TPU v7x, 128 devices: a whole 4x4x4 slice. The times are simulated.
128 devices in a mesh: ty: 8 (over y, core), tx: 16 (over z, x).
Axes of the slice: x: 4, y: 4, z: 4, core: 2. Of those that a mesh axis runs over, the one named last changes fastest.
Arguments:
- section_a: bfloat16 [4096, 8192], P('ty', 'tx'), may hold values from -6 to 6
- section_b: bfloat16 [4096, 8192], P('ty', 'tx'), may hold values from -6 to 6
- template_corner: int32 [2, 8, 128], P(None, 'ty', 'tx'), may hold values from 0 to 384
- template_slot: int32 [8, 128], P('ty', 'tx'), may hold values from 0 to 31, as said below
- window_corner: int32 [2, 8, 128], P(None, 'ty', 'tx'), may hold values from 0 to 384
- window_slot: int32 [8, 128], P('ty', 'tx'), may hold values from 0 to 31, as said below
- node_mask: int32 [256, 512], P('ty', 'tx'), may hold values 0 or 1
Outputs:
- owner_flow: float32 [2, 8, 128], P(None, 'ty', 'tx')
- source_flow: float32 [2, 8, 128], P(None, 'ty', 'tx')
- displacement: float32 [2, 256, 512], P(None, 'ty', 'tx')
Inputs may be any that keep to these rules, and one draw needn't show every extreme that they name: `template_slot`: entry j of a row belongs to owner device j // 8 of that ty row; its value is s * 2 + k for the k-th pair that source device s sends to it; the values of one device's list are distinct; each owner gets exactly 2 pairs from each of 4 sources. `window_slot`: entry m of a row belongs to source device m // 8 of that ty row; its value is o * 2 + k for the k-th pair that it sends to owner device o; the values of one device's list are distinct; together with template_slot every pair of a row appears once on each side.
All inputs are finite; a program needn't handle non-finite values. No bound on the sum of `node_mask` on one device may be relied on, other than what follows from the above.
Results may differ from a plain program's by a relative error of at most 0.0003.
Values may be sent and summed in bfloat16 or wider, within the bound.
No kernel may reach another device: no remote copies, remote signals or barrier semaphores. Data moves between devices by JAX's collectives and lax.ppermute only.
A program may use at most 64 MiB of HBM per device.

v0:
```python
import jax
import jax.numpy as jnp
from jax import lax
from jax.sharding import PartitionSpec as P

PATCH = 128
SHIFTS = 65
RADIUS = 32
WIN = 192
CAP = 2
ITERS_R = 3


SHARPNESS = 256.0
SPRING_RATE = 0.25
FLOW_RATE = 0.5
FLOW_UNIT = 8.0
EPSILON = 1e-05


def padded_2(cells, sides, width):
    for axis, dim in sides:
        count = lax.axis_size(axis)
        ends = count - 1
        head = lax.slice_in_dim(cells, 0, width, axis=dim)
        tail = lax.slice_in_dim(cells, cells.shape[dim] - width, cells.shape[dim], axis=dim)
        cells = jnp.concatenate(
            [
                lax.ppermute(tail, axis, [(i, (i + 1) % count) for i in range(ends)]),
                cells,
                lax.ppermute(head, axis, [((i + 1) % count, i) for i in range(ends)]),
            ],
            axis=dim,
        )
    return cells


def shift_tables():
    rows_out = jnp.arange(SHIFTS * PATCH, dtype=jnp.int32)
    wanted = rows_out // PATCH + rows_out % PATCH
    row_shift = (wanted[:, None] == jnp.arange(WIN, dtype=jnp.int32)[None, :]).astype(jnp.bfloat16)
    cols_out = jnp.arange(SHIFTS * WIN, dtype=jnp.int32)
    source_col = cols_out % WIN - cols_out // WIN
    col_shift = (jnp.arange(PATCH, dtype=jnp.int32)[:, None] == source_col[None, :]).astype(
        jnp.bfloat16
    )
    return (row_shift, col_shift)


def make_block_flow(row_shift, col_shift):

    def block_flow(pair):
        template, window = pair
        moved_rows = jnp.dot(row_shift, window, preferred_element_type=jnp.float32).astype(
            jnp.bfloat16
        )
        moved_rows = moved_rows.reshape(SHIFTS, PATCH, WIN)
        placed = jnp.dot(template, col_shift, preferred_element_type=jnp.float32).astype(
            jnp.bfloat16
        )
        placed = placed.reshape(PATCH, SHIFTS, WIN)
        corr = jnp.einsum("dia,ixa->dx", moved_rows, placed, preferred_element_type=jnp.float32)
        temp_f = template.astype(jnp.float32)
        wind_f = window.astype(jnp.float32)
        energy_t = jnp.mean(temp_f * temp_f)
        energy_w = jnp.mean(wind_f * wind_f)
        scores = (
            SHARPNESS
            * corr
            / (PATCH * PATCH * jnp.sqrt((energy_t + EPSILON) * (energy_w + EPSILON)))
        )
        weights = jnp.exp(scores - jnp.max(scores))
        weights = weights / jnp.sum(weights)
        shift_vals = (jnp.arange(SHIFTS) - RADIUS).astype(jnp.float32)
        flow_y = jnp.sum(weights * shift_vals[:, None]) / FLOW_UNIT
        flow_x = jnp.sum(weights * shift_vals[None, :]) / FLOW_UNIT
        return jnp.stack([flow_y, flow_x])

    return block_flow


def relax_sweep(padded, mask_pad, target, count):
    centre = padded[:, 1:-1, 1:-1]
    mask_c = mask_pad[1:-1, 1:-1]
    height = centre.shape[1]
    width = centre.shape[2]
    spring = jnp.zeros_like(centre)
    for row_step, col_step in ((0, 1), (2, 1), (1, 0), (1, 2)):
        nearby = padded[:, row_step : row_step + height, col_step : col_step + width]
        mask_n = mask_pad[row_step : row_step + height, col_step : col_step + width]
        spring = spring + mask_c * mask_n * (nearby - centre)
    return centre + SPRING_RATE * spring + FLOW_RATE * (target - count * centre)


def cut_blocks(image, tops, lefts, extent):
    return jax.vmap(
        lambda top_row, left_col: lax.dynamic_slice(image, (top_row, left_col), (extent, extent))
    )(tops, lefts)


def select_rows(picker, values):
    flat = values.reshape(values.shape[0], -1)
    chosen = jnp.dot(picker, flat, preferred_element_type=jnp.float32).astype(jnp.bfloat16)
    return chosen.reshape((picker.shape[0],) + values.shape[1:])


def shards(
    section_a, section_b, template_corner, template_slot, window_corner, window_slot, node_mask
):
    tile_size = section_a.shape[0]
    slot_count = lax.axis_size("tx") * CAP
    slot_ids = jnp.arange(slot_count, dtype=jnp.int32)
    owner_picker = template_slot[0][:, None] == slot_ids[None, :]
    source_picker = window_slot[0][:, None] == slot_ids[None, :]
    row_shift, col_shift = shift_tables()
    block_flow = make_block_flow(row_shift, col_shift)
    b_wide = padded_2(section_b, (("ty", 0), ("tx", 1)), RADIUS)
    templates = cut_blocks(section_a, template_corner[0, 0], template_corner[1, 0], PATCH)
    windows = cut_blocks(b_wide, window_corner[0, 0], window_corner[1, 0], WIN)
    highest = lax.Precision.HIGHEST
    outgoing = select_rows(source_picker.T.astype(jnp.bfloat16), windows)
    arrived = lax.all_to_all(outgoing, "tx", split_axis=0, concat_axis=0, tiled=True)
    matched = select_rows(owner_picker.astype(jnp.bfloat16), arrived)
    flows = lax.map(block_flow, (templates, matched)).T
    returned = jnp.dot(flows, owner_picker.astype(jnp.float32), precision=highest)
    landed = lax.all_to_all(returned, "tx", split_axis=1, concat_axis=1, tiled=True)
    source_flow = -jnp.dot(landed, source_picker.T.astype(jnp.float32), precision=highest)
    node_rows, node_cols = node_mask.shape
    centre_y = (window_corner[0, 0] + PATCH // 2) * node_rows // tile_size
    centre_x = (window_corner[1, 0] + PATCH // 2) * node_cols // tile_size
    node_ids = centre_y * node_cols + centre_x
    node_picker = (
        node_ids[:, None] == jnp.arange(node_rows * node_cols, dtype=jnp.int32)[None, :]
    ).astype(jnp.float32)
    target = jnp.dot(source_flow, node_picker, precision=highest).reshape(2, node_rows, node_cols)
    count = jnp.sum(node_picker, axis=0).reshape(node_rows, node_cols)
    mask = node_mask.astype(jnp.float32)
    mask_wide = padded_2(mask, (("ty", 0), ("tx", 1)), 1)
    displace = jnp.zeros((2, node_rows, node_cols), jnp.float32)
    for sweep in range(ITERS_R):
        padded = padded_2(displace, (("ty", 1), ("tx", 2)), 1)
        displace = relax_sweep(padded, mask_wide, target, count)
    return (flows[:, None, :], source_flow[:, None, :], displace)


def solution(mesh):
    placed = (
        P("ty", "tx"),
        P("ty", "tx"),
        P(None, "ty", "tx"),
        P("ty", "tx"),
        P(None, "ty", "tx"),
        P("ty", "tx"),
        P("ty", "tx"),
    )
    return jax.shard_map(
        shards,
        mesh=mesh,
        in_specs=placed,
        out_specs=(P(None, "ty", "tx"), P(None, "ty", "tx"), P(None, "ty", "tx")),
        check_vma=False,
    )
```

profile of v0, /device:TPU:48, one launch (start us, length us, event | category | flops | bytes accessed | tf_op | source)
XLA Modules:
  0.0 367.0 jit_solution(18386269829610975597)
XLA Ops:
  2.6 3.6 collective-permute-start.7
  8.9 3.6 collective-permute-start.1
  20.6 4.2 %collective-permute-start.3 = (bf16[576,32]{1,0:T(8,128)(2,1)S(1)}, bf16[576,32]{1,0:T(8,128)(2,1)S(1)}, u32[]{:S(2)}, u32[]{:S(2)}) collective-permute-start(bf16[576,32]{1,0:T(8,128)(2,1)S(1)} %get-tuple-element.163), channel_id=1, source_target_pairs={{1,0},{2,1},{3,2},{4,3},{5,4},{6,5},{7,6},{8,7},{9,8},{10,9},{11,1... | collective-permute-start | bytes 110600 | tf_op jit(solution)/shard_map/ppermute | solution.py:31
  30.6 4.1 %collective-permute-done.2 = bf16[576,32]{1,0:T(8,128)(2,1)S(1)} collective-permute-done((bf16[576,32]{1,0:T(8,128)(2,1)S(1)}, bf16[576,32]{1,0:T(8,128)(2,1)S(1)}, u32[]{:S(2)}, u32[]{:S(2)}) %collective-permute-start.2) | collective-permute-done | bytes 36896 | tf_op jit(solution)/shard_map/ppermute | solution.py:29
  35.2 17.1 %while.15 = (s32[]{:T(128)}, bf16[576,576]{1,0:T(8,128)(2,1)S(1)}, s32[8,2]{0,1:T(2,128)S(1)}, bf16[8,192,192]{2,1,0:T(8,128)(2,1)S(1)}, s32[]{:T(128)}) while((s32[]{:T(128)}, bf16[576,576]{1,0:T(8,128)(2,1)S(1)}, s32[8,2]{0,1:T(2,128)S(1)}, bf16[8,192,192]{2,1,0:T(8,128)(2,1)S(1)}, s32[]{:T(128)}) %tuple.85), condition=%wide.while_cond, body=%wide.while_body.sunk | while | flops 2 | bytes 196725 | solution.py:97
  54.1 4.6 %reshape.256 = bf16[32,192,192]{2,1,0:T(8,128)(2,1)} reshape(bf16[32,36864]{1,0:T(8,128)(2,1)S(1)} %convolution_convert_fusion.2) | data formatting | bytes 4718592 | tf_op jit(solution)/shard_map/reshape | solution.py:104
  58.6 5.7 %all-to-all-start = ((bf16[32,192,192]{2,1,0:T(8,128)(2,1)}), bf16[32,192,192]{2,1,0:T(8,128)(2,1)S(1)}, u32[]{:S(2)}, u32[]{:S(2)}) async-start(bf16[32,192,192]{2,1,0:T(8,128)(2,1)} %reshape.256), calls=%async_computation | async-start | bytes 6291456 | tf_op jit(solution)/shard_map/all_to_all | solution.py:122
  64.4 27.7 %while.16 = (s32[]{:T(128)}, bf16[512,512]{1,0:T(8,128)(2,1)}, s32[8,2]{0,1:T(2,128)S(1)}, bf16[8,128,128]{2,1,0:T(8,128)(2,1)}, s32[]{:T(128)}) while((s32[]{:T(128)}, bf16[512,512]{1,0:T(8,128)(2,1)}, s32[8,2]{0,1:T(2,128)S(1)}, bf16[8,128,128]{2,1,0:T(8,128)(2,1)}, s32[]{:T(128)}) %tuple.88), condition=%wide.while_cond.1, body=%wide.while_body.1.sunk | while | flops 2 | bytes 66669 | solution.py:97
  96.3 4.5 %collective-permute-start.10 = (f32[34,1]{1,0:T(8,128)}, f32[34,1]{1,0:T(8,128)}, u32[]{:S(2)}, u32[]{:S(2)}) collective-permute-start(f32[34,1]{1,0:T(8,128)} %get-tuple-element.177), channel_id=1, source_target_pairs={{1,0},{2,1},{3,2},{4,3},{5,4},{6,5},{7,6},{8,7},{9,8},{10,9},{11,1... | collective-permute-start | bytes 416 | tf_op jit(solution)/shard_map/ppermute | solution.py:31
  107.4 5.8 %all-to-all-done = bf16[32,192,192]{2,1,0:T(8,128)(2,1)S(1)} async-done(((bf16[32,192,192]{2,1,0:T(8,128)(2,1)}), bf16[32,192,192]{2,1,0:T(8,128)(2,1)S(1)}, u32[]{:S(2)}, u32[]{:S(2)}) %all-to-all-start) | async-done | bytes 2359328 | tf_op jit(solution)/shard_map/all_to_all | solution.py:122
  113.2 4.2 %reshape.257 = bf16[32,36864]{1,0:T(8,128)(2,1)} reshape(bf16[32,192,192]{2,1,0:T(8,128)(2,1)S(1)} %all-to-all-done) | data formatting | bytes 4718592 | tf_op jit(solution)/shard_map/reshape | solution.py:102
  121.4 191.9 %while.17 = (s32[]{:T(128)}, f32[8,2]{1,0:T(8,128)}, bf16[8,192,192]{2,1,0:T(8,128)(2,1)}, bf16[8,128,128]{2,1,0:T(8,128)(2,1)}, s32[8320]{0:T(1024)}, /*index=5...) while((s32[]{:T(128)}, f32[8,2]{1,0:T(8,128)}, ...), condition=%wide.region_7.8_spmd.clone, body=%wide.region_0.7_spmd.clone.sunk | while | flops 1239819776 | bytes 19549576 | solution.py:124
  130.0 4.3 %reshape.302 = bf16[65,128,192]{1,0,2:T(8,128)(2,1)S(1)} reshape(bf16[8320,192]{0,1:T(8,128)(2,1)} %fusion.130) | data formatting | bytes 6389760 | tf_op jit(solution)/shard_map/while/body/eval_jaxpr/reshape | solution.py:57
  150.4 3.6 fusion.130
  154.0 4.3 %reshape.302 = bf16[65,128,192]{1,0,2:T(8,128)(2,1)S(1)} reshape(bf16[8320,192]{0,1:T(8,128)(2,1)} %fusion.130) | data formatting | bytes 6389760 | tf_op jit(solution)/shard_map/while/body/eval_jaxpr/reshape | solution.py:57
  174.4 3.6 fusion.130
  178.0 4.3 %reshape.302 = bf16[65,128,192]{1,0,2:T(8,128)(2,1)S(1)} reshape(bf16[8320,192]{0,1:T(8,128)(2,1)} %fusion.130) | data formatting | bytes 6389760 | tf_op jit(solution)/shard_map/while/body/eval_jaxpr/reshape | solution.py:57
  198.4 3.6 fusion.130
  202.0 4.3 %reshape.302 = bf16[65,128,192]{1,0,2:T(8,128)(2,1)S(1)} reshape(bf16[8320,192]{0,1:T(8,128)(2,1)} %fusion.130) | data formatting | bytes 6389760 | tf_op jit(solution)/shard_map/while/body/eval_jaxpr/reshape | solution.py:57
  222.3 3.6 fusion.130
  225.9 4.3 %reshape.302 = bf16[65,128,192]{1,0,2:T(8,128)(2,1)S(1)} reshape(bf16[8320,192]{0,1:T(8,128)(2,1)} %fusion.130) | data formatting | bytes 6389760 | tf_op jit(solution)/shard_map/while/body/eval_jaxpr/reshape | solution.py:57
  246.3 3.6 fusion.130
  249.9 4.3 %reshape.302 = bf16[65,128,192]{1,0,2:T(8,128)(2,1)S(1)} reshape(bf16[8320,192]{0,1:T(8,128)(2,1)} %fusion.130) | data formatting | bytes 6389760 | tf_op jit(solution)/shard_map/while/body/eval_jaxpr/reshape | solution.py:57
  270.3 3.6 fusion.130
  273.9 4.3 %reshape.302 = bf16[65,128,192]{1,0,2:T(8,128)(2,1)S(1)} reshape(bf16[8320,192]{0,1:T(8,128)(2,1)} %fusion.130) | data formatting | bytes 6389760 | tf_op jit(solution)/shard_map/while/body/eval_jaxpr/reshape | solution.py:57
  294.3 3.6 fusion.130
  297.9 4.3 %reshape.302 = bf16[65,128,192]{1,0,2:T(8,128)(2,1)S(1)} reshape(bf16[8320,192]{0,1:T(8,128)(2,1)} %fusion.130) | data formatting | bytes 6389760 | tf_op jit(solution)/shard_map/while/body/eval_jaxpr/reshape | solution.py:57
  314.9 6.4 %all-to-all-start.1 = ((f32[2,16,2]{2,0,1:T(2,128)}), f32[2,16,2]{2,0,1:T(2,128)S(1)}, u32[]{:S(2)}, u32[]{:S(2)}) async-start(f32[2,16,2]{2,0,1:T(2,128)} %copy.26), calls=%async_computation.1 | async-start | bytes 32768 | tf_op jit(solution)/shard_map/all_to_all | solution.py:126
  322.3 5.2 %all-to-all-done.1 = f32[2,16,2]{2,0,1:T(2,128)S(1)} async-done(((f32[2,16,2]{2,0,1:T(2,128)}), f32[2,16,2]{2,0,1:T(2,128)S(1)}, u32[]{:S(2)}, u32[]{:S(2)}) %all-to-all-start.1) | async-done | bytes 288 | tf_op jit(solution)/shard_map/all_to_all | solution.py:126
  337.3 4.0 %collective-permute-start.15 = (f32[2,34,1]{2,1,0:T(8,128)S(1)}, f32[2,34,1]{2,1,0:T(8,128)S(1)}, u32[]{:S(2)}, u32[]{:S(2)}) collective-permute-start(f32[2,34,1]{2,1,0:T(8,128)S(1)} %get-tuple-element.169), channel_id=1, source_target_pairs={{1,0},{2,1},{3,2},{4,3},{5,4},{6,5},{7,6},{8,7},{9,8},{10,9},{11,1... | collective-permute-start | bytes 824 | tf_op jit(solution)/shard_map/ppermute | solution.py:31
  343.2 6.1 %collective-permute-done.14 = f32[2,34,1]{2,1,0:T(8,128)S(1)} collective-permute-done((f32[2,34,1]{2,1,0:T(8,128)S(1)}, f32[2,34,1]{2,1,0:T(8,128)S(1)}, u32[]{:S(2)}, u32[]{:S(2)}) %collective-permute-start.14) | collective-permute-done | bytes 304 | tf_op jit(solution)/shard_map/ppermute | solution.py:29
  358.2 3.9 %collective-permute-start.18 = (f32[2,34,1]{2,1,0:T(8,128)S(1)}, f32[2,34,1]{2,1,0:T(8,128)S(1)}, u32[]{:S(2)}, u32[]{:S(2)}) collective-permute-start(f32[2,34,1]{2,1,0:T(8,128)S(1)} %get-tuple-element.166), channel_id=1, source_target_pairs={{0,1},{1,2},{2,3},{3,4},{4,5},{5,6},{6,7},{7,8},{8,9},{9,10},{10,1... | collective-permute-start | bytes 824 | tf_op jit(solution)/shard_map/ppermute | solution.py:29
  (239 shorter events, 219.1 us)
Async XLA Ops:
  0.6 52.5 %copy-start.8 = (s32[1,8]{1,0:T(1,128)S(1)}, s32[1,8]{1,0:T(1,128)}, u32[]{:S(2)}) copy-start(s32[1,8]{1,0:T(1,128)} %param.14) | copy-start | bytes 100
  0.7 100.1 %collective-permute-start.5 = (f32[2,1,32]{2,1,0:T(1,128)S(1)}, f32[2,1,32]{2,1,0:T(1,128)S(1)}, u32[]{:S(2)}, u32[]{:S(2)}) collective-permute-start(f32[2,1,32]{2,1,0:T(1,128)S(1)} %broadcast.300), channel_id=1, source_target_pairs={{0,16},{16,32},{32,48},{48,64},{64,80},{80,96},{96,112},{1,17},{17... | collective-permute-start | bytes 776 | tf_op jit(solution)/shard_map/ppermute | solution.py:29
  2.6 98.2 %collective-permute-start.7 = (f32[2,1,32]{2,1,0:T(1,128)S(1)}, f32[2,1,32]{2,1,0:T(1,128)S(1)}, u32[]{:S(2)}, u32[]{:S(2)}) collective-permute-start(f32[2,1,32]{2,1,0:T(1,128)S(1)} %broadcast.300), channel_id=1, source_target_pairs={{16,0},{32,16},{48,32},{64,48},{80,64},{96,80},{112,96},{17,1},{33... | collective-permute-start | bytes 776 | tf_op jit(solution)/shard_map/ppermute | solution.py:31
  7.0 12.3 %collective-permute-start = (bf16[32,512]{1,0:T(8,128)(2,1)S(1)}, bf16[32,512]{1,0:T(8,128)(2,1)S(1)}, u32[]{:S(2)}, u32[]{:S(2)}) collective-permute-start(bf16[32,512]{1,0:T(8,128)(2,1)S(1)} %get-tuple-element.165), channel_id=1, source_target_pairs={{0,16},{16,32},{32,48},{48,64},{64,80},{80,96},{96,112},{1,17},{17... | collective-permute-start | bytes 98312 | tf_op jit(solution)/shard_map/ppermute | solution.py:29
  8.9 11.5 %collective-permute-start.1 = (bf16[32,512]{1,0:T(8,128)(2,1)S(1)}, bf16[32,512]{1,0:T(8,128)(2,1)S(1)}, u32[]{:S(2)}, u32[]{:S(2)}) collective-permute-start(bf16[32,512]{1,0:T(8,128)(2,1)S(1)} %get-tuple-element.164), channel_id=1, source_target_pairs={{16,0},{32,16},{48,32},{64,48},{80,64},{96,80},{112,96},{17,1},{33... | collective-permute-start | bytes 98312 | tf_op jit(solution)/shard_map/ppermute | solution.py:31
  13.3 78.8 %copy-start.1 = (f32[32,32]{1,0:T(8,128)}, f32[32,32]{1,0:T(8,128)S(1)}, u32[]{:S(2)}) copy-start(f32[32,32]{1,0:T(8,128)S(1)} %convert_element_type.72) | copy-start | bytes 12292
  13.3 78.8 %collective-permute-start.6 = (f32[1,32]{1,0:T(1,128)S(1)}, f32[1,32]{1,0:T(1,128)S(1)}, u32[]{:S(2)}, u32[]{:S(2)}) collective-permute-start(f32[1,32]{1,0:T(1,128)S(1)} %get-tuple-element.183), channel_id=1, source_target_pairs={{16,0},{32,16},{48,32},{64,48},{80,64},{96,80},{112,96},{17,1},{33... | collective-permute-start | bytes 392 | tf_op jit(solution)/shard_map/ppermute | solution.py:31
  20.6 8.1 %collective-permute-start.3 = (bf16[576,32]{1,0:T(8,128)(2,1)S(1)}, bf16[576,32]{1,0:T(8,128)(2,1)S(1)}, u32[]{:S(2)}, u32[]{:S(2)}) collective-permute-start(bf16[576,32]{1,0:T(8,128)(2,1)S(1)} %get-tuple-element.163), channel_id=1, source_target_pairs={{1,0},{2,1},{3,2},{4,3},{5,4},{6,5},{7,6},{8,7},{9,8},{10,9},{11,1... | collective-permute-start | bytes 110600 | tf_op jit(solution)/shard_map/ppermute | solution.py:31
  24.8 10.0 %collective-permute-start.2 = (bf16[576,32]{1,0:T(8,128)(2,1)S(1)}, bf16[576,32]{1,0:T(8,128)(2,1)S(1)}, u32[]{:S(2)}, u32[]{:S(2)}) collective-permute-start(bf16[576,32]{1,0:T(8,128)(2,1)S(1)} %get-tuple-element.162), channel_id=1, source_target_pairs={{0,1},{1,2},{2,3},{3,4},{4,5},{5,6},{6,7},{7,8},{8,9},{9,10},{10,1... | collective-permute-start | bytes 110600 | tf_op jit(solution)/shard_map/ppermute | solution.py:29
  28.7 63.4 %collective-permute-start.4 = (f32[1,32]{1,0:T(1,128)S(1)}, f32[1,32]{1,0:T(1,128)S(1)}, u32[]{:S(2)}, u32[]{:S(2)}) collective-permute-start(f32[1,32]{1,0:T(1,128)S(1)} %get-tuple-element.182), channel_id=1, source_target_pairs={{0,16},{16,32},{32,48},{48,64},{64,80},{80,96},{96,112},{1,17},{17... | collective-permute-start | bytes 392 | tf_op jit(solution)/shard_map/ppermute | solution.py:29
  58.6 54.6 %all-to-all-start = ((bf16[32,192,192]{2,1,0:T(8,128)(2,1)}), bf16[32,192,192]{2,1,0:T(8,128)(2,1)S(1)}, u32[]{:S(2)}, u32[]{:S(2)}) async-start(bf16[32,192,192]{2,1,0:T(8,128)(2,1)} %reshape.256), calls=%async_computation | async-start | bytes 6291456 | tf_op jit(solution)/shard_map/all_to_all | solution.py:122
  64.3 53.1 %copy-start.7 = (s32[1,8]{1,0:T(1,128)S(1)}, s32[1,8]{1,0:T(1,128)}, u32[]{:S(2)}) copy-start(s32[1,8]{1,0:T(1,128)} %param.12) | copy-start | bytes 100
  92.1 27.5 %copy-start.5 = (f32[1,32]{1,0:T(1,128)}, f32[1,32]{1,0:T(1,128)S(1)}, u32[]{:S(2)}) copy-start(f32[1,32]{1,0:T(1,128)S(1)} %collective-permute-done.6) | copy-start | bytes 388
  92.1 27.5 %copy-start.6 = (f32[1,32]{1,0:T(1,128)}, f32[1,32]{1,0:T(1,128)S(1)}, u32[]{:S(2)}) copy-start(f32[1,32]{1,0:T(1,128)S(1)} %collective-permute-done.4) | copy-start | bytes 388
  92.8 228.4 %collective-permute-start.8 = (f32[34,1]{1,0:T(8,128)}, f32[34,1]{1,0:T(8,128)}, u32[]{:S(2)}, u32[]{:S(2)}) collective-permute-start(f32[34,1]{1,0:T(8,128)} %get-tuple-element.176), channel_id=1, source_target_pairs={{0,1},{1,2},{2,3},{3,4},{4,5},{5,6},{6,7},{7,8},{8,9},{9,10},{10,1... | collective-permute-start | bytes 416 | tf_op jit(solution)/shard_map/ppermute | solution.py:29
  96.3 225.0 %collective-permute-start.10 = (f32[34,1]{1,0:T(8,128)}, f32[34,1]{1,0:T(8,128)}, u32[]{:S(2)}, u32[]{:S(2)}) collective-permute-start(f32[34,1]{1,0:T(8,128)} %get-tuple-element.177), channel_id=1, source_target_pairs={{1,0},{2,1},{3,2},{4,3},{5,4},{6,5},{7,6},{8,7},{9,8},{10,9},{11,1... | collective-permute-start | bytes 416 | tf_op jit(solution)/shard_map/ppermute | solution.py:31
  100.8 18.8 %copy-start.3 = (f32[2,1,32]{2,1,0:T(1,128)}, f32[2,1,32]{2,1,0:T(1,128)S(1)}, u32[]{:S(2)}) copy-start(f32[2,1,32]{2,1,0:T(1,128)S(1)} %collective-permute-done.5) | copy-start | bytes 772
  100.8 18.8 %copy-start.4 = (f32[2,1,32]{2,1,0:T(1,128)}, f32[2,1,32]{2,1,0:T(1,128)S(1)}, u32[]{:S(2)}) copy-start(f32[2,1,32]{2,1,0:T(1,128)S(1)} %collective-permute-done.7) | copy-start | bytes 772
  101.6 227.8 %collective-permute-start.11 = (f32[2,34,1]{2,1,0:T(8,128)}, f32[2,34,1]{2,1,0:T(8,128)}, u32[]{:S(2)}, u32[]{:S(2)}) collective-permute-start(f32[2,34,1]{2,1,0:T(8,128)} %get-tuple-element.171), channel_id=1, source_target_pairs={{1,0},{2,1},{3,2},{4,3},{5,4},{6,5},{7,6},{8,7},{9,8},{10,9},{11,1... | collective-permute-start | bytes 824 | tf_op jit(solution)/shard_map/ppermute | solution.py:31
  104.2 225.2 %collective-permute-start.9 = (f32[2,34,1]{2,1,0:T(8,128)}, f32[2,34,1]{2,1,0:T(8,128)}, u32[]{:S(2)}, u32[]{:S(2)}) collective-permute-start(f32[2,34,1]{2,1,0:T(8,128)} %get-tuple-element.170), channel_id=1, source_target_pairs={{0,1},{1,2},{2,3},{3,4},{4,5},{5,6},{6,7},{7,8},{8,9},{9,10},{10,1... | collective-permute-start | bytes 824 | tf_op jit(solution)/shard_map/ppermute | solution.py:29
  160.6 4.2 %copy-start.2 = (f32[65]{0:T(128)S(1)}, f32[65]{0:T(128)}, u32[]{:S(2)}) copy-start(f32[65]{0:T(128)} %add_convert_fusion.2) | copy-start | bytes 784 | tf_op jit(solution)/shard_map/while
  280.5 4.2 %copy-start.2 = (f32[65]{0:T(128)S(1)}, f32[65]{0:T(128)}, u32[]{:S(2)}) copy-start(f32[65]{0:T(128)} %add_convert_fusion.2) | copy-start | bytes 784 | tf_op jit(solution)/shard_map/while
  314.9 12.6 %all-to-all-start.1 = ((f32[2,16,2]{2,0,1:T(2,128)}), f32[2,16,2]{2,0,1:T(2,128)S(1)}, u32[]{:S(2)}, u32[]{:S(2)}) async-start(f32[2,16,2]{2,0,1:T(2,128)} %copy.26), calls=%async_computation.1 | async-start | bytes 32768 | tf_op jit(solution)/shard_map/all_to_all | solution.py:126
  328.4 38.5 %copy-start.10 = (f32[2,8]{1,0:T(2,128)}, f32[2,8]{1,0:T(2,128)S(1)}, u32[]{:S(2)}) copy-start(f32[2,8]{1,0:T(2,128)S(1)} %convolution_negate_fusion) | copy-start | bytes 196
  330.4 4.3 %collective-permute-start.13 = (f32[2,1,32]{2,1,0:T(1,128)S(1)}, f32[2,1,32]{2,1,0:T(1,128)S(1)}, u32[]{:S(2)}, u32[]{:S(2)}) collective-permute-start(f32[2,1,32]{2,1,0:T(1,128)S(1)} %get-tuple-element.175), channel_id=1, source_target_pairs={{16,0},{32,16},{48,32},{64,48},{80,64},{96,80},{112,96},{17,1},{33... | collective-permute-start | bytes 776 | tf_op jit(solution)/shard_map/ppermute | solution.py:31
  332.3 4.9 %collective-permute-start.12 = (f32[2,1,32]{2,1,0:T(1,128)S(1)}, f32[2,1,32]{2,1,0:T(1,128)S(1)}, u32[]{:S(2)}, u32[]{:S(2)}) collective-permute-start(f32[2,1,32]{2,1,0:T(1,128)S(1)} %get-tuple-element.174), channel_id=1, source_target_pairs={{0,16},{16,32},{32,48},{48,64},{64,80},{80,96},{96,112},{1,17},{17... | collective-permute-start | bytes 776 | tf_op jit(solution)/shard_map/ppermute | solution.py:29
  337.3 5.9 %collective-permute-start.15 = (f32[2,34,1]{2,1,0:T(8,128)S(1)}, f32[2,34,1]{2,1,0:T(8,128)S(1)}, u32[]{:S(2)}, u32[]{:S(2)}) collective-permute-start(f32[2,34,1]{2,1,0:T(8,128)S(1)} %get-tuple-element.169), channel_id=1, source_target_pairs={{1,0},{2,1},{3,2},{4,3},{5,4},{6,5},{7,6},{8,7},{9,8},{10,9},{11,1... | collective-permute-start | bytes 824 | tf_op jit(solution)/shard_map/ppermute | solution.py:31
  341.3 8.0 %collective-permute-start.14 = (f32[2,34,1]{2,1,0:T(8,128)S(1)}, f32[2,34,1]{2,1,0:T(8,128)S(1)}, u32[]{:S(2)}, u32[]{:S(2)}) collective-permute-start(f32[2,34,1]{2,1,0:T(8,128)S(1)} %get-tuple-element.168), channel_id=1, source_target_pairs={{0,1},{1,2},{2,3},{3,4},{4,5},{5,6},{6,7},{7,8},{8,9},{9,10},{10,1... | collective-permute-start | bytes 824 | tf_op jit(solution)/shard_map/ppermute | solution.py:29
  349.4 4.3 %collective-permute-start.17 = (f32[2,1,32]{2,1,0:T(1,128)S(1)}, f32[2,1,32]{2,1,0:T(1,128)S(1)}, u32[]{:S(2)}, u32[]{:S(2)}) collective-permute-start(f32[2,1,32]{2,1,0:T(1,128)S(1)} %get-tuple-element.173), channel_id=1, source_target_pairs={{16,0},{32,16},{48,32},{64,48},{80,64},{96,80},{112,96},{17,1},{33... | collective-permute-start | bytes 776 | tf_op jit(solution)/shard_map/ppermute | solution.py:31
  351.3 4.9 %collective-permute-start.16 = (f32[2,1,32]{2,1,0:T(1,128)S(1)}, f32[2,1,32]{2,1,0:T(1,128)S(1)}, u32[]{:S(2)}, u32[]{:S(2)}) collective-permute-start(f32[2,1,32]{2,1,0:T(1,128)S(1)} %get-tuple-element.172), channel_id=1, source_target_pairs={{0,16},{16,32},{32,48},{48,64},{64,80},{80,96},{96,112},{1,17},{17... | collective-permute-start | bytes 776 | tf_op jit(solution)/shard_map/ppermute | solution.py:29
  356.3 7.2 %collective-permute-start.19 = (f32[2,34,1]{2,1,0:T(8,128)S(1)}, f32[2,34,1]{2,1,0:T(8,128)S(1)}, u32[]{:S(2)}, u32[]{:S(2)}) collective-permute-start(f32[2,34,1]{2,1,0:T(8,128)S(1)} %get-tuple-element.167), channel_id=1, source_target_pairs={{1,0},{2,1},{3,2},{4,3},{5,4},{6,5},{7,6},{8,7},{9,8},{10,9},{11,1... | collective-permute-start | bytes 824 | tf_op jit(solution)/shard_map/ppermute | solution.py:31
  358.2 8.0 %collective-permute-start.18 = (f32[2,34,1]{2,1,0:T(8,128)S(1)}, f32[2,34,1]{2,1,0:T(8,128)S(1)}, u32[]{:S(2)}, u32[]{:S(2)}) collective-permute-start(f32[2,34,1]{2,1,0:T(8,128)S(1)} %get-tuple-element.166), channel_id=1, source_target_pairs={{0,1},{1,2},{2,3},{3,4},{4,5},{5,6},{6,7},{7,8},{8,9},{9,10},{10,1... | collective-permute-start | bytes 824 | tf_op jit(solution)/shard_map/ppermute | solution.py:29
  (8 other events, 31.2 us)
where the time goes:
time: 372 us; the launch traced here: 367 us
  local copies, waits for them, and re-layouts  106 us (28%)
  matrix products  76.9 us (21%)
  starting transfers between devices  67.4 us (18%)
  other arithmetic  62.9 us (17%)
  waiting for transfers between devices  30.9 us (8%)
  loops' own time  21.6 us (6%)
    gather x48, local copies, waits for them, and re-layouts  44.7 us
    reshape x8, local copies, waits for them, and re-layouts, block_flow(): moved_rows = moved_rows.reshape(SHIFTS, PATCH, WIN)  34 us
    ppermute x10, starting transfers between devices, padded_2(): lax.ppermute(head, axis, [((i + 1) % count, i) for i in range(ends)])  30.2 us
    dot_general x8, matrix products, block_flow(): jnp.dot(row_shift, window, preferred_element_type=jnp.float32)  28.8 us
    ppermute x10, starting transfers between devices, padded_2(): lax.ppermute(tail, axis, [(i, (i + 1) % count) for i in range(ends)])  25 us
    dot_general x8, matrix products, block_flow(): jnp.einsum('dia,ixa->dx', moved_rows, placed, preferred_element_type=jnp....  23.8 us
    another operation x1, loops' own time, shards(): flows = lax.map(block_flow, (templates, matched)).T  21.4 us
    dot_general x8, matrix products, block_flow(): jnp.dot(template, col_shift, preferred_element_type=jnp.float32)  18.8 us
  transfers between devices with their start and end apart: 22, of which 8 were waited for; matrix products, arithmetic and copies ran while one was open for 66% of the time, Pallas kernels for 0%

commit v1 on v0

--- a/solution.py
+++ b/solution.py
@@ -2,6 +2,8 @@
 import jax.numpy as jnp
 from jax import lax
 from jax.sharding import PartitionSpec as P
+from jax.experimental import pallas as pl
+from jax.experimental.pallas import tpu as pltpu
 
 PATCH = 128
 SHIFTS = 65
@@ -16,6 +18,64 @@
 FLOW_RATE = 0.5
 FLOW_UNIT = 8.0
 EPSILON = 1e-05
+
+from jax.experimental import pallas as pl
+from jax.experimental.pallas import tpu as pltpu
+
+
+def flow_kernel(tf_ref, w_ref, out_ref, wpad, tpad, corr):
+    wpad[...] = jnp.zeros(wpad.shape, jnp.float32)
+    wf = w_ref[0].astype(jnp.float32)
+    wpad[0:WIN, 0:WIN] = wf
+    tfv = tf_ref[0].astype(jnp.float32)
+    tpad[...] = jnp.zeros(tpad.shape, jnp.float32)
+    tpad[:, 0:PATCH] = tfv
+    wb = wpad[...].astype(jnp.bfloat16)
+    tp = tpad[...]
+    corr[...] = jnp.zeros(corr.shape, jnp.float32)
+
+    def step(dy, carry):
+        lhs = pltpu.roll(tp, dy, axis=1).astype(jnp.bfloat16)
+        m = jnp.dot(lhs, wb, preferred_element_type=jnp.float32)
+        r = pltpu.roll(m, 0, axis=1, stride=1, stride_axis=0)
+        corr[pl.ds(dy, 1), :] = jnp.sum(r, axis=0, keepdims=True)
+        return carry
+    lax.fori_loop(0, SHIFTS, step, 0, unroll=5)
+
+    c = corr[...]
+    rows = lax.broadcasted_iota(jnp.int32, c.shape, 0)
+    lanes = lax.broadcasted_iota(jnp.int32, c.shape, 1)
+    valid = (rows < SHIFTS) & (lanes >= PATCH - 1) & (lanes < PATCH - 1 + SHIFTS)
+    e_t = jnp.sum(tfv * tfv, keepdims=True) / float(PATCH * PATCH)
+    e_w = jnp.sum(wf * wf, keepdims=True) / float(WIN * WIN)
+    denom = float(PATCH * PATCH) * jnp.sqrt((e_t + EPSILON) * (e_w + EPSILON))
+    scores = SHARPNESS * c / denom
+    scores = jnp.where(valid, scores, -jnp.inf)
+    mx = jnp.max(scores, keepdims=True)
+    e = jnp.where(valid, jnp.exp(scores - mx), 0.0)
+    w = e / jnp.sum(e, keepdims=True)
+    sy = (rows - RADIUS).astype(jnp.float32)
+    sx = (lanes - (PATCH - 1) - RADIUS).astype(jnp.float32)
+    fy = jnp.sum(w * sy, keepdims=True) / FLOW_UNIT
+    fx = jnp.sum(w * sx, keepdims=True) / FLOW_UNIT
+    orow = lax.broadcasted_iota(jnp.int32, (8, 128), 0)
+    out_ref[0] = jnp.where(orow == 0, fy, jnp.where(orow == 1, fx, 0.0))
+
+def flows_of(templates, windows):
+    n = templates.shape[0]
+    tf = jnp.flip(templates, axis=2).transpose(0, 2, 1)
+    out = pl.pallas_call(
+        flow_kernel,
+        grid=(n,),
+        in_specs=[pl.BlockSpec((1, PATCH, PATCH), lambda i: (i, 0, 0)),
+                  pl.BlockSpec((1, WIN, WIN), lambda i: (i, 0, 0))],
+        out_specs=pl.BlockSpec((1, 8, 128), lambda i: (i, 0, 0)),
+        out_shape=jax.ShapeDtypeStruct((n, 8, 128), jnp.float32),
+        scratch_shapes=[pltpu.VMEM((256, 256), jnp.float32),
+                        pltpu.VMEM((PATCH, 256), jnp.float32),
+                        pltpu.VMEM((72, 256), jnp.float32)],
+    )(tf, windows)
+    return out[:, 0:2, 0].T
 
 
 def padded_2(cells, sides, width):
@@ -121,7 +181,7 @@
     outgoing = select_rows(source_picker.T.astype(jnp.bfloat16), windows)
     arrived = lax.all_to_all(outgoing, "tx", split_axis=0, concat_axis=0, tiled=True)
     matched = select_rows(owner_picker.astype(jnp.bfloat16), arrived)
-    flows = lax.map(block_flow, (templates, matched)).T
+    flows = flows_of(templates, matched)
     returned = jnp.dot(flows, owner_picker.astype(jnp.float32), precision=highest)
     landed = lax.all_to_all(returned, "tx", split_axis=1, concat_axis=1, tiled=True)
     source_flow = -jnp.dot(landed, source_picker.T.astype(jnp.float32), precision=highest)

time: 372 us -> 225 us (0.60)
  the two profiles are of different devices: /device:TPU:48 before, /device:TPU:7 now
where the time goes in v1:
time: 225 us; the launch traced here: 223 us
  starting transfers between devices  72.9 us (32%)
  local copies, waits for them, and re-layouts  57.5 us (26%)
  Pallas kernels  55.9 us (25%)
  waiting for transfers between devices  28.3 us (13%)
  other arithmetic  3.66 us (2%)
  matrix products  3.61 us (2%)
    pallas_call x1, Pallas kernels, flows_of(): pl.pallas_call(flow_kernel, grid=(n,), in_specs=[pl.BlockSpec((1, PATCH,...  55.9 us
    gather x64, local copies, waits for them, and re-layouts  39.4 us
    ppermute x10, starting transfers between devices, padded_2(): lax.ppermute(tail, axis, [(i, (i + 1) % count) for i in range(ends)])  37.8 us
    ppermute x10, starting transfers between devices, padded_2(): lax.ppermute(head, axis, [((i + 1) % count, i) for i in range(ends)])  21.9 us
    ppermute x10, waiting for transfers between devices, padded_2(): lax.ppermute(head, axis, [((i + 1) % count, i) for i in range(ends)])  18.5 us
    all_to_all x1, starting transfers between devices, shards(): lax.all_to_all(outgoing, 'tx', split_axis=0, concat_axis=0, tiled=True)  7.12 us
    reshape x2, local copies, waits for them, and re-layouts, select_rows(): return chosen.reshape((picker.shape[0],) + values.shape[1:])  6.37 us
    all_to_all x1, starting transfers between devices, shards(): lax.all_to_all(returned, 'tx', split_axis=1, concat_axis=1, tiled=True)  6.16 us
  transfers between devices with their start and end apart: 22, of which 9 were waited for; matrix products, arithmetic and copies ran while one was open for 28% of the time, Pallas kernels for 25%

profile of v1, /device:TPU:7, one launch (start us, length us, event | category | flops | bytes accessed | tf_op | source)
XLA Modules:
  0.0 223.2 jit_solution(11809833359167679224)
XLA Ops:
  0.6 3.8 %collective-permute-start.5 = (f32[2,1,32]{2,1,0:T(1,128)S(1)}, f32[2,1,32]{2,1,0:T(1,128)S(1)}, u32[]{:S(2)}, u32[]{:S(2)}) collective-permute-start(f32[2,1,32]{2,1,0:T(1,128)S(1)} %broadcast.209), channel_id=1, source_target_pairs={{0,16},{16,32},{32,48},{48,64},{64,80},{80,96},{96,112},{1,17},{17... | collective-permute-start | bytes 776 | tf_op jit(solution)/shard_map/ppermute | solution.py:89
  7.1 3.6 %collective-permute-start.4 = (f32[1,32]{1,0:T(1,128)S(1)}, f32[1,32]{1,0:T(1,128)S(1)}, u32[]{:S(2)}, u32[]{:S(2)}) collective-permute-start(f32[1,32]{1,0:T(1,128)S(1)} %get-tuple-element.71), channel_id=1, source_target_pairs={{0,16},{16,32},{32,48},{48,64},{64,80},{80,96},{96,112},{1,17},{17... | collective-permute-start | bytes 392 | tf_op jit(solution)/shard_map/ppermute | solution.py:89
  13.4 2.4 %collective-permute-start.1 = (bf16[32,512]{1,0:T(8,128)(2,1)S(1)}, bf16[32,512]{1,0:T(8,128)(2,1)S(1)}, u32[]{:S(2)}, u32[]{:S(2)}) collective-permute-start(bf16[32,512]{1,0:T(8,128)(2,1)S(1)} %get-tuple-element.53), channel_id=1, source_target_pairs={{16,0},{32,16},{48,32},{64,48},{80,64},{96,80},{112,96},{17,1},{33... | collective-permute-start | bytes 98312 | tf_op jit(solution)/shard_map/ppermute | solution.py:91
  18.8 3.5 %collective-permute-start.2 = (bf16[576,32]{1,0:T(8,128)(2,1)S(1)}, bf16[576,32]{1,0:T(8,128)(2,1)S(1)}, u32[]{:S(2)}, u32[]{:S(2)}) collective-permute-start(bf16[576,32]{1,0:T(8,128)(2,1)S(1)} %get-tuple-element.51), channel_id=1, source_target_pairs={{0,1},{1,2},{2,3},{3,4},{4,5},{5,6},{6,7},{7,8},{8,9},{9,10},{10,1... | collective-permute-start | bytes 110600 | tf_op jit(solution)/shard_map/ppermute | solution.py:89
  27.9 3.8 %collective-permute-done.3 = bf16[576,32]{1,0:T(8,128)(2,1)S(1)} collective-permute-done((bf16[576,32]{1,0:T(8,128)(2,1)S(1)}, bf16[576,32]{1,0:T(8,128)(2,1)S(1)}, u32[]{:S(2)}, u32[]{:S(2)}) %collective-permute-start.3) | collective-permute-done | bytes 36896 | tf_op jit(solution)/shard_map/ppermute | solution.py:91
  32.1 15.7 %while.3 = (s32[]{:T(128)}, bf16[576,576]{1,0:T(8,128)(2,1)S(1)}, s32[8,2]{0,1:T(2,128)S(1)}, bf16[8,192,192]{2,1,0:T(8,128)(2,1)S(1)}, s32[]{:T(128)}) while((s32[]{:T(128)}, bf16[576,576]{1,0:T(8,128)(2,1)S(1)}, s32[8,2]{0,1:T(2,128)S(1)}, bf16[8,192,192]{2,1,0:T(8,128)(2,1)S(1)}, s32[]{:T(128)}) %tuple.58), condition=%wide.while_cond.1, body=%wide.while_body.1.sunk | while | flops 2 | bytes 196717 | solution.py:157
  49.5 4.6 %reshape.213 = bf16[32,192,192]{2,1,0:T(8,128)(2,1)} reshape(bf16[32,36864]{1,0:T(8,128)(2,1)S(1)} %convolution_convert_fusion) | data formatting | bytes 4718592 | tf_op jit(solution)/shard_map/reshape | solution.py:164
  54.0 7.1 %all-to-all-start = ((bf16[32,192,192]{2,1,0:T(8,128)(2,1)}), bf16[32,192,192]{2,1,0:T(8,128)(2,1)S(1)}, u32[]{:S(2)}, u32[]{:S(2)}) async-start(bf16[32,192,192]{2,1,0:T(8,128)(2,1)} %reshape.213), calls=%async_computation | async-start | bytes 6291456 | tf_op jit(solution)/shard_map/all_to_all | solution.py:182
  61.2 24.2 %while.2 = (s32[]{:T(128)}, bf16[512,512]{1,0:T(8,128)(2,1)}, s32[8,2]{0,1:T(2,128)S(1)}, bf16[8,128,128]{1,2,0:T(8,128)(2,1)S(1)}, s32[]{:T(128)}) while((s32[]{:T(128)}, bf16[512,512]{1,0:T(8,128)(2,1)}, s32[8,2]{0,1:T(2,128)S(1)}, bf16[8,128,128]{1,2,0:T(8,128)(2,1)S(1)}, s32[]{:T(128)}) %tuple.55), condition=%wide.while_cond, body=%wide.while_body.sunk | while | flops 2 | bytes 196717 | solution.py:157
  61.8 2.3 %dynamic-slice_bitcast_fusion.2 = bf16[1,128,128]{2,1,0:T(8,128)(2,1)S(1)} fusion(bf16[512,512]{1,0:T(8,128)(2,1)} %get-tuple-element.146, s32[]{:T(128)} %bitcast.62, s32[]{:T(128)} %bitcast.63), kind=kLoop, calls=%fused_computation.clone.1 | loop fusion | bytes 65544 | tf_op jit(solution)/shard_map/vmap()/gather
  64.8 2.3 %dynamic-slice_bitcast_fusion.2 = bf16[1,128,128]{2,1,0:T(8,128)(2,1)S(1)} fusion(bf16[512,512]{1,0:T(8,128)(2,1)} %get-tuple-element.146, s32[]{:T(128)} %bitcast.62, s32[]{:T(128)} %bitcast.63), kind=kLoop, calls=%fused_computation.clone.1 | loop fusion | bytes 65544 | tf_op jit(solution)/shard_map/vmap()/gather
  67.8 2.3 %dynamic-slice_bitcast_fusion.2 = bf16[1,128,128]{2,1,0:T(8,128)(2,1)S(1)} fusion(bf16[512,512]{1,0:T(8,128)(2,1)} %get-tuple-element.146, s32[]{:T(128)} %bitcast.62, s32[]{:T(128)} %bitcast.63), kind=kLoop, calls=%fused_computation.clone.1 | loop fusion | bytes 65544 | tf_op jit(solution)/shard_map/vmap()/gather
  70.8 2.3 %dynamic-slice_bitcast_fusion.2 = bf16[1,128,128]{2,1,0:T(8,128)(2,1)S(1)} fusion(bf16[512,512]{1,0:T(8,128)(2,1)} %get-tuple-element.146, s32[]{:T(128)} %bitcast.62, s32[]{:T(128)} %bitcast.63), kind=kLoop, calls=%fused_computation.clone.1 | loop fusion | bytes 65544 | tf_op jit(solution)/shard_map/vmap()/gather
  73.8 2.3 %dynamic-slice_bitcast_fusion.2 = bf16[1,128,128]{2,1,0:T(8,128)(2,1)S(1)} fusion(bf16[512,512]{1,0:T(8,128)(2,1)} %get-tuple-element.146, s32[]{:T(128)} %bitcast.62, s32[]{:T(128)} %bitcast.63), kind=kLoop, calls=%fused_computation.clone.1 | loop fusion | bytes 65544 | tf_op jit(solution)/shard_map/vmap()/gather
  79.9 2.3 %dynamic-slice_bitcast_fusion.2 = bf16[1,128,128]{2,1,0:T(8,128)(2,1)S(1)} fusion(bf16[512,512]{1,0:T(8,128)(2,1)} %get-tuple-element.146, s32[]{:T(128)} %bitcast.62, s32[]{:T(128)} %bitcast.63), kind=kLoop, calls=%fused_computation.clone.1 | loop fusion | bytes 65544 | tf_op jit(solution)/shard_map/vmap()/gather
  85.5 2.6 %rev.4 = bf16[8,128,128]{1,2,0:T(8,128)(2,1)} reverse(bf16[8,128,128]{1,2,0:T(8,128)(2,1)S(1)} %get-tuple-element.10), dimensions={2} | reverse | bytes 524288 | tf_op jit(solution)/shard_map/jit(_flip)/rev | solution.py:66
  88.2 2.5 %collective-permute-start.10 = (f32[34,1]{1,0:T(8,128)S(1)}, f32[34,1]{1,0:T(8,128)S(1)}, u32[]{:S(2)}, u32[]{:S(2)}) collective-permute-start(f32[34,1]{1,0:T(8,128)S(1)} %get-tuple-element.66), channel_id=1, source_target_pairs={{1,0},{2,1},{3,2},{4,3},{5,4},{6,5},{7,6},{8,7},{9,8},{10,9},{11,1... | collective-permute-start | bytes 416 | tf_op jit(solution)/shard_map/ppermute | solution.py:91
  90.6 4.9 %collective-permute-start.8 = (f32[34,1]{1,0:T(8,128)S(1)}, f32[34,1]{1,0:T(8,128)S(1)}, u32[]{:S(2)}, u32[]{:S(2)}) collective-permute-start(f32[34,1]{1,0:T(8,128)S(1)} %get-tuple-element.65), channel_id=1, source_target_pairs={{0,1},{1,2},{2,3},{3,4},{4,5},{5,6},{6,7},{7,8},{8,9},{9,10},{10,1... | collective-permute-start | bytes 416 | tf_op jit(solution)/shard_map/ppermute | solution.py:89
  97.6 5.5 %collective-permute-start.9 = (f32[2,34,1]{2,1,0:T(8,128)S(1)}, f32[2,34,1]{2,1,0:T(8,128)S(1)}, u32[]{:S(2)}, u32[]{:S(2)}) collective-permute-start(f32[2,34,1]{2,1,0:T(8,128)S(1)} %get-tuple-element.59), channel_id=1, source_target_pairs={{0,1},{1,2},{2,3},{3,4},{4,5},{5,6},{6,7},{7,8},{8,9},{9,10},{10,1... | collective-permute-start | bytes 824 | tf_op jit(solution)/shard_map/ppermute | solution.py:89
  103.1 3.5 %all-to-all-done = bf16[32,192,192]{2,1,0:T(8,128)(2,1)S(1)} async-done(((bf16[32,192,192]{2,1,0:T(8,128)(2,1)}), bf16[32,192,192]{2,1,0:T(8,128)(2,1)S(1)}, u32[]{:S(2)}, u32[]{:S(2)}) %all-to-all-start) | async-done | bytes 2359328 | tf_op jit(solution)/shard_map/all_to_all | solution.py:182
  106.6 4.2 %reshape.214 = bf16[32,36864]{1,0:T(8,128)(2,1)} reshape(bf16[32,192,192]{2,1,0:T(8,128)(2,1)S(1)} %all-to-all-done) | data formatting | bytes 4718592 | tf_op jit(solution)/shard_map/reshape | solution.py:162
  114.8 55.9 %shard_map.94 = f32[8,8,128]{2,1,0:T(8,128)} custom-call(bf16[8,128,128]{2,1,0:T(8,128)(2,1)} %bitcast.67, bf16[8,192,192]{2,1,0:T(8,128)(2,1)} %reshape.215.w_ref), custom_call_target="tpu_custom_call" | custom-call | tf_op jit(solution)/shard_map/pallas_call | solution.py:67
  172.5 6.2 %all-to-all-start.1 = ((f32[2,16,2]{0,2,1:T(2,128)}), f32[2,16,2]{0,2,1:T(2,128)S(1)}, u32[]{:S(2)}, u32[]{:S(2)}) async-start(f32[2,16,2]{0,2,1:T(2,128)} %copy.28), calls=%async_computation.1 | async-start | bytes 32768 | tf_op jit(solution)/shard_map/all_to_all | solution.py:186
  178.8 4.7 %all-to-all-done.1 = f32[2,16,2]{0,2,1:T(2,128)S(1)} async-done(((f32[2,16,2]{0,2,1:T(2,128)}), f32[2,16,2]{0,2,1:T(2,128)S(1)}, u32[]{:S(2)}, u32[]{:S(2)}) %all-to-all-start.1) | async-done | bytes 288 | tf_op jit(solution)/shard_map/all_to_all | solution.py:186
  184.0 5.6 %collective-permute-start.12 = (f32[2,1,32]{2,1,0:T(1,128)S(1)}, f32[2,1,32]{2,1,0:T(1,128)S(1)}, u32[]{:S(2)}, u32[]{:S(2)}) collective-permute-start(f32[2,1,32]{2,1,0:T(1,128)S(1)} %get-tuple-element.63), channel_id=1, source_target_pairs={{0,16},{16,32},{32,48},{48,64},{64,80},{80,96},{96,112},{1,17},{17... | collective-permute-start | bytes 776 | tf_op jit(solution)/shard_map/ppermute | solution.py:89
  191.6 3.0 %collective-permute-done.13 = f32[2,1,32]{2,1,0:T(1,128)S(1)} collective-permute-done((f32[2,1,32]{2,1,0:T(1,128)S(1)}, f32[2,1,32]{2,1,0:T(1,128)S(1)}, u32[]{:S(2)}, u32[]{:S(2)}) %collective-permute-start.13) | collective-permute-done | bytes 288 | tf_op jit(solution)/shard_map/ppermute | solution.py:91
  194.7 3.7 %collective-permute-start.14 = (f32[2,34,1]{2,1,0:T(8,128)S(1)}, f32[2,34,1]{2,1,0:T(8,128)S(1)}, u32[]{:S(2)}, u32[]{:S(2)}) collective-permute-start(f32[2,34,1]{2,1,0:T(8,128)S(1)} %get-tuple-element.57), channel_id=1, source_target_pairs={{0,1},{1,2},{2,3},{3,4},{4,5},{5,6},{6,7},{7,8},{8,9},{9,10},{10,1... | collective-permute-start | bytes 824 | tf_op jit(solution)/shard_map/ppermute | solution.py:89
  200.3 4.9 %collective-permute-done.15 = f32[2,34,1]{2,1,0:T(8,128)S(1)} collective-permute-done((f32[2,34,1]{2,1,0:T(8,128)S(1)}, f32[2,34,1]{2,1,0:T(8,128)S(1)}, u32[]{:S(2)}, u32[]{:S(2)}) %collective-permute-start.15) | collective-permute-done | bytes 304 | tf_op jit(solution)/shard_map/ppermute | solution.py:91
  205.3 3.4 %collective-permute-start.16 = (f32[2,1,32]{2,1,0:T(1,128)S(1)}, f32[2,1,32]{2,1,0:T(1,128)S(1)}, u32[]{:S(2)}, u32[]{:S(2)}) collective-permute-start(f32[2,1,32]{2,1,0:T(1,128)S(1)} %get-tuple-element.61), channel_id=1, source_target_pairs={{0,16},{16,32},{32,48},{48,64},{64,80},{80,96},{96,112},{1,17},{17... | collective-permute-start | bytes 776 | tf_op jit(solution)/shard_map/ppermute | solution.py:89
  210.7 3.0 %collective-permute-done.17 = f32[2,1,32]{2,1,0:T(1,128)S(1)} collective-permute-done((f32[2,1,32]{2,1,0:T(1,128)S(1)}, f32[2,1,32]{2,1,0:T(1,128)S(1)}, u32[]{:S(2)}, u32[]{:S(2)}) %collective-permute-start.17) | collective-permute-done | bytes 288 | tf_op jit(solution)/shard_map/ppermute | solution.py:91
  215.6 3.4 %collective-permute-start.19 = (f32[2,34,1]{2,1,0:T(8,128)S(1)}, f32[2,34,1]{2,1,0:T(8,128)S(1)}, u32[]{:S(2)}, u32[]{:S(2)}) collective-permute-start(f32[2,34,1]{2,1,0:T(8,128)S(1)} %get-tuple-element.56), channel_id=1, source_target_pairs={{1,0},{2,1},{3,2},{4,3},{5,4},{6,5},{7,6},{8,7},{9,8},{10,9},{11,1... | collective-permute-start | bytes 824 | tf_op jit(solution)/shard_map/ppermute | solution.py:91
  219.0 3.5 %collective-permute-done.19 = f32[2,34,1]{2,1,0:T(8,128)S(1)} collective-permute-done((f32[2,34,1]{2,1,0:T(8,128)S(1)}, f32[2,34,1]{2,1,0:T(8,128)S(1)}, u32[]{:S(2)}, u32[]{:S(2)}) %collective-permute-start.19) | collective-permute-done | bytes 304 | tf_op jit(solution)/shard_map/ppermute | solution.py:91
  (138 shorter events, 59.1 us)
Async XLA Ops:
  0.6 94.9 %collective-permute-start.5 = (f32[2,1,32]{2,1,0:T(1,128)S(1)}, f32[2,1,32]{2,1,0:T(1,128)S(1)}, u32[]{:S(2)}, u32[]{:S(2)}) collective-permute-start(f32[2,1,32]{2,1,0:T(1,128)S(1)} %broadcast.209), channel_id=1, source_target_pairs={{0,16},{16,32},{32,48},{48,64},{64,80},{80,96},{96,112},{1,17},{17... | collective-permute-start | bytes 776 | tf_op jit(solution)/shard_map/ppermute | solution.py:89
  4.4 91.2 %collective-permute-start.7 = (f32[2,1,32]{2,1,0:T(1,128)S(1)}, f32[2,1,32]{2,1,0:T(1,128)S(1)}, u32[]{:S(2)}, u32[]{:S(2)}) collective-permute-start(f32[2,1,32]{2,1,0:T(1,128)S(1)} %broadcast.209), channel_id=1, source_target_pairs={{16,0},{32,16},{48,32},{64,48},{80,64},{96,80},{112,96},{17,1},{33... | collective-permute-start | bytes 776 | tf_op jit(solution)/shard_map/ppermute | solution.py:91
  7.1 81.0 %collective-permute-start.4 = (f32[1,32]{1,0:T(1,128)S(1)}, f32[1,32]{1,0:T(1,128)S(1)}, u32[]{:S(2)}, u32[]{:S(2)}) collective-permute-start(f32[1,32]{1,0:T(1,128)S(1)} %get-tuple-element.71), channel_id=1, source_target_pairs={{0,16},{16,32},{32,48},{48,64},{64,80},{80,96},{96,112},{1,17},{17... | collective-permute-start | bytes 392 | tf_op jit(solution)/shard_map/ppermute | solution.py:89
  11.5 5.7 %collective-permute-start = (bf16[32,512]{1,0:T(8,128)(2,1)S(1)}, bf16[32,512]{1,0:T(8,128)(2,1)S(1)}, u32[]{:S(2)}, u32[]{:S(2)}) collective-permute-start(bf16[32,512]{1,0:T(8,128)(2,1)S(1)} %get-tuple-element.54), channel_id=1, source_target_pairs={{0,16},{16,32},{32,48},{48,64},{64,80},{80,96},{96,112},{1,17},{17... | collective-permute-start | bytes 98312 | tf_op jit(solution)/shard_map/ppermute | solution.py:89
  13.4 5.2 %collective-permute-start.1 = (bf16[32,512]{1,0:T(8,128)(2,1)S(1)}, bf16[32,512]{1,0:T(8,128)(2,1)S(1)}, u32[]{:S(2)}, u32[]{:S(2)}) collective-permute-start(bf16[32,512]{1,0:T(8,128)(2,1)S(1)} %get-tuple-element.53), channel_id=1, source_target_pairs={{16,0},{32,16},{48,32},{64,48},{80,64},{96,80},{112,96},{17,1},{33... | collective-permute-start | bytes 98312 | tf_op jit(solution)/shard_map/ppermute | solution.py:91
  18.6 30.0 %copy-start.3 = (s32[1,8]{1,0:T(1,128)S(1)}, s32[1,8]{1,0:T(1,128)}, u32[]{:S(2)}) copy-start(s32[1,8]{1,0:T(1,128)} %param.12) | copy-start | bytes 100
  18.8 7.0 %collective-permute-start.2 = (bf16[576,32]{1,0:T(8,128)(2,1)S(1)}, bf16[576,32]{1,0:T(8,128)(2,1)S(1)}, u32[]{:S(2)}, u32[]{:S(2)}) collective-permute-start(bf16[576,32]{1,0:T(8,128)(2,1)S(1)} %get-tuple-element.51), channel_id=1, source_target_pairs={{0,1},{1,2},{2,3},{3,4},{4,5},{5,6},{6,7},{7,8},{8,9},{9,10},{10,1... | collective-permute-start | bytes 110600 | tf_op jit(solution)/shard_map/ppermute | solution.py:89
  22.2 9.5 %collective-permute-start.3 = (bf16[576,32]{1,0:T(8,128)(2,1)S(1)}, bf16[576,32]{1,0:T(8,128)(2,1)S(1)}, u32[]{:S(2)}, u32[]{:S(2)}) collective-permute-start(bf16[576,32]{1,0:T(8,128)(2,1)S(1)} %get-tuple-element.52), channel_id=1, source_target_pairs={{1,0},{2,1},{3,2},{4,3},{5,4},{6,5},{7,6},{8,7},{9,8},{10,9},{11,1... | collective-permute-start | bytes 110600 | tf_op jit(solution)/shard_map/ppermute | solution.py:91
  25.7 62.3 %collective-permute-start.6 = (f32[1,32]{1,0:T(1,128)S(1)}, f32[1,32]{1,0:T(1,128)S(1)}, u32[]{:S(2)}, u32[]{:S(2)}) collective-permute-start(f32[1,32]{1,0:T(1,128)S(1)} %get-tuple-element.72), channel_id=1, source_target_pairs={{16,0},{32,16},{48,32},{64,48},{80,64},{96,80},{112,96},{17,1},{33... | collective-permute-start | bytes 392 | tf_op jit(solution)/shard_map/ppermute | solution.py:91
  54.0 31.3 %copy-start.1 = (s32[2,1,8]{2,1,0:T(1,128)S(1)}, s32[2,1,8]{2,1,0:T(1,128)}, u32[]{:S(2)}) copy-start(s32[2,1,8]{2,1,0:T(1,128)} %param.11) | copy-start | bytes 196
  54.0 52.6 %all-to-all-start = ((bf16[32,192,192]{2,1,0:T(8,128)(2,1)}), bf16[32,192,192]{2,1,0:T(8,128)(2,1)S(1)}, u32[]{:S(2)}, u32[]{:S(2)}) async-start(bf16[32,192,192]{2,1,0:T(8,128)(2,1)} %reshape.213), calls=%async_computation | async-start | bytes 6291456 | tf_op jit(solution)/shard_map/all_to_all | solution.py:182
  88.2 90.5 %collective-permute-start.10 = (f32[34,1]{1,0:T(8,128)S(1)}, f32[34,1]{1,0:T(8,128)S(1)}, u32[]{:S(2)}, u32[]{:S(2)}) collective-permute-start(f32[34,1]{1,0:T(8,128)S(1)} %get-tuple-element.66), channel_id=1, source_target_pairs={{1,0},{2,1},{3,2},{4,3},{5,4},{6,5},{7,6},{8,7},{9,8},{10,9},{11,1... | collective-permute-start | bytes 416 | tf_op jit(solution)/shard_map/ppermute | solution.py:91
  90.6 88.0 %collective-permute-start.8 = (f32[34,1]{1,0:T(8,128)S(1)}, f32[34,1]{1,0:T(8,128)S(1)}, u32[]{:S(2)}, u32[]{:S(2)}) collective-permute-start(f32[34,1]{1,0:T(8,128)S(1)} %get-tuple-element.65), channel_id=1, source_target_pairs={{0,1},{1,2},{2,3},{3,4},{4,5},{5,6},{6,7},{7,8},{8,9},{9,10},{10,1... | collective-permute-start | bytes 416 | tf_op jit(solution)/shard_map/ppermute | solution.py:89
  95.7 88.2 %collective-permute-start.11 = (f32[2,34,1]{2,1,0:T(8,128)S(1)}, f32[2,34,1]{2,1,0:T(8,128)S(1)}, u32[]{:S(2)}, u32[]{:S(2)}) collective-permute-start(f32[2,34,1]{2,1,0:T(8,128)S(1)} %get-tuple-element.60), channel_id=1, source_target_pairs={{1,0},{2,1},{3,2},{4,3},{5,4},{6,5},{7,6},{8,7},{9,8},{10,9},{11,1... | collective-permute-start | bytes 824 | tf_op jit(solution)/shard_map/ppermute | solution.py:91
  97.6 13.2 %copy-start.2 = (s32[1,8]{1,0:T(1,128)S(1)}, s32[1,8]{1,0:T(1,128)}, u32[]{:S(2)}) copy-start(s32[1,8]{1,0:T(1,128)} %param.10) | copy-start | bytes 100
  97.6 86.3 %collective-permute-start.9 = (f32[2,34,1]{2,1,0:T(8,128)S(1)}, f32[2,34,1]{2,1,0:T(8,128)S(1)}, u32[]{:S(2)}, u32[]{:S(2)}) collective-permute-start(f32[2,34,1]{2,1,0:T(8,128)S(1)} %get-tuple-element.59), channel_id=1, source_target_pairs={{0,1},{1,2},{2,3},{3,4},{4,5},{5,6},{6,7},{7,8},{8,9},{9,10},{10,1... | collective-permute-start | bytes 824 | tf_op jit(solution)/shard_map/ppermute | solution.py:89
  171.6 51.6 %copy-start = (f32[8,2,1]{0,1,2:T(2,128)}, f32[8,2,1]{0,1,2:T(2,128)S(1)}, u32[]{:S(2)}) copy-start(f32[8,2,1]{0,1,2:T(2,128)S(1)} %copy.27) | copy-start | bytes 196
  172.5 10.9 %all-to-all-start.1 = ((f32[2,16,2]{0,2,1:T(2,128)}), f32[2,16,2]{0,2,1:T(2,128)S(1)}, u32[]{:S(2)}, u32[]{:S(2)}) async-start(f32[2,16,2]{0,2,1:T(2,128)} %copy.28), calls=%async_computation.1 | async-start | bytes 32768 | tf_op jit(solution)/shard_map/all_to_all | solution.py:186
  183.6 39.6 %copy-start.4 = (f32[2,8]{1,0:T(2,128)}, f32[2,8]{1,0:T(2,128)S(1)}, u32[]{:S(2)}) copy-start(f32[2,8]{1,0:T(2,128)S(1)} %convolution_negate_fusion) | copy-start | bytes 196
  184.0 7.6 %collective-permute-start.12 = (f32[2,1,32]{2,1,0:T(1,128)S(1)}, f32[2,1,32]{2,1,0:T(1,128)S(1)}, u32[]{:S(2)}, u32[]{:S(2)}) collective-permute-start(f32[2,1,32]{2,1,0:T(1,128)S(1)} %get-tuple-element.63), channel_id=1, source_target_pairs={{0,16},{16,32},{32,48},{48,64},{64,80},{80,96},{96,112},{1,17},{17... | collective-permute-start | bytes 776 | tf_op jit(solution)/shard_map/ppermute | solution.py:89
  189.7 4.9 %collective-permute-start.13 = (f32[2,1,32]{2,1,0:T(1,128)S(1)}, f32[2,1,32]{2,1,0:T(1,128)S(1)}, u32[]{:S(2)}, u32[]{:S(2)}) collective-permute-start(f32[2,1,32]{2,1,0:T(1,128)S(1)} %get-tuple-element.64), channel_id=1, source_target_pairs={{16,0},{32,16},{48,32},{64,48},{80,64},{96,80},{112,96},{17,1},{33... | collective-permute-start | bytes 776 | tf_op jit(solution)/shard_map/ppermute | solution.py:91
  194.7 5.6 %collective-permute-start.14 = (f32[2,34,1]{2,1,0:T(8,128)S(1)}, f32[2,34,1]{2,1,0:T(8,128)S(1)}, u32[]{:S(2)}, u32[]{:S(2)}) collective-permute-start(f32[2,34,1]{2,1,0:T(8,128)S(1)} %get-tuple-element.57), channel_id=1, source_target_pairs={{0,1},{1,2},{2,3},{3,4},{4,5},{5,6},{6,7},{7,8},{8,9},{9,10},{10,1... | collective-permute-start | bytes 824 | tf_op jit(solution)/shard_map/ppermute | solution.py:89
  198.4 6.9 %collective-permute-start.15 = (f32[2,34,1]{2,1,0:T(8,128)S(1)}, f32[2,34,1]{2,1,0:T(8,128)S(1)}, u32[]{:S(2)}, u32[]{:S(2)}) collective-permute-start(f32[2,34,1]{2,1,0:T(8,128)S(1)} %get-tuple-element.58), channel_id=1, source_target_pairs={{1,0},{2,1},{3,2},{4,3},{5,4},{6,5},{7,6},{8,7},{9,8},{10,9},{11,1... | collective-permute-start | bytes 824 | tf_op jit(solution)/shard_map/ppermute | solution.py:91
  205.3 5.3 %collective-permute-start.16 = (f32[2,1,32]{2,1,0:T(1,128)S(1)}, f32[2,1,32]{2,1,0:T(1,128)S(1)}, u32[]{:S(2)}, u32[]{:S(2)}) collective-permute-start(f32[2,1,32]{2,1,0:T(1,128)S(1)} %get-tuple-element.61), channel_id=1, source_target_pairs={{0,16},{16,32},{32,48},{48,64},{64,80},{80,96},{96,112},{1,17},{17... | collective-permute-start | bytes 776 | tf_op jit(solution)/shard_map/ppermute | solution.py:89
  208.7 4.9 %collective-permute-start.17 = (f32[2,1,32]{2,1,0:T(1,128)S(1)}, f32[2,1,32]{2,1,0:T(1,128)S(1)}, u32[]{:S(2)}, u32[]{:S(2)}) collective-permute-start(f32[2,1,32]{2,1,0:T(1,128)S(1)} %get-tuple-element.62), channel_id=1, source_target_pairs={{16,0},{32,16},{48,32},{64,48},{80,64},{96,80},{112,96},{17,1},{33... | collective-permute-start | bytes 776 | tf_op jit(solution)/shard_map/ppermute | solution.py:91
  213.7 5.3 %collective-permute-start.18 = (f32[2,34,1]{2,1,0:T(8,128)S(1)}, f32[2,34,1]{2,1,0:T(8,128)S(1)}, u32[]{:S(2)}, u32[]{:S(2)}) collective-permute-start(f32[2,34,1]{2,1,0:T(8,128)S(1)} %get-tuple-element.55), channel_id=1, source_target_pairs={{0,1},{1,2},{2,3},{3,4},{4,5},{5,6},{6,7},{7,8},{8,9},{9,10},{10,1... | collective-permute-start | bytes 824 | tf_op jit(solution)/shard_map/ppermute | solution.py:89
  215.6 6.9 %collective-permute-start.19 = (f32[2,34,1]{2,1,0:T(8,128)S(1)}, f32[2,34,1]{2,1,0:T(8,128)S(1)}, u32[]{:S(2)}, u32[]{:S(2)}) collective-permute-start(f32[2,34,1]{2,1,0:T(8,128)S(1)} %get-tuple-element.56), channel_id=1, source_target_pairs={{1,0},{2,1},{3,2},{4,3},{5,4},{6,5},{7,6},{8,7},{9,8},{10,9},{11,1... | collective-permute-start | bytes 824 | tf_op jit(solution)/shard_map/ppermute | solution.py:91

commit v2 on v1

v2 whole, which is shorter than its diff:
```python
import jax
import jax.numpy as jnp
from jax import lax
from jax.sharding import PartitionSpec as P
from jax.experimental import pallas as pl
from jax.experimental.pallas import tpu as pltpu

PATCH = 128
SHIFTS = 65
RADIUS = 32
WIN = 192
CAP = 2
ITERS_R = 3


SHARPNESS = 256.0
SPRING_RATE = 0.25
FLOW_RATE = 0.5
FLOW_UNIT = 8.0
EPSILON = 1e-05

LANES = 256


def flow_kernel(tf_ref, w_ref, out_ref, wpad, tpad, corr):
    wpad[...] = jnp.zeros(wpad.shape, jnp.float32)
    wf = w_ref[0].astype(jnp.float32)
    wpad[0:WIN, 0:WIN] = wf
    tfv = tf_ref[0].astype(jnp.float32)
    tpad[...] = jnp.zeros(tpad.shape, jnp.float32)
    tpad[:, 0:PATCH] = tfv
    wb = wpad[...].astype(jnp.bfloat16)
    tp = tpad[...]
    corr[...] = jnp.zeros(corr.shape, jnp.float32)

    def step(dy, carry):
        lhs = pltpu.roll(tp, dy, axis=1).astype(jnp.bfloat16)
        m = jnp.dot(lhs, wb, preferred_element_type=jnp.float32)
        r = pltpu.roll(m, 0, axis=1, stride=1, stride_axis=0)
        corr[pl.ds(dy, 1), :] = jnp.sum(r, axis=0, keepdims=True)
        return carry

    lax.fori_loop(0, SHIFTS, step, 0, unroll=5)

    c = corr[...]
    rows = lax.broadcasted_iota(jnp.int32, c.shape, 0)
    lanes = lax.broadcasted_iota(jnp.int32, c.shape, 1)
    valid = (rows < SHIFTS) & (lanes >= PATCH - 1) & (lanes < PATCH - 1 + SHIFTS)
    e_t = jnp.sum(tfv * tfv, keepdims=True) / float(PATCH * PATCH)
    e_w = jnp.sum(wf * wf, keepdims=True) / float(WIN * WIN)
    denom = float(PATCH * PATCH) * jnp.sqrt((e_t + EPSILON) * (e_w + EPSILON))
    scores = SHARPNESS * c / denom
    scores = jnp.where(valid, scores, -jnp.inf)
    mx = jnp.max(scores, keepdims=True)
    e = jnp.where(valid, jnp.exp(scores - mx), 0.0)
    w = e / jnp.sum(e, keepdims=True)
    sy = (rows - RADIUS).astype(jnp.float32)
    sx = (lanes - (PATCH - 1) - RADIUS).astype(jnp.float32)
    fy = jnp.sum(w * sy, keepdims=True) / FLOW_UNIT
    fx = jnp.sum(w * sx, keepdims=True) / FLOW_UNIT
    orow = lax.broadcasted_iota(jnp.int32, (8, 128), 0)
    out_ref[0] = jnp.where(orow == 0, fy, jnp.where(orow == 1, fx, 0.0))


def flows_of(tflipped, windows):
    n = tflipped.shape[0]
    out = pl.pallas_call(
        flow_kernel,
        grid=(n,),
        in_specs=[
            pl.BlockSpec((1, PATCH, PATCH), lambda i: (i, 0, 0)),
            pl.BlockSpec((1, WIN, WIN), lambda i: (i, 0, 0)),
        ],
        out_specs=pl.BlockSpec((1, 8, 128), lambda i: (i, 0, 0)),
        out_shape=jax.ShapeDtypeStruct((n, 8, 128), jnp.float32),
        scratch_shapes=[
            pltpu.VMEM((LANES, LANES), jnp.float32),
            pltpu.VMEM((PATCH, LANES), jnp.float32),
            pltpu.VMEM((72, LANES), jnp.float32),
        ],
    )(tflipped, windows)
    return out[:, 0:2, 0].T


def halo(cells, width):
    n_ty = lax.axis_size("ty")
    n_tx = lax.axis_size("tx")
    height, breadth = cells.shape[-2], cells.shape[-1]
    pieces = {}
    for dy in (-1, 0, 1):
        for dx in (-1, 0, 1):
            if dy == 0 and dx == 0:
                pieces[(dy, dx)] = cells
                continue
            rows = {-1: (height - width, height), 0: (0, height), 1: (0, width)}[dy]
            cols = {-1: (breadth - width, breadth), 0: (0, breadth), 1: (0, width)}[dx]
            part = cells[..., rows[0] : rows[1], cols[0] : cols[1]]
            pairs = []
            for i in range(n_ty):
                for j in range(n_tx):
                    si, sj = i + dy, j + dx
                    if 0 <= si < n_ty and 0 <= sj < n_tx:
                        pairs.append((si * n_tx + sj, i * n_tx + j))
            pieces[(dy, dx)] = lax.ppermute(part, ("ty", "tx"), pairs)
    bands = [
        jnp.concatenate([pieces[(dy, -1)], pieces[(dy, 0)], pieces[(dy, 1)]], axis=-1)
        for dy in (-1, 0, 1)
    ]
    return jnp.concatenate(bands, axis=-2)


def relax_sweep(padded, mask_pad, target, count):
    centre = padded[:, 1:-1, 1:-1]
    mask_c = mask_pad[1:-1, 1:-1]
    height = centre.shape[1]
    width = centre.shape[2]
    spring = jnp.zeros_like(centre)
    for row_step, col_step in ((0, 1), (2, 1), (1, 0), (1, 2)):
        nearby = padded[:, row_step : row_step + height, col_step : col_step + width]
        mask_n = mask_pad[row_step : row_step + height, col_step : col_step + width]
        spring = spring + mask_c * mask_n * (nearby - centre)
    return centre + SPRING_RATE * spring + FLOW_RATE * (target - count * centre)


def one_hot(starts, size, extent, flip=False):
    offs = jnp.arange(size, dtype=jnp.int32)
    if flip:
        offs = size - 1 - offs
    want = starts[:, None, None] + offs[None, :, None]
    return (want == jnp.arange(extent, dtype=jnp.int32)[None, None, :]).astype(jnp.bfloat16)


def shards(
    section_a, section_b, template_corner, template_slot, window_corner, window_slot, node_mask
):
    tile_size = section_a.shape[0]
    slot_count = lax.axis_size("tx") * CAP
    slot_ids = jnp.arange(slot_count, dtype=jnp.int32)
    owner_picker = template_slot[0][:, None] == slot_ids[None, :]
    source_picker = window_slot[0][:, None] == slot_ids[None, :]
    f32 = jnp.float32

    col_pick = one_hot(template_corner[1, 0], PATCH, section_a.shape[1], flip=True)
    row_pick = one_hot(template_corner[0, 0], PATCH, section_a.shape[0])
    by_col = jnp.einsum("krc,ac->kra", col_pick, section_a, preferred_element_type=f32)
    tflipped = jnp.einsum(
        "kra,kia->kri", by_col.astype(jnp.bfloat16), row_pick, preferred_element_type=f32
    ).astype(jnp.bfloat16)
    outgoing = jnp.einsum(
        "ks,kri->sri", owner_picker.astype(jnp.bfloat16), tflipped, preferred_element_type=f32
    ).astype(jnp.bfloat16)
    arrived = lax.all_to_all(outgoing, "tx", split_axis=0, concat_axis=0, tiled=True)

    b_wide = halo(section_b, RADIUS)
    wrow_pick = one_hot(window_corner[0, 0], WIN, b_wide.shape[0])
    wcol_pick = one_hot(window_corner[1, 0], WIN, b_wide.shape[1])
    by_row = jnp.einsum("mra,ac->mrc", wrow_pick, b_wide, preferred_element_type=f32)
    windows = jnp.einsum(
        "mrc,msc->mrs", by_row.astype(jnp.bfloat16), wcol_pick, preferred_element_type=f32
    ).astype(jnp.bfloat16)
    matched = jnp.einsum(
        "ms,sri->mri", source_picker.astype(jnp.bfloat16), arrived, preferred_element_type=f32
    ).astype(jnp.bfloat16)

    flows = flows_of(matched, windows)
    source_flow = -flows

    returned = jnp.sum(jnp.where(source_picker[None], flows[:, :, None], 0.0), axis=1)
    landed = lax.all_to_all(returned, "tx", split_axis=1, concat_axis=1, tiled=True)
    owner_flow = jnp.sum(jnp.where(owner_picker[None], landed[:, None, :], 0.0), axis=2)

    node_rows, node_cols = node_mask.shape
    centre_y = (window_corner[0, 0] + PATCH // 2) * node_rows // tile_size
    centre_x = (window_corner[1, 0] + PATCH // 2) * node_cols // tile_size
    attach = (centre_y[:, None, None] == jnp.arange(node_rows, dtype=jnp.int32)[None, :, None]) & (
        centre_x[:, None, None] == jnp.arange(node_cols, dtype=jnp.int32)[None, None, :]
    )
    target = jnp.sum(jnp.where(attach[None], source_flow[:, :, None, None], 0.0), axis=1)
    count = jnp.sum(attach.astype(f32), axis=0)
    mask = node_mask.astype(f32)
    fields = jnp.concatenate([target, count[None], mask[None]], axis=0)
    wide = halo(fields, ITERS_R)
    displace = jnp.zeros((2,) + wide.shape[1:], f32)
    for sweep in range(ITERS_R):
        lo_m, hi_m = sweep, wide.shape[1] - sweep
        lo_t, hi_t = sweep + 1, wide.shape[1] - sweep - 1
        displace = relax_sweep(
            displace,
            wide[3, lo_m:hi_m, lo_m:hi_m],
            wide[0:2, lo_t:hi_t, lo_t:hi_t],
            wide[2, lo_t:hi_t, lo_t:hi_t],
        )
    return (owner_flow[:, None, :], source_flow[:, None, :], displace)


def solution(mesh):
    placed = (
        P("ty", "tx"),
        P("ty", "tx"),
        P(None, "ty", "tx"),
        P("ty", "tx"),
        P(None, "ty", "tx"),
        P("ty", "tx"),
        P("ty", "tx"),
    )
    return jax.shard_map(
        shards,
        mesh=mesh,
        in_specs=placed,
        out_specs=(P(None, "ty", "tx"), P(None, "ty", "tx"), P(None, "ty", "tx")),
        check_vma=False,
    )
```

time: 225 us -> 148 us (0.66)
  the two profiles are of different devices: /device:TPU:7 before, /device:TPU:48 now
where the time goes in v2:
time: 148 us; the launch traced here: 147 us
  starting transfers between devices  64.8 us (44%)
  Pallas kernels  55.9 us (38%)
  waiting for transfers between devices  11.1 us (8%)
  matrix products  6.09 us (4%)
  local copies, waits for them, and re-layouts  5.25 us (4%)
  other arithmetic  2.83 us (2%)
    pallas_call x1, Pallas kernels, flows_of(): pl.pallas_call(flow_kernel, grid=(n,), in_specs=[pl.BlockSpec((1, PATCH,...  55.9 us
    ppermute x16, starting transfers between devices, halo(): pieces[dy, dx] = lax.ppermute(part, ('ty', 'tx'), pairs)  52 us
    ppermute x16, waiting for transfers between devices, halo(): pieces[dy, dx] = lax.ppermute(part, ('ty', 'tx'), pairs)  11.1 us
    all_to_all x1, starting transfers between devices, shards(): lax.all_to_all(outgoing, 'tx', split_axis=0, concat_axis=0, tiled=True)  8.04 us
    all_to_all x1, starting transfers between devices, shards(): lax.all_to_all(returned, 'tx', split_axis=1, concat_axis=1, tiled=True)  4.82 us
    dot_general x1, matrix products, shards(): jnp.einsum('mrc,msc->mrs', by_row.astype(jnp.bfloat16), wcol_pick, prefer...  3.75 us
  transfers between devices with their start and end apart: 18, of which 2 were waited for; matrix products, arithmetic and copies ran while one was open for 4% of the time, Pallas kernels for 0%

profile of v2, /device:TPU:48, one launch (start us, length us, event | category | flops | bytes accessed | tf_op | source)
XLA Modules:
  0.0 147.0 jit_solution(16651045213659906165)
XLA Ops:
  0.7 0.7 slice_bitcast_fusion.7
  1.7 1.1 fusion.11
  2.9 0.6 convolution_convert_fusion
  3.4 1.4 copy.28
  4.8 8.0 %all-to-all-start = ((bf16[32,128,128]{2,1,0:T(8,128)(2,1)}), bf16[32,128,128]{2,1,0:T(8,128)(2,1)S(1)}, u32[]{:S(2)}, u32[]{:S(2)}) async-start(bf16[32,128,128]{2,1,0:T(8,128)(2,1)} %copy.28), calls=%async_computation | async-start | bytes 2097152 | tf_op jit(solution)/shard_map/all_to_all | solution.py:152
  12.9 3.3 %collective-permute-start.7 = (bf16[32,32]{1,0:T(8,128)(2,1)S(1)}, bf16[32,32]{1,0:T(8,128)(2,1)S(1)}, u32[]{:S(2)}, u32[]{:S(2)}) collective-permute-start(bf16[32,32]{1,0:T(8,128)(2,1)S(1)} %get-tuple-element.18), channel_id=1, source_target_pairs={{17,0},{18,1},{19,2},{20,3},{21,4},{22,5},{23,6},{24,7},{25,8},{26... | collective-permute-start | bytes 6152 | tf_op jit(solution)/shard_map/ppermute | solution.py:104
  16.3 3.3 %collective-permute-start.6 = (bf16[32,512]{1,0:T(8,128)(2,1)S(1)}, bf16[32,512]{1,0:T(8,128)(2,1)S(1)}, u32[]{:S(2)}, u32[]{:S(2)}) collective-permute-start(bf16[32,512]{1,0:T(8,128)(2,1)S(1)} %get-tuple-element.20), channel_id=1, source_target_pairs={{16,0},{17,1},{18,2},{19,3},{20,4},{21,5},{22,6},{23,7},{24,8},{25... | collective-permute-start | bytes 98312 | tf_op jit(solution)/shard_map/ppermute | solution.py:104
  19.6 1.9 %collective-permute-start.5 = (bf16[32,32]{1,0:T(8,128)(2,1)S(1)}, bf16[32,32]{1,0:T(8,128)(2,1)S(1)}, u32[]{:S(2)}, u32[]{:S(2)}) collective-permute-start(bf16[32,32]{1,0:T(8,128)(2,1)S(1)} %get-tuple-element.16), channel_id=1, source_target_pairs={{16,1},{17,2},{18,3},{19,4},{20,5},{21,6},{22,7},{23,8},{24,9},{25... | collective-permute-start | bytes 6152 | tf_op jit(solution)/shard_map/ppermute | solution.py:104
  21.6 5.5 %collective-permute-start.4 = (bf16[512,32]{1,0:T(8,128)(2,1)S(1)}, bf16[512,32]{1,0:T(8,128)(2,1)S(1)}, u32[]{:S(2)}, u32[]{:S(2)}) collective-permute-start(bf16[512,32]{1,0:T(8,128)(2,1)S(1)} %get-tuple-element.22), channel_id=1, source_target_pairs={{1,0},{2,1},{3,2},{4,3},{5,4},{6,5},{7,6},{8,7},{9,8},{10,9},{11,1... | collective-permute-start | bytes 98312 | tf_op jit(solution)/shard_map/ppermute | solution.py:104
  27.1 2.2 %collective-permute-start.2 = (bf16[32,32]{1,0:T(8,128)(2,1)S(1)}, bf16[32,32]{1,0:T(8,128)(2,1)S(1)}, u32[]{:S(2)}, u32[]{:S(2)}) collective-permute-start(bf16[32,32]{1,0:T(8,128)(2,1)S(1)} %get-tuple-element.17), channel_id=1, source_target_pairs={{1,16},{2,17},{3,18},{4,19},{5,20},{6,21},{7,22},{8,23},{9,24},{10... | collective-permute-start | bytes 6152 | tf_op jit(solution)/shard_map/ppermute | solution.py:104
  29.8 3.6 %collective-permute-start.3 = (bf16[512,32]{1,0:T(8,128)(2,1)S(1)}, bf16[512,32]{1,0:T(8,128)(2,1)S(1)}, u32[]{:S(2)}, u32[]{:S(2)}) collective-permute-start(bf16[512,32]{1,0:T(8,128)(2,1)S(1)} %get-tuple-element.21), channel_id=1, source_target_pairs={{0,1},{1,2},{2,3},{3,4},{4,5},{5,6},{6,7},{7,8},{8,9},{9,10},{10,1... | collective-permute-start | bytes 98312 | tf_op jit(solution)/shard_map/ppermute | solution.py:104
  33.5 2.8 %collective-permute-start.1 = (bf16[32,512]{1,0:T(8,128)(2,1)S(1)}, bf16[32,512]{1,0:T(8,128)(2,1)S(1)}, u32[]{:S(2)}, u32[]{:S(2)}) collective-permute-start(bf16[32,512]{1,0:T(8,128)(2,1)S(1)} %get-tuple-element.19), channel_id=1, source_target_pairs={{0,16},{1,17},{2,18},{3,19},{4,20},{5,21},{6,22},{7,23},{8,24},{9,... | collective-permute-start | bytes 98312 | tf_op jit(solution)/shard_map/ppermute | solution.py:104
  36.2 2.4 %collective-permute-start = (bf16[32,32]{1,0:T(8,128)(2,1)S(1)}, bf16[32,32]{1,0:T(8,128)(2,1)S(1)}, u32[]{:S(2)}, u32[]{:S(2)}) collective-permute-start(bf16[32,32]{1,0:T(8,128)(2,1)S(1)} %get-tuple-element.15), channel_id=1, source_target_pairs={{0,17},{1,18},{2,19},{3,20},{4,21},{5,22},{6,23},{7,24},{8,25},{9,... | collective-permute-start | bytes 6152 | tf_op jit(solution)/shard_map/ppermute | solution.py:104
  38.7 5.6 %collective-permute-done = bf16[32,32]{1,0:T(8,128)(2,1)S(1)} collective-permute-done((bf16[32,32]{1,0:T(8,128)(2,1)S(1)}, bf16[32,32]{1,0:T(8,128)(2,1)S(1)}, u32[]{:S(2)}, u32[]{:S(2)}) %collective-permute-start) | collective-permute-done | bytes 2080 | tf_op jit(solution)/shard_map/ppermute | solution.py:104
  44.4 3.8 %fusion.8.w_ref = bf16[8,192,192]{2,1,0:T(8,128)(2,1)} fusion(s32[8,192]{1,0:T(8,128)S(1)} %get-tuple-element.51, s32[8,192]{1,0:T(8,128)S(1)} %get-tuple-element.52, bf16[32,32]{1,0:T(8,128)(2,1)S(1)} %collective-permute-done.7, bf16[32,512]{1,0:T(8,128)(2,1)S(1)} %collective-permute-done.6, bf16[32,32]{1,0:T(8,128)(2,1)S(1)} %collective-permute-done.5, ...), kind=kOutput, calls=%fused_computation.13 | convolution fusion | flops 1367875584 | bytes 1265664 | tf_op jit(solution)/shard_map/mrc,msc->mrs/dot_general | solution.py:158
  48.1 0.7 fusion.12
  48.8 0.8 copy.41.tf_ref
  49.5 55.9 %shard_map.94 = f32[8,8,128]{2,1,0:T(8,128)} custom-call(bf16[8,128,128]{2,1,0:T(8,128)(2,1)} %copy.41.tf_ref, bf16[8,192,192]{2,1,0:T(8,128)(2,1)} %fusion.8.w_ref), custom_call_target="tpu_custom_call" | custom-call | tf_op jit(solution)/shard_map/pallas_call | solution.py:67
  105.4 0.8 slice.214
  106.8 0.6 copy.32
  107.4 4.8 %all-to-all-start.1 = ((f32[2,16,2]{2,0,1:T(2,128)}), f32[2,16,2]{2,0,1:T(2,128)S(1)}, u32[]{:S(2)}, u32[]{:S(2)}) async-start(f32[2,16,2]{2,0,1:T(2,128)} %copy.32), calls=%async_computation.1 | async-start | bytes 32768 | tf_op jit(solution)/shard_map/all_to_all | solution.py:169
  112.2 3.6 %collective-permute-start.15 = (f32[4,3,3]{2,1,0:T(4,128)S(1)}, f32[4,3,3]{2,1,0:T(4,128)S(1)}, u32[]{:S(2)}, u32[]{:S(2)}) collective-permute-start(f32[4,3,3]{2,1,0:T(4,128)S(1)} %get-tuple-element.29), channel_id=1, source_target_pairs={{17,0},{18,1},{19,2},{20,3},{21,4},{22,5},{23,6},{24,7},{25,8},{26... | collective-permute-start | bytes 440 | tf_op jit(solution)/shard_map/ppermute | solution.py:104
  115.8 3.0 %collective-permute-start.14 = (f32[4,3,32]{2,1,0:T(4,128)S(1)}, f32[4,3,32]{2,1,0:T(4,128)S(1)}, u32[]{:S(2)}, u32[]{:S(2)}) collective-permute-start(f32[4,3,32]{2,1,0:T(4,128)S(1)} %get-tuple-element.32), channel_id=1, source_target_pairs={{16,0},{17,1},{18,2},{19,3},{20,4},{21,5},{22,6},{23,7},{24,8},{25... | collective-permute-start | bytes 4616 | tf_op jit(solution)/shard_map/ppermute | solution.py:104
  118.9 1.9 %collective-permute-start.13 = (f32[4,3,3]{2,1,0:T(4,128)S(1)}, f32[4,3,3]{2,1,0:T(4,128)S(1)}, u32[]{:S(2)}, u32[]{:S(2)}) collective-permute-start(f32[4,3,3]{2,1,0:T(4,128)S(1)} %get-tuple-element.28), channel_id=1, source_target_pairs={{16,1},{17,2},{18,3},{19,4},{20,5},{21,6},{22,7},{23,8},{24,9},{25... | collective-permute-start | bytes 440 | tf_op jit(solution)/shard_map/ppermute | solution.py:104
  120.8 5.5 %collective-permute-start.12 = (f32[4,32,3]{2,1,0:T(8,128)S(1)}, f32[4,32,3]{2,1,0:T(8,128)S(1)}, u32[]{:S(2)}, u32[]{:S(2)}) collective-permute-start(f32[4,32,3]{2,1,0:T(8,128)S(1)} %get-tuple-element.34), channel_id=1, source_target_pairs={{1,0},{2,1},{3,2},{4,3},{5,4},{6,5},{7,6},{8,7},{9,8},{10,9},{11,1... | collective-permute-start | bytes 4616 | tf_op jit(solution)/shard_map/ppermute | solution.py:104
  126.3 1.9 %collective-permute-start.11 = (f32[4,32,3]{2,1,0:T(8,128)S(1)}, f32[4,32,3]{2,1,0:T(8,128)S(1)}, u32[]{:S(2)}, u32[]{:S(2)}) collective-permute-start(f32[4,32,3]{2,1,0:T(8,128)S(1)} %get-tuple-element.33), channel_id=1, source_target_pairs={{0,1},{1,2},{2,3},{3,4},{4,5},{5,6},{6,7},{7,8},{8,9},{9,10},{10,1... | collective-permute-start | bytes 4616 | tf_op jit(solution)/shard_map/ppermute | solution.py:104
  128.3 5.7 %collective-permute-start.10 = (f32[4,3,3]{2,1,0:T(4,128)S(1)}, f32[4,3,3]{2,1,0:T(4,128)S(1)}, u32[]{:S(2)}, u32[]{:S(2)}) collective-permute-start(f32[4,3,3]{2,1,0:T(4,128)S(1)} %get-tuple-element.30), channel_id=1, source_target_pairs={{1,16},{2,17},{3,18},{4,19},{5,20},{6,21},{7,22},{8,23},{9,24},{10... | collective-permute-start | bytes 440 | tf_op jit(solution)/shard_map/ppermute | solution.py:104
  134.1 3.3 %collective-permute-start.9 = (f32[4,3,32]{2,1,0:T(4,128)S(1)}, f32[4,3,32]{2,1,0:T(4,128)S(1)}, u32[]{:S(2)}, u32[]{:S(2)}) collective-permute-start(f32[4,3,32]{2,1,0:T(4,128)S(1)} %get-tuple-element.31), channel_id=1, source_target_pairs={{0,16},{1,17},{2,18},{3,19},{4,20},{5,21},{6,22},{7,23},{8,24},{9,... | collective-permute-start | bytes 4616 | tf_op jit(solution)/shard_map/ppermute | solution.py:104
  137.4 1.9 %collective-permute-start.8 = (f32[4,3,3]{2,1,0:T(4,128)S(1)}, f32[4,3,3]{2,1,0:T(4,128)S(1)}, u32[]{:S(2)}, u32[]{:S(2)}) collective-permute-start(f32[4,3,3]{2,1,0:T(4,128)S(1)} %get-tuple-element.27), channel_id=1, source_target_pairs={{0,17},{1,18},{2,19},{3,20},{4,21},{5,22},{6,23},{7,24},{8,25},{9,... | collective-permute-start | bytes 440 | tf_op jit(solution)/shard_map/ppermute | solution.py:104
  139.4 0.7 select_reduce_fusion.1
  140.0 5.4 %collective-permute-done.8 = f32[4,3,3]{2,1,0:T(4,128)S(1)} collective-permute-done((f32[4,3,3]{2,1,0:T(4,128)S(1)}, f32[4,3,3]{2,1,0:T(4,128)S(1)}, u32[]{:S(2)}, u32[]{:S(2)}) %collective-permute-start.8) | collective-permute-done | bytes 176 | tf_op jit(solution)/shard_map/ppermute | solution.py:104
  146.2 0.7 fusion.69
  (64 shorter events, 2.5 us)
Async XLA Ops:
  0.6 1.1 copy-start
  1.7 1.1 copy-start.5
  4.8 8.1 %copy-start.1 = (bf16[512,512]{1,0:T(8,128)(2,1)S(1)}, bf16[512,512]{1,0:T(8,128)(2,1)}, u32[]{:S(2)}) copy-start(bf16[512,512]{1,0:T(8,128)(2,1)} %param.8) | copy-start | bytes 1572868
  4.8 24.5 %copy-start.4 = (s32[2,1,8]{2,1,0:T(1,128)S(1)}, s32[2,1,8]{2,1,0:T(1,128)}, u32[]{:S(2)}) copy-start(s32[2,1,8]{2,1,0:T(1,128)} %param.11) | copy-start | bytes 196
  4.8 24.6 %copy-start.2 = (s32[32,32]{1,0:T(8,128)S(1)}, s32[32,32]{1,0:T(8,128)}, u32[]{:S(2)}) copy-start(s32[32,32]{1,0:T(8,128)} %param.13) | copy-start | bytes 12292
  4.8 24.9 %copy-start.6 = (s32[1,8]{1,0:T(1,128)S(1)}, s32[1,8]{1,0:T(1,128)}, u32[]{:S(2)}) copy-start(s32[1,8]{1,0:T(1,128)} %param.12) | copy-start | bytes 100
  4.8 43.3 %all-to-all-start = ((bf16[32,128,128]{2,1,0:T(8,128)(2,1)}), bf16[32,128,128]{2,1,0:T(8,128)(2,1)S(1)}, u32[]{:S(2)}, u32[]{:S(2)}) async-start(bf16[32,128,128]{2,1,0:T(8,128)(2,1)} %copy.28), calls=%async_computation | async-start | bytes 2097152 | tf_op jit(solution)/shard_map/all_to_all | solution.py:152
  12.9 16.9 %collective-permute-start.7 = (bf16[32,32]{1,0:T(8,128)(2,1)S(1)}, bf16[32,32]{1,0:T(8,128)(2,1)S(1)}, u32[]{:S(2)}, u32[]{:S(2)}) collective-permute-start(bf16[32,32]{1,0:T(8,128)(2,1)S(1)} %get-tuple-element.18), channel_id=1, source_target_pairs={{17,0},{18,1},{19,2},{20,3},{21,4},{22,5},{23,6},{24,7},{25,8},{26... | collective-permute-start | bytes 6152 | tf_op jit(solution)/shard_map/ppermute | solution.py:104
  16.3 28.0 %collective-permute-start.6 = (bf16[32,512]{1,0:T(8,128)(2,1)S(1)}, bf16[32,512]{1,0:T(8,128)(2,1)S(1)}, u32[]{:S(2)}, u32[]{:S(2)}) collective-permute-start(bf16[32,512]{1,0:T(8,128)(2,1)S(1)} %get-tuple-element.20), channel_id=1, source_target_pairs={{16,0},{17,1},{18,2},{19,3},{20,4},{21,5},{22,6},{23,7},{24,8},{25... | collective-permute-start | bytes 98312 | tf_op jit(solution)/shard_map/ppermute | solution.py:104
  19.6 13.8 %collective-permute-start.5 = (bf16[32,32]{1,0:T(8,128)(2,1)S(1)}, bf16[32,32]{1,0:T(8,128)(2,1)S(1)}, u32[]{:S(2)}, u32[]{:S(2)}) collective-permute-start(bf16[32,32]{1,0:T(8,128)(2,1)S(1)} %get-tuple-element.16), channel_id=1, source_target_pairs={{16,1},{17,2},{18,3},{19,4},{20,5},{21,6},{22,7},{23,8},{24,9},{25... | collective-permute-start | bytes 6152 | tf_op jit(solution)/shard_map/ppermute | solution.py:104
  21.6 22.7 %collective-permute-start.4 = (bf16[512,32]{1,0:T(8,128)(2,1)S(1)}, bf16[512,32]{1,0:T(8,128)(2,1)S(1)}, u32[]{:S(2)}, u32[]{:S(2)}) collective-permute-start(bf16[512,32]{1,0:T(8,128)(2,1)S(1)} %get-tuple-element.22), channel_id=1, source_target_pairs={{1,0},{2,1},{3,2},{4,3},{5,4},{6,5},{7,6},{8,7},{9,8},{10,9},{11,1... | collective-permute-start | bytes 98312 | tf_op jit(solution)/shard_map/ppermute | solution.py:104
  27.1 9.1 %collective-permute-start.2 = (bf16[32,32]{1,0:T(8,128)(2,1)S(1)}, bf16[32,32]{1,0:T(8,128)(2,1)S(1)}, u32[]{:S(2)}, u32[]{:S(2)}) collective-permute-start(bf16[32,32]{1,0:T(8,128)(2,1)S(1)} %get-tuple-element.17), channel_id=1, source_target_pairs={{1,16},{2,17},{3,18},{4,19},{5,20},{6,21},{7,22},{8,23},{9,24},{10... | collective-permute-start | bytes 6152 | tf_op jit(solution)/shard_map/ppermute | solution.py:104
  29.8 14.5 %collective-permute-start.3 = (bf16[512,32]{1,0:T(8,128)(2,1)S(1)}, bf16[512,32]{1,0:T(8,128)(2,1)S(1)}, u32[]{:S(2)}, u32[]{:S(2)}) collective-permute-start(bf16[512,32]{1,0:T(8,128)(2,1)S(1)} %get-tuple-element.21), channel_id=1, source_target_pairs={{0,1},{1,2},{2,3},{3,4},{4,5},{5,6},{6,7},{7,8},{8,9},{9,10},{10,1... | collective-permute-start | bytes 98312 | tf_op jit(solution)/shard_map/ppermute | solution.py:104
  33.5 10.9 %collective-permute-start.1 = (bf16[32,512]{1,0:T(8,128)(2,1)S(1)}, bf16[32,512]{1,0:T(8,128)(2,1)S(1)}, u32[]{:S(2)}, u32[]{:S(2)}) collective-permute-start(bf16[32,512]{1,0:T(8,128)(2,1)S(1)} %get-tuple-element.19), channel_id=1, source_target_pairs={{0,16},{1,17},{2,18},{3,19},{4,20},{5,21},{6,22},{7,23},{8,24},{9,... | collective-permute-start | bytes 98312 | tf_op jit(solution)/shard_map/ppermute | solution.py:104
  36.2 8.1 %collective-permute-start = (bf16[32,32]{1,0:T(8,128)(2,1)S(1)}, bf16[32,32]{1,0:T(8,128)(2,1)S(1)}, u32[]{:S(2)}, u32[]{:S(2)}) collective-permute-start(bf16[32,32]{1,0:T(8,128)(2,1)S(1)} %get-tuple-element.15), channel_id=1, source_target_pairs={{0,17},{1,18},{2,19},{3,20},{4,21},{5,22},{6,23},{7,24},{8,25},{9,... | collective-permute-start | bytes 6152 | tf_op jit(solution)/shard_map/ppermute | solution.py:104
  106.3 39.9 %copy-start.3 = (f32[2,8]{1,0:T(2,128)}, f32[2,8]{1,0:T(2,128)S(1)}, u32[]{:S(2)}) copy-start(f32[2,8]{1,0:T(2,128)S(1)} %bitcast_negate_fusion) | copy-start | bytes 196
  107.4 20.8 %all-to-all-start.1 = ((f32[2,16,2]{2,0,1:T(2,128)}), f32[2,16,2]{2,0,1:T(2,128)S(1)}, u32[]{:S(2)}, u32[]{:S(2)}) async-start(f32[2,16,2]{2,0,1:T(2,128)} %copy.32), calls=%async_computation.1 | async-start | bytes 32768 | tf_op jit(solution)/shard_map/all_to_all | solution.py:169
  112.2 16.1 %collective-permute-start.15 = (f32[4,3,3]{2,1,0:T(4,128)S(1)}, f32[4,3,3]{2,1,0:T(4,128)S(1)}, u32[]{:S(2)}, u32[]{:S(2)}) collective-permute-start(f32[4,3,3]{2,1,0:T(4,128)S(1)} %get-tuple-element.29), channel_id=1, source_target_pairs={{17,0},{18,1},{19,2},{20,3},{21,4},{22,5},{23,6},{24,7},{25,8},{26... | collective-permute-start | bytes 440 | tf_op jit(solution)/shard_map/ppermute | solution.py:104
  115.8 29.6 %collective-permute-start.14 = (f32[4,3,32]{2,1,0:T(4,128)S(1)}, f32[4,3,32]{2,1,0:T(4,128)S(1)}, u32[]{:S(2)}, u32[]{:S(2)}) collective-permute-start(f32[4,3,32]{2,1,0:T(4,128)S(1)} %get-tuple-element.32), channel_id=1, source_target_pairs={{16,0},{17,1},{18,2},{19,3},{20,4},{21,5},{22,6},{23,7},{24,8},{25... | collective-permute-start | bytes 4616 | tf_op jit(solution)/shard_map/ppermute | solution.py:104
  118.9 15.2 %collective-permute-start.13 = (f32[4,3,3]{2,1,0:T(4,128)S(1)}, f32[4,3,3]{2,1,0:T(4,128)S(1)}, u32[]{:S(2)}, u32[]{:S(2)}) collective-permute-start(f32[4,3,3]{2,1,0:T(4,128)S(1)} %get-tuple-element.28), channel_id=1, source_target_pairs={{16,1},{17,2},{18,3},{19,4},{20,5},{21,6},{22,7},{23,8},{24,9},{25... | collective-permute-start | bytes 440 | tf_op jit(solution)/shard_map/ppermute | solution.py:104
  120.8 24.6 %collective-permute-start.12 = (f32[4,32,3]{2,1,0:T(8,128)S(1)}, f32[4,32,3]{2,1,0:T(8,128)S(1)}, u32[]{:S(2)}, u32[]{:S(2)}) collective-permute-start(f32[4,32,3]{2,1,0:T(8,128)S(1)} %get-tuple-element.34), channel_id=1, source_target_pairs={{1,0},{2,1},{3,2},{4,3},{5,4},{6,5},{7,6},{8,7},{9,8},{10,9},{11,1... | collective-permute-start | bytes 4616 | tf_op jit(solution)/shard_map/ppermute | solution.py:104
  126.3 19.2 %collective-permute-start.11 = (f32[4,32,3]{2,1,0:T(8,128)S(1)}, f32[4,32,3]{2,1,0:T(8,128)S(1)}, u32[]{:S(2)}, u32[]{:S(2)}) collective-permute-start(f32[4,32,3]{2,1,0:T(8,128)S(1)} %get-tuple-element.33), channel_id=1, source_target_pairs={{0,1},{1,2},{2,3},{3,4},{4,5},{5,6},{6,7},{7,8},{8,9},{9,10},{10,1... | collective-permute-start | bytes 4616 | tf_op jit(solution)/shard_map/ppermute | solution.py:104
  128.3 9.1 %collective-permute-start.10 = (f32[4,3,3]{2,1,0:T(4,128)S(1)}, f32[4,3,3]{2,1,0:T(4,128)S(1)}, u32[]{:S(2)}, u32[]{:S(2)}) collective-permute-start(f32[4,3,3]{2,1,0:T(4,128)S(1)} %get-tuple-element.30), channel_id=1, source_target_pairs={{1,16},{2,17},{3,18},{4,19},{5,20},{6,21},{7,22},{8,23},{9,24},{10... | collective-permute-start | bytes 440 | tf_op jit(solution)/shard_map/ppermute | solution.py:104
  134.1 11.4 %collective-permute-start.9 = (f32[4,3,32]{2,1,0:T(4,128)S(1)}, f32[4,3,32]{2,1,0:T(4,128)S(1)}, u32[]{:S(2)}, u32[]{:S(2)}) collective-permute-start(f32[4,3,32]{2,1,0:T(4,128)S(1)} %get-tuple-element.31), channel_id=1, source_target_pairs={{0,16},{1,17},{2,18},{3,19},{4,20},{5,21},{6,22},{7,23},{8,24},{9,... | collective-permute-start | bytes 4616 | tf_op jit(solution)/shard_map/ppermute | solution.py:104
  137.4 8.0 %collective-permute-start.8 = (f32[4,3,3]{2,1,0:T(4,128)S(1)}, f32[4,3,3]{2,1,0:T(4,128)S(1)}, u32[]{:S(2)}, u32[]{:S(2)}) collective-permute-start(f32[4,3,3]{2,1,0:T(4,128)S(1)} %get-tuple-element.27), channel_id=1, source_target_pairs={{0,17},{1,18},{2,19},{3,20},{4,21},{5,22},{6,23},{7,24},{8,25},{9,... | collective-permute-start | bytes 440 | tf_op jit(solution)/shard_map/ppermute | solution.py:104

commit v3 on v2

--- a/solution.py
+++ b/solution.py
@@ -19,33 +19,35 @@
 FLOW_UNIT = 8.0
 EPSILON = 1e-05
 
-LANES = 256
-
-
-def flow_kernel(tf_ref, w_ref, out_ref, wpad, tpad, corr):
-    wpad[...] = jnp.zeros(wpad.shape, jnp.float32)
+HALF = PATCH // 2
+
+
+def flow_kernel(tf_ref, w_ref, out_ref, wlo, whi, corr):
     wf = w_ref[0].astype(jnp.float32)
-    wpad[0:WIN, 0:WIN] = wf
+    wlo[...] = wf[:, 0:PATCH]
+    whi[...] = jnp.zeros(whi.shape, jnp.float32)
+    whi[:, 0:WIN - HALF] = wf[:, HALF:WIN]
     tfv = tf_ref[0].astype(jnp.float32)
-    tpad[...] = jnp.zeros(tpad.shape, jnp.float32)
-    tpad[:, 0:PATCH] = tfv
-    wb = wpad[...].astype(jnp.bfloat16)
-    tp = tpad[...]
+    t_top = tf_ref[0, 0:HALF, :]
+    t_bot = tf_ref[0, HALF:PATCH, :]
     corr[...] = jnp.zeros(corr.shape, jnp.float32)
 
     def step(dy, carry):
-        lhs = pltpu.roll(tp, dy, axis=1).astype(jnp.bfloat16)
-        m = jnp.dot(lhs, wb, preferred_element_type=jnp.float32)
-        r = pltpu.roll(m, 0, axis=1, stride=1, stride_axis=0)
-        corr[pl.ds(dy, 1), :] = jnp.sum(r, axis=0, keepdims=True)
+        w_lo = wlo[pl.ds(dy, PATCH), :].astype(jnp.bfloat16)
+        w_hi = whi[pl.ds(dy, PATCH), :].astype(jnp.bfloat16)
+        m_top = jnp.dot(t_top, w_hi, preferred_element_type=jnp.float32)
+        m_bot = jnp.dot(t_bot, w_lo, preferred_element_type=jnp.float32)
+        r_top = pltpu.roll(m_top, 0, axis=1, stride=1, stride_axis=0)
+        r_bot = pltpu.roll(m_bot, 0, axis=1, stride=1, stride_axis=0)
+        corr[pl.ds(dy, 1), :] = jnp.sum(r_top + r_bot, axis=0, keepdims=True)
         return carry
 
-    lax.fori_loop(0, SHIFTS, step, 0, unroll=5)
+    lax.fori_loop(0, SHIFTS, step, 0, unroll=SHIFTS)
 
     c = corr[...]
     rows = lax.broadcasted_iota(jnp.int32, c.shape, 0)
     lanes = lax.broadcasted_iota(jnp.int32, c.shape, 1)
-    valid = (rows < SHIFTS) & (lanes >= PATCH - 1) & (lanes < PATCH - 1 + SHIFTS)
+    valid = (rows < SHIFTS) & (lanes >= HALF - 1)
     e_t = jnp.sum(tfv * tfv, keepdims=True) / float(PATCH * PATCH)
     e_w = jnp.sum(wf * wf, keepdims=True) / float(WIN * WIN)
     denom = float(PATCH * PATCH) * jnp.sqrt((e_t + EPSILON) * (e_w + EPSILON))
@@ -55,29 +57,24 @@
     e = jnp.where(valid, jnp.exp(scores - mx), 0.0)
     w = e / jnp.sum(e, keepdims=True)
     sy = (rows - RADIUS).astype(jnp.float32)
-    sx = (lanes - (PATCH - 1) - RADIUS).astype(jnp.float32)
+    sx = (lanes - (HALF - 1) - RADIUS).astype(jnp.float32)
     fy = jnp.sum(w * sy, keepdims=True) / FLOW_UNIT
     fx = jnp.sum(w * sx, keepdims=True) / FLOW_UNIT
     orow = lax.broadcasted_iota(jnp.int32, (8, 128), 0)
     out_ref[0] = jnp.where(orow == 0, fy, jnp.where(orow == 1, fx, 0.0))
-
 
 def flows_of(tflipped, windows):
     n = tflipped.shape[0]
     out = pl.pallas_call(
         flow_kernel,
         grid=(n,),
-        in_specs=[
-            pl.BlockSpec((1, PATCH, PATCH), lambda i: (i, 0, 0)),
-            pl.BlockSpec((1, WIN, WIN), lambda i: (i, 0, 0)),
-        ],
+        in_specs=[pl.BlockSpec((1, PATCH, PATCH), lambda i: (i, 0, 0)),
+                  pl.BlockSpec((1, WIN, WIN), lambda i: (i, 0, 0))],
         out_specs=pl.BlockSpec((1, 8, 128), lambda i: (i, 0, 0)),
         out_shape=jax.ShapeDtypeStruct((n, 8, 128), jnp.float32),
-        scratch_shapes=[
-            pltpu.VMEM((LANES, LANES), jnp.float32),
-            pltpu.VMEM((PATCH, LANES), jnp.float32),
-            pltpu.VMEM((72, LANES), jnp.float32),
-        ],
+        scratch_shapes=[pltpu.VMEM((WIN, PATCH), jnp.float32),
+                        pltpu.VMEM((WIN, PATCH), jnp.float32),
+                        pltpu.VMEM((72, PATCH), jnp.float32)],
     )(tflipped, windows)
     return out[:, 0:2, 0].T
 

time: 148 us -> 108 us (0.73)
  Pallas kernels: 55.9 us -> 16 us
    pallas_call x1, Pallas kernels: 55.9 us -> 16 us  [flows_of(): pl.pallas_call(flow_kernel, grid=(n,), in_specs=[pl.BlockSpec((1, PATCH,...]
  transfers between devices with their start and end apart: 18 -> 18, of which waited for: 2 -> 2; matrix products, arithmetic and copies ran while one was open for 4% -> 5% of each run, Pallas kernels for 0% -> 0%
where the time goes in v3:
time: 108 us; the launch traced here: 107 us
  starting transfers between devices  64.8 us (60%)
  Pallas kernels  16 us (15%)
  waiting for transfers between devices  11.1 us (10%)
  matrix products  6.09 us (6%)
  local copies, waits for them, and re-layouts  5.25 us (5%)
  other arithmetic  2.83 us (3%)
    ppermute x16, starting transfers between devices, halo(): pieces[dy, dx] = lax.ppermute(part, ('ty', 'tx'), pairs)  52 us
    pallas_call x1, Pallas kernels, flows_of(): pl.pallas_call(flow_kernel, grid=(n,), in_specs=[pl.BlockSpec((1, PATCH,...  16 us
    ppermute x16, waiting for transfers between devices, halo(): pieces[dy, dx] = lax.ppermute(part, ('ty', 'tx'), pairs)  11.1 us
    all_to_all x1, starting transfers between devices, shards(): lax.all_to_all(outgoing, 'tx', split_axis=0, concat_axis=0, tiled=True)  8.04 us
    all_to_all x1, starting transfers between devices, shards(): lax.all_to_all(returned, 'tx', split_axis=1, concat_axis=1, tiled=True)  4.82 us
    dot_general x1, matrix products, shards(): jnp.einsum('mrc,msc->mrs', by_row.astype(jnp.bfloat16), wcol_pick, prefer...  3.75 us
  transfers between devices with their start and end apart: 18, of which 2 were waited for; matrix products, arithmetic and copies ran while one was open for 5% of the time, Pallas kernels for 0%

profile of v3, /device:TPU:48, one launch (start us, length us, event | category | flops | bytes accessed | tf_op | source)
XLA Modules:
  0.0 107.1 jit_solution(15402100875496068518)
XLA Ops:
  0.7 0.7 slice_bitcast_fusion.7
  1.7 1.1 %fusion.11 = bf16[8,128,128]{2,1,0:T(8,128)(2,1)S(1)} fusion(s32[8,128]{1,0:T(8,128)S(1)} %get-tuple-element.49, s32[8,128]{1,0:T(8,128)S(1)} %get-tuple-element.50, bf16[512,512]{1,0:T(8,128)(2,1)S(1)} %copy-done), kind=kOutput, calls=%fused_computation.14 | convolution fusion | flops 672792576 | bytes 794624 | tf_op jit(solution)/shard_map/kra,kia->kri/dot_general | solution.py:143
  2.9 0.6 convolution_convert_fusion
  3.4 1.4 %copy.28 = bf16[32,128,128]{2,1,0:T(8,128)(2,1)} copy(bf16[32,128,128]{2,0,1:T(8,128)(2,1)S(1)} %convolution_convert_fusion) | data formatting | bytes 2097152 | tf_op jit(solution)/shard_map/convert_element_type | solution.py:148
  4.8 8.0 %all-to-all-start = ((bf16[32,128,128]{2,1,0:T(8,128)(2,1)}), bf16[32,128,128]{2,1,0:T(8,128)(2,1)S(1)}, u32[]{:S(2)}, u32[]{:S(2)}) async-start(bf16[32,128,128]{2,1,0:T(8,128)(2,1)} %copy.28), calls=%async_computation | async-start | bytes 2097152 | tf_op jit(solution)/shard_map/all_to_all | solution.py:149
  12.9 3.3 %collective-permute-start.7 = (bf16[32,32]{1,0:T(8,128)(2,1)S(1)}, bf16[32,32]{1,0:T(8,128)(2,1)S(1)}, u32[]{:S(2)}, u32[]{:S(2)}) collective-permute-start(bf16[32,32]{1,0:T(8,128)(2,1)S(1)} %get-tuple-element.18), channel_id=1, source_target_pairs={{17,0},{18,1},{19,2},{20,3},{21,4},{22,5},{23,6},{24,7},{25,8},{26... | collective-permute-start | bytes 6152 | tf_op jit(solution)/shard_map/ppermute | solution.py:101
  16.3 3.3 %collective-permute-start.6 = (bf16[32,512]{1,0:T(8,128)(2,1)S(1)}, bf16[32,512]{1,0:T(8,128)(2,1)S(1)}, u32[]{:S(2)}, u32[]{:S(2)}) collective-permute-start(bf16[32,512]{1,0:T(8,128)(2,1)S(1)} %get-tuple-element.20), channel_id=1, source_target_pairs={{16,0},{17,1},{18,2},{19,3},{20,4},{21,5},{22,6},{23,7},{24,8},{25... | collective-permute-start | bytes 98312 | tf_op jit(solution)/shard_map/ppermute | solution.py:101
  19.6 1.9 %collective-permute-start.5 = (bf16[32,32]{1,0:T(8,128)(2,1)S(1)}, bf16[32,32]{1,0:T(8,128)(2,1)S(1)}, u32[]{:S(2)}, u32[]{:S(2)}) collective-permute-start(bf16[32,32]{1,0:T(8,128)(2,1)S(1)} %get-tuple-element.16), channel_id=1, source_target_pairs={{16,1},{17,2},{18,3},{19,4},{20,5},{21,6},{22,7},{23,8},{24,9},{25... | collective-permute-start | bytes 6152 | tf_op jit(solution)/shard_map/ppermute | solution.py:101
  21.6 5.5 %collective-permute-start.4 = (bf16[512,32]{1,0:T(8,128)(2,1)S(1)}, bf16[512,32]{1,0:T(8,128)(2,1)S(1)}, u32[]{:S(2)}, u32[]{:S(2)}) collective-permute-start(bf16[512,32]{1,0:T(8,128)(2,1)S(1)} %get-tuple-element.22), channel_id=1, source_target_pairs={{1,0},{2,1},{3,2},{4,3},{5,4},{6,5},{7,6},{8,7},{9,8},{10,9},{11,1... | collective-permute-start | bytes 98312 | tf_op jit(solution)/shard_map/ppermute | solution.py:101
  27.1 2.2 %collective-permute-start.2 = (bf16[32,32]{1,0:T(8,128)(2,1)S(1)}, bf16[32,32]{1,0:T(8,128)(2,1)S(1)}, u32[]{:S(2)}, u32[]{:S(2)}) collective-permute-start(bf16[32,32]{1,0:T(8,128)(2,1)S(1)} %get-tuple-element.17), channel_id=1, source_target_pairs={{1,16},{2,17},{3,18},{4,19},{5,20},{6,21},{7,22},{8,23},{9,24},{10... | collective-permute-start | bytes 6152 | tf_op jit(solution)/shard_map/ppermute | solution.py:101
  29.8 3.6 %collective-permute-start.3 = (bf16[512,32]{1,0:T(8,128)(2,1)S(1)}, bf16[512,32]{1,0:T(8,128)(2,1)S(1)}, u32[]{:S(2)}, u32[]{:S(2)}) collective-permute-start(bf16[512,32]{1,0:T(8,128)(2,1)S(1)} %get-tuple-element.21), channel_id=1, source_target_pairs={{0,1},{1,2},{2,3},{3,4},{4,5},{5,6},{6,7},{7,8},{8,9},{9,10},{10,1... | collective-permute-start | bytes 98312 | tf_op jit(solution)/shard_map/ppermute | solution.py:101
  33.5 2.8 %collective-permute-start.1 = (bf16[32,512]{1,0:T(8,128)(2,1)S(1)}, bf16[32,512]{1,0:T(8,128)(2,1)S(1)}, u32[]{:S(2)}, u32[]{:S(2)}) collective-permute-start(bf16[32,512]{1,0:T(8,128)(2,1)S(1)} %get-tuple-element.19), channel_id=1, source_target_pairs={{0,16},{1,17},{2,18},{3,19},{4,20},{5,21},{6,22},{7,23},{8,24},{9,... | collective-permute-start | bytes 98312 | tf_op jit(solution)/shard_map/ppermute | solution.py:101
  36.2 2.4 %collective-permute-start = (bf16[32,32]{1,0:T(8,128)(2,1)S(1)}, bf16[32,32]{1,0:T(8,128)(2,1)S(1)}, u32[]{:S(2)}, u32[]{:S(2)}) collective-permute-start(bf16[32,32]{1,0:T(8,128)(2,1)S(1)} %get-tuple-element.15), channel_id=1, source_target_pairs={{0,17},{1,18},{2,19},{3,20},{4,21},{5,22},{6,23},{7,24},{8,25},{9,... | collective-permute-start | bytes 6152 | tf_op jit(solution)/shard_map/ppermute | solution.py:101
  38.7 5.6 %collective-permute-done = bf16[32,32]{1,0:T(8,128)(2,1)S(1)} collective-permute-done((bf16[32,32]{1,0:T(8,128)(2,1)S(1)}, bf16[32,32]{1,0:T(8,128)(2,1)S(1)}, u32[]{:S(2)}, u32[]{:S(2)}) %collective-permute-start) | collective-permute-done | bytes 2080 | tf_op jit(solution)/shard_map/ppermute | solution.py:101
  44.4 3.8 %fusion.8.w_ref = bf16[8,192,192]{2,1,0:T(8,128)(2,1)} fusion(s32[8,192]{1,0:T(8,128)S(1)} %get-tuple-element.51, s32[8,192]{1,0:T(8,128)S(1)} %get-tuple-element.52, bf16[32,32]{1,0:T(8,128)(2,1)S(1)} %collective-permute-done.7, bf16[32,512]{1,0:T(8,128)(2,1)S(1)} %collective-permute-done.6, bf16[32,32]{1,0:T(8,128)(2,1)S(1)} %collective-permute-done.5, ...), kind=kOutput, calls=%fused_computation.13 | convolution fusion | flops 1367875584 | bytes 1265664 | tf_op jit(solution)/shard_map/mrc,msc->mrs/dot_general | solution.py:155
  48.1 0.7 fusion.12
  48.8 0.8 copy.41.tf_ref
  49.5 16.0 %shard_map.94 = f32[8,8,128]{2,1,0:T(8,128)} custom-call(bf16[8,128,128]{2,1,0:T(8,128)(2,1)} %copy.41.tf_ref, bf16[8,192,192]{2,1,0:T(8,128)(2,1)} %fusion.8.w_ref), custom_call_target="tpu_custom_call" | custom-call | tf_op jit(solution)/shard_map/pallas_call | solution.py:68
  65.5 0.8 slice.214
  66.9 0.6 copy.32
  67.5 4.8 %all-to-all-start.1 = ((f32[2,16,2]{2,0,1:T(2,128)}), f32[2,16,2]{2,0,1:T(2,128)S(1)}, u32[]{:S(2)}, u32[]{:S(2)}) async-start(f32[2,16,2]{2,0,1:T(2,128)} %copy.32), calls=%async_computation.1 | async-start | bytes 32768 | tf_op jit(solution)/shard_map/all_to_all | solution.py:166
  72.3 3.6 %collective-permute-start.15 = (f32[4,3,3]{2,1,0:T(4,128)S(1)}, f32[4,3,3]{2,1,0:T(4,128)S(1)}, u32[]{:S(2)}, u32[]{:S(2)}) collective-permute-start(f32[4,3,3]{2,1,0:T(4,128)S(1)} %get-tuple-element.29), channel_id=1, source_target_pairs={{17,0},{18,1},{19,2},{20,3},{21,4},{22,5},{23,6},{24,7},{25,8},{26... | collective-permute-start | bytes 440 | tf_op jit(solution)/shard_map/ppermute | solution.py:101
  75.9 3.0 %collective-permute-start.14 = (f32[4,3,32]{2,1,0:T(4,128)S(1)}, f32[4,3,32]{2,1,0:T(4,128)S(1)}, u32[]{:S(2)}, u32[]{:S(2)}) collective-permute-start(f32[4,3,32]{2,1,0:T(4,128)S(1)} %get-tuple-element.32), channel_id=1, source_target_pairs={{16,0},{17,1},{18,2},{19,3},{20,4},{21,5},{22,6},{23,7},{24,8},{25... | collective-permute-start | bytes 4616 | tf_op jit(solution)/shard_map/ppermute | solution.py:101
  79.0 1.9 %collective-permute-start.13 = (f32[4,3,3]{2,1,0:T(4,128)S(1)}, f32[4,3,3]{2,1,0:T(4,128)S(1)}, u32[]{:S(2)}, u32[]{:S(2)}) collective-permute-start(f32[4,3,3]{2,1,0:T(4,128)S(1)} %get-tuple-element.28), channel_id=1, source_target_pairs={{16,1},{17,2},{18,3},{19,4},{20,5},{21,6},{22,7},{23,8},{24,9},{25... | collective-permute-start | bytes 440 | tf_op jit(solution)/shard_map/ppermute | solution.py:101
  80.9 5.5 %collective-permute-start.12 = (f32[4,32,3]{2,1,0:T(8,128)S(1)}, f32[4,32,3]{2,1,0:T(8,128)S(1)}, u32[]{:S(2)}, u32[]{:S(2)}) collective-permute-start(f32[4,32,3]{2,1,0:T(8,128)S(1)} %get-tuple-element.34), channel_id=1, source_target_pairs={{1,0},{2,1},{3,2},{4,3},{5,4},{6,5},{7,6},{8,7},{9,8},{10,9},{11,1... | collective-permute-start | bytes 4616 | tf_op jit(solution)/shard_map/ppermute | solution.py:101
  86.4 1.9 %collective-permute-start.11 = (f32[4,32,3]{2,1,0:T(8,128)S(1)}, f32[4,32,3]{2,1,0:T(8,128)S(1)}, u32[]{:S(2)}, u32[]{:S(2)}) collective-permute-start(f32[4,32,3]{2,1,0:T(8,128)S(1)} %get-tuple-element.33), channel_id=1, source_target_pairs={{0,1},{1,2},{2,3},{3,4},{4,5},{5,6},{6,7},{7,8},{8,9},{9,10},{10,1... | collective-permute-start | bytes 4616 | tf_op jit(solution)/shard_map/ppermute | solution.py:101
  88.4 5.7 %collective-permute-start.10 = (f32[4,3,3]{2,1,0:T(4,128)S(1)}, f32[4,3,3]{2,1,0:T(4,128)S(1)}, u32[]{:S(2)}, u32[]{:S(2)}) collective-permute-start(f32[4,3,3]{2,1,0:T(4,128)S(1)} %get-tuple-element.30), channel_id=1, source_target_pairs={{1,16},{2,17},{3,18},{4,19},{5,20},{6,21},{7,22},{8,23},{9,24},{10... | collective-permute-start | bytes 440 | tf_op jit(solution)/shard_map/ppermute | solution.py:101
  94.2 3.4 %collective-permute-start.9 = (f32[4,3,32]{2,1,0:T(4,128)S(1)}, f32[4,3,32]{2,1,0:T(4,128)S(1)}, u32[]{:S(2)}, u32[]{:S(2)}) collective-permute-start(f32[4,3,32]{2,1,0:T(4,128)S(1)} %get-tuple-element.31), channel_id=1, source_target_pairs={{0,16},{1,17},{2,18},{3,19},{4,20},{5,21},{6,22},{7,23},{8,24},{9,... | collective-permute-start | bytes 4616 | tf_op jit(solution)/shard_map/ppermute | solution.py:101
  97.6 1.9 %collective-permute-start.8 = (f32[4,3,3]{2,1,0:T(4,128)S(1)}, f32[4,3,3]{2,1,0:T(4,128)S(1)}, u32[]{:S(2)}, u32[]{:S(2)}) collective-permute-start(f32[4,3,3]{2,1,0:T(4,128)S(1)} %get-tuple-element.27), channel_id=1, source_target_pairs={{0,17},{1,18},{2,19},{3,20},{4,21},{5,22},{6,23},{7,24},{8,25},{9,... | collective-permute-start | bytes 440 | tf_op jit(solution)/shard_map/ppermute | solution.py:101
  99.5 0.7 select_reduce_fusion.1
  100.1 5.4 %collective-permute-done.8 = f32[4,3,3]{2,1,0:T(4,128)S(1)} collective-permute-done((f32[4,3,3]{2,1,0:T(4,128)S(1)}, f32[4,3,3]{2,1,0:T(4,128)S(1)}, u32[]{:S(2)}, u32[]{:S(2)}) %collective-permute-start.8) | collective-permute-done | bytes 176 | tf_op jit(solution)/shard_map/ppermute | solution.py:101
  106.4 0.7 fusion.69
  (64 shorter events, 2.5 us)
Async XLA Ops:
  0.6 1.1 %copy-start = (bf16[512,512]{1,0:T(8,128)(2,1)S(1)}, bf16[512,512]{1,0:T(8,128)(2,1)}, u32[]{:S(2)}) copy-start(bf16[512,512]{1,0:T(8,128)(2,1)} %param.7) | copy-start | bytes 1572868
  1.7 1.1 %copy-start.5 = (s32[1,8]{1,0:T(1,128)S(1)}, s32[1,8]{1,0:T(1,128)}, u32[]{:S(2)}) copy-start(s32[1,8]{1,0:T(1,128)} %param.10) | copy-start | bytes 100
  4.8 8.1 %copy-start.1 = (bf16[512,512]{1,0:T(8,128)(2,1)S(1)}, bf16[512,512]{1,0:T(8,128)(2,1)}, u32[]{:S(2)}) copy-start(bf16[512,512]{1,0:T(8,128)(2,1)} %param.8) | copy-start | bytes 1572868
  4.8 24.5 %copy-start.4 = (s32[2,1,8]{2,1,0:T(1,128)S(1)}, s32[2,1,8]{2,1,0:T(1,128)}, u32[]{:S(2)}) copy-start(s32[2,1,8]{2,1,0:T(1,128)} %param.11) | copy-start | bytes 196
  4.8 24.6 %copy-start.2 = (s32[32,32]{1,0:T(8,128)S(1)}, s32[32,32]{1,0:T(8,128)}, u32[]{:S(2)}) copy-start(s32[32,32]{1,0:T(8,128)} %param.13) | copy-start | bytes 12292
  4.8 24.9 %copy-start.6 = (s32[1,8]{1,0:T(1,128)S(1)}, s32[1,8]{1,0:T(1,128)}, u32[]{:S(2)}) copy-start(s32[1,8]{1,0:T(1,128)} %param.12) | copy-start | bytes 100
  4.8 43.3 %all-to-all-start = ((bf16[32,128,128]{2,1,0:T(8,128)(2,1)}), bf16[32,128,128]{2,1,0:T(8,128)(2,1)S(1)}, u32[]{:S(2)}, u32[]{:S(2)}) async-start(bf16[32,128,128]{2,1,0:T(8,128)(2,1)} %copy.28), calls=%async_computation | async-start | bytes 2097152 | tf_op jit(solution)/shard_map/all_to_all | solution.py:149
  12.9 16.9 %collective-permute-start.7 = (bf16[32,32]{1,0:T(8,128)(2,1)S(1)}, bf16[32,32]{1,0:T(8,128)(2,1)S(1)}, u32[]{:S(2)}, u32[]{:S(2)}) collective-permute-start(bf16[32,32]{1,0:T(8,128)(2,1)S(1)} %get-tuple-element.18), channel_id=1, source_target_pairs={{17,0},{18,1},{19,2},{20,3},{21,4},{22,5},{23,6},{24,7},{25,8},{26... | collective-permute-start | bytes 6152 | tf_op jit(solution)/shard_map/ppermute | solution.py:101
  16.3 28.0 %collective-permute-start.6 = (bf16[32,512]{1,0:T(8,128)(2,1)S(1)}, bf16[32,512]{1,0:T(8,128)(2,1)S(1)}, u32[]{:S(2)}, u32[]{:S(2)}) collective-permute-start(bf16[32,512]{1,0:T(8,128)(2,1)S(1)} %get-tuple-element.20), channel_id=1, source_target_pairs={{16,0},{17,1},{18,2},{19,3},{20,4},{21,5},{22,6},{23,7},{24,8},{25... | collective-permute-start | bytes 98312 | tf_op jit(solution)/shard_map/ppermute | solution.py:101
  19.6 13.8 %collective-permute-start.5 = (bf16[32,32]{1,0:T(8,128)(2,1)S(1)}, bf16[32,32]{1,0:T(8,128)(2,1)S(1)}, u32[]{:S(2)}, u32[]{:S(2)}) collective-permute-start(bf16[32,32]{1,0:T(8,128)(2,1)S(1)} %get-tuple-element.16), channel_id=1, source_target_pairs={{16,1},{17,2},{18,3},{19,4},{20,5},{21,6},{22,7},{23,8},{24,9},{25... | collective-permute-start | bytes 6152 | tf_op jit(solution)/shard_map/ppermute | solution.py:101
  21.6 22.7 %collective-permute-start.4 = (bf16[512,32]{1,0:T(8,128)(2,1)S(1)}, bf16[512,32]{1,0:T(8,128)(2,1)S(1)}, u32[]{:S(2)}, u32[]{:S(2)}) collective-permute-start(bf16[512,32]{1,0:T(8,128)(2,1)S(1)} %get-tuple-element.22), channel_id=1, source_target_pairs={{1,0},{2,1},{3,2},{4,3},{5,4},{6,5},{7,6},{8,7},{9,8},{10,9},{11,1... | collective-permute-start | bytes 98312 | tf_op jit(solution)/shard_map/ppermute | solution.py:101
  27.1 9.1 %collective-permute-start.2 = (bf16[32,32]{1,0:T(8,128)(2,1)S(1)}, bf16[32,32]{1,0:T(8,128)(2,1)S(1)}, u32[]{:S(2)}, u32[]{:S(2)}) collective-permute-start(bf16[32,32]{1,0:T(8,128)(2,1)S(1)} %get-tuple-element.17), channel_id=1, source_target_pairs={{1,16},{2,17},{3,18},{4,19},{5,20},{6,21},{7,22},{8,23},{9,24},{10... | collective-permute-start | bytes 6152 | tf_op jit(solution)/shard_map/ppermute | solution.py:101
  29.8 14.5 %collective-permute-start.3 = (bf16[512,32]{1,0:T(8,128)(2,1)S(1)}, bf16[512,32]{1,0:T(8,128)(2,1)S(1)}, u32[]{:S(2)}, u32[]{:S(2)}) collective-permute-start(bf16[512,32]{1,0:T(8,128)(2,1)S(1)} %get-tuple-element.21), channel_id=1, source_target_pairs={{0,1},{1,2},{2,3},{3,4},{4,5},{5,6},{6,7},{7,8},{8,9},{9,10},{10,1... | collective-permute-start | bytes 98312 | tf_op jit(solution)/shard_map/ppermute | solution.py:101
  33.5 10.9 %collective-permute-start.1 = (bf16[32,512]{1,0:T(8,128)(2,1)S(1)}, bf16[32,512]{1,0:T(8,128)(2,1)S(1)}, u32[]{:S(2)}, u32[]{:S(2)}) collective-permute-start(bf16[32,512]{1,0:T(8,128)(2,1)S(1)} %get-tuple-element.19), channel_id=1, source_target_pairs={{0,16},{1,17},{2,18},{3,19},{4,20},{5,21},{6,22},{7,23},{8,24},{9,... | collective-permute-start | bytes 98312 | tf_op jit(solution)/shard_map/ppermute | solution.py:101
  36.2 8.1 %collective-permute-start = (bf16[32,32]{1,0:T(8,128)(2,1)S(1)}, bf16[32,32]{1,0:T(8,128)(2,1)S(1)}, u32[]{:S(2)}, u32[]{:S(2)}) collective-permute-start(bf16[32,32]{1,0:T(8,128)(2,1)S(1)} %get-tuple-element.15), channel_id=1, source_target_pairs={{0,17},{1,18},{2,19},{3,20},{4,21},{5,22},{6,23},{7,24},{8,25},{9,... | collective-permute-start | bytes 6152 | tf_op jit(solution)/shard_map/ppermute | solution.py:101
  66.4 39.9 %copy-start.3 = (f32[2,8]{1,0:T(2,128)}, f32[2,8]{1,0:T(2,128)S(1)}, u32[]{:S(2)}) copy-start(f32[2,8]{1,0:T(2,128)S(1)} %bitcast_negate_fusion) | copy-start | bytes 196
  67.5 20.8 %all-to-all-start.1 = ((f32[2,16,2]{2,0,1:T(2,128)}), f32[2,16,2]{2,0,1:T(2,128)S(1)}, u32[]{:S(2)}, u32[]{:S(2)}) async-start(f32[2,16,2]{2,0,1:T(2,128)} %copy.32), calls=%async_computation.1 | async-start | bytes 32768 | tf_op jit(solution)/shard_map/all_to_all | solution.py:166
  72.3 16.1 %collective-permute-start.15 = (f32[4,3,3]{2,1,0:T(4,128)S(1)}, f32[4,3,3]{2,1,0:T(4,128)S(1)}, u32[]{:S(2)}, u32[]{:S(2)}) collective-permute-start(f32[4,3,3]{2,1,0:T(4,128)S(1)} %get-tuple-element.29), channel_id=1, source_target_pairs={{17,0},{18,1},{19,2},{20,3},{21,4},{22,5},{23,6},{24,7},{25,8},{26... | collective-permute-start | bytes 440 | tf_op jit(solution)/shard_map/ppermute | solution.py:101
  75.9 29.6 %collective-permute-start.14 = (f32[4,3,32]{2,1,0:T(4,128)S(1)}, f32[4,3,32]{2,1,0:T(4,128)S(1)}, u32[]{:S(2)}, u32[]{:S(2)}) collective-permute-start(f32[4,3,32]{2,1,0:T(4,128)S(1)} %get-tuple-element.32), channel_id=1, source_target_pairs={{16,0},{17,1},{18,2},{19,3},{20,4},{21,5},{22,6},{23,7},{24,8},{25... | collective-permute-start | bytes 4616 | tf_op jit(solution)/shard_map/ppermute | solution.py:101
  79.0 15.2 %collective-permute-start.13 = (f32[4,3,3]{2,1,0:T(4,128)S(1)}, f32[4,3,3]{2,1,0:T(4,128)S(1)}, u32[]{:S(2)}, u32[]{:S(2)}) collective-permute-start(f32[4,3,3]{2,1,0:T(4,128)S(1)} %get-tuple-element.28), channel_id=1, source_target_pairs={{16,1},{17,2},{18,3},{19,4},{20,5},{21,6},{22,7},{23,8},{24,9},{25... | collective-permute-start | bytes 440 | tf_op jit(solution)/shard_map/ppermute | solution.py:101
  80.9 24.7 %collective-permute-start.12 = (f32[4,32,3]{2,1,0:T(8,128)S(1)}, f32[4,32,3]{2,1,0:T(8,128)S(1)}, u32[]{:S(2)}, u32[]{:S(2)}) collective-permute-start(f32[4,32,3]{2,1,0:T(8,128)S(1)} %get-tuple-element.34), channel_id=1, source_target_pairs={{1,0},{2,1},{3,2},{4,3},{5,4},{6,5},{7,6},{8,7},{9,8},{10,9},{11,1... | collective-permute-start | bytes 4616 | tf_op jit(solution)/shard_map/ppermute | solution.py:101
  86.4 19.2 %collective-permute-start.11 = (f32[4,32,3]{2,1,0:T(8,128)S(1)}, f32[4,32,3]{2,1,0:T(8,128)S(1)}, u32[]{:S(2)}, u32[]{:S(2)}) collective-permute-start(f32[4,32,3]{2,1,0:T(8,128)S(1)} %get-tuple-element.33), channel_id=1, source_target_pairs={{0,1},{1,2},{2,3},{3,4},{4,5},{5,6},{6,7},{7,8},{8,9},{9,10},{10,1... | collective-permute-start | bytes 4616 | tf_op jit(solution)/shard_map/ppermute | solution.py:101
  88.4 9.1 %collective-permute-start.10 = (f32[4,3,3]{2,1,0:T(4,128)S(1)}, f32[4,3,3]{2,1,0:T(4,128)S(1)}, u32[]{:S(2)}, u32[]{:S(2)}) collective-permute-start(f32[4,3,3]{2,1,0:T(4,128)S(1)} %get-tuple-element.30), channel_id=1, source_target_pairs={{1,16},{2,17},{3,18},{4,19},{5,20},{6,21},{7,22},{8,23},{9,24},{10... | collective-permute-start | bytes 440 | tf_op jit(solution)/shard_map/ppermute | solution.py:101
  94.2 11.4 %collective-permute-start.9 = (f32[4,3,32]{2,1,0:T(4,128)S(1)}, f32[4,3,32]{2,1,0:T(4,128)S(1)}, u32[]{:S(2)}, u32[]{:S(2)}) collective-permute-start(f32[4,3,32]{2,1,0:T(4,128)S(1)} %get-tuple-element.31), channel_id=1, source_target_pairs={{0,16},{1,17},{2,18},{3,19},{4,20},{5,21},{6,22},{7,23},{8,24},{9,... | collective-permute-start | bytes 4616 | tf_op jit(solution)/shard_map/ppermute | solution.py:101
  97.6 8.0 %collective-permute-start.8 = (f32[4,3,3]{2,1,0:T(4,128)S(1)}, f32[4,3,3]{2,1,0:T(4,128)S(1)}, u32[]{:S(2)}, u32[]{:S(2)}) collective-permute-start(f32[4,3,3]{2,1,0:T(4,128)S(1)} %get-tuple-element.27), channel_id=1, source_target_pairs={{0,17},{1,18},{2,19},{3,20},{4,21},{5,22},{6,23},{7,24},{8,25},{9,... | collective-permute-start | bytes 440 | tf_op jit(solution)/shard_map/ppermute | solution.py:101

commit v4 on v3

--- a/solution.py
+++ b/solution.py
@@ -162,30 +162,90 @@
     flows = flows_of(matched, windows)
     source_flow = -flows
 
-    returned = jnp.sum(jnp.where(source_picker[None], flows[:, :, None], 0.0), axis=1)
-    landed = lax.all_to_all(returned, "tx", split_axis=1, concat_axis=1, tiled=True)
-    owner_flow = jnp.sum(jnp.where(owner_picker[None], landed[:, None, :], 0.0), axis=2)
-
+    n_ty = lax.axis_size("ty")
+    n_tx = lax.axis_size("tx")
+    me_y = lax.axis_index("ty")
+    me_x = lax.axis_index("tx")
     node_rows, node_cols = node_mask.shape
-    centre_y = (window_corner[0, 0] + PATCH // 2) * node_rows // tile_size
-    centre_x = (window_corner[1, 0] + PATCH // 2) * node_cols // tile_size
-    attach = (centre_y[:, None, None] == jnp.arange(node_rows, dtype=jnp.int32)[None, :, None]) & (
-        centre_x[:, None, None] == jnp.arange(node_cols, dtype=jnp.int32)[None, None, :]
-    )
-    target = jnp.sum(jnp.where(attach[None], source_flow[:, :, None, None], 0.0), axis=1)
-    count = jnp.sum(attach.astype(f32), axis=0)
-    mask = node_mask.astype(f32)
-    fields = jnp.concatenate([target, count[None], mask[None]], axis=0)
-    wide = halo(fields, ITERS_R)
-    displace = jnp.zeros((2,) + wide.shape[1:], f32)
+    w = ITERS_R
+    strips = jnp.concatenate(
+        [
+            node_mask[0:w, :].reshape(-1),
+            node_mask[node_rows - w :, :].reshape(-1),
+            node_mask[:, 0:w].reshape(-1),
+            node_mask[:, node_cols - w :].reshape(-1),
+        ]
+    )
+    facts = jnp.concatenate(
+        [window_slot[0], window_corner[0, 0], window_corner[1, 0], strips]
+    ).astype(f32)
+    all_facts = lax.all_gather(facts, ("ty", "tx")).astype(jnp.int32)
+    all_flows = lax.all_gather(flows.reshape(-1), ("ty", "tx"))
+    items = flows.shape[1]
+
+    row_flows = lax.dynamic_slice_in_dim(all_flows, me_y * n_tx, n_tx, axis=0).reshape(n_tx, 2, items)
+    row_slots = lax.dynamic_slice_in_dim(all_facts, me_y * n_tx, n_tx, axis=0)[:, 0:items]
+    src = template_slot[0] // CAP
+    rank = template_slot[0] % CAP
+    match = (jnp.arange(n_tx, dtype=jnp.int32)[None, :, None] == src[:, None, None]) & (
+        row_slots[None, :, :] == (me_x * CAP + rank)[:, None, None]
+    )
+    owner_flow = jnp.sum(
+        jnp.where(match[None], jnp.transpose(row_flows, (1, 0, 2))[:, None, :, :], 0.0), axis=(2, 3)
+    )
+
+    ext_r = node_rows + 2 * w
+    ext_c = node_cols + 2 * w
+    ids_r = jnp.arange(ext_r, dtype=jnp.int32)
+    ids_c = jnp.arange(ext_c, dtype=jnp.int32)
+    target = jnp.zeros((2, ext_r, ext_c), f32)
+    count = jnp.zeros((ext_r, ext_c), f32)
+    mask_rows = []
+    for dy in (-1, 0, 1):
+        mask_band = []
+        for dx in (-1, 0, 1):
+            ny = me_y + dy
+            nx = me_x + dx
+            inside = (ny >= 0) & (ny < n_ty) & (nx >= 0) & (nx < n_tx)
+            who = jnp.clip(ny, 0, n_ty - 1) * n_tx + jnp.clip(nx, 0, n_tx - 1)
+            fact = lax.dynamic_index_in_dim(all_facts, who, axis=0, keepdims=False)
+            flow = lax.dynamic_index_in_dim(all_flows, who, axis=0, keepdims=False).reshape(2, items)
+            corner_y = fact[items : 2 * items]
+            corner_x = fact[2 * items : 3 * items]
+            at_y = dy * node_rows + w + (corner_y + PATCH // 2) * node_rows // tile_size
+            at_x = dx * node_cols + w + (corner_x + PATCH // 2) * node_cols // tile_size
+            hit = (
+                inside
+                & (at_y[:, None, None] == ids_r[None, :, None])
+                & (at_x[:, None, None] == ids_c[None, None, :])
+            )
+            target = target + jnp.sum(jnp.where(hit[None], -flow[:, :, None, None], 0.0), axis=1)
+            count = count + jnp.sum(hit.astype(f32), axis=0)
+            base = 3 * items
+            top = fact[base : base + w * node_cols].reshape(w, node_cols)
+            bottom = fact[base + w * node_cols : base + 2 * w * node_cols].reshape(w, node_cols)
+            left = fact[base + 2 * w * node_cols : base + 2 * w * node_cols + node_rows * w].reshape(node_rows, w)
+            right = fact[base + 2 * w * node_cols + node_rows * w :].reshape(node_rows, w)
+            if dy == 0 and dx == 0:
+                piece = node_mask
+            elif dy == 0:
+                piece = right if dx == -1 else left
+            else:
+                band = bottom if dy == -1 else top
+                piece = {-1: band[:, node_cols - w :], 0: band, 1: band[:, 0:w]}[dx]
+            mask_band.append(jnp.where(inside, piece, 0).astype(f32))
+        mask_rows.append(jnp.concatenate(mask_band, axis=1))
+    mask_wide = jnp.concatenate(mask_rows, axis=0)
+
+    displace = jnp.zeros((2, ext_r, ext_c), f32)
     for sweep in range(ITERS_R):
-        lo_m, hi_m = sweep, wide.shape[1] - sweep
-        lo_t, hi_t = sweep + 1, wide.shape[1] - sweep - 1
+        lo_m, hi_m = sweep, ext_r - sweep
+        lo_c, hi_c = sweep, ext_c - sweep
         displace = relax_sweep(
             displace,
-            wide[3, lo_m:hi_m, lo_m:hi_m],
-            wide[0:2, lo_t:hi_t, lo_t:hi_t],
-            wide[2, lo_t:hi_t, lo_t:hi_t],
+            mask_wide[lo_m:hi_m, lo_c:hi_c],
+            target[:, lo_m + 1 : hi_m - 1, lo_c + 1 : hi_c - 1],
+            count[lo_m + 1 : hi_m - 1, lo_c + 1 : hi_c - 1],
         )
     return (owner_flow[:, None, :], source_flow[:, None, :], displace)
 

time: 108 us -> 181 us (1.68)
  the two profiles are of different devices: /device:TPU:48 before, /device:TPU:1 now
where the time goes in v4:
time: 181 us
  blocking collectives  117 us (65%)
  starting transfers between devices  24.2 us (13%)
  Pallas kernels  16 us (9%)
  other arithmetic  8.39 us (5%)
  matrix products  7.03 us (4%)
  local copies, waits for them, and re-layouts  6.93 us (4%)
    all_gather x1, blocking collectives, shards(): all_facts = lax.all_gather(facts, ('ty', 'tx')).astype(jnp.int32)  66.8 us
    all_gather x1, blocking collectives, shards(): all_flows = lax.all_gather(flows.reshape(-1), ('ty', 'tx'))  49.7 us
    pallas_call x1, Pallas kernels, flows_of(): pl.pallas_call(flow_kernel, grid=(n,), in_specs=[pl.BlockSpec((1, PATCH,...  16 us
    ppermute x8, starting transfers between devices, halo(): pieces[dy, dx] = lax.ppermute(part, ('ty', 'tx'), pairs)  15.7 us
    all_to_all x1, starting transfers between devices, shards(): lax.all_to_all(outgoing, 'tx', split_axis=0, concat_axis=0, tiled=True)  8.56 us
    dot_general x1, matrix products, shards(): jnp.einsum('mrc,msc->mrs', by_row.astype(jnp.bfloat16), wcol_pick, prefer...  4.69 us
  transfers between devices with their start and end apart: 9, of which 1 were waited for; matrix products, arithmetic and copies ran while one was open for 6% of the time, Pallas kernels for 0%

profile of v4, /device:TPU:1, one launch (start us, length us, event | category | flops | bytes accessed | tf_op | source)
XLA Modules:
  0.0 180.8 jit_solution(7206727391420773949)
XLA Ops:
  0.7 0.7 slice_bitcast_fusion.1
  1.5 0.2 copy-done
  1.7 1.1 fusion.11
  2.9 0.6 convolution_convert_fusion
  3.4 1.4 copy.40
  4.8 8.6 %all-to-all-start = ((bf16[32,128,128]{2,1,0:T(8,128)(2,1)}), bf16[32,128,128]{2,1,0:T(8,128)(2,1)S(1)}, u32[]{:S(2)}, u32[]{:S(2)}) async-start(bf16[32,128,128]{2,1,0:T(8,128)(2,1)} %copy.40), calls=%async_computation | async-start | bytes 2097152 | tf_op jit(solution)/shard_map/all_to_all | solution.py:149
  13.5 1.3 collective-permute-start.7
  14.8 2.9 %collective-permute-start.6 = (bf16[32,512]{1,0:T(8,128)(2,1)S(1)}, bf16[32,512]{1,0:T(8,128)(2,1)S(1)}, u32[]{:S(2)}, u32[]{:S(2)}) collective-permute-start(bf16[32,512]{1,0:T(8,128)(2,1)S(1)} %get-tuple-element.32), channel_id=1, source_target_pairs={{16,0},{17,1},{18,2},{19,3},{20,4},{21,5},{22,6},{23,7},{24,8},{25... | collective-permute-start | bytes 98312 | tf_op jit(solution)/shard_map/ppermute | solution.py:101
  17.7 2.8 %collective-permute-start.5 = (bf16[32,32]{1,0:T(8,128)(2,1)S(1)}, bf16[32,32]{1,0:T(8,128)(2,1)S(1)}, u32[]{:S(2)}, u32[]{:S(2)}) collective-permute-start(bf16[32,32]{1,0:T(8,128)(2,1)S(1)} %get-tuple-element.28), channel_id=1, source_target_pairs={{16,1},{17,2},{18,3},{19,4},{20,5},{21,6},{22,7},{23,8},{24,9},{25... | collective-permute-start | bytes 6152 | tf_op jit(solution)/shard_map/ppermute | solution.py:101
  20.6 1.3 collective-permute-start.4
  21.9 1.3 collective-permute-start.2
  23.8 66.8 %all-gather = f32[128,1,408]{2,1,0:T(1,128)S(1)} all-gather(f32[1,1,408]{2,1,0:T(1,128)S(1)} %convert_bitcast_fusion), channel_id=1, replica_groups=mesh['ty'=8,'tx'=16] {'ty','tx'}, dimensions={0}, use_global_device_ids=true | all-gather | bytes 210528 | tf_op jit(solution)/shard_map/all_gather | solution.py:182
  96.4 2.9 %collective-permute-start.3 = (bf16[512,32]{1,0:T(8,128)(2,1)S(1)}, bf16[512,32]{1,0:T(8,128)(2,1)S(1)}, u32[]{:S(2)}, u32[]{:S(2)}) collective-permute-start(bf16[512,32]{1,0:T(8,128)(2,1)S(1)} %get-tuple-element.33), channel_id=1, source_target_pairs={{0,1},{1,2},{2,3},{3,4},{4,5},{5,6},{6,7},{7,8},{8,9},{9,10},{10,1... | collective-permute-start | bytes 98312 | tf_op jit(solution)/shard_map/ppermute | solution.py:101
  99.3 1.9 %collective-permute-start.1 = (bf16[32,512]{1,0:T(8,128)(2,1)S(1)}, bf16[32,512]{1,0:T(8,128)(2,1)S(1)}, u32[]{:S(2)}, u32[]{:S(2)}) collective-permute-start(bf16[32,512]{1,0:T(8,128)(2,1)S(1)} %get-tuple-element.31), channel_id=1, source_target_pairs={{0,16},{1,17},{2,18},{3,19},{4,20},{5,21},{6,22},{7,23},{8,24},{9,... | collective-permute-start | bytes 98312 | tf_op jit(solution)/shard_map/ppermute | solution.py:101
  101.2 1.3 collective-permute-start
  102.8 0.5 collective-permute-done
  103.3 4.7 %fusion.8.w_ref = bf16[8,192,192]{2,1,0:T(8,128)(2,1)} fusion(s32[8,192]{1,0:T(8,128)S(1)} %get-tuple-element.86, s32[8,192]{1,0:T(8,128)S(1)} %get-tuple-element.87, bf16[32,32]{1,0:T(8,128)(2,1)S(1)} %collective-permute-done.7, bf16[32,512]{1,0:T(8,128)(2,1)S(1)} %collective-permute-done.6, bf16[32,32]{1,0:T(8,128)(2,1)S(1)} %collective-permute-done.5, ...), kind=kOutput, calls=%fused_computation.13 | convolution fusion | flops 1367875584 | bytes 1265664 | tf_op jit(solution)/shard_map/mrc,msc->mrs/dot_general | solution.py:155
  108.0 0.7 fusion.12
  108.7 0.7 copy.54.tf_ref
  109.4 16.0 %shard_map.94 = f32[8,8,128]{2,1,0:T(8,128)} custom-call(bf16[8,128,128]{2,1,0:T(8,128)(2,1)} %copy.54.tf_ref, bf16[8,192,192]{2,1,0:T(8,128)(2,1)} %fusion.8.w_ref), custom_call_target="tpu_custom_call" | custom-call | tf_op jit(solution)/shard_map/pallas_call | solution.py:68
  125.5 0.8 slice.363
  126.3 0.6 bitcast_negate_fusion
  127.0 49.7 %all-gather.1 = f32[128,1,16]{2,1,0:T(1,128)S(1)} all-gather(f32[1,1,16]{2,1,0:T(1,128)S(1)} %reshape.1379), channel_id=1, replica_groups=mesh['ty'=8,'tx'=16] {'ty','tx'}, dimensions={0}, use_global_device_ids=true | all-gather | bytes 8256 | tf_op jit(solution)/shard_map/all_gather | solution.py:183
  177.5 0.7 select_reduce_fusion.9
  178.4 0.2 select_reduce_fusion.1
  178.6 0.2 select_reduce_fusion.2
  178.8 0.2 select_reduce_fusion.3
  178.9 0.2 select_reduce_fusion.4
  179.1 0.2 select_reduce_fusion.5
  179.3 0.2 select_reduce_fusion.6
  179.7 0.2 select_reduce_fusion.7
  180.1 0.7 fusion.66
  (128 shorter events, 8.2 us)
Async XLA Ops:
  0.6 1.1 copy-start
  1.7 1.1 copy-start.3
  4.8 8.6 %copy-start.1 = (bf16[512,512]{1,0:T(8,128)(2,1)S(1)}, bf16[512,512]{1,0:T(8,128)(2,1)}, u32[]{:S(2)}) copy-start(bf16[512,512]{1,0:T(8,128)(2,1)} %param.8) | copy-start | bytes 1572868
  4.8 18.4 %copy-start.2 = (s32[32,32]{1,0:T(8,128)S(1)}, s32[32,32]{1,0:T(8,128)}, u32[]{:S(2)}) copy-start(s32[32,32]{1,0:T(8,128)} %param.13) | copy-start | bytes 12292
  4.8 18.5 %copy-start.5 = (s32[2,1,8]{2,1,0:T(1,128)S(1)}, s32[2,1,8]{2,1,0:T(1,128)}, u32[]{:S(2)}) copy-start(s32[2,1,8]{2,1,0:T(1,128)} %param.11) | copy-start | bytes 196
  4.8 18.9 %copy-start.4 = (s32[1,8]{1,0:T(1,128)S(1)}, s32[1,8]{1,0:T(1,128)}, u32[]{:S(2)}) copy-start(s32[1,8]{1,0:T(1,128)} %param.12) | copy-start | bytes 100
  4.8 103.2 %all-to-all-start = ((bf16[32,128,128]{2,1,0:T(8,128)(2,1)}), bf16[32,128,128]{2,1,0:T(8,128)(2,1)S(1)}, u32[]{:S(2)}, u32[]{:S(2)}) async-start(bf16[32,128,128]{2,1,0:T(8,128)(2,1)} %copy.40), calls=%async_computation | async-start | bytes 2097152 | tf_op jit(solution)/shard_map/all_to_all | solution.py:149
  13.5 82.9 %collective-permute-start.7 = (bf16[32,32]{1,0:T(8,128)(2,1)S(1)}, bf16[32,32]{1,0:T(8,128)(2,1)S(1)}, u32[]{:S(2)}, u32[]{:S(2)}) collective-permute-start(bf16[32,32]{1,0:T(8,128)(2,1)S(1)} %get-tuple-element.30), channel_id=1, source_target_pairs={{17,0},{18,1},{19,2},{20,3},{21,4},{22,5},{23,6},{24,7},{25,8},{26... | collective-permute-start | bytes 6152 | tf_op jit(solution)/shard_map/ppermute | solution.py:101
  14.8 88.5 %collective-permute-start.6 = (bf16[32,512]{1,0:T(8,128)(2,1)S(1)}, bf16[32,512]{1,0:T(8,128)(2,1)S(1)}, u32[]{:S(2)}, u32[]{:S(2)}) collective-permute-start(bf16[32,512]{1,0:T(8,128)(2,1)S(1)} %get-tuple-element.32), channel_id=1, source_target_pairs={{16,0},{17,1},{18,2},{19,3},{20,4},{21,5},{22,6},{23,7},{24,8},{25... | collective-permute-start | bytes 98312 | tf_op jit(solution)/shard_map/ppermute | solution.py:101
  17.7 81.6 %collective-permute-start.5 = (bf16[32,32]{1,0:T(8,128)(2,1)S(1)}, bf16[32,32]{1,0:T(8,128)(2,1)S(1)}, u32[]{:S(2)}, u32[]{:S(2)}) collective-permute-start(bf16[32,32]{1,0:T(8,128)(2,1)S(1)} %get-tuple-element.28), channel_id=1, source_target_pairs={{16,1},{17,2},{18,3},{19,4},{20,5},{21,6},{22,7},{23,8},{24,9},{25... | collective-permute-start | bytes 6152 | tf_op jit(solution)/shard_map/ppermute | solution.py:101
  20.6 82.7 %collective-permute-start.4 = (bf16[512,32]{1,0:T(8,128)(2,1)S(1)}, bf16[512,32]{1,0:T(8,128)(2,1)}, u32[]{:S(2)}, u32[]{:S(2)}) collective-permute-start(bf16[512,32]{1,0:T(8,128)(2,1)S(1)} %get-tuple-element.34), channel_id=1, source_target_pairs={{1,0},{2,1},{3,2},{4,3},{5,4},{6,5},{7,6},{8,7},{9,8},{10,9},{11,1... | collective-permute-start | bytes 98312 | tf_op jit(solution)/shard_map/ppermute | solution.py:101
  21.9 79.3 %collective-permute-start.2 = (bf16[32,32]{1,0:T(8,128)(2,1)S(1)}, bf16[32,32]{1,0:T(8,128)(2,1)}, u32[]{:S(2)}, u32[]{:S(2)}) collective-permute-start(bf16[32,32]{1,0:T(8,128)(2,1)S(1)} %get-tuple-element.29), channel_id=1, source_target_pairs={{1,16},{2,17},{3,18},{4,19},{5,20},{6,21},{7,22},{8,23},{9,24},{10... | collective-permute-start | bytes 6152 | tf_op jit(solution)/shard_map/ppermute | solution.py:101
  96.4 6.9 %collective-permute-start.3 = (bf16[512,32]{1,0:T(8,128)(2,1)S(1)}, bf16[512,32]{1,0:T(8,128)(2,1)S(1)}, u32[]{:S(2)}, u32[]{:S(2)}) collective-permute-start(bf16[512,32]{1,0:T(8,128)(2,1)S(1)} %get-tuple-element.33), channel_id=1, source_target_pairs={{0,1},{1,2},{2,3},{3,4},{4,5},{5,6},{6,7},{7,8},{8,9},{9,10},{10,1... | collective-permute-start | bytes 98312 | tf_op jit(solution)/shard_map/ppermute | solution.py:101
  99.3 4.0 %collective-permute-start.1 = (bf16[32,512]{1,0:T(8,128)(2,1)S(1)}, bf16[32,512]{1,0:T(8,128)(2,1)S(1)}, u32[]{:S(2)}, u32[]{:S(2)}) collective-permute-start(bf16[32,512]{1,0:T(8,128)(2,1)S(1)} %get-tuple-element.31), channel_id=1, source_target_pairs={{0,16},{1,17},{2,18},{3,19},{4,20},{5,21},{6,22},{7,23},{8,24},{9,... | collective-permute-start | bytes 98312 | tf_op jit(solution)/shard_map/ppermute | solution.py:101
  101.2 2.1 %collective-permute-start = (bf16[32,32]{1,0:T(8,128)(2,1)S(1)}, bf16[32,32]{1,0:T(8,128)(2,1)S(1)}, u32[]{:S(2)}, u32[]{:S(2)}) collective-permute-start(bf16[32,32]{1,0:T(8,128)(2,1)S(1)} %get-tuple-element.27), channel_id=1, source_target_pairs={{0,17},{1,18},{2,19},{3,20},{4,21},{5,22},{6,23},{7,24},{8,25},{9,... | collective-permute-start | bytes 6152 | tf_op jit(solution)/shard_map/ppermute | solution.py:101

commit v5 on v3

--- a/solution.py
+++ b/solution.py
@@ -146,9 +146,89 @@
     outgoing = jnp.einsum(
         "ks,kri->sri", owner_picker.astype(jnp.bfloat16), tflipped, preferred_element_type=f32
     ).astype(jnp.bfloat16)
-    arrived = lax.all_to_all(outgoing, "tx", split_axis=0, concat_axis=0, tiled=True)
-
-    b_wide = halo(section_b, RADIUS)
+
+    n_tx = lax.axis_size("tx")
+    n_ty = lax.axis_size("ty")
+    me_x = lax.axis_index("tx")
+    tx_ids = jnp.arange(n_tx, dtype=jnp.int32)
+    to_left = (tx_ids == me_x - 1)[:, None]
+    to_right = (tx_ids == me_x + 1)[:, None]
+
+    def side_payload(left, right):
+        lf = left.reshape(1, -1)
+        rf = right.reshape(1, -1)
+        return jnp.where(to_left, lf, jnp.where(to_right, rf, jnp.zeros_like(lf)))
+
+    def side_arrivals(got, shape):
+        left = lax.dynamic_index_in_dim(got, jnp.maximum(me_x - 1, 0), axis=0, keepdims=False)
+        right = lax.dynamic_index_in_dim(got, jnp.minimum(me_x + 1, n_tx - 1), axis=0, keepdims=False)
+        left = jnp.where(me_x >= 1, left, jnp.zeros_like(left)).reshape(shape)
+        right = jnp.where(me_x + 1 < n_tx, right, jnp.zeros_like(right)).reshape(shape)
+        return left, right
+
+    def rows_exchange(cells, width):
+        count = n_ty
+        height = cells.shape[-2]
+        head = cells[..., 0:width, :]
+        tail = cells[..., height - width : height, :]
+        above = lax.ppermute(tail, "ty", [(i, i + 1) for i in range(count - 1)])
+        below = lax.ppermute(head, "ty", [(i + 1, i) for i in range(count - 1)])
+        return above, below
+
+    node_rows, node_cols = node_mask.shape
+    centre_y = (window_corner[0, 0] + PATCH // 2) * node_rows // tile_size
+    centre_x = (window_corner[1, 0] + PATCH // 2) * node_cols // tile_size
+    attach = (centre_y[:, None, None] == jnp.arange(node_rows, dtype=jnp.int32)[None, :, None]) & (
+        centre_x[:, None, None] == jnp.arange(node_cols, dtype=jnp.int32)[None, None, :]
+    )
+    count = jnp.sum(attach.astype(f32), axis=0)
+    mask = node_mask.astype(f32)
+    fixed = jnp.stack([count, mask]).astype(jnp.bfloat16)
+    w = ITERS_R
+    b_cols = section_b.shape[1]
+    send = jnp.concatenate(
+        [
+            outgoing.reshape(n_tx, -1),
+            side_payload(section_b[:, 0:RADIUS], section_b[:, b_cols - RADIUS :]),
+            side_payload(fixed[:, :, 0:w], fixed[:, :, node_cols - w :]),
+        ],
+        axis=1,
+    )
+    got = lax.all_to_all(send, "tx", split_axis=0, concat_axis=0, tiled=True)
+    t_len = outgoing.size // n_tx
+    b_len = section_b.shape[0] * RADIUS
+    arrived = got[:, 0:t_len].reshape(outgoing.shape)
+    b_left, b_right = side_arrivals(got[:, t_len : t_len + b_len], (section_b.shape[0], RADIUS))
+    f_left, f_right = side_arrivals(got[:, t_len + b_len :], (2, node_rows, w))
+    b_tx = jnp.concatenate([b_left, section_b, b_right], axis=1)
+    fixed_tx = jnp.concatenate([f_left, fixed, f_right], axis=2)
+
+    b_len_row = RADIUS * b_tx.shape[1]
+    stacked_head = jnp.concatenate(
+        [b_tx[0:RADIUS].reshape(-1), fixed_tx[:, 0:w].reshape(-1)]
+    )
+    stacked_tail = jnp.concatenate(
+        [b_tx[b_tx.shape[0] - RADIUS :].reshape(-1), fixed_tx[:, node_rows - w :].reshape(-1)]
+    )
+    above = lax.ppermute(stacked_tail, "ty", [(i, i + 1) for i in range(n_ty - 1)])
+    below = lax.ppermute(stacked_head, "ty", [(i + 1, i) for i in range(n_ty - 1)])
+    b_wide = jnp.concatenate(
+        [
+            above[0:b_len_row].reshape(RADIUS, -1),
+            b_tx,
+            below[0:b_len_row].reshape(RADIUS, -1),
+        ],
+        axis=0,
+    )
+    fixed_wide = jnp.concatenate(
+        [
+            above[b_len_row:].reshape(2, w, -1),
+            fixed_tx,
+            below[b_len_row:].reshape(2, w, -1),
+        ],
+        axis=1,
+    ).astype(f32)
+
     wrow_pick = one_hot(window_corner[0, 0], WIN, b_wide.shape[0])
     wcol_pick = one_hot(window_corner[1, 0], WIN, b_wide.shape[1])
     by_row = jnp.einsum("mra,ac->mrc", wrow_pick, b_wide, preferred_element_type=f32)
@@ -162,21 +242,24 @@
     flows = flows_of(matched, windows)
     source_flow = -flows
 
+    target = jnp.sum(jnp.where(attach[None], source_flow[:, :, None, None], 0.0), axis=1)
     returned = jnp.sum(jnp.where(source_picker[None], flows[:, :, None], 0.0), axis=1)
-    landed = lax.all_to_all(returned, "tx", split_axis=1, concat_axis=1, tiled=True)
+    back = jnp.concatenate(
+        [
+            returned.reshape(2, n_tx, CAP).transpose(1, 0, 2).reshape(n_tx, -1),
+            side_payload(target[:, :, 0:w], target[:, :, node_cols - w :]),
+        ],
+        axis=1,
+    )
+    came = lax.all_to_all(back, "tx", split_axis=0, concat_axis=0, tiled=True)
+    landed = came[:, 0 : 2 * CAP].reshape(n_tx, 2, CAP).transpose(1, 0, 2).reshape(2, -1)
     owner_flow = jnp.sum(jnp.where(owner_picker[None], landed[:, None, :], 0.0), axis=2)
-
-    node_rows, node_cols = node_mask.shape
-    centre_y = (window_corner[0, 0] + PATCH // 2) * node_rows // tile_size
-    centre_x = (window_corner[1, 0] + PATCH // 2) * node_cols // tile_size
-    attach = (centre_y[:, None, None] == jnp.arange(node_rows, dtype=jnp.int32)[None, :, None]) & (
-        centre_x[:, None, None] == jnp.arange(node_cols, dtype=jnp.int32)[None, None, :]
-    )
-    target = jnp.sum(jnp.where(attach[None], source_flow[:, :, None, None], 0.0), axis=1)
-    count = jnp.sum(attach.astype(f32), axis=0)
-    mask = node_mask.astype(f32)
-    fields = jnp.concatenate([target, count[None], mask[None]], axis=0)
-    wide = halo(fields, ITERS_R)
+    t_left, t_right = side_arrivals(came[:, 2 * CAP :], (2, node_rows, w))
+    target_tx = jnp.concatenate([t_left, target, t_right], axis=2)
+    t_above, t_below = rows_exchange(target_tx, w)
+    target_wide = jnp.concatenate([t_above, target_tx, t_below], axis=1)
+
+    wide = jnp.concatenate([target_wide, fixed_wide], axis=0)
     displace = jnp.zeros((2,) + wide.shape[1:], f32)
     for sweep in range(ITERS_R):
         lo_m, hi_m = sweep, wide.shape[1] - sweep

time: 108 us -> 117 us (1.083)
  the two profiles are of different devices: /device:TPU:48 before, /device:TPU:1 now
where the time goes in v5:
time: 117 us
  waiting for transfers between devices  30.1 us (26%)
  local copies, waits for them, and re-layouts  26.6 us (23%)
  starting transfers between devices  26.2 us (22%)
  Pallas kernels  16 us (14%)
  other arithmetic  9.88 us (8%)
  matrix products  6.74 us (6%)
    all_to_all x1, waiting for transfers between devices, shards(): got = lax.all_to_all(send, 'tx', split_axis=0, concat_axis=0, tiled=True)  21.7 us
    pallas_call x1, Pallas kernels, flows_of(): pl.pallas_call(flow_kernel, grid=(n,), in_specs=[pl.BlockSpec((1, PATCH,...  16 us
    unnamed x20, local copies, waits for them, and re-layouts  14.4 us
    all_to_all x1, starting transfers between devices, shards(): got = lax.all_to_all(send, 'tx', split_axis=0, concat_axis=0, tiled=True)  8.55 us
    all_to_all x1, waiting for transfers between devices, shards(): came = lax.all_to_all(back, 'tx', split_axis=0, concat_axis=0, tiled=True)  6.21 us
    ppermute x1, starting transfers between devices, shards(): lax.ppermute(stacked_tail, 'ty', [(i, i + 1) for i in range(n_ty - 1)])  5.46 us
    ppermute x1, starting transfers between devices, rows_exchange(): above = lax.ppermute(tail, 'ty', [(i, i + 1) for i in range(count - 1)])  4.66 us
    dot_general x1, matrix products, shards(): jnp.einsum('mrc,msc->mrs', by_row.astype(jnp.bfloat16), wcol_pick, prefer...  3.75 us
  transfers between devices with their start and end apart: 6, of which 4 were waited for; matrix products, arithmetic and copies ran while one was open for 6% of the time, Pallas kernels for 0%

profile of v5, /device:TPU:1, one launch (start us, length us, event | category | flops | bytes accessed | tf_op | source)
XLA Modules:
  0.0 116.6 jit_solution(16898040314976739061)
XLA Ops:
  0.7 0.7 and_select_fusion.1
  1.4 0.7 fusion.63
  2.7 1.1 fusion.72
  4.0 0.7 slice_bitcast_fusion.8
  4.8 1.1 fusion.11
  8.3 2.5 %reduce.16 = bf16[16,49344]{1,0:T(8,128)(2,1)} reduce(bf16[16,1,49344]{2,0,1:T(8,128)(2,1)S(1)} %maximum_bitcast_fusion, bf16[]{:T(256)} %broadcast.351), dimensions={1}, to_apply=%copy.54.reduce_sub_computation | reduce | bytes 3158018 | tf_op jit(solution)/shard_map/all_to_all | solution.py:197
  10.8 3.1 %reshape.402 = bf16[16,2,24672]{2,1,0:T(2,128)(2,1)} reshape(bf16[16,49344]{1,0:T(8,128)(2,1)} %reduce.16) | data formatting | bytes 3158016
  13.8 8.5 %all-to-all-start = ((bf16[16,2,24672]{2,1,0:T(2,128)(2,1)}), bf16[16,2,24672]{2,1,0:T(2,128)(2,1)S(1)}, u32[]{:S(2)}, u32[]{:S(2)}) async-start(bf16[16,2,24672]{2,1,0:T(2,128)(2,1)} %reshape.402), calls=%async_computation | async-start | bytes 3162112 | tf_op jit(solution)/shard_map/all_to_all | solution.py:197
  22.4 0.6 iota_compare_fusion.27
  23.1 0.6 iota_compare_fusion.26
  23.9 21.7 %all-to-all-done = bf16[16,2,24672]{2,1,0:T(2,128)(2,1)S(1)} async-done(((bf16[16,2,24672]{2,1,0:T(2,128)(2,1)}), bf16[16,2,24672]{2,1,0:T(2,128)(2,1)S(1)}, u32[]{:S(2)}, u32[]{:S(2)}) %all-to-all-start) | async-done | bytes 1579040 | tf_op jit(solution)/shard_map/all_to_all | solution.py:197
  45.6 9.0 %reshape.403 = bf16[16,1,49344]{2,1,0:T(2,128)(2,1)} reshape(bf16[16,2,24672]{2,1,0:T(2,128)(2,1)S(1)} %all-to-all-done) | data formatting | bytes 3158016
  54.6 2.1 %copy.75 = bf16[16,1,49344]{2,0,1:T(8,128)(2,1)S(1)} copy(bf16[16,1,49344]{2,1,0:T(2,128)(2,1)} %reshape.403) | data formatting | bytes 3158016
  58.5 5.5 %collective-permute-start = (bf16[18660]{0:T(1024)(128)(2,1)S(1)}, bf16[18660]{0:T(1024)(128)(2,1)}, u32[]{:S(2)}, u32[]{:S(2)}) collective-permute-start(bf16[18660]{0:T(1024)(128)(2,1)S(1)} %pad_maximum_fusion.4), channel_id=1, source_target_pairs={{0,16},{16,32},{32,48},{48,64},{64,80},{80,96},{96,112},{1,17},{17... | collective-permute-start | bytes 111968 | tf_op jit(solution)/shard_map/ppermute | solution.py:213
  64.8 2.1 %collective-permute-start.1 = (bf16[18660]{0:T(1024)(128)(2,1)}, bf16[18660]{0:T(1024)(128)(2,1)}, u32[]{:S(2)}, u32[]{:S(2)}) collective-permute-start(bf16[18660]{0:T(1024)(128)(2,1)} %pad_maximum_fusion.5), channel_id=1, source_target_pairs={{16,0},{32,16},{48,32},{64,48},{80,64},{96,80},{112,96},{17,1},{33... | collective-permute-start | bytes 111968 | tf_op jit(solution)/shard_map/ppermute | solution.py:214
  67.4 1.3 %fusion.12 = bf16[8,128,128]{2,0,1:T(8,128)(2,1)S(1)} fusion(bf16[32,128,128]{2,1,0:T(8,128)(2,1)S(1)} %reshape.370, s32[8]{0:T(128)} %bitcast.86), kind=kOutput, calls=%fused_computation.17 | convolution fusion | flops 8388864 | bytes 1310752 | tf_op jit(solution)/shard_map/ms,sri->mri/dot_general | solution.py:238
  68.7 0.7 copy.74.tf_ref
  69.5 0.7 slice.249
  70.4 0.7 slice.250
  71.6 0.8 slice.243
  72.5 0.8 slice.244
  73.4 3.7 %fusion.8.w_ref = bf16[8,192,192]{2,1,0:T(8,128)(2,1)} fusion(s32[8,192]{1,0:T(8,128)S(1)} %get-tuple-element.60, s32[8,192]{1,0:T(8,128)S(1)} %get-tuple-element.61, bf16[32,576]{1,0:T(8,128)(2,1)S(1)} %reshape.376, bf16[512,32]{1,0:T(8,128)(2,1)S(1)} %select_n.137, bf16[512,512]{1,0:T(8,128)(2,1)S(1)} %copy-done.1, bf16[512,32]{1,0:T(8,128)(2,1)S(1)} %select_n.133, ...), kind=kOutput, calls=%fused_computation.15 | convolution fusion | flops 1365221376 | bytes 1265664 | tf_op jit(solution)/shard_map/mrc,msc->mrs/dot_general | solution.py:235
  77.1 16.0 %shard_map.94 = f32[8,8,128]{2,1,0:T(8,128)} custom-call(bf16[8,128,128]{2,1,0:T(8,128)(2,1)} %copy.74.tf_ref, bf16[8,192,192]{2,1,0:T(8,128)(2,1)} %fusion.8.w_ref), custom_call_target="tpu_custom_call" | custom-call | tf_op jit(solution)/shard_map/pallas_call | solution.py:68
  93.1 0.8 slice.245
  95.0 0.6 copy.60
  95.6 3.5 %all-to-all-start.1 = ((f32[16,1,196]{2,1,0:T(1,128)}), f32[16,1,196]{2,1,0:T(1,128)S(1)}, u32[]{:S(2)}, u32[]{:S(2)}) async-start(f32[16,1,196]{2,1,0:T(1,128)} %copy.60), calls=%async_computation.1 | async-start | bytes 32768 | tf_op jit(solution)/shard_map/all_to_all | solution.py:254
  99.3 6.2 %all-to-all-done.1 = f32[16,1,196]{2,1,0:T(1,128)S(1)} async-done(((f32[16,1,196]{2,1,0:T(1,128)}), f32[16,1,196]{2,1,0:T(1,128)S(1)}, u32[]{:S(2)}, u32[]{:S(2)}) %all-to-all-start.1) | async-done | bytes 12576 | tf_op jit(solution)/shard_map/all_to_all | solution.py:254
  105.9 4.7 %collective-permute-start.2 = (f32[2,3,38]{2,1,0:T(4,128)S(1)}, f32[2,3,38]{2,1,0:T(4,128)S(1)}, u32[]{:S(2)}, u32[]{:S(2)}) collective-permute-start(f32[2,3,38]{2,1,0:T(4,128)S(1)} %get-tuple-element.28), channel_id=1, source_target_pairs={{0,16},{16,32},{32,48},{48,64},{64,80},{80,96},{96,112},{1,17},{17... | collective-permute-start | bytes 2744 | tf_op jit(solution)/shard_map/ppermute | solution.py:174
  110.6 1.9 %collective-permute-start.3 = (f32[2,3,38]{2,1,0:T(4,128)S(1)}, f32[2,3,38]{2,1,0:T(4,128)S(1)}, u32[]{:S(2)}, u32[]{:S(2)}) collective-permute-start(f32[2,3,38]{2,1,0:T(4,128)S(1)} %get-tuple-element.29), channel_id=1, source_target_pairs={{16,0},{32,16},{48,32},{64,48},{80,64},{96,80},{112,96},{17,1},{33... | collective-permute-start | bytes 2744 | tf_op jit(solution)/shard_map/ppermute | solution.py:175
  112.8 0.7 select_reduce_fusion.1
  113.5 2.1 %collective-permute-done.3 = f32[2,3,38]{2,1,0:T(4,128)S(1)} collective-permute-done((f32[2,3,38]{2,1,0:T(4,128)S(1)}, f32[2,3,38]{2,1,0:T(4,128)S(1)}, u32[]{:S(2)}, u32[]{:S(2)}) %collective-permute-start.3) | collective-permute-done | bytes 944 | tf_op jit(solution)/shard_map/ppermute | solution.py:175
  115.9 0.7 fusion.55
  (94 shorter events, 9.6 us)
Async XLA Ops:
  0.6 4.2 %copy-start = (bf16[512,512]{1,0:T(8,128)(2,1)S(1)}, bf16[512,512]{1,0:T(8,128)(2,1)}, u32[]{:S(2)}) copy-start(bf16[512,512]{1,0:T(8,128)(2,1)} %param.7) | copy-start | bytes 1572868
  4.0 1.9 %copy-start.6 = (s32[1,8]{1,0:T(1,128)S(1)}, s32[1,8]{1,0:T(1,128)}, u32[]{:S(2)}) copy-start(s32[1,8]{1,0:T(1,128)} %param.10) | copy-start | bytes 100
  13.8 8.6 %copy-start.3 = (s32[2,1,8]{2,1,0:T(1,128)S(1)}, s32[2,1,8]{2,1,0:T(1,128)}, u32[]{:S(2)}) copy-start(s32[2,1,8]{2,1,0:T(1,128)} %param.11) | copy-start | bytes 196
  13.8 9.2 %copy-start.7 = (s32[1,8]{1,0:T(1,128)S(1)}, s32[1,8]{1,0:T(1,128)}, u32[]{:S(2)}) copy-start(s32[1,8]{1,0:T(1,128)} %param.12) | copy-start | bytes 100
  13.8 31.8 %all-to-all-start = ((bf16[16,2,24672]{2,1,0:T(2,128)(2,1)}), bf16[16,2,24672]{2,1,0:T(2,128)(2,1)S(1)}, u32[]{:S(2)}, u32[]{:S(2)}) async-start(bf16[16,2,24672]{2,1,0:T(2,128)(2,1)} %reshape.402), calls=%async_computation | async-start | bytes 3162112 | tf_op jit(solution)/shard_map/all_to_all | solution.py:197
  56.7 1.0 copy-start.1
  58.5 11.0 %collective-permute-start = (bf16[18660]{0:T(1024)(128)(2,1)S(1)}, bf16[18660]{0:T(1024)(128)(2,1)}, u32[]{:S(2)}, u32[]{:S(2)}) collective-permute-start(bf16[18660]{0:T(1024)(128)(2,1)S(1)} %pad_maximum_fusion.4), channel_id=1, source_target_pairs={{0,16},{16,32},{32,48},{48,64},{64,80},{80,96},{96,112},{1,17},{17... | collective-permute-start | bytes 111968 | tf_op jit(solution)/shard_map/ppermute | solution.py:213
  64.8 5.6 %collective-permute-start.1 = (bf16[18660]{0:T(1024)(128)(2,1)}, bf16[18660]{0:T(1024)(128)(2,1)}, u32[]{:S(2)}, u32[]{:S(2)}) collective-permute-start(bf16[18660]{0:T(1024)(128)(2,1)} %pad_maximum_fusion.5), channel_id=1, source_target_pairs={{16,0},{32,16},{48,32},{64,48},{80,64},{96,80},{112,96},{17,1},{33... | collective-permute-start | bytes 111968 | tf_op jit(solution)/shard_map/ppermute | solution.py:214
  73.4 21.1 %copy-start.5 = (pred[8,32]{1,0:T(8,128)(4,1)S(1)}, pred[8,32]{1,0:T(8,128)(4,1)}, u32[]{:S(2)}) copy-start(pred[8,32]{1,0:T(8,128)(4,1)} %iota_compare_fusion.26) | copy-start | bytes 772
  77.1 35.7 %copy-start.4 = (pred[8,32]{1,0:T(8,128)(4,1)S(1)}, pred[8,32]{1,0:T(8,128)(4,1)}, u32[]{:S(2)}) copy-start(pred[8,32]{1,0:T(8,128)(4,1)} %iota_compare_fusion.27) | copy-start | bytes 772
  94.0 22.6 %copy-start.2 = (f32[2,8]{1,0:T(2,128)}, f32[2,8]{1,0:T(2,128)S(1)}, u32[]{:S(2)}) copy-start(f32[2,8]{1,0:T(2,128)S(1)} %bitcast_negate_fusion) | copy-start | bytes 196
  95.6 9.9 %all-to-all-start.1 = ((f32[16,1,196]{2,1,0:T(1,128)}), f32[16,1,196]{2,1,0:T(1,128)S(1)}, u32[]{:S(2)}, u32[]{:S(2)}) async-start(f32[16,1,196]{2,1,0:T(1,128)} %copy.60), calls=%async_computation.1 | async-start | bytes 32768 | tf_op jit(solution)/shard_map/all_to_all | solution.py:254
  105.9 7.5 %collective-permute-start.2 = (f32[2,3,38]{2,1,0:T(4,128)S(1)}, f32[2,3,38]{2,1,0:T(4,128)S(1)}, u32[]{:S(2)}, u32[]{:S(2)}) collective-permute-start(f32[2,3,38]{2,1,0:T(4,128)S(1)} %get-tuple-element.28), channel_id=1, source_target_pairs={{0,16},{16,32},{32,48},{48,64},{64,80},{80,96},{96,112},{1,17},{17... | collective-permute-start | bytes 2744 | tf_op jit(solution)/shard_map/ppermute | solution.py:174
  110.6 4.9 %collective-permute-start.3 = (f32[2,3,38]{2,1,0:T(4,128)S(1)}, f32[2,3,38]{2,1,0:T(4,128)S(1)}, u32[]{:S(2)}, u32[]{:S(2)}) collective-permute-start(f32[2,3,38]{2,1,0:T(4,128)S(1)} %get-tuple-element.29), channel_id=1, source_target_pairs={{16,0},{32,16},{48,32},{64,48},{80,64},{96,80},{112,96},{17,1},{33... | collective-permute-start | bytes 2744 | tf_op jit(solution)/shard_map/ppermute | solution.py:175

commit v6 on v5

--- a/solution.py
+++ b/solution.py
@@ -183,51 +183,9 @@
     )
     count = jnp.sum(attach.astype(f32), axis=0)
     mask = node_mask.astype(f32)
-    fixed = jnp.stack([count, mask]).astype(jnp.bfloat16)
     w = ITERS_R
-    b_cols = section_b.shape[1]
-    send = jnp.concatenate(
-        [
-            outgoing.reshape(n_tx, -1),
-            side_payload(section_b[:, 0:RADIUS], section_b[:, b_cols - RADIUS :]),
-            side_payload(fixed[:, :, 0:w], fixed[:, :, node_cols - w :]),
-        ],
-        axis=1,
-    )
-    got = lax.all_to_all(send, "tx", split_axis=0, concat_axis=0, tiled=True)
-    t_len = outgoing.size // n_tx
-    b_len = section_b.shape[0] * RADIUS
-    arrived = got[:, 0:t_len].reshape(outgoing.shape)
-    b_left, b_right = side_arrivals(got[:, t_len : t_len + b_len], (section_b.shape[0], RADIUS))
-    f_left, f_right = side_arrivals(got[:, t_len + b_len :], (2, node_rows, w))
-    b_tx = jnp.concatenate([b_left, section_b, b_right], axis=1)
-    fixed_tx = jnp.concatenate([f_left, fixed, f_right], axis=2)
-
-    b_len_row = RADIUS * b_tx.shape[1]
-    stacked_head = jnp.concatenate(
-        [b_tx[0:RADIUS].reshape(-1), fixed_tx[:, 0:w].reshape(-1)]
-    )
-    stacked_tail = jnp.concatenate(
-        [b_tx[b_tx.shape[0] - RADIUS :].reshape(-1), fixed_tx[:, node_rows - w :].reshape(-1)]
-    )
-    above = lax.ppermute(stacked_tail, "ty", [(i, i + 1) for i in range(n_ty - 1)])
-    below = lax.ppermute(stacked_head, "ty", [(i + 1, i) for i in range(n_ty - 1)])
-    b_wide = jnp.concatenate(
-        [
-            above[0:b_len_row].reshape(RADIUS, -1),
-            b_tx,
-            below[0:b_len_row].reshape(RADIUS, -1),
-        ],
-        axis=0,
-    )
-    fixed_wide = jnp.concatenate(
-        [
-            above[b_len_row:].reshape(2, w, -1),
-            fixed_tx,
-            below[b_len_row:].reshape(2, w, -1),
-        ],
-        axis=1,
-    ).astype(f32)
+    arrived = lax.all_to_all(outgoing, "tx", split_axis=0, concat_axis=0, tiled=True)
+    b_wide = halo(section_b, RADIUS)
 
     wrow_pick = one_hot(window_corner[0, 0], WIN, b_wide.shape[0])
     wcol_pick = one_hot(window_corner[1, 0], WIN, b_wide.shape[1])
@@ -243,23 +201,23 @@
     source_flow = -flows
 
     target = jnp.sum(jnp.where(attach[None], source_flow[:, :, None, None], 0.0), axis=1)
+    fields = jnp.concatenate([target, count[None], mask[None]], axis=0)
     returned = jnp.sum(jnp.where(source_picker[None], flows[:, :, None], 0.0), axis=1)
     back = jnp.concatenate(
         [
             returned.reshape(2, n_tx, CAP).transpose(1, 0, 2).reshape(n_tx, -1),
-            side_payload(target[:, :, 0:w], target[:, :, node_cols - w :]),
+            side_payload(fields[:, :, 0:w], fields[:, :, node_cols - w :]),
         ],
         axis=1,
     )
     came = lax.all_to_all(back, "tx", split_axis=0, concat_axis=0, tiled=True)
     landed = came[:, 0 : 2 * CAP].reshape(n_tx, 2, CAP).transpose(1, 0, 2).reshape(2, -1)
     owner_flow = jnp.sum(jnp.where(owner_picker[None], landed[:, None, :], 0.0), axis=2)
-    t_left, t_right = side_arrivals(came[:, 2 * CAP :], (2, node_rows, w))
-    target_tx = jnp.concatenate([t_left, target, t_right], axis=2)
-    t_above, t_below = rows_exchange(target_tx, w)
-    target_wide = jnp.concatenate([t_above, target_tx, t_below], axis=1)
-
-    wide = jnp.concatenate([target_wide, fixed_wide], axis=0)
+    f_left, f_right = side_arrivals(came[:, 2 * CAP :], (fields.shape[0], node_rows, w))
+    fields_tx = jnp.concatenate([f_left, fields, f_right], axis=2)
+    f_above, f_below = rows_exchange(fields_tx, w)
+    wide = jnp.concatenate([f_above, fields_tx, f_below], axis=1)
+
     displace = jnp.zeros((2,) + wide.shape[1:], f32)
     for sweep in range(ITERS_R):
         lo_m, hi_m = sweep, wide.shape[1] - sweep

time: 117 us -> 90.9 us (0.78)
  local copies, waits for them, and re-layouts: 26.6 us -> 6.44 us
  starting transfers between devices: 26.2 us -> 45 us
  waiting for transfers between devices: 30.1 us -> 12.7 us
  other arithmetic: 9.88 us -> 3.09 us
    all_to_all x1, waiting for transfers between devices: 21.7 us -> 0.01 us  [shards(): lax.all_to_all(outgoing, 'tx', split_axis=0, concat_axis=0, tiled=True)]
    unnamed x20 -> x15, local copies, waits for them, and re-layouts: 14.4 us -> 0.28 us
    ppermute x2 -> x8, starting transfers between devices: 7.55 us -> 18.2 us  [halo(): pieces[dy, dx] = lax.ppermute(part, ('ty', 'tx'), pairs)]
    all_to_all x1, starting transfers between devices: 3.49 us -> 11.1 us  [shards(): came = lax.all_to_all(back, 'tx', split_axis=0, concat_axis=0, tiled=True)]
    ppermute x2 -> x8, waiting for transfers between devices: 0.14 us -> 6.24 us  [halo(): pieces[dy, dx] = lax.ppermute(part, ('ty', 'tx'), pairs)]
    slice x10 -> x5, local copies, waits for them, and re-layouts: 4.23 us -> 0.35 us  [the longest x3 0.19 us: halo(): part = cells[..., rows[0]:rows[1], cols[0]:cols[1]]]
    all_to_all x3 -> x0, other arithmetic: 2.69 us -> none  [the longest x2 2.6 us: shards(): got = lax.all_to_all(send, 'tx', split_axis=0, concat_axis=0, tiled=True)]
    ppermute x1, waiting for transfers between devices: 2.07 us -> 0.01 us  [rows_exchange(): below = lax.ppermute(head, 'ty', [(i + 1, i) for i in range(count - 1)])]
  transfers between devices with their start and end apart: 6 -> 12, of which waited for: 4 -> 4; matrix products, arithmetic and copies ran while one was open for 6% -> 6% of each run, Pallas kernels for 0% -> 0%
where the time goes in v6:
time: 90.9 us; the launch traced here: 90.3 us
  starting transfers between devices  45 us (50%)
  Pallas kernels  16 us (18%)
  waiting for transfers between devices  12.7 us (14%)
  local copies, waits for them, and re-layouts  6.44 us (7%)
  matrix products  6.1 us (7%)
  other arithmetic  3.09 us (3%)
  between operations  1 us (1%)
    ppermute x8, starting transfers between devices, halo(): pieces[dy, dx] = lax.ppermute(part, ('ty', 'tx'), pairs)  18.2 us
    pallas_call x1, Pallas kernels, flows_of(): pl.pallas_call(flow_kernel, grid=(n,), in_specs=[pl.BlockSpec((1, PATCH,...  16 us
    all_to_all x1, starting transfers between devices, shards(): came = lax.all_to_all(back, 'tx', split_axis=0, concat_axis=0, tiled=True)  11.1 us
    all_to_all x1, starting transfers between devices, shards(): lax.all_to_all(outgoing, 'tx', split_axis=0, concat_axis=0, tiled=True)  8.56 us
    all_to_all x1, waiting for transfers between devices, shards(): came = lax.all_to_all(back, 'tx', split_axis=0, concat_axis=0, tiled=True)  6.38 us
    ppermute x8, waiting for transfers between devices, halo(): pieces[dy, dx] = lax.ppermute(part, ('ty', 'tx'), pairs)  6.24 us
    ppermute x1, starting transfers between devices, rows_exchange(): above = lax.ppermute(tail, 'ty', [(i, i + 1) for i in range(count - 1)])  3.88 us
    dot_general x1, matrix products, shards(): jnp.einsum('mrc,msc->mrs', by_row.astype(jnp.bfloat16), wcol_pick, prefer...  3.76 us
  transfers between devices with their start and end apart: 12, of which 4 were waited for; matrix products, arithmetic and copies ran while one was open for 6% of the time, Pallas kernels for 0%

profile of v6, /device:TPU:1, one launch (start us, length us, event | category | flops | bytes accessed | tf_op | source)
XLA Modules:
  0.0 90.3 jit_solution(6179149573505791191)
XLA Ops:
  0.7 0.7 slice_bitcast_fusion.7
  1.5 0.2 copy-done
  1.7 1.1 %fusion.11 = bf16[8,128,128]{2,1,0:T(8,128)(2,1)S(1)} fusion(s32[8,128]{1,0:T(8,128)S(1)} %get-tuple-element.49, s32[8,128]{1,0:T(8,128)S(1)} %get-tuple-element.50, bf16[512,512]{1,0:T(8,128)(2,1)S(1)} %copy-done), kind=kOutput, calls=%fused_computation.14 | convolution fusion | flops 672792576 | bytes 794624 | tf_op jit(solution)/shard_map/kra,kia->kri/dot_general | solution.py:143
  2.9 0.6 convolution_convert_fusion
  3.4 1.4 %copy.36 = bf16[32,128,128]{2,1,0:T(8,128)(2,1)} copy(bf16[32,128,128]{2,0,1:T(8,128)(2,1)S(1)} %convolution_convert_fusion) | data formatting | bytes 2097152 | tf_op jit(solution)/shard_map/convert_element_type | solution.py:148
  4.8 8.6 %all-to-all-start = ((bf16[32,128,128]{2,1,0:T(8,128)(2,1)}), bf16[32,128,128]{2,1,0:T(8,128)(2,1)S(1)}, u32[]{:S(2)}, u32[]{:S(2)}) async-start(bf16[32,128,128]{2,1,0:T(8,128)(2,1)} %copy.36), calls=%async_computation | async-start | bytes 2097152 | tf_op jit(solution)/shard_map/all_to_all | solution.py:187
  13.5 1.3 %collective-permute-start.7 = (bf16[32,32]{1,0:T(8,128)(2,1)S(1)}, bf16[32,32]{1,0:T(8,128)(2,1)S(1)}, u32[]{:S(2)}, u32[]{:S(2)}) collective-permute-start(bf16[32,32]{1,0:T(8,128)(2,1)S(1)} %get-tuple-element.20), channel_id=1, source_target_pairs={{17,0},{18,1},{19,2},{20,3},{21,4},{22,5},{23,6},{24,7},{25,8},{26... | collective-permute-start | bytes 6152 | tf_op jit(solution)/shard_map/ppermute | solution.py:101
  14.8 2.9 %collective-permute-start.6 = (bf16[32,512]{1,0:T(8,128)(2,1)S(1)}, bf16[32,512]{1,0:T(8,128)(2,1)S(1)}, u32[]{:S(2)}, u32[]{:S(2)}) collective-permute-start(bf16[32,512]{1,0:T(8,128)(2,1)S(1)} %get-tuple-element.22), channel_id=1, source_target_pairs={{16,0},{17,1},{18,2},{19,3},{20,4},{21,5},{22,6},{23,7},{24,8},{25... | collective-permute-start | bytes 98312 | tf_op jit(solution)/shard_map/ppermute | solution.py:101
  17.7 2.8 %collective-permute-start.5 = (bf16[32,32]{1,0:T(8,128)(2,1)S(1)}, bf16[32,32]{1,0:T(8,128)(2,1)S(1)}, u32[]{:S(2)}, u32[]{:S(2)}) collective-permute-start(bf16[32,32]{1,0:T(8,128)(2,1)S(1)} %get-tuple-element.18), channel_id=1, source_target_pairs={{16,1},{17,2},{18,3},{19,4},{20,5},{21,6},{22,7},{23,8},{24,9},{25... | collective-permute-start | bytes 6152 | tf_op jit(solution)/shard_map/ppermute | solution.py:101
  20.6 1.3 %collective-permute-start.4 = (bf16[512,32]{1,0:T(8,128)(2,1)S(1)}, bf16[512,32]{1,0:T(8,128)(2,1)S(1)}, u32[]{:S(2)}, u32[]{:S(2)}) collective-permute-start(bf16[512,32]{1,0:T(8,128)(2,1)S(1)} %get-tuple-element.24), channel_id=1, source_target_pairs={{1,0},{2,1},{3,2},{4,3},{5,4},{6,5},{7,6},{8,7},{9,8},{10,9},{11,1... | collective-permute-start | bytes 98312 | tf_op jit(solution)/shard_map/ppermute | solution.py:101
  21.9 1.3 %collective-permute-start.2 = (bf16[32,32]{1,0:T(8,128)(2,1)S(1)}, bf16[32,32]{1,0:T(8,128)(2,1)S(1)}, u32[]{:S(2)}, u32[]{:S(2)}) collective-permute-start(bf16[32,32]{1,0:T(8,128)(2,1)S(1)} %get-tuple-element.19), channel_id=1, source_target_pairs={{1,16},{2,17},{3,18},{4,19},{5,20},{6,21},{7,22},{8,23},{9,24},{10... | collective-permute-start | bytes 6152 | tf_op jit(solution)/shard_map/ppermute | solution.py:101
  23.7 5.5 %collective-permute-done.7 = bf16[32,32]{1,0:T(8,128)(2,1)S(1)} collective-permute-done((bf16[32,32]{1,0:T(8,128)(2,1)S(1)}, bf16[32,32]{1,0:T(8,128)(2,1)S(1)}, u32[]{:S(2)}, u32[]{:S(2)}) %collective-permute-start.7) | collective-permute-done | bytes 2080 | tf_op jit(solution)/shard_map/ppermute | solution.py:101
  29.2 1.6 %collective-permute-start.3 = (bf16[512,32]{1,0:T(8,128)(2,1)S(1)}, bf16[512,32]{1,0:T(8,128)(2,1)S(1)}, u32[]{:S(2)}, u32[]{:S(2)}) collective-permute-start(bf16[512,32]{1,0:T(8,128)(2,1)S(1)} %get-tuple-element.23), channel_id=1, source_target_pairs={{0,1},{1,2},{2,3},{3,4},{4,5},{5,6},{6,7},{7,8},{8,9},{9,10},{10,1... | collective-permute-start | bytes 98312 | tf_op jit(solution)/shard_map/ppermute | solution.py:101
  30.7 2.6 %collective-permute-start.1 = (bf16[32,512]{1,0:T(8,128)(2,1)S(1)}, bf16[32,512]{1,0:T(8,128)(2,1)S(1)}, u32[]{:S(2)}, u32[]{:S(2)}) collective-permute-start(bf16[32,512]{1,0:T(8,128)(2,1)S(1)} %get-tuple-element.21), channel_id=1, source_target_pairs={{0,16},{1,17},{2,18},{3,19},{4,20},{5,21},{6,22},{7,23},{8,24},{9,... | collective-permute-start | bytes 98312 | tf_op jit(solution)/shard_map/ppermute | solution.py:101
  33.4 4.5 %collective-permute-start = (bf16[32,32]{1,0:T(8,128)(2,1)S(1)}, bf16[32,32]{1,0:T(8,128)(2,1)S(1)}, u32[]{:S(2)}, u32[]{:S(2)}) collective-permute-start(bf16[32,32]{1,0:T(8,128)(2,1)S(1)} %get-tuple-element.17), channel_id=1, source_target_pairs={{0,17},{1,18},{2,19},{3,20},{4,21},{5,22},{6,23},{7,24},{8,25},{9,... | collective-permute-start | bytes 6152 | tf_op jit(solution)/shard_map/ppermute | solution.py:101
  37.9 0.8 collective-permute-done
  38.7 3.8 %fusion.8.w_ref = bf16[8,192,192]{2,1,0:T(8,128)(2,1)} fusion(s32[8,192]{1,0:T(8,128)S(1)} %get-tuple-element.51, s32[8,192]{1,0:T(8,128)S(1)} %get-tuple-element.52, bf16[32,32]{1,0:T(8,128)(2,1)S(1)} %collective-permute-done.7, bf16[32,512]{1,0:T(8,128)(2,1)S(1)} %collective-permute-done.6, bf16[32,32]{1,0:T(8,128)(2,1)S(1)} %collective-permute-done.5, ...), kind=kOutput, calls=%fused_computation.13 | convolution fusion | flops 1367875584 | bytes 1265664 | tf_op jit(solution)/shard_map/mrc,msc->mrs/dot_general | solution.py:193
  42.5 0.7 fusion.12
  43.1 0.8 copy.53.tf_ref
  43.9 16.0 %shard_map.94 = f32[8,8,128]{2,1,0:T(8,128)} custom-call(bf16[8,128,128]{2,1,0:T(8,128)(2,1)} %copy.53.tf_ref, bf16[8,192,192]{2,1,0:T(8,128)(2,1)} %fusion.8.w_ref), custom_call_target="tpu_custom_call" | custom-call | tf_op jit(solution)/shard_map/pallas_call | solution.py:68
  59.9 0.8 slice.206
  61.0 0.2 broadcast_in_dim.163
  61.2 0.2 broadcast_in_dim.160
  61.9 0.6 all_to_all.12
  62.5 11.1 %all-to-all-start.1 = ((f32[16,1,388]{2,1,0:T(1,128)}), f32[16,1,388]{2,1,0:T(1,128)S(1)}, u32[]{:S(2)}, u32[]{:S(2)}) async-start(f32[16,1,388]{2,1,0:T(1,128)} %all_to_all.12), calls=%async_computation.1 | async-start | bytes 65536 | tf_op jit(solution)/shard_map/all_to_all | solution.py:213
  73.8 6.4 %all-to-all-done.1 = f32[16,1,388]{2,1,0:T(1,128)S(1)} async-done(((f32[16,1,388]{2,1,0:T(1,128)}), f32[16,1,388]{2,1,0:T(1,128)S(1)}, u32[]{:S(2)}, u32[]{:S(2)}) %all-to-all-start.1) | async-done | bytes 24864 | tf_op jit(solution)/shard_map/all_to_all | solution.py:213
  80.5 0.2 select_n.76
  80.7 0.2 select_n.72
  81.0 3.1 %collective-permute-start.9 = (f32[4,3,38]{2,1,0:T(4,128)S(1)}, f32[4,3,38]{2,1,0:T(4,128)S(1)}, u32[]{:S(2)}, u32[]{:S(2)}) collective-permute-start(f32[4,3,38]{2,1,0:T(4,128)S(1)} %get-tuple-element.26), channel_id=1, source_target_pairs={{16,0},{32,16},{48,32},{64,48},{80,64},{96,80},{112,96},{17,1},{33... | collective-permute-start | bytes 5480 | tf_op jit(solution)/shard_map/ppermute | solution.py:175
  84.2 3.9 %collective-permute-start.8 = (f32[4,3,38]{2,1,0:T(4,128)S(1)}, f32[4,3,38]{2,1,0:T(4,128)S(1)}, u32[]{:S(2)}, u32[]{:S(2)}) collective-permute-start(f32[4,3,38]{2,1,0:T(4,128)S(1)} %get-tuple-element.25), channel_id=1, source_target_pairs={{0,16},{16,32},{32,48},{48,64},{64,80},{80,96},{96,112},{1,17},{17... | collective-permute-start | bytes 5480 | tf_op jit(solution)/shard_map/ppermute | solution.py:174
  88.0 0.7 select_reduce_fusion.1
  89.6 0.7 fusion.69
  (65 shorter events, 2.9 us)
Async XLA Ops:
  0.6 1.1 %copy-start = (bf16[512,512]{1,0:T(8,128)(2,1)S(1)}, bf16[512,512]{1,0:T(8,128)(2,1)}, u32[]{:S(2)}) copy-start(bf16[512,512]{1,0:T(8,128)(2,1)} %param.7) | copy-start | bytes 1572868
  1.7 1.1 %copy-start.6 = (s32[1,8]{1,0:T(1,128)S(1)}, s32[1,8]{1,0:T(1,128)}, u32[]{:S(2)}) copy-start(s32[1,8]{1,0:T(1,128)} %param.10) | copy-start | bytes 100
  4.8 8.6 %copy-start.1 = (bf16[512,512]{1,0:T(8,128)(2,1)S(1)}, bf16[512,512]{1,0:T(8,128)(2,1)}, u32[]{:S(2)}) copy-start(bf16[512,512]{1,0:T(8,128)(2,1)} %param.8) | copy-start | bytes 1572868
  4.8 18.4 %copy-start.4 = (s32[2,1,8]{2,1,0:T(1,128)S(1)}, s32[2,1,8]{2,1,0:T(1,128)}, u32[]{:S(2)}) copy-start(s32[2,1,8]{2,1,0:T(1,128)} %param.11) | copy-start | bytes 196
  4.8 18.4 %copy-start.2 = (s32[32,32]{1,0:T(8,128)S(1)}, s32[32,32]{1,0:T(8,128)}, u32[]{:S(2)}) copy-start(s32[32,32]{1,0:T(8,128)} %param.13) | copy-start | bytes 12292
  4.8 18.6 %copy-start.5 = (s32[1,8]{1,0:T(1,128)S(1)}, s32[1,8]{1,0:T(1,128)}, u32[]{:S(2)}) copy-start(s32[1,8]{1,0:T(1,128)} %param.12) | copy-start | bytes 100
  4.8 37.6 %all-to-all-start = ((bf16[32,128,128]{2,1,0:T(8,128)(2,1)}), bf16[32,128,128]{2,1,0:T(8,128)(2,1)S(1)}, u32[]{:S(2)}, u32[]{:S(2)}) async-start(bf16[32,128,128]{2,1,0:T(8,128)(2,1)} %copy.36), calls=%async_computation | async-start | bytes 2097152 | tf_op jit(solution)/shard_map/all_to_all | solution.py:187
  13.5 15.7 %collective-permute-start.7 = (bf16[32,32]{1,0:T(8,128)(2,1)S(1)}, bf16[32,32]{1,0:T(8,128)(2,1)S(1)}, u32[]{:S(2)}, u32[]{:S(2)}) collective-permute-start(bf16[32,32]{1,0:T(8,128)(2,1)S(1)} %get-tuple-element.20), channel_id=1, source_target_pairs={{17,0},{18,1},{19,2},{20,3},{21,4},{22,5},{23,6},{24,7},{25,8},{26... | collective-permute-start | bytes 6152 | tf_op jit(solution)/shard_map/ppermute | solution.py:101
  14.8 23.9 %collective-permute-start.6 = (bf16[32,512]{1,0:T(8,128)(2,1)S(1)}, bf16[32,512]{1,0:T(8,128)(2,1)S(1)}, u32[]{:S(2)}, u32[]{:S(2)}) collective-permute-start(bf16[32,512]{1,0:T(8,128)(2,1)S(1)} %get-tuple-element.22), channel_id=1, source_target_pairs={{16,0},{17,1},{18,2},{19,3},{20,4},{21,5},{22,6},{23,7},{24,8},{25... | collective-permute-start | bytes 98312 | tf_op jit(solution)/shard_map/ppermute | solution.py:101
  17.7 13.1 %collective-permute-start.5 = (bf16[32,32]{1,0:T(8,128)(2,1)S(1)}, bf16[32,32]{1,0:T(8,128)(2,1)S(1)}, u32[]{:S(2)}, u32[]{:S(2)}) collective-permute-start(bf16[32,32]{1,0:T(8,128)(2,1)S(1)} %get-tuple-element.18), channel_id=1, source_target_pairs={{16,1},{17,2},{18,3},{19,4},{20,5},{21,6},{22,7},{23,8},{24,9},{25... | collective-permute-start | bytes 6152 | tf_op jit(solution)/shard_map/ppermute | solution.py:101
  20.6 18.1 %collective-permute-start.4 = (bf16[512,32]{1,0:T(8,128)(2,1)S(1)}, bf16[512,32]{1,0:T(8,128)(2,1)S(1)}, u32[]{:S(2)}, u32[]{:S(2)}) collective-permute-start(bf16[512,32]{1,0:T(8,128)(2,1)S(1)} %get-tuple-element.24), channel_id=1, source_target_pairs={{1,0},{2,1},{3,2},{4,3},{5,4},{6,5},{7,6},{8,7},{9,8},{10,9},{11,1... | collective-permute-start | bytes 98312 | tf_op jit(solution)/shard_map/ppermute | solution.py:101
  21.9 11.5 %collective-permute-start.2 = (bf16[32,32]{1,0:T(8,128)(2,1)S(1)}, bf16[32,32]{1,0:T(8,128)(2,1)S(1)}, u32[]{:S(2)}, u32[]{:S(2)}) collective-permute-start(bf16[32,32]{1,0:T(8,128)(2,1)S(1)} %get-tuple-element.19), channel_id=1, source_target_pairs={{1,16},{2,17},{3,18},{4,19},{5,20},{6,21},{7,22},{8,23},{9,24},{10... | collective-permute-start | bytes 6152 | tf_op jit(solution)/shard_map/ppermute | solution.py:101
  29.2 9.5 %collective-permute-start.3 = (bf16[512,32]{1,0:T(8,128)(2,1)S(1)}, bf16[512,32]{1,0:T(8,128)(2,1)S(1)}, u32[]{:S(2)}, u32[]{:S(2)}) collective-permute-start(bf16[512,32]{1,0:T(8,128)(2,1)S(1)} %get-tuple-element.23), channel_id=1, source_target_pairs={{0,1},{1,2},{2,3},{3,4},{4,5},{5,6},{6,7},{7,8},{8,9},{9,10},{10,1... | collective-permute-start | bytes 98312 | tf_op jit(solution)/shard_map/ppermute | solution.py:101
  30.7 8.0 %collective-permute-start.1 = (bf16[32,512]{1,0:T(8,128)(2,1)S(1)}, bf16[32,512]{1,0:T(8,128)(2,1)S(1)}, u32[]{:S(2)}, u32[]{:S(2)}) collective-permute-start(bf16[32,512]{1,0:T(8,128)(2,1)S(1)} %get-tuple-element.21), channel_id=1, source_target_pairs={{0,16},{1,17},{2,18},{3,19},{4,20},{5,21},{6,22},{7,23},{8,24},{9,... | collective-permute-start | bytes 98312 | tf_op jit(solution)/shard_map/ppermute | solution.py:101
  33.4 5.3 %collective-permute-start = (bf16[32,32]{1,0:T(8,128)(2,1)S(1)}, bf16[32,32]{1,0:T(8,128)(2,1)S(1)}, u32[]{:S(2)}, u32[]{:S(2)}) collective-permute-start(bf16[32,32]{1,0:T(8,128)(2,1)S(1)} %get-tuple-element.17), channel_id=1, source_target_pairs={{0,17},{1,18},{2,19},{3,20},{4,21},{5,22},{6,23},{7,24},{8,25},{9,... | collective-permute-start | bytes 6152 | tf_op jit(solution)/shard_map/ppermute | solution.py:101
  60.8 28.5 %copy-start.3 = (f32[2,8]{1,0:T(2,128)}, f32[2,8]{1,0:T(2,128)S(1)}, u32[]{:S(2)}) copy-start(f32[2,8]{1,0:T(2,128)S(1)} %bitcast_negate_fusion) | copy-start | bytes 196
  62.5 17.6 %all-to-all-start.1 = ((f32[16,1,388]{2,1,0:T(1,128)}), f32[16,1,388]{2,1,0:T(1,128)S(1)}, u32[]{:S(2)}, u32[]{:S(2)}) async-start(f32[16,1,388]{2,1,0:T(1,128)} %all_to_all.12), calls=%async_computation.1 | async-start | bytes 65536 | tf_op jit(solution)/shard_map/all_to_all | solution.py:213
  81.0 7.7 %collective-permute-start.9 = (f32[4,3,38]{2,1,0:T(4,128)S(1)}, f32[4,3,38]{2,1,0:T(4,128)S(1)}, u32[]{:S(2)}, u32[]{:S(2)}) collective-permute-start(f32[4,3,38]{2,1,0:T(4,128)S(1)} %get-tuple-element.26), channel_id=1, source_target_pairs={{16,0},{32,16},{48,32},{64,48},{80,64},{96,80},{112,96},{17,1},{33... | collective-permute-start | bytes 5480 | tf_op jit(solution)/shard_map/ppermute | solution.py:175
  84.2 4.7 %collective-permute-start.8 = (f32[4,3,38]{2,1,0:T(4,128)S(1)}, f32[4,3,38]{2,1,0:T(4,128)S(1)}, u32[]{:S(2)}, u32[]{:S(2)}) collective-permute-start(f32[4,3,38]{2,1,0:T(4,128)S(1)} %get-tuple-element.25), channel_id=1, source_target_pairs={{0,16},{16,32},{32,48},{48,64},{64,80},{80,96},{96,112},{1,17},{17... | collective-permute-start | bytes 5480 | tf_op jit(solution)/shard_map/ppermute | solution.py:174

commit v7 on v6

--- a/solution.py
+++ b/solution.py
@@ -184,8 +184,18 @@
     count = jnp.sum(attach.astype(f32), axis=0)
     mask = node_mask.astype(f32)
     w = ITERS_R
-    arrived = lax.all_to_all(outgoing, "tx", split_axis=0, concat_axis=0, tiled=True)
-    b_wide = halo(section_b, RADIUS)
+    b_rows, b_cols = section_b.shape
+    rim_send = side_payload(section_b[:, 0:RADIUS], section_b[:, b_cols - RADIUS :])
+    slot_shape = outgoing.shape[1:]
+    send = jnp.concatenate(
+        [outgoing.reshape((n_tx, CAP) + slot_shape), rim_send.reshape((n_tx, 1) + slot_shape)], axis=1
+    )
+    got = lax.all_to_all(send, "tx", split_axis=0, concat_axis=0, tiled=True)
+    arrived = got[:, 0:CAP].reshape(outgoing.shape)
+    b_left, b_right = side_arrivals(got[:, CAP].reshape(n_tx, -1), (b_rows, RADIUS))
+    b_tx = jnp.concatenate([b_left, section_b, b_right], axis=1)
+    b_above, b_below = rows_exchange(b_tx, RADIUS)
+    b_wide = jnp.concatenate([b_above, b_tx, b_below], axis=0)
 
     wrow_pick = one_hot(window_corner[0, 0], WIN, b_wide.shape[0])
     wcol_pick = one_hot(window_corner[1, 0], WIN, b_wide.shape[1])

time: 90.9 us -> 94.4 us (1.039)
  waiting for transfers between devices: 12.7 us -> 33.6 us
  starting transfers between devices: 45 us -> 24.4 us
  other arithmetic: 3.09 us -> 5.06 us
  local copies, waits for them, and re-layouts: 6.44 us -> 8.07 us
    all_to_all x1, waiting for transfers between devices: 0.01 us -> 22.6 us  [shards(): got = lax.all_to_all(send, 'tx', split_axis=0, concat_axis=0, tiled=True)]
    ppermute x8 -> x0, starting transfers between devices: 18.2 us -> none  [halo(): pieces[dy, dx] = lax.ppermute(part, ('ty', 'tx'), pairs)]
    all_to_all x1, starting transfers between devices: 11.1 us -> 3.5 us  [shards(): came = lax.all_to_all(back, 'tx', split_axis=0, concat_axis=0, tiled=True)]
    ppermute x8 -> x0, waiting for transfers between devices: 6.24 us -> none  [halo(): pieces[dy, dx] = lax.ppermute(part, ('ty', 'tx'), pairs)]
    ppermute x1 -> x2, waiting for transfers between devices: 0.01 us -> 4.71 us  [rows_exchange(): below = lax.ppermute(head, 'ty', [(i + 1, i) for i in range(count - 1)])]
    ppermute x1 -> x2, starting transfers between devices: 3.88 us -> 8.53 us  [rows_exchange(): above = lax.ppermute(tail, 'ty', [(i, i + 1) for i in range(count - 1)])]
    slice x3 -> x4, local copies, waits for them, and re-layouts: 0.19 us -> 2.25 us  [the longest x2 1.15 us: shards(): arrived = got[:, 0:CAP].reshape(outgoing.shape)]
    convert_element_type x1 -> x0, local copies, waits for them, and re-layouts: 1.4 us -> none  [shards(): outgoing = jnp.einsum('ks,kri->sri', owner_picker.astype(jnp.bfloat16), t...]
  transfers between devices with their start and end apart: 12 -> 6, of which waited for: 4 -> 4; matrix products, arithmetic and copies ran while one was open for 6% -> 2% of each run, Pallas kernels for 0% -> 0%
where the time goes in v7:
time: 94.4 us; the launch traced here: 93.9 us
  waiting for transfers between devices  33.6 us (36%)
  starting transfers between devices  24.4 us (26%)
  Pallas kernels  16 us (17%)
  local copies, waits for them, and re-layouts  8.07 us (9%)
  matrix products  5.73 us (6%)
  other arithmetic  5.06 us (5%)
  between operations  1.02 us (1%)
    all_to_all x1, waiting for transfers between devices, shards(): got = lax.all_to_all(send, 'tx', split_axis=0, concat_axis=0, tiled=True)  22.6 us
    pallas_call x1, Pallas kernels, flows_of(): pl.pallas_call(flow_kernel, grid=(n,), in_specs=[pl.BlockSpec((1, PATCH,...  16 us
    all_to_all x1, starting transfers between devices, shards(): got = lax.all_to_all(send, 'tx', split_axis=0, concat_axis=0, tiled=True)  8.55 us
    ppermute x2, starting transfers between devices, rows_exchange(): above = lax.ppermute(tail, 'ty', [(i, i + 1) for i in range(count - 1)])  8.53 us
    all_to_all x1, waiting for transfers between devices, shards(): came = lax.all_to_all(back, 'tx', split_axis=0, concat_axis=0, tiled=True)  6.31 us
    ppermute x2, waiting for transfers between devices, rows_exchange(): below = lax.ppermute(head, 'ty', [(i + 1, i) for i in range(count - 1)])  4.71 us
    ppermute x2, starting transfers between devices, rows_exchange(): below = lax.ppermute(head, 'ty', [(i + 1, i) for i in range(count - 1)])  3.84 us
    dot_general x1, matrix products, shards(): jnp.einsum('mrc,msc->mrs', by_row.astype(jnp.bfloat16), wcol_pick, prefer...  3.74 us
  transfers between devices with their start and end apart: 6, of which 4 were waited for; matrix products, arithmetic and copies ran while one was open for 2% of the time, Pallas kernels for 0%

profile of v7, /device:TPU:1, one launch (start us, length us, event | category | flops | bytes accessed | tf_op | source)
XLA Modules:
  0.0 93.9 jit_solution(1985155871791582984)
XLA Ops:
  0.7 0.7 slice_bitcast_fusion.7
  1.4 1.1 %fusion.68 = (bf16[512,32]{1,0:T(8,128)(2,1)S(1)}, bf16[512,32]{1,0:T(8,128)(2,1)S(1)}) fusion(bf16[512,512]{1,0:T(8,128)(2,1)} %param.8), kind=kLoop, calls=%fused_computation.139 | loop fusion | bytes 131072 | tf_op jit(solution)/shard_map/slice | solution.py:188
  2.8 1.1 %fusion.11 = bf16[8,128,128]{2,1,0:T(8,128)(2,1)S(1)} fusion(s32[8,128]{1,0:T(8,128)S(1)} %get-tuple-element.49, s32[8,128]{1,0:T(8,128)S(1)} %get-tuple-element.50, bf16[512,512]{1,0:T(8,128)(2,1)S(1)} %copy-done), kind=kOutput, calls=%fused_computation.15 | convolution fusion | flops 672792576 | bytes 794624 | tf_op jit(solution)/shard_map/kra,kia->kri/dot_general | solution.py:143
  4.0 0.6 convolution_convert_fusion
  4.5 0.4 copy.38
  4.9 0.1 select_select_fusion
  5.1 1.3 %pad_maximum_fusion = bf16[16,3,128,128]{3,2,1,0:T(8,128)(2,1)} fusion(bf16[16,1,128,128]{3,2,1,0:T(8,128)(2,1)S(1)} %select_select_fusion, bf16[16,2,128,128]{3,2,1,0:T(8,128)(2,1)S(1)} %copy.38), kind=kLoop, calls=%fused_computation.11 | loop fusion | flops 786432 | bytes 3145728 | tf_op jit(solution)/shard_map/concatenate | solution.py:190
  6.4 8.5 %all-to-all-start = ((bf16[16,3,128,128]{3,2,1,0:T(8,128)(2,1)}), bf16[16,3,128,128]{3,2,1,0:T(8,128)(2,1)S(1)}, u32[]{:S(2)}, u32[]{:S(2)}) async-start(bf16[16,3,128,128]{3,2,1,0:T(8,128)(2,1)} %pad_maximum_fusion), calls=%async_computation | async-start | bytes 3145728 | tf_op jit(solution)/shard_map/all_to_all | solution.py:193
  15.5 22.6 %all-to-all-done = bf16[16,3,128,128]{3,2,1,0:T(8,128)(2,1)S(1)} async-done(((bf16[16,3,128,128]{3,2,1,0:T(8,128)(2,1)}), bf16[16,3,128,128]{3,2,1,0:T(8,128)(2,1)S(1)}, u32[]{:S(2)}, u32[]{:S(2)}) %all-to-all-start) | async-done | bytes 1572896 | tf_op jit(solution)/shard_map/all_to_all | solution.py:193
  38.1 1.1 %copy.39 = bf16[16,2,128,128]{3,1,0,2:T(2,128)(2,1)S(1)} copy(bf16[16,2,128,128]{3,2,1,0:T(8,128)(2,1)S(1)} %slice.198) | data formatting | bytes 2097152 | tf_op jit(solution)/shard_map/slice | solution.py:194
  39.3 0.3 copy.56
  39.6 0.4 fusion.34
  40.4 5.5 %collective-permute-start = (bf16[32,576]{1,0:T(8,128)(2,1)S(1)}, bf16[32,576]{1,0:T(8,128)(2,1)S(1)}, u32[]{:S(2)}, u32[]{:S(2)}) collective-permute-start(bf16[32,576]{1,0:T(8,128)(2,1)S(1)} %get-tuple-element.19), channel_id=1, source_target_pairs={{0,16},{16,32},{32,48},{48,64},{64,80},{80,96},{96,112},{1,17},{17... | collective-permute-start | bytes 110600 | tf_op jit(solution)/shard_map/ppermute | solution.py:174
  45.9 1.9 %collective-permute-start.1 = (bf16[32,576]{1,0:T(8,128)(2,1)S(1)}, bf16[32,576]{1,0:T(8,128)(2,1)S(1)}, u32[]{:S(2)}, u32[]{:S(2)}) collective-permute-start(bf16[32,576]{1,0:T(8,128)(2,1)S(1)} %get-tuple-element.20), channel_id=1, source_target_pairs={{16,0},{32,16},{48,32},{64,48},{80,64},{96,80},{112,96},{17,1},{33... | collective-permute-start | bytes 110600 | tf_op jit(solution)/shard_map/ppermute | solution.py:175
  47.8 0.3 fusion.62
  48.1 0.8 copy.55.tf_ref
  48.9 2.3 %collective-permute-done.1 = bf16[32,576]{1,0:T(8,128)(2,1)S(1)} collective-permute-done((bf16[32,576]{1,0:T(8,128)(2,1)S(1)}, bf16[32,576]{1,0:T(8,128)(2,1)S(1)}, u32[]{:S(2)}, u32[]{:S(2)}) %collective-permute-start.1) | collective-permute-done | bytes 36896 | tf_op jit(solution)/shard_map/ppermute | solution.py:175
  51.2 3.7 %fusion.8.w_ref = bf16[8,192,192]{2,1,0:T(8,128)(2,1)} fusion(s32[8,192]{1,0:T(8,128)S(1)} %get-tuple-element.51, s32[8,192]{1,0:T(8,128)S(1)} %get-tuple-element.52, bf16[32,576]{1,0:T(8,128)(2,1)S(1)} %collective-permute-done.1, bf16[512,32]{1,0:T(8,128)(2,1)S(1)} %select_n.118, bf16[512,512]{1,0:T(8,128)(2,1)S(1)} %copy-done.1, ...), kind=kOutput, calls=%fused_computation.14 | convolution fusion | flops 1365221376 | bytes 1265664 | tf_op jit(solution)/shard_map/mrc,msc->mrs/dot_general | solution.py:203
  54.9 16.0 %shard_map.94 = f32[8,8,128]{2,1,0:T(8,128)} custom-call(bf16[8,128,128]{2,1,0:T(8,128)(2,1)} %copy.55.tf_ref, bf16[8,192,192]{2,1,0:T(8,128)(2,1)} %fusion.8.w_ref), custom_call_target="tpu_custom_call" | custom-call | tf_op jit(solution)/shard_map/pallas_call | solution.py:68
  70.9 0.8 slice.200
  72.4 0.2 broadcast_in_dim.212
  72.6 0.2 broadcast_in_dim.215
  72.9 0.6 all_to_all.12
  73.6 3.5 %all-to-all-start.1 = ((f32[16,1,388]{2,1,0:T(1,128)}), f32[16,1,388]{2,1,0:T(1,128)S(1)}, u32[]{:S(2)}, u32[]{:S(2)}) async-start(f32[16,1,388]{2,1,0:T(1,128)} %all_to_all.12), calls=%async_computation.1 | async-start | bytes 65536 | tf_op jit(solution)/shard_map/all_to_all | solution.py:223
  77.2 6.3 %all-to-all-done.1 = f32[16,1,388]{2,1,0:T(1,128)S(1)} async-done(((f32[16,1,388]{2,1,0:T(1,128)}), f32[16,1,388]{2,1,0:T(1,128)S(1)}, u32[]{:S(2)}, u32[]{:S(2)}) %all-to-all-start.1) | async-done | bytes 24864 | tf_op jit(solution)/shard_map/all_to_all | solution.py:223
  83.9 0.2 select_n.128
  84.1 0.2 select_n.131
  84.4 3.1 %collective-permute-start.2 = (f32[4,3,38]{2,1,0:T(4,128)S(1)}, f32[4,3,38]{2,1,0:T(4,128)S(1)}, u32[]{:S(2)}, u32[]{:S(2)}) collective-permute-start(f32[4,3,38]{2,1,0:T(4,128)S(1)} %get-tuple-element.23), channel_id=1, source_target_pairs={{0,16},{16,32},{32,48},{48,64},{64,80},{80,96},{96,112},{1,17},{17... | collective-permute-start | bytes 5480 | tf_op jit(solution)/shard_map/ppermute | solution.py:174
  87.4 1.9 %collective-permute-start.3 = (f32[4,3,38]{2,1,0:T(4,128)S(1)}, f32[4,3,38]{2,1,0:T(4,128)S(1)}, u32[]{:S(2)}, u32[]{:S(2)}) collective-permute-start(f32[4,3,38]{2,1,0:T(4,128)S(1)} %get-tuple-element.24), channel_id=1, source_target_pairs={{16,0},{32,16},{48,32},{64,48},{80,64},{96,80},{112,96},{17,1},{33... | collective-permute-start | bytes 5480 | tf_op jit(solution)/shard_map/ppermute | solution.py:175
  89.4 0.7 select_reduce_fusion.1
  90.0 2.4 %collective-permute-done.3 = f32[4,3,38]{2,1,0:T(4,128)S(1)} collective-permute-done((f32[4,3,38]{2,1,0:T(4,128)S(1)}, f32[4,3,38]{2,1,0:T(4,128)S(1)}, u32[]{:S(2)}, u32[]{:S(2)}) %collective-permute-start.3) | collective-permute-done | bytes 1856 | tf_op jit(solution)/shard_map/ppermute | solution.py:175
  93.2 0.7 fusion.53
  (63 shorter events, 3.3 us)
Async XLA Ops:
  0.6 2.2 %copy-start = (bf16[512,512]{1,0:T(8,128)(2,1)S(1)}, bf16[512,512]{1,0:T(8,128)(2,1)}, u32[]{:S(2)}) copy-start(bf16[512,512]{1,0:T(8,128)(2,1)} %param.7) | copy-start | bytes 1572868
  2.8 1.1 %copy-start.6 = (s32[1,8]{1,0:T(1,128)S(1)}, s32[1,8]{1,0:T(1,128)}, u32[]{:S(2)}) copy-start(s32[1,8]{1,0:T(1,128)} %param.10) | copy-start | bytes 100
  6.4 8.6 %copy-start.4 = (s32[2,1,8]{2,1,0:T(1,128)S(1)}, s32[2,1,8]{2,1,0:T(1,128)}, u32[]{:S(2)}) copy-start(s32[2,1,8]{2,1,0:T(1,128)} %param.11) | copy-start | bytes 196
  6.4 8.8 %copy-start.5 = (s32[1,8]{1,0:T(1,128)S(1)}, s32[1,8]{1,0:T(1,128)}, u32[]{:S(2)}) copy-start(s32[1,8]{1,0:T(1,128)} %param.12) | copy-start | bytes 100
  6.4 9.0 %copy-start.2 = (s32[32,32]{1,0:T(8,128)S(1)}, s32[32,32]{1,0:T(8,128)}, u32[]{:S(2)}) copy-start(s32[32,32]{1,0:T(8,128)} %param.13) | copy-start | bytes 12292
  6.4 31.6 %all-to-all-start = ((bf16[16,3,128,128]{3,2,1,0:T(8,128)(2,1)}), bf16[16,3,128,128]{3,2,1,0:T(8,128)(2,1)S(1)}, u32[]{:S(2)}, u32[]{:S(2)}) async-start(bf16[16,3,128,128]{3,2,1,0:T(8,128)(2,1)} %pad_maximum_fusion), calls=%async_computation | async-start | bytes 3145728 | tf_op jit(solution)/shard_map/all_to_all | solution.py:193
  39.2 1.0 %copy-start.1 = (bf16[512,512]{1,0:T(8,128)(2,1)S(1)}, bf16[512,512]{1,0:T(8,128)(2,1)}, u32[]{:S(2)}) copy-start(bf16[512,512]{1,0:T(8,128)(2,1)} %param.8) | copy-start | bytes 1572868
  40.4 8.5 %collective-permute-start = (bf16[32,576]{1,0:T(8,128)(2,1)S(1)}, bf16[32,576]{1,0:T(8,128)(2,1)S(1)}, u32[]{:S(2)}, u32[]{:S(2)}) collective-permute-start(bf16[32,576]{1,0:T(8,128)(2,1)S(1)} %get-tuple-element.19), channel_id=1, source_target_pairs={{0,16},{16,32},{32,48},{48,64},{64,80},{80,96},{96,112},{1,17},{17... | collective-permute-start | bytes 110600 | tf_op jit(solution)/shard_map/ppermute | solution.py:174
  45.9 5.3 %collective-permute-start.1 = (bf16[32,576]{1,0:T(8,128)(2,1)S(1)}, bf16[32,576]{1,0:T(8,128)(2,1)S(1)}, u32[]{:S(2)}, u32[]{:S(2)}) collective-permute-start(bf16[32,576]{1,0:T(8,128)(2,1)S(1)} %get-tuple-element.20), channel_id=1, source_target_pairs={{16,0},{32,16},{48,32},{64,48},{80,64},{96,80},{112,96},{17,1},{33... | collective-permute-start | bytes 110600 | tf_op jit(solution)/shard_map/ppermute | solution.py:175
  71.8 22.1 %copy-start.3 = (f32[2,8]{1,0:T(2,128)}, f32[2,8]{1,0:T(2,128)S(1)}, u32[]{:S(2)}) copy-start(f32[2,8]{1,0:T(2,128)S(1)} %bitcast_negate_fusion) | copy-start | bytes 196
  73.6 9.9 %all-to-all-start.1 = ((f32[16,1,388]{2,1,0:T(1,128)}), f32[16,1,388]{2,1,0:T(1,128)S(1)}, u32[]{:S(2)}, u32[]{:S(2)}) async-start(f32[16,1,388]{2,1,0:T(1,128)} %all_to_all.12), calls=%async_computation.1 | async-start | bytes 65536 | tf_op jit(solution)/shard_map/all_to_all | solution.py:223
  84.4 5.6 %collective-permute-start.2 = (f32[4,3,38]{2,1,0:T(4,128)S(1)}, f32[4,3,38]{2,1,0:T(4,128)S(1)}, u32[]{:S(2)}, u32[]{:S(2)}) collective-permute-start(f32[4,3,38]{2,1,0:T(4,128)S(1)} %get-tuple-element.23), channel_id=1, source_target_pairs={{0,16},{16,32},{32,48},{48,64},{64,80},{80,96},{96,112},{1,17},{17... | collective-permute-start | bytes 5480 | tf_op jit(solution)/shard_map/ppermute | solution.py:174
  87.4 5.0 %collective-permute-start.3 = (f32[4,3,38]{2,1,0:T(4,128)S(1)}, f32[4,3,38]{2,1,0:T(4,128)S(1)}, u32[]{:S(2)}, u32[]{:S(2)}) collective-permute-start(f32[4,3,38]{2,1,0:T(4,128)S(1)} %get-tuple-element.24), channel_id=1, source_target_pairs={{16,0},{32,16},{48,32},{64,48},{80,64},{96,80},{112,96},{17,1},{33... | collective-permute-start | bytes 5480 | tf_op jit(solution)/shard_map/ppermute | solution.py:175

commit v8 on v6

--- a/solution.py
+++ b/solution.py
@@ -203,17 +203,18 @@
     target = jnp.sum(jnp.where(attach[None], source_flow[:, :, None, None], 0.0), axis=1)
     fields = jnp.concatenate([target, count[None], mask[None]], axis=0)
     returned = jnp.sum(jnp.where(source_picker[None], flows[:, :, None], 0.0), axis=1)
+    lane = 128
+    sides = side_payload(fields[:, :, 0:w], fields[:, :, node_cols - w :])
+    flows_out = returned.reshape(2, n_tx, CAP).transpose(1, 0, 2).reshape(n_tx, -1)
+    side_len = sides.shape[1]
+    chunk = -(-(side_len + flows_out.shape[1]) // lane) * lane
     back = jnp.concatenate(
-        [
-            returned.reshape(2, n_tx, CAP).transpose(1, 0, 2).reshape(n_tx, -1),
-            side_payload(fields[:, :, 0:w], fields[:, :, node_cols - w :]),
-        ],
-        axis=1,
-    )
-    came = lax.all_to_all(back, "tx", split_axis=0, concat_axis=0, tiled=True)
-    landed = came[:, 0 : 2 * CAP].reshape(n_tx, 2, CAP).transpose(1, 0, 2).reshape(2, -1)
+        [sides, flows_out, jnp.zeros((n_tx, chunk - side_len - flows_out.shape[1]), f32)], axis=1
+    ).reshape(n_tx, chunk // lane, lane)
+    came = lax.all_to_all(back, "tx", split_axis=0, concat_axis=0, tiled=True).reshape(n_tx, chunk)
+    landed = came[:, side_len : side_len + 2 * CAP].reshape(n_tx, 2, CAP).transpose(1, 0, 2).reshape(2, -1)
     owner_flow = jnp.sum(jnp.where(owner_picker[None], landed[:, None, :], 0.0), axis=2)
-    f_left, f_right = side_arrivals(came[:, 2 * CAP :], (fields.shape[0], node_rows, w))
+    f_left, f_right = side_arrivals(came[:, 0:side_len], (fields.shape[0], node_rows, w))
     fields_tx = jnp.concatenate([f_left, fields, f_right], axis=2)
     f_above, f_below = rows_exchange(fields_tx, w)
     wide = jnp.concatenate([f_above, fields_tx, f_below], axis=1)

time: 90.9 us -> 90.8 us (level)
  no operation moved by 1% of the time
where the time goes in v8:
time: 90.8 us; the launch traced here: 90.2 us
  starting transfers between devices  45 us (50%)
  Pallas kernels  16 us (18%)
  waiting for transfers between devices  12.7 us (14%)
  local copies, waits for them, and re-layouts  6.43 us (7%)
  matrix products  6.09 us (7%)
  other arithmetic  3.03 us (3%)
  between operations  1.01 us (1%)
    ppermute x8, starting transfers between devices, halo(): pieces[dy, dx] = lax.ppermute(part, ('ty', 'tx'), pairs)  18.2 us
    pallas_call x1, Pallas kernels, flows_of(): pl.pallas_call(flow_kernel, grid=(n,), in_specs=[pl.BlockSpec((1, PATCH,...  16 us
    all_to_all x1, starting transfers between devices, shards(): lax.all_to_all(back, 'tx', split_axis=0, concat_axis=0, tiled=True)  11.1 us
    all_to_all x1, starting transfers between devices, shards(): lax.all_to_all(outgoing, 'tx', split_axis=0, concat_axis=0, tiled=True)  8.56 us
    all_to_all x1, waiting for transfers between devices, shards(): lax.all_to_all(back, 'tx', split_axis=0, concat_axis=0, tiled=True)  6.38 us
    ppermute x8, waiting for transfers between devices, halo(): pieces[dy, dx] = lax.ppermute(part, ('ty', 'tx'), pairs)  6.15 us
    ppermute x1, starting transfers between devices, rows_exchange(): above = lax.ppermute(tail, 'ty', [(i, i + 1) for i in range(count - 1)])  3.88 us
    dot_general x1, matrix products, shards(): jnp.einsum('mrc,msc->mrs', by_row.astype(jnp.bfloat16), wcol_pick, prefer...  3.75 us
  transfers between devices with their start and end apart: 12, of which 4 were waited for; matrix products, arithmetic and copies ran while one was open for 6% of the time, Pallas kernels for 0%

profile of v8, /device:TPU:1, one launch (start us, length us, event | category | flops | bytes accessed | tf_op | source)
XLA Modules:
  0.0 90.2 jit_solution(10933625264624682788)
XLA Ops:
  0.7 0.7 slice_bitcast_fusion.5
  1.5 0.2 copy-done
  1.7 1.1 %fusion.11 = bf16[8,128,128]{2,1,0:T(8,128)(2,1)S(1)} fusion(s32[8,128]{1,0:T(8,128)S(1)} %get-tuple-element.47, s32[8,128]{1,0:T(8,128)S(1)} %get-tuple-element.48, bf16[512,512]{1,0:T(8,128)(2,1)S(1)} %copy-done), kind=kOutput, calls=%fused_computation.14 | convolution fusion | flops 672792576 | bytes 794624 | tf_op jit(solution)/shard_map/kra,kia->kri/dot_general | solution.py:143
  2.9 0.6 convolution_convert_fusion
  3.4 1.4 %copy.36 = bf16[32,128,128]{2,1,0:T(8,128)(2,1)} copy(bf16[32,128,128]{2,0,1:T(8,128)(2,1)S(1)} %convolution_convert_fusion) | data formatting | bytes 2097152 | tf_op jit(solution)/shard_map/convert_element_type | solution.py:148
  4.8 8.6 %all-to-all-start = ((bf16[32,128,128]{2,1,0:T(8,128)(2,1)}), bf16[32,128,128]{2,1,0:T(8,128)(2,1)S(1)}, u32[]{:S(2)}, u32[]{:S(2)}) async-start(bf16[32,128,128]{2,1,0:T(8,128)(2,1)} %copy.36), calls=%async_computation | async-start | bytes 2097152 | tf_op jit(solution)/shard_map/all_to_all | solution.py:187
  13.5 1.3 %collective-permute-start.7 = (bf16[32,32]{1,0:T(8,128)(2,1)S(1)}, bf16[32,32]{1,0:T(8,128)(2,1)S(1)}, u32[]{:S(2)}, u32[]{:S(2)}) collective-permute-start(bf16[32,32]{1,0:T(8,128)(2,1)S(1)} %get-tuple-element.20), channel_id=1, source_target_pairs={{17,0},{18,1},{19,2},{20,3},{21,4},{22,5},{23,6},{24,7},{25,8},{26... | collective-permute-start | bytes 6152 | tf_op jit(solution)/shard_map/ppermute | solution.py:101
  14.8 2.9 %collective-permute-start.6 = (bf16[32,512]{1,0:T(8,128)(2,1)S(1)}, bf16[32,512]{1,0:T(8,128)(2,1)S(1)}, u32[]{:S(2)}, u32[]{:S(2)}) collective-permute-start(bf16[32,512]{1,0:T(8,128)(2,1)S(1)} %get-tuple-element.22), channel_id=1, source_target_pairs={{16,0},{17,1},{18,2},{19,3},{20,4},{21,5},{22,6},{23,7},{24,8},{25... | collective-permute-start | bytes 98312 | tf_op jit(solution)/shard_map/ppermute | solution.py:101
  17.7 2.8 %collective-permute-start.5 = (bf16[32,32]{1,0:T(8,128)(2,1)S(1)}, bf16[32,32]{1,0:T(8,128)(2,1)S(1)}, u32[]{:S(2)}, u32[]{:S(2)}) collective-permute-start(bf16[32,32]{1,0:T(8,128)(2,1)S(1)} %get-tuple-element.18), channel_id=1, source_target_pairs={{16,1},{17,2},{18,3},{19,4},{20,5},{21,6},{22,7},{23,8},{24,9},{25... | collective-permute-start | bytes 6152 | tf_op jit(solution)/shard_map/ppermute | solution.py:101
  20.6 1.3 %collective-permute-start.4 = (bf16[512,32]{1,0:T(8,128)(2,1)S(1)}, bf16[512,32]{1,0:T(8,128)(2,1)S(1)}, u32[]{:S(2)}, u32[]{:S(2)}) collective-permute-start(bf16[512,32]{1,0:T(8,128)(2,1)S(1)} %get-tuple-element.24), channel_id=1, source_target_pairs={{1,0},{2,1},{3,2},{4,3},{5,4},{6,5},{7,6},{8,7},{9,8},{10,9},{11,1... | collective-permute-start | bytes 98312 | tf_op jit(solution)/shard_map/ppermute | solution.py:101
  21.9 1.3 %collective-permute-start.2 = (bf16[32,32]{1,0:T(8,128)(2,1)S(1)}, bf16[32,32]{1,0:T(8,128)(2,1)S(1)}, u32[]{:S(2)}, u32[]{:S(2)}) collective-permute-start(bf16[32,32]{1,0:T(8,128)(2,1)S(1)} %get-tuple-element.19), channel_id=1, source_target_pairs={{1,16},{2,17},{3,18},{4,19},{5,20},{6,21},{7,22},{8,23},{9,24},{10... | collective-permute-start | bytes 6152 | tf_op jit(solution)/shard_map/ppermute | solution.py:101
  23.7 5.5 %collective-permute-done.7 = bf16[32,32]{1,0:T(8,128)(2,1)S(1)} collective-permute-done((bf16[32,32]{1,0:T(8,128)(2,1)S(1)}, bf16[32,32]{1,0:T(8,128)(2,1)S(1)}, u32[]{:S(2)}, u32[]{:S(2)}) %collective-permute-start.7) | collective-permute-done | bytes 2080 | tf_op jit(solution)/shard_map/ppermute | solution.py:101
  29.2 1.6 %collective-permute-start.3 = (bf16[512,32]{1,0:T(8,128)(2,1)S(1)}, bf16[512,32]{1,0:T(8,128)(2,1)S(1)}, u32[]{:S(2)}, u32[]{:S(2)}) collective-permute-start(bf16[512,32]{1,0:T(8,128)(2,1)S(1)} %get-tuple-element.23), channel_id=1, source_target_pairs={{0,1},{1,2},{2,3},{3,4},{4,5},{5,6},{6,7},{7,8},{8,9},{9,10},{10,1... | collective-permute-start | bytes 98312 | tf_op jit(solution)/shard_map/ppermute | solution.py:101
  30.7 2.6 %collective-permute-start.1 = (bf16[32,512]{1,0:T(8,128)(2,1)S(1)}, bf16[32,512]{1,0:T(8,128)(2,1)S(1)}, u32[]{:S(2)}, u32[]{:S(2)}) collective-permute-start(bf16[32,512]{1,0:T(8,128)(2,1)S(1)} %get-tuple-element.21), channel_id=1, source_target_pairs={{0,16},{1,17},{2,18},{3,19},{4,20},{5,21},{6,22},{7,23},{8,24},{9,... | collective-permute-start | bytes 98312 | tf_op jit(solution)/shard_map/ppermute | solution.py:101
  33.4 4.5 %collective-permute-start = (bf16[32,32]{1,0:T(8,128)(2,1)S(1)}, bf16[32,32]{1,0:T(8,128)(2,1)S(1)}, u32[]{:S(2)}, u32[]{:S(2)}) collective-permute-start(bf16[32,32]{1,0:T(8,128)(2,1)S(1)} %get-tuple-element.17), channel_id=1, source_target_pairs={{0,17},{1,18},{2,19},{3,20},{4,21},{5,22},{6,23},{7,24},{8,25},{9,... | collective-permute-start | bytes 6152 | tf_op jit(solution)/shard_map/ppermute | solution.py:101
  38.0 0.7 collective-permute-done
  38.7 3.8 %fusion.8.w_ref = bf16[8,192,192]{2,1,0:T(8,128)(2,1)} fusion(s32[8,192]{1,0:T(8,128)S(1)} %get-tuple-element.49, s32[8,192]{1,0:T(8,128)S(1)} %get-tuple-element.50, bf16[32,32]{1,0:T(8,128)(2,1)S(1)} %collective-permute-done.7, bf16[32,512]{1,0:T(8,128)(2,1)S(1)} %collective-permute-done.6, bf16[32,32]{1,0:T(8,128)(2,1)S(1)} %collective-permute-done.5, ...), kind=kOutput, calls=%fused_computation.13 | convolution fusion | flops 1367875584 | bytes 1265664 | tf_op jit(solution)/shard_map/mrc,msc->mrs/dot_general | solution.py:193
  42.5 0.7 fusion.12
  43.1 0.8 copy.53.tf_ref
  43.9 16.0 %shard_map.94 = f32[8,8,128]{2,1,0:T(8,128)} custom-call(bf16[8,128,128]{2,1,0:T(8,128)(2,1)} %copy.53.tf_ref, bf16[8,192,192]{2,1,0:T(8,128)(2,1)} %fusion.8.w_ref), custom_call_target="tpu_custom_call" | custom-call | tf_op jit(solution)/shard_map/pallas_call | solution.py:68
  59.9 0.8 slice.206
  61.3 0.2 broadcast_in_dim.163
  61.5 0.2 broadcast_in_dim.160
  61.8 0.6 reshape.316
  62.5 11.1 %all-to-all-start.1 = ((f32[16,4,128]{2,1,0:T(4,128)}), f32[16,4,128]{2,1,0:T(4,128)S(1)}, u32[]{:S(2)}, u32[]{:S(2)}) async-start(f32[16,4,128]{2,1,0:T(4,128)} %reshape.316), calls=%async_computation.1 | async-start | bytes 65536 | tf_op jit(solution)/shard_map/all_to_all | solution.py:214
  73.7 6.4 %all-to-all-done.1 = f32[16,4,128]{2,1,0:T(4,128)S(1)} async-done(((f32[16,4,128]{2,1,0:T(4,128)}), f32[16,4,128]{2,1,0:T(4,128)S(1)}, u32[]{:S(2)}, u32[]{:S(2)}) %all-to-all-start.1) | async-done | bytes 32800 | tf_op jit(solution)/shard_map/all_to_all | solution.py:214
  80.4 0.2 select_n.76
  80.6 0.2 select_n.72
  80.9 3.1 %collective-permute-start.9 = (f32[4,3,38]{2,1,0:T(4,128)S(1)}, f32[4,3,38]{2,1,0:T(4,128)S(1)}, u32[]{:S(2)}, u32[]{:S(2)}) collective-permute-start(f32[4,3,38]{2,1,0:T(4,128)S(1)} %get-tuple-element.26), channel_id=1, source_target_pairs={{16,0},{32,16},{48,32},{64,48},{80,64},{96,80},{112,96},{17,1},{33... | collective-permute-start | bytes 5480 | tf_op jit(solution)/shard_map/ppermute | solution.py:175
  84.0 3.9 %collective-permute-start.8 = (f32[4,3,38]{2,1,0:T(4,128)S(1)}, f32[4,3,38]{2,1,0:T(4,128)S(1)}, u32[]{:S(2)}, u32[]{:S(2)}) collective-permute-start(f32[4,3,38]{2,1,0:T(4,128)S(1)} %get-tuple-element.25), channel_id=1, source_target_pairs={{0,16},{16,32},{32,48},{48,64},{64,80},{80,96},{96,112},{1,17},{17... | collective-permute-start | bytes 5480 | tf_op jit(solution)/shard_map/ppermute | solution.py:174
  87.9 0.7 select_reduce_fusion.1
  89.4 0.7 fusion.69
  (67 shorter events, 2.9 us)
Async XLA Ops:
  0.6 1.1 %copy-start = (bf16[512,512]{1,0:T(8,128)(2,1)S(1)}, bf16[512,512]{1,0:T(8,128)(2,1)}, u32[]{:S(2)}) copy-start(bf16[512,512]{1,0:T(8,128)(2,1)} %param.7) | copy-start | bytes 1572868
  1.7 1.1 %copy-start.6 = (s32[1,8]{1,0:T(1,128)S(1)}, s32[1,8]{1,0:T(1,128)}, u32[]{:S(2)}) copy-start(s32[1,8]{1,0:T(1,128)} %param.10) | copy-start | bytes 100
  4.8 8.6 %copy-start.1 = (bf16[512,512]{1,0:T(8,128)(2,1)S(1)}, bf16[512,512]{1,0:T(8,128)(2,1)}, u32[]{:S(2)}) copy-start(bf16[512,512]{1,0:T(8,128)(2,1)} %param.8) | copy-start | bytes 1572868
  4.8 18.4 %copy-start.4 = (s32[2,1,8]{2,1,0:T(1,128)S(1)}, s32[2,1,8]{2,1,0:T(1,128)}, u32[]{:S(2)}) copy-start(s32[2,1,8]{2,1,0:T(1,128)} %param.11) | copy-start | bytes 196
  4.8 18.4 %copy-start.2 = (s32[32,32]{1,0:T(8,128)S(1)}, s32[32,32]{1,0:T(8,128)}, u32[]{:S(2)}) copy-start(s32[32,32]{1,0:T(8,128)} %param.13) | copy-start | bytes 12292
  4.8 18.6 %copy-start.5 = (s32[1,8]{1,0:T(1,128)S(1)}, s32[1,8]{1,0:T(1,128)}, u32[]{:S(2)}) copy-start(s32[1,8]{1,0:T(1,128)} %param.12) | copy-start | bytes 100
  4.8 37.6 %all-to-all-start = ((bf16[32,128,128]{2,1,0:T(8,128)(2,1)}), bf16[32,128,128]{2,1,0:T(8,128)(2,1)S(1)}, u32[]{:S(2)}, u32[]{:S(2)}) async-start(bf16[32,128,128]{2,1,0:T(8,128)(2,1)} %copy.36), calls=%async_computation | async-start | bytes 2097152 | tf_op jit(solution)/shard_map/all_to_all | solution.py:187
  13.5 15.7 %collective-permute-start.7 = (bf16[32,32]{1,0:T(8,128)(2,1)S(1)}, bf16[32,32]{1,0:T(8,128)(2,1)S(1)}, u32[]{:S(2)}, u32[]{:S(2)}) collective-permute-start(bf16[32,32]{1,0:T(8,128)(2,1)S(1)} %get-tuple-element.20), channel_id=1, source_target_pairs={{17,0},{18,1},{19,2},{20,3},{21,4},{22,5},{23,6},{24,7},{25,8},{26... | collective-permute-start | bytes 6152 | tf_op jit(solution)/shard_map/ppermute | solution.py:101
  14.8 23.9 %collective-permute-start.6 = (bf16[32,512]{1,0:T(8,128)(2,1)S(1)}, bf16[32,512]{1,0:T(8,128)(2,1)S(1)}, u32[]{:S(2)}, u32[]{:S(2)}) collective-permute-start(bf16[32,512]{1,0:T(8,128)(2,1)S(1)} %get-tuple-element.22), channel_id=1, source_target_pairs={{16,0},{17,1},{18,2},{19,3},{20,4},{21,5},{22,6},{23,7},{24,8},{25... | collective-permute-start | bytes 98312 | tf_op jit(solution)/shard_map/ppermute | solution.py:101
  17.7 13.1 %collective-permute-start.5 = (bf16[32,32]{1,0:T(8,128)(2,1)S(1)}, bf16[32,32]{1,0:T(8,128)(2,1)S(1)}, u32[]{:S(2)}, u32[]{:S(2)}) collective-permute-start(bf16[32,32]{1,0:T(8,128)(2,1)S(1)} %get-tuple-element.18), channel_id=1, source_target_pairs={{16,1},{17,2},{18,3},{19,4},{20,5},{21,6},{22,7},{23,8},{24,9},{25... | collective-permute-start | bytes 6152 | tf_op jit(solution)/shard_map/ppermute | solution.py:101
  20.6 18.1 %collective-permute-start.4 = (bf16[512,32]{1,0:T(8,128)(2,1)S(1)}, bf16[512,32]{1,0:T(8,128)(2,1)S(1)}, u32[]{:S(2)}, u32[]{:S(2)}) collective-permute-start(bf16[512,32]{1,0:T(8,128)(2,1)S(1)} %get-tuple-element.24), channel_id=1, source_target_pairs={{1,0},{2,1},{3,2},{4,3},{5,4},{6,5},{7,6},{8,7},{9,8},{10,9},{11,1... | collective-permute-start | bytes 98312 | tf_op jit(solution)/shard_map/ppermute | solution.py:101
  21.9 11.5 %collective-permute-start.2 = (bf16[32,32]{1,0:T(8,128)(2,1)S(1)}, bf16[32,32]{1,0:T(8,128)(2,1)S(1)}, u32[]{:S(2)}, u32[]{:S(2)}) collective-permute-start(bf16[32,32]{1,0:T(8,128)(2,1)S(1)} %get-tuple-element.19), channel_id=1, source_target_pairs={{1,16},{2,17},{3,18},{4,19},{5,20},{6,21},{7,22},{8,23},{9,24},{10... | collective-permute-start | bytes 6152 | tf_op jit(solution)/shard_map/ppermute | solution.py:101
  29.2 9.5 %collective-permute-start.3 = (bf16[512,32]{1,0:T(8,128)(2,1)S(1)}, bf16[512,32]{1,0:T(8,128)(2,1)S(1)}, u32[]{:S(2)}, u32[]{:S(2)}) collective-permute-start(bf16[512,32]{1,0:T(8,128)(2,1)S(1)} %get-tuple-element.23), channel_id=1, source_target_pairs={{0,1},{1,2},{2,3},{3,4},{4,5},{5,6},{6,7},{7,8},{8,9},{9,10},{10,1... | collective-permute-start | bytes 98312 | tf_op jit(solution)/shard_map/ppermute | solution.py:101
  30.7 8.0 %collective-permute-start.1 = (bf16[32,512]{1,0:T(8,128)(2,1)S(1)}, bf16[32,512]{1,0:T(8,128)(2,1)S(1)}, u32[]{:S(2)}, u32[]{:S(2)}) collective-permute-start(bf16[32,512]{1,0:T(8,128)(2,1)S(1)} %get-tuple-element.21), channel_id=1, source_target_pairs={{0,16},{1,17},{2,18},{3,19},{4,20},{5,21},{6,22},{7,23},{8,24},{9,... | collective-permute-start | bytes 98312 | tf_op jit(solution)/shard_map/ppermute | solution.py:101
  33.4 5.3 %collective-permute-start = (bf16[32,32]{1,0:T(8,128)(2,1)S(1)}, bf16[32,32]{1,0:T(8,128)(2,1)S(1)}, u32[]{:S(2)}, u32[]{:S(2)}) collective-permute-start(bf16[32,32]{1,0:T(8,128)(2,1)S(1)} %get-tuple-element.17), channel_id=1, source_target_pairs={{0,17},{1,18},{2,19},{3,20},{4,21},{5,22},{6,23},{7,24},{8,25},{9,... | collective-permute-start | bytes 6152 | tf_op jit(solution)/shard_map/ppermute | solution.py:101
  60.8 28.4 %copy-start.3 = (f32[2,8]{1,0:T(2,128)}, f32[2,8]{1,0:T(2,128)S(1)}, u32[]{:S(2)}) copy-start(f32[2,8]{1,0:T(2,128)S(1)} %bitcast_negate_fusion) | copy-start | bytes 196
  62.5 17.6 %all-to-all-start.1 = ((f32[16,4,128]{2,1,0:T(4,128)}), f32[16,4,128]{2,1,0:T(4,128)S(1)}, u32[]{:S(2)}, u32[]{:S(2)}) async-start(f32[16,4,128]{2,1,0:T(4,128)} %reshape.316), calls=%async_computation.1 | async-start | bytes 65536 | tf_op jit(solution)/shard_map/all_to_all | solution.py:214
  80.9 7.7 %collective-permute-start.9 = (f32[4,3,38]{2,1,0:T(4,128)S(1)}, f32[4,3,38]{2,1,0:T(4,128)S(1)}, u32[]{:S(2)}, u32[]{:S(2)}) collective-permute-start(f32[4,3,38]{2,1,0:T(4,128)S(1)} %get-tuple-element.26), channel_id=1, source_target_pairs={{16,0},{32,16},{48,32},{64,48},{80,64},{96,80},{112,96},{17,1},{33... | collective-permute-start | bytes 5480 | tf_op jit(solution)/shard_map/ppermute | solution.py:175
  84.0 4.7 %collective-permute-start.8 = (f32[4,3,38]{2,1,0:T(4,128)S(1)}, f32[4,3,38]{2,1,0:T(4,128)S(1)}, u32[]{:S(2)}, u32[]{:S(2)}) collective-permute-start(f32[4,3,38]{2,1,0:T(4,128)S(1)} %get-tuple-element.25), channel_id=1, source_target_pairs={{0,16},{16,32},{32,48},{48,64},{64,80},{80,96},{96,112},{1,17},{17... | collective-permute-start | bytes 5480 | tf_op jit(solution)/shard_map/ppermute | solution.py:174

commit v9 on v8

--- a/solution.py
+++ b/solution.py
@@ -28,18 +28,16 @@
     whi[...] = jnp.zeros(whi.shape, jnp.float32)
     whi[:, 0:WIN - HALF] = wf[:, HALF:WIN]
     tfv = tf_ref[0].astype(jnp.float32)
-    t_top = tf_ref[0, 0:HALF, :]
-    t_bot = tf_ref[0, HALF:PATCH, :]
+    t_cat = jnp.concatenate([tf_ref[0, 0:HALF, :], tf_ref[0, HALF:PATCH, :]], axis=1)
     corr[...] = jnp.zeros(corr.shape, jnp.float32)
 
     def step(dy, carry):
-        w_lo = wlo[pl.ds(dy, PATCH), :].astype(jnp.bfloat16)
-        w_hi = whi[pl.ds(dy, PATCH), :].astype(jnp.bfloat16)
-        m_top = jnp.dot(t_top, w_hi, preferred_element_type=jnp.float32)
-        m_bot = jnp.dot(t_bot, w_lo, preferred_element_type=jnp.float32)
-        r_top = pltpu.roll(m_top, 0, axis=1, stride=1, stride_axis=0)
-        r_bot = pltpu.roll(m_bot, 0, axis=1, stride=1, stride_axis=0)
-        corr[pl.ds(dy, 1), :] = jnp.sum(r_top + r_bot, axis=0, keepdims=True)
+        w_cat = jnp.concatenate(
+            [whi[pl.ds(dy, PATCH), :], wlo[pl.ds(dy, PATCH), :]], axis=0
+        ).astype(jnp.bfloat16)
+        m = jnp.dot(t_cat, w_cat, preferred_element_type=jnp.float32)
+        r = pltpu.roll(m, 0, axis=1, stride=1, stride_axis=0)
+        corr[pl.ds(dy, 1), :] = jnp.sum(r, axis=0, keepdims=True)
         return carry
 
     lax.fori_loop(0, SHIFTS, step, 0, unroll=SHIFTS)

time: 90.8 us -> 86.7 us (0.955)
  Pallas kernels: 16 us -> 11.9 us
    pallas_call x1, Pallas kernels: 16 us -> 11.9 us  [flows_of(): pl.pallas_call(flow_kernel, grid=(n,), in_specs=[pl.BlockSpec((1, PATCH,...]
where the time goes in v9:
time: 86.7 us; the launch traced here: 86.1 us
  starting transfers between devices  45 us (52%)
  waiting for transfers between devices  12.7 us (15%)
  Pallas kernels  11.9 us (14%)
  local copies, waits for them, and re-layouts  6.43 us (7%)
  matrix products  6.09 us (7%)
  other arithmetic  3.03 us (3%)
  between operations  1.01 us (1%)
    ppermute x8, starting transfers between devices, halo(): pieces[dy, dx] = lax.ppermute(part, ('ty', 'tx'), pairs)  18.2 us
    pallas_call x1, Pallas kernels, flows_of(): pl.pallas_call(flow_kernel, grid=(n,), in_specs=[pl.BlockSpec((1, PATCH,...  11.9 us
    all_to_all x1, starting transfers between devices, shards(): lax.all_to_all(back, 'tx', split_axis=0, concat_axis=0, tiled=True)  11.1 us
    all_to_all x1, starting transfers between devices, shards(): lax.all_to_all(outgoing, 'tx', split_axis=0, concat_axis=0, tiled=True)  8.56 us
    all_to_all x1, waiting for transfers between devices, shards(): lax.all_to_all(back, 'tx', split_axis=0, concat_axis=0, tiled=True)  6.38 us
    ppermute x8, waiting for transfers between devices, halo(): pieces[dy, dx] = lax.ppermute(part, ('ty', 'tx'), pairs)  6.15 us
    ppermute x1, starting transfers between devices, rows_exchange(): above = lax.ppermute(tail, 'ty', [(i, i + 1) for i in range(count - 1)])  3.88 us
    dot_general x1, matrix products, shards(): jnp.einsum('mrc,msc->mrs', by_row.astype(jnp.bfloat16), wcol_pick, prefer...  3.75 us
  transfers between devices with their start and end apart: 12, of which 4 were waited for; matrix products, arithmetic and copies ran while one was open for 6% of the time, Pallas kernels for 0%

profile of v9, /device:TPU:1, one launch (start us, length us, event | category | flops | bytes accessed | tf_op | source)
XLA Modules:
  0.0 86.1 jit_solution(6692075324182687443)
XLA Ops:
  0.7 0.7 slice_bitcast_fusion.5
  1.5 0.2 copy-done
  1.7 1.1 %fusion.11 = bf16[8,128,128]{2,1,0:T(8,128)(2,1)S(1)} fusion(s32[8,128]{1,0:T(8,128)S(1)} %get-tuple-element.47, s32[8,128]{1,0:T(8,128)S(1)} %get-tuple-element.48, bf16[512,512]{1,0:T(8,128)(2,1)S(1)} %copy-done), kind=kOutput, calls=%fused_computation.14 | convolution fusion | flops 672792576 | bytes 794624 | tf_op jit(solution)/shard_map/kra,kia->kri/dot_general | solution.py:141
  2.9 0.6 convolution_convert_fusion
  3.4 1.4 %copy.36 = bf16[32,128,128]{2,1,0:T(8,128)(2,1)} copy(bf16[32,128,128]{2,0,1:T(8,128)(2,1)S(1)} %convolution_convert_fusion) | data formatting | bytes 2097152 | tf_op jit(solution)/shard_map/convert_element_type | solution.py:146
  4.8 8.6 %all-to-all-start = ((bf16[32,128,128]{2,1,0:T(8,128)(2,1)}), bf16[32,128,128]{2,1,0:T(8,128)(2,1)S(1)}, u32[]{:S(2)}, u32[]{:S(2)}) async-start(bf16[32,128,128]{2,1,0:T(8,128)(2,1)} %copy.36), calls=%async_computation | async-start | bytes 2097152 | tf_op jit(solution)/shard_map/all_to_all | solution.py:185
  13.5 1.3 %collective-permute-start.7 = (bf16[32,32]{1,0:T(8,128)(2,1)S(1)}, bf16[32,32]{1,0:T(8,128)(2,1)S(1)}, u32[]{:S(2)}, u32[]{:S(2)}) collective-permute-start(bf16[32,32]{1,0:T(8,128)(2,1)S(1)} %get-tuple-element.20), channel_id=1, source_target_pairs={{17,0},{18,1},{19,2},{20,3},{21,4},{22,5},{23,6},{24,7},{25,8},{26... | collective-permute-start | bytes 6152 | tf_op jit(solution)/shard_map/ppermute | solution.py:99
  14.8 2.9 %collective-permute-start.6 = (bf16[32,512]{1,0:T(8,128)(2,1)S(1)}, bf16[32,512]{1,0:T(8,128)(2,1)S(1)}, u32[]{:S(2)}, u32[]{:S(2)}) collective-permute-start(bf16[32,512]{1,0:T(8,128)(2,1)S(1)} %get-tuple-element.22), channel_id=1, source_target_pairs={{16,0},{17,1},{18,2},{19,3},{20,4},{21,5},{22,6},{23,7},{24,8},{25... | collective-permute-start | bytes 98312 | tf_op jit(solution)/shard_map/ppermute | solution.py:99
  17.7 2.8 %collective-permute-start.5 = (bf16[32,32]{1,0:T(8,128)(2,1)S(1)}, bf16[32,32]{1,0:T(8,128)(2,1)S(1)}, u32[]{:S(2)}, u32[]{:S(2)}) collective-permute-start(bf16[32,32]{1,0:T(8,128)(2,1)S(1)} %get-tuple-element.18), channel_id=1, source_target_pairs={{16,1},{17,2},{18,3},{19,4},{20,5},{21,6},{22,7},{23,8},{24,9},{25... | collective-permute-start | bytes 6152 | tf_op jit(solution)/shard_map/ppermute | solution.py:99
  20.6 1.3 %collective-permute-start.4 = (bf16[512,32]{1,0:T(8,128)(2,1)S(1)}, bf16[512,32]{1,0:T(8,128)(2,1)S(1)}, u32[]{:S(2)}, u32[]{:S(2)}) collective-permute-start(bf16[512,32]{1,0:T(8,128)(2,1)S(1)} %get-tuple-element.24), channel_id=1, source_target_pairs={{1,0},{2,1},{3,2},{4,3},{5,4},{6,5},{7,6},{8,7},{9,8},{10,9},{11,1... | collective-permute-start | bytes 98312 | tf_op jit(solution)/shard_map/ppermute | solution.py:99
  21.9 1.3 %collective-permute-start.2 = (bf16[32,32]{1,0:T(8,128)(2,1)S(1)}, bf16[32,32]{1,0:T(8,128)(2,1)S(1)}, u32[]{:S(2)}, u32[]{:S(2)}) collective-permute-start(bf16[32,32]{1,0:T(8,128)(2,1)S(1)} %get-tuple-element.19), channel_id=1, source_target_pairs={{1,16},{2,17},{3,18},{4,19},{5,20},{6,21},{7,22},{8,23},{9,24},{10... | collective-permute-start | bytes 6152 | tf_op jit(solution)/shard_map/ppermute | solution.py:99
  23.7 5.5 %collective-permute-done.7 = bf16[32,32]{1,0:T(8,128)(2,1)S(1)} collective-permute-done((bf16[32,32]{1,0:T(8,128)(2,1)S(1)}, bf16[32,32]{1,0:T(8,128)(2,1)S(1)}, u32[]{:S(2)}, u32[]{:S(2)}) %collective-permute-start.7) | collective-permute-done | bytes 2080 | tf_op jit(solution)/shard_map/ppermute | solution.py:99
  29.2 1.6 %collective-permute-start.3 = (bf16[512,32]{1,0:T(8,128)(2,1)S(1)}, bf16[512,32]{1,0:T(8,128)(2,1)S(1)}, u32[]{:S(2)}, u32[]{:S(2)}) collective-permute-start(bf16[512,32]{1,0:T(8,128)(2,1)S(1)} %get-tuple-element.23), channel_id=1, source_target_pairs={{0,1},{1,2},{2,3},{3,4},{4,5},{5,6},{6,7},{7,8},{8,9},{9,10},{10,1... | collective-permute-start | bytes 98312 | tf_op jit(solution)/shard_map/ppermute | solution.py:99
  30.7 2.6 %collective-permute-start.1 = (bf16[32,512]{1,0:T(8,128)(2,1)S(1)}, bf16[32,512]{1,0:T(8,128)(2,1)S(1)}, u32[]{:S(2)}, u32[]{:S(2)}) collective-permute-start(bf16[32,512]{1,0:T(8,128)(2,1)S(1)} %get-tuple-element.21), channel_id=1, source_target_pairs={{0,16},{1,17},{2,18},{3,19},{4,20},{5,21},{6,22},{7,23},{8,24},{9,... | collective-permute-start | bytes 98312 | tf_op jit(solution)/shard_map/ppermute | solution.py:99
  33.4 4.5 %collective-permute-start = (bf16[32,32]{1,0:T(8,128)(2,1)S(1)}, bf16[32,32]{1,0:T(8,128)(2,1)S(1)}, u32[]{:S(2)}, u32[]{:S(2)}) collective-permute-start(bf16[32,32]{1,0:T(8,128)(2,1)S(1)} %get-tuple-element.17), channel_id=1, source_target_pairs={{0,17},{1,18},{2,19},{3,20},{4,21},{5,22},{6,23},{7,24},{8,25},{9,... | collective-permute-start | bytes 6152 | tf_op jit(solution)/shard_map/ppermute | solution.py:99
  38.0 0.7 collective-permute-done
  38.7 3.8 %fusion.8.w_ref = bf16[8,192,192]{2,1,0:T(8,128)(2,1)} fusion(s32[8,192]{1,0:T(8,128)S(1)} %get-tuple-element.49, s32[8,192]{1,0:T(8,128)S(1)} %get-tuple-element.50, bf16[32,32]{1,0:T(8,128)(2,1)S(1)} %collective-permute-done.7, bf16[32,512]{1,0:T(8,128)(2,1)S(1)} %collective-permute-done.6, bf16[32,32]{1,0:T(8,128)(2,1)S(1)} %collective-permute-done.5, ...), kind=kOutput, calls=%fused_computation.13 | convolution fusion | flops 1367875584 | bytes 1265664 | tf_op jit(solution)/shard_map/mrc,msc->mrs/dot_general | solution.py:191
  42.5 0.7 fusion.12
  43.1 0.8 copy.53.tf_ref
  43.9 11.9 %shard_map.94 = f32[8,8,128]{2,1,0:T(8,128)} custom-call(bf16[8,128,128]{2,1,0:T(8,128)(2,1)} %copy.53.tf_ref, bf16[8,192,192]{2,1,0:T(8,128)(2,1)} %fusion.8.w_ref), custom_call_target="tpu_custom_call" | custom-call | tf_op jit(solution)/shard_map/pallas_call | solution.py:66
  55.8 0.8 slice.206
  57.2 0.2 broadcast_in_dim.163
  57.4 0.2 broadcast_in_dim.160
  57.7 0.6 reshape.316
  58.4 11.1 %all-to-all-start.1 = ((f32[16,4,128]{2,1,0:T(4,128)}), f32[16,4,128]{2,1,0:T(4,128)S(1)}, u32[]{:S(2)}, u32[]{:S(2)}) async-start(f32[16,4,128]{2,1,0:T(4,128)} %reshape.316), calls=%async_computation.1 | async-start | bytes 65536 | tf_op jit(solution)/shard_map/all_to_all | solution.py:212
  69.6 6.4 %all-to-all-done.1 = f32[16,4,128]{2,1,0:T(4,128)S(1)} async-done(((f32[16,4,128]{2,1,0:T(4,128)}), f32[16,4,128]{2,1,0:T(4,128)S(1)}, u32[]{:S(2)}, u32[]{:S(2)}) %all-to-all-start.1) | async-done | bytes 32800 | tf_op jit(solution)/shard_map/all_to_all | solution.py:212
  76.3 0.2 select_n.76
  76.5 0.2 select_n.72
  76.8 3.1 %collective-permute-start.9 = (f32[4,3,38]{2,1,0:T(4,128)S(1)}, f32[4,3,38]{2,1,0:T(4,128)S(1)}, u32[]{:S(2)}, u32[]{:S(2)}) collective-permute-start(f32[4,3,38]{2,1,0:T(4,128)S(1)} %get-tuple-element.26), channel_id=1, source_target_pairs={{16,0},{32,16},{48,32},{64,48},{80,64},{96,80},{112,96},{17,1},{33... | collective-permute-start | bytes 5480 | tf_op jit(solution)/shard_map/ppermute | solution.py:173
  79.9 3.9 %collective-permute-start.8 = (f32[4,3,38]{2,1,0:T(4,128)S(1)}, f32[4,3,38]{2,1,0:T(4,128)S(1)}, u32[]{:S(2)}, u32[]{:S(2)}) collective-permute-start(f32[4,3,38]{2,1,0:T(4,128)S(1)} %get-tuple-element.25), channel_id=1, source_target_pairs={{0,16},{16,32},{32,48},{48,64},{64,80},{80,96},{96,112},{1,17},{17... | collective-permute-start | bytes 5480 | tf_op jit(solution)/shard_map/ppermute | solution.py:172
  83.8 0.7 select_reduce_fusion.1
  85.3 0.7 fusion.69
  (67 shorter events, 2.9 us)
Async XLA Ops:
  0.6 1.1 %copy-start = (bf16[512,512]{1,0:T(8,128)(2,1)S(1)}, bf16[512,512]{1,0:T(8,128)(2,1)}, u32[]{:S(2)}) copy-start(bf16[512,512]{1,0:T(8,128)(2,1)} %param.7) | copy-start | bytes 1572868
  1.7 1.1 %copy-start.6 = (s32[1,8]{1,0:T(1,128)S(1)}, s32[1,8]{1,0:T(1,128)}, u32[]{:S(2)}) copy-start(s32[1,8]{1,0:T(1,128)} %param.10) | copy-start | bytes 100
  4.8 8.6 %copy-start.1 = (bf16[512,512]{1,0:T(8,128)(2,1)S(1)}, bf16[512,512]{1,0:T(8,128)(2,1)}, u32[]{:S(2)}) copy-start(bf16[512,512]{1,0:T(8,128)(2,1)} %param.8) | copy-start | bytes 1572868
  4.8 18.4 %copy-start.4 = (s32[2,1,8]{2,1,0:T(1,128)S(1)}, s32[2,1,8]{2,1,0:T(1,128)}, u32[]{:S(2)}) copy-start(s32[2,1,8]{2,1,0:T(1,128)} %param.11) | copy-start | bytes 196
  4.8 18.4 %copy-start.2 = (s32[32,32]{1,0:T(8,128)S(1)}, s32[32,32]{1,0:T(8,128)}, u32[]{:S(2)}) copy-start(s32[32,32]{1,0:T(8,128)} %param.13) | copy-start | bytes 12292
  4.8 18.6 %copy-start.5 = (s32[1,8]{1,0:T(1,128)S(1)}, s32[1,8]{1,0:T(1,128)}, u32[]{:S(2)}) copy-start(s32[1,8]{1,0:T(1,128)} %param.12) | copy-start | bytes 100
  4.8 37.6 %all-to-all-start = ((bf16[32,128,128]{2,1,0:T(8,128)(2,1)}), bf16[32,128,128]{2,1,0:T(8,128)(2,1)S(1)}, u32[]{:S(2)}, u32[]{:S(2)}) async-start(bf16[32,128,128]{2,1,0:T(8,128)(2,1)} %copy.36), calls=%async_computation | async-start | bytes 2097152 | tf_op jit(solution)/shard_map/all_to_all | solution.py:185
  13.5 15.7 %collective-permute-start.7 = (bf16[32,32]{1,0:T(8,128)(2,1)S(1)}, bf16[32,32]{1,0:T(8,128)(2,1)S(1)}, u32[]{:S(2)}, u32[]{:S(2)}) collective-permute-start(bf16[32,32]{1,0:T(8,128)(2,1)S(1)} %get-tuple-element.20), channel_id=1, source_target_pairs={{17,0},{18,1},{19,2},{20,3},{21,4},{22,5},{23,6},{24,7},{25,8},{26... | collective-permute-start | bytes 6152 | tf_op jit(solution)/shard_map/ppermute | solution.py:99
  14.8 23.9 %collective-permute-start.6 = (bf16[32,512]{1,0:T(8,128)(2,1)S(1)}, bf16[32,512]{1,0:T(8,128)(2,1)S(1)}, u32[]{:S(2)}, u32[]{:S(2)}) collective-permute-start(bf16[32,512]{1,0:T(8,128)(2,1)S(1)} %get-tuple-element.22), channel_id=1, source_target_pairs={{16,0},{17,1},{18,2},{19,3},{20,4},{21,5},{22,6},{23,7},{24,8},{25... | collective-permute-start | bytes 98312 | tf_op jit(solution)/shard_map/ppermute | solution.py:99
  17.7 13.1 %collective-permute-start.5 = (bf16[32,32]{1,0:T(8,128)(2,1)S(1)}, bf16[32,32]{1,0:T(8,128)(2,1)S(1)}, u32[]{:S(2)}, u32[]{:S(2)}) collective-permute-start(bf16[32,32]{1,0:T(8,128)(2,1)S(1)} %get-tuple-element.18), channel_id=1, source_target_pairs={{16,1},{17,2},{18,3},{19,4},{20,5},{21,6},{22,7},{23,8},{24,9},{25... | collective-permute-start | bytes 6152 | tf_op jit(solution)/shard_map/ppermute | solution.py:99
  20.6 18.1 %collective-permute-start.4 = (bf16[512,32]{1,0:T(8,128)(2,1)S(1)}, bf16[512,32]{1,0:T(8,128)(2,1)S(1)}, u32[]{:S(2)}, u32[]{:S(2)}) collective-permute-start(bf16[512,32]{1,0:T(8,128)(2,1)S(1)} %get-tuple-element.24), channel_id=1, source_target_pairs={{1,0},{2,1},{3,2},{4,3},{5,4},{6,5},{7,6},{8,7},{9,8},{10,9},{11,1... | collective-permute-start | bytes 98312 | tf_op jit(solution)/shard_map/ppermute | solution.py:99
  21.9 11.5 %collective-permute-start.2 = (bf16[32,32]{1,0:T(8,128)(2,1)S(1)}, bf16[32,32]{1,0:T(8,128)(2,1)S(1)}, u32[]{:S(2)}, u32[]{:S(2)}) collective-permute-start(bf16[32,32]{1,0:T(8,128)(2,1)S(1)} %get-tuple-element.19), channel_id=1, source_target_pairs={{1,16},{2,17},{3,18},{4,19},{5,20},{6,21},{7,22},{8,23},{9,24},{10... | collective-permute-start | bytes 6152 | tf_op jit(solution)/shard_map/ppermute | solution.py:99
  29.2 9.5 %collective-permute-start.3 = (bf16[512,32]{1,0:T(8,128)(2,1)S(1)}, bf16[512,32]{1,0:T(8,128)(2,1)S(1)}, u32[]{:S(2)}, u32[]{:S(2)}) collective-permute-start(bf16[512,32]{1,0:T(8,128)(2,1)S(1)} %get-tuple-element.23), channel_id=1, source_target_pairs={{0,1},{1,2},{2,3},{3,4},{4,5},{5,6},{6,7},{7,8},{8,9},{9,10},{10,1... | collective-permute-start | bytes 98312 | tf_op jit(solution)/shard_map/ppermute | solution.py:99
  30.7 8.0 %collective-permute-start.1 = (bf16[32,512]{1,0:T(8,128)(2,1)S(1)}, bf16[32,512]{1,0:T(8,128)(2,1)S(1)}, u32[]{:S(2)}, u32[]{:S(2)}) collective-permute-start(bf16[32,512]{1,0:T(8,128)(2,1)S(1)} %get-tuple-element.21), channel_id=1, source_target_pairs={{0,16},{1,17},{2,18},{3,19},{4,20},{5,21},{6,22},{7,23},{8,24},{9,... | collective-permute-start | bytes 98312 | tf_op jit(solution)/shard_map/ppermute | solution.py:99
  33.4 5.3 %collective-permute-start = (bf16[32,32]{1,0:T(8,128)(2,1)S(1)}, bf16[32,32]{1,0:T(8,128)(2,1)S(1)}, u32[]{:S(2)}, u32[]{:S(2)}) collective-permute-start(bf16[32,32]{1,0:T(8,128)(2,1)S(1)} %get-tuple-element.17), channel_id=1, source_target_pairs={{0,17},{1,18},{2,19},{3,20},{4,21},{5,22},{6,23},{7,24},{8,25},{9,... | collective-permute-start | bytes 6152 | tf_op jit(solution)/shard_map/ppermute | solution.py:99
  56.7 28.4 %copy-start.3 = (f32[2,8]{1,0:T(2,128)}, f32[2,8]{1,0:T(2,128)S(1)}, u32[]{:S(2)}) copy-start(f32[2,8]{1,0:T(2,128)S(1)} %bitcast_negate_fusion) | copy-start | bytes 196
  58.4 17.6 %all-to-all-start.1 = ((f32[16,4,128]{2,1,0:T(4,128)}), f32[16,4,128]{2,1,0:T(4,128)S(1)}, u32[]{:S(2)}, u32[]{:S(2)}) async-start(f32[16,4,128]{2,1,0:T(4,128)} %reshape.316), calls=%async_computation.1 | async-start | bytes 65536 | tf_op jit(solution)/shard_map/all_to_all | solution.py:212
  76.8 7.7 %collective-permute-start.9 = (f32[4,3,38]{2,1,0:T(4,128)S(1)}, f32[4,3,38]{2,1,0:T(4,128)S(1)}, u32[]{:S(2)}, u32[]{:S(2)}) collective-permute-start(f32[4,3,38]{2,1,0:T(4,128)S(1)} %get-tuple-element.26), channel_id=1, source_target_pairs={{16,0},{32,16},{48,32},{64,48},{80,64},{96,80},{112,96},{17,1},{33... | collective-permute-start | bytes 5480 | tf_op jit(solution)/shard_map/ppermute | solution.py:173
  79.9 4.7 %collective-permute-start.8 = (f32[4,3,38]{2,1,0:T(4,128)S(1)}, f32[4,3,38]{2,1,0:T(4,128)S(1)}, u32[]{:S(2)}, u32[]{:S(2)}) collective-permute-start(f32[4,3,38]{2,1,0:T(4,128)S(1)} %get-tuple-element.25), channel_id=1, source_target_pairs={{0,16},{16,32},{32,48},{48,64},{64,80},{80,96},{96,112},{1,17},{17... | collective-permute-start | bytes 5480 | tf_op jit(solution)/shard_map/ppermute | solution.py:172

commit v10 on v9

--- a/solution.py
+++ b/solution.py
@@ -75,6 +75,23 @@
                         pltpu.VMEM((72, PATCH), jnp.float32)],
     )(tflipped, windows)
     return out[:, 0:2, 0].T
+
+
+def padded_2(cells, sides, width):
+    for axis, dim in sides:
+        count = lax.axis_size(axis)
+        ends = count - 1
+        head = lax.slice_in_dim(cells, 0, width, axis=dim)
+        tail = lax.slice_in_dim(cells, cells.shape[dim] - width, cells.shape[dim], axis=dim)
+        cells = jnp.concatenate(
+            [
+                lax.ppermute(tail, axis, [(i, (i + 1) % count) for i in range(ends)]),
+                cells,
+                lax.ppermute(head, axis, [((i + 1) % count, i) for i in range(ends)]),
+            ],
+            axis=dim,
+        )
+    return cells
 
 
 def halo(cells, width):
@@ -183,7 +200,7 @@
     mask = node_mask.astype(f32)
     w = ITERS_R
     arrived = lax.all_to_all(outgoing, "tx", split_axis=0, concat_axis=0, tiled=True)
-    b_wide = halo(section_b, RADIUS)
+    b_wide = padded_2(section_b, (("ty", 0), ("tx", 1)), RADIUS)
 
     wrow_pick = one_hot(window_corner[0, 0], WIN, b_wide.shape[0])
     wcol_pick = one_hot(window_corner[1, 0], WIN, b_wide.shape[1])

time: 86.7 us -> 76.9 us (0.89)
  starting transfers between devices: 45 us -> 36.4 us
  waiting for transfers between devices: 12.7 us -> 11.6 us
    ppermute x8 -> x4, starting transfers between devices: 18.2 us -> 11.4 us  [the longest x2 8.22 us: padded_2(): lax.ppermute(tail, axis, [(i, (i + 1) % count) for i in range(ends)])]
    all_to_all x1, starting transfers between devices: 11.1 us -> 9.27 us  [shards(): lax.all_to_all(back, 'tx', split_axis=0, concat_axis=0, tiled=True)]
    ppermute x8 -> x4, waiting for transfers between devices: 6.15 us -> 5.01 us  [the longest x2 4.98 us: padded_2(): lax.ppermute(head, axis, [((i + 1) % count, i) for i in range(ends)])]
    ppermute x1, starting transfers between devices: 3.88 us -> 4.84 us  [rows_exchange(): above = lax.ppermute(tail, 'ty', [(i, i + 1) for i in range(count - 1)])]
  transfers between devices with their start and end apart: 12 -> 8, of which waited for: 4 -> 4; matrix products, arithmetic and copies ran while one was open for 6% -> 7% of each run, Pallas kernels for 0% -> 0%
where the time goes in v10:
time: 76.9 us; the launch traced here: 76.4 us
  starting transfers between devices  36.4 us (47%)
  Pallas kernels  11.9 us (15%)
  waiting for transfers between devices  11.6 us (15%)
  local copies, waits for them, and re-layouts  6.38 us (8%)
  matrix products  6.14 us (8%)
  other arithmetic  3.03 us (4%)
  between operations  0.97 us (1%)
    pallas_call x1, Pallas kernels, flows_of(): pl.pallas_call(flow_kernel, grid=(n,), in_specs=[pl.BlockSpec((1, PATCH,...  11.9 us
    all_to_all x1, starting transfers between devices, shards(): lax.all_to_all(back, 'tx', split_axis=0, concat_axis=0, tiled=True)  9.27 us
    all_to_all x1, starting transfers between devices, shards(): lax.all_to_all(outgoing, 'tx', split_axis=0, concat_axis=0, tiled=True)  8.56 us
    ppermute x2, starting transfers between devices, padded_2(): lax.ppermute(tail, axis, [(i, (i + 1) % count) for i in range(ends)])  8.22 us
    all_to_all x1, waiting for transfers between devices, shards(): lax.all_to_all(back, 'tx', split_axis=0, concat_axis=0, tiled=True)  6.43 us
    ppermute x2, waiting for transfers between devices, padded_2(): lax.ppermute(head, axis, [((i + 1) % count, i) for i in range(ends)])  4.98 us
    ppermute x1, starting transfers between devices, rows_exchange(): above = lax.ppermute(tail, 'ty', [(i, i + 1) for i in range(count - 1)])  4.84 us
    dot_general x1, matrix products, shards(): jnp.einsum('mrc,msc->mrs', by_row.astype(jnp.bfloat16), wcol_pick, prefer...  3.8 us
  transfers between devices with their start and end apart: 8, of which 4 were waited for; matrix products, arithmetic and copies ran while one was open for 7% of the time, Pallas kernels for 0%

profile of v10, /device:TPU:1, one launch (start us, length us, event | category | flops | bytes accessed | tf_op | source)
XLA Modules:
  0.0 76.4 jit_solution(15577852478845660712)
XLA Ops:
  0.7 0.7 slice_bitcast_fusion.5
  1.5 0.2 copy-done
  1.7 1.1 %fusion.11 = bf16[8,128,128]{2,1,0:T(8,128)(2,1)S(1)} fusion(s32[8,128]{1,0:T(8,128)S(1)} %get-tuple-element.43, s32[8,128]{1,0:T(8,128)S(1)} %get-tuple-element.44, bf16[512,512]{1,0:T(8,128)(2,1)S(1)} %copy-done), kind=kOutput, calls=%fused_computation.14 | convolution fusion | flops 672792576 | bytes 794624 | tf_op jit(solution)/shard_map/kra,kia->kri/dot_general | solution.py:158
  2.9 0.6 convolution_convert_fusion
  3.4 1.4 %copy.36 = bf16[32,128,128]{2,1,0:T(8,128)(2,1)} copy(bf16[32,128,128]{2,0,1:T(8,128)(2,1)S(1)} %convolution_convert_fusion) | data formatting | bytes 2097152 | tf_op jit(solution)/shard_map/convert_element_type | solution.py:163
  4.8 8.6 %all-to-all-start = ((bf16[32,128,128]{2,1,0:T(8,128)(2,1)}), bf16[32,128,128]{2,1,0:T(8,128)(2,1)S(1)}, u32[]{:S(2)}, u32[]{:S(2)}) async-start(bf16[32,128,128]{2,1,0:T(8,128)(2,1)} %copy.36), calls=%async_computation | async-start | bytes 2097152 | tf_op jit(solution)/shard_map/all_to_all | solution.py:202
  13.4 4.0 %collective-permute-start = (bf16[32,512]{1,0:T(8,128)(2,1)S(1)}, bf16[32,512]{1,0:T(8,128)(2,1)S(1)}, u32[]{:S(2)}, u32[]{:S(2)}) collective-permute-start(bf16[32,512]{1,0:T(8,128)(2,1)S(1)} %get-tuple-element.20), channel_id=1, source_target_pairs={{0,16},{16,32},{32,48},{48,64},{64,80},{80,96},{96,112},{1,17},{17... | collective-permute-start | bytes 98312 | tf_op jit(solution)/shard_map/ppermute | solution.py:88
  17.4 1.9 %collective-permute-start.1 = (bf16[32,512]{1,0:T(8,128)(2,1)S(1)}, bf16[32,512]{1,0:T(8,128)(2,1)S(1)}, u32[]{:S(2)}, u32[]{:S(2)}) collective-permute-start(bf16[32,512]{1,0:T(8,128)(2,1)S(1)} %get-tuple-element.19), channel_id=1, source_target_pairs={{16,0},{32,16},{48,32},{64,48},{80,64},{96,80},{112,96},{17,1},{33... | collective-permute-start | bytes 98312 | tf_op jit(solution)/shard_map/ppermute | solution.py:90
  19.9 3.0 %collective-permute-done.1 = bf16[32,512]{1,0:T(8,128)(2,1)S(1)} collective-permute-done((bf16[32,512]{1,0:T(8,128)(2,1)S(1)}, bf16[32,512]{1,0:T(8,128)(2,1)S(1)}, u32[]{:S(2)}, u32[]{:S(2)}) %collective-permute-start.1) | collective-permute-done | bytes 32800 | tf_op jit(solution)/shard_map/ppermute | solution.py:90
  23.0 0.1 fusion.59
  23.1 1.3 %collective-permute-start.3 = (bf16[576,32]{1,0:T(8,128)(2,1)S(1)}, bf16[576,32]{1,0:T(8,128)(2,1)S(1)}, u32[]{:S(2)}, u32[]{:S(2)}) collective-permute-start(bf16[576,32]{1,0:T(8,128)(2,1)S(1)} %get-tuple-element.18), channel_id=1, source_target_pairs={{1,0},{2,1},{3,2},{4,3},{5,4},{6,5},{7,6},{8,7},{9,8},{10,9},{11,1... | collective-permute-start | bytes 110600 | tf_op jit(solution)/shard_map/ppermute | solution.py:90
  24.4 4.2 %collective-permute-start.2 = (bf16[576,32]{1,0:T(8,128)(2,1)S(1)}, bf16[576,32]{1,0:T(8,128)(2,1)S(1)}, u32[]{:S(2)}, u32[]{:S(2)}) collective-permute-start(bf16[576,32]{1,0:T(8,128)(2,1)S(1)} %get-tuple-element.17), channel_id=1, source_target_pairs={{0,1},{1,2},{2,3},{3,4},{4,5},{5,6},{6,7},{7,8},{8,9},{9,10},{10,1... | collective-permute-start | bytes 110600 | tf_op jit(solution)/shard_map/ppermute | solution.py:88
  28.7 2.0 %collective-permute-done.3 = bf16[576,32]{1,0:T(8,128)(2,1)S(1)} collective-permute-done((bf16[576,32]{1,0:T(8,128)(2,1)S(1)}, bf16[576,32]{1,0:T(8,128)(2,1)S(1)}, u32[]{:S(2)}, u32[]{:S(2)}) %collective-permute-start.3) | collective-permute-done | bytes 36896 | tf_op jit(solution)/shard_map/ppermute | solution.py:90
  30.7 3.8 %fusion.8.w_ref = bf16[8,192,192]{2,1,0:T(8,128)(2,1)} fusion(s32[8,192]{1,0:T(8,128)S(1)} %get-tuple-element.45, s32[8,192]{1,0:T(8,128)S(1)} %get-tuple-element.46, bf16[576,32]{1,0:T(8,128)(2,1)S(1)} %collective-permute-done.3, bf16[576,512]{1,0:T(8,128)(2,1)S(1)} %constant_dynamic-update-slice_fusion, bf16[576,32]{1,0:T(8,128)(2,1)S(1)} %collective-permute-done.2), kind=kOutput, calls=%fused_computation.13 | convolution fusion | flops 1363894272 | bytes 1265664 | tf_op jit(solution)/shard_map/mrc,msc->mrs/dot_general | solution.py:208
  34.5 0.7 fusion.12
  35.1 0.8 copy.53.tf_ref
  35.9 11.9 %shard_map.94 = f32[8,8,128]{2,1,0:T(8,128)} custom-call(bf16[8,128,128]{2,1,0:T(8,128)(2,1)} %copy.53.tf_ref, bf16[8,192,192]{2,1,0:T(8,128)(2,1)} %fusion.8.w_ref), custom_call_target="tpu_custom_call" | custom-call | tf_op jit(solution)/shard_map/pallas_call | solution.py:66
  47.8 0.8 slice.192
  49.2 0.2 broadcast_in_dim.163
  49.4 0.2 broadcast_in_dim.160
  49.7 0.6 reshape.316
  50.4 9.3 %all-to-all-start.1 = ((f32[16,4,128]{2,1,0:T(4,128)}), f32[16,4,128]{2,1,0:T(4,128)S(1)}, u32[]{:S(2)}, u32[]{:S(2)}) async-start(f32[16,4,128]{2,1,0:T(4,128)} %reshape.316), calls=%async_computation.1 | async-start | bytes 65536 | tf_op jit(solution)/shard_map/all_to_all | solution.py:229
  59.7 6.4 %all-to-all-done.1 = f32[16,4,128]{2,1,0:T(4,128)S(1)} async-done(((f32[16,4,128]{2,1,0:T(4,128)}), f32[16,4,128]{2,1,0:T(4,128)S(1)}, u32[]{:S(2)}, u32[]{:S(2)}) %all-to-all-start.1) | async-done | bytes 32800 | tf_op jit(solution)/shard_map/all_to_all | solution.py:229
  66.5 0.2 select_n.76
  66.7 0.2 select_n.72
  67.0 2.3 %collective-permute-start.5 = (f32[4,3,38]{2,1,0:T(4,128)S(1)}, f32[4,3,38]{2,1,0:T(4,128)S(1)}, u32[]{:S(2)}, u32[]{:S(2)}) collective-permute-start(f32[4,3,38]{2,1,0:T(4,128)S(1)} %get-tuple-element.22), channel_id=1, source_target_pairs={{16,0},{32,16},{48,32},{64,48},{80,64},{96,80},{112,96},{17,1},{33... | collective-permute-start | bytes 5480 | tf_op jit(solution)/shard_map/ppermute | solution.py:190
  69.3 4.8 %collective-permute-start.4 = (f32[4,3,38]{2,1,0:T(4,128)S(1)}, f32[4,3,38]{2,1,0:T(4,128)S(1)}, u32[]{:S(2)}, u32[]{:S(2)}) collective-permute-start(f32[4,3,38]{2,1,0:T(4,128)S(1)} %get-tuple-element.21), channel_id=1, source_target_pairs={{0,16},{16,32},{32,48},{48,64},{64,80},{80,96},{96,112},{1,17},{17... | collective-permute-start | bytes 5480 | tf_op jit(solution)/shard_map/ppermute | solution.py:189
  74.2 0.7 select_reduce_fusion.1
  74.8 0.1 collective-permute-done.4
  74.9 0.1 pad_maximum_fusion
  75.6 0.1 fusion.29
  75.7 0.7 fusion.45
  (61 shorter events, 2.4 us)
Async XLA Ops:
  0.6 1.1 %copy-start = (bf16[512,512]{1,0:T(8,128)(2,1)S(1)}, bf16[512,512]{1,0:T(8,128)(2,1)}, u32[]{:S(2)}) copy-start(bf16[512,512]{1,0:T(8,128)(2,1)} %param.7) | copy-start | bytes 1572868
  1.7 1.1 %copy-start.6 = (s32[1,8]{1,0:T(1,128)S(1)}, s32[1,8]{1,0:T(1,128)}, u32[]{:S(2)}) copy-start(s32[1,8]{1,0:T(1,128)} %param.10) | copy-start | bytes 100
  4.8 8.6 %copy-start.1 = (bf16[512,512]{1,0:T(8,128)(2,1)S(1)}, bf16[512,512]{1,0:T(8,128)(2,1)}, u32[]{:S(2)}) copy-start(bf16[512,512]{1,0:T(8,128)(2,1)} %param.8) | copy-start | bytes 1572868
  4.8 14.6 %copy-start.4 = (s32[2,1,8]{2,1,0:T(1,128)S(1)}, s32[2,1,8]{2,1,0:T(1,128)}, u32[]{:S(2)}) copy-start(s32[2,1,8]{2,1,0:T(1,128)} %param.11) | copy-start | bytes 196
  4.8 14.6 %copy-start.5 = (s32[1,8]{1,0:T(1,128)S(1)}, s32[1,8]{1,0:T(1,128)}, u32[]{:S(2)}) copy-start(s32[1,8]{1,0:T(1,128)} %param.12) | copy-start | bytes 100
  4.8 14.7 %copy-start.2 = (s32[32,32]{1,0:T(8,128)S(1)}, s32[32,32]{1,0:T(8,128)}, u32[]{:S(2)}) copy-start(s32[32,32]{1,0:T(8,128)} %param.13) | copy-start | bytes 12292
  4.8 29.6 %all-to-all-start = ((bf16[32,128,128]{2,1,0:T(8,128)(2,1)}), bf16[32,128,128]{2,1,0:T(8,128)(2,1)S(1)}, u32[]{:S(2)}, u32[]{:S(2)}) async-start(bf16[32,128,128]{2,1,0:T(8,128)(2,1)} %copy.36), calls=%async_computation | async-start | bytes 2097152 | tf_op jit(solution)/shard_map/all_to_all | solution.py:202
  13.4 6.5 %collective-permute-start = (bf16[32,512]{1,0:T(8,128)(2,1)S(1)}, bf16[32,512]{1,0:T(8,128)(2,1)S(1)}, u32[]{:S(2)}, u32[]{:S(2)}) collective-permute-start(bf16[32,512]{1,0:T(8,128)(2,1)S(1)} %get-tuple-element.20), channel_id=1, source_target_pairs={{0,16},{16,32},{32,48},{48,64},{64,80},{80,96},{96,112},{1,17},{17... | collective-permute-start | bytes 98312 | tf_op jit(solution)/shard_map/ppermute | solution.py:88
  17.4 5.5 %collective-permute-start.1 = (bf16[32,512]{1,0:T(8,128)(2,1)S(1)}, bf16[32,512]{1,0:T(8,128)(2,1)S(1)}, u32[]{:S(2)}, u32[]{:S(2)}) collective-permute-start(bf16[32,512]{1,0:T(8,128)(2,1)S(1)} %get-tuple-element.19), channel_id=1, source_target_pairs={{16,0},{32,16},{48,32},{64,48},{80,64},{96,80},{112,96},{17,1},{33... | collective-permute-start | bytes 98312 | tf_op jit(solution)/shard_map/ppermute | solution.py:90
  23.1 7.5 %collective-permute-start.3 = (bf16[576,32]{1,0:T(8,128)(2,1)S(1)}, bf16[576,32]{1,0:T(8,128)(2,1)S(1)}, u32[]{:S(2)}, u32[]{:S(2)}) collective-permute-start(bf16[576,32]{1,0:T(8,128)(2,1)S(1)} %get-tuple-element.18), channel_id=1, source_target_pairs={{1,0},{2,1},{3,2},{4,3},{5,4},{6,5},{7,6},{8,7},{9,8},{10,9},{11,1... | collective-permute-start | bytes 110600 | tf_op jit(solution)/shard_map/ppermute | solution.py:90
  24.4 6.3 %collective-permute-start.2 = (bf16[576,32]{1,0:T(8,128)(2,1)S(1)}, bf16[576,32]{1,0:T(8,128)(2,1)S(1)}, u32[]{:S(2)}, u32[]{:S(2)}) collective-permute-start(bf16[576,32]{1,0:T(8,128)(2,1)S(1)} %get-tuple-element.17), channel_id=1, source_target_pairs={{0,1},{1,2},{2,3},{3,4},{4,5},{5,6},{6,7},{7,8},{8,9},{9,10},{10,1... | collective-permute-start | bytes 110600 | tf_op jit(solution)/shard_map/ppermute | solution.py:88
  48.7 26.7 %copy-start.3 = (f32[2,8]{1,0:T(2,128)}, f32[2,8]{1,0:T(2,128)S(1)}, u32[]{:S(2)}) copy-start(f32[2,8]{1,0:T(2,128)S(1)} %bitcast_negate_fusion) | copy-start | bytes 196
  50.4 15.8 %all-to-all-start.1 = ((f32[16,4,128]{2,1,0:T(4,128)}), f32[16,4,128]{2,1,0:T(4,128)S(1)}, u32[]{:S(2)}, u32[]{:S(2)}) async-start(f32[16,4,128]{2,1,0:T(4,128)} %reshape.316), calls=%async_computation.1 | async-start | bytes 65536 | tf_op jit(solution)/shard_map/all_to_all | solution.py:229
  67.0 7.9 %collective-permute-start.5 = (f32[4,3,38]{2,1,0:T(4,128)S(1)}, f32[4,3,38]{2,1,0:T(4,128)S(1)}, u32[]{:S(2)}, u32[]{:S(2)}) collective-permute-start(f32[4,3,38]{2,1,0:T(4,128)S(1)} %get-tuple-element.22), channel_id=1, source_target_pairs={{16,0},{32,16},{48,32},{64,48},{80,64},{96,80},{112,96},{17,1},{33... | collective-permute-start | bytes 5480 | tf_op jit(solution)/shard_map/ppermute | solution.py:190
  69.3 5.6 %collective-permute-start.4 = (f32[4,3,38]{2,1,0:T(4,128)S(1)}, f32[4,3,38]{2,1,0:T(4,128)S(1)}, u32[]{:S(2)}, u32[]{:S(2)}) collective-permute-start(f32[4,3,38]{2,1,0:T(4,128)S(1)} %get-tuple-element.21), channel_id=1, source_target_pairs={{0,16},{16,32},{32,48},{48,64},{64,80},{80,96},{96,112},{1,17},{17... | collective-permute-start | bytes 5480 | tf_op jit(solution)/shard_map/ppermute | solution.py:189

commit v11 on v10

--- a/solution.py
+++ b/solution.py
@@ -61,6 +61,7 @@
     orow = lax.broadcasted_iota(jnp.int32, (8, 128), 0)
     out_ref[0] = jnp.where(orow == 0, fy, jnp.where(orow == 1, fx, 0.0))
 
+
 def flows_of(tflipped, windows):
     n = tflipped.shape[0]
     out = pl.pallas_call(
@@ -94,33 +95,6 @@
     return cells
 
 
-def halo(cells, width):
-    n_ty = lax.axis_size("ty")
-    n_tx = lax.axis_size("tx")
-    height, breadth = cells.shape[-2], cells.shape[-1]
-    pieces = {}
-    for dy in (-1, 0, 1):
-        for dx in (-1, 0, 1):
-            if dy == 0 and dx == 0:
-                pieces[(dy, dx)] = cells
-                continue
-            rows = {-1: (height - width, height), 0: (0, height), 1: (0, width)}[dy]
-            cols = {-1: (breadth - width, breadth), 0: (0, breadth), 1: (0, width)}[dx]
-            part = cells[..., rows[0] : rows[1], cols[0] : cols[1]]
-            pairs = []
-            for i in range(n_ty):
-                for j in range(n_tx):
-                    si, sj = i + dy, j + dx
-                    if 0 <= si < n_ty and 0 <= sj < n_tx:
-                        pairs.append((si * n_tx + sj, i * n_tx + j))
-            pieces[(dy, dx)] = lax.ppermute(part, ("ty", "tx"), pairs)
-    bands = [
-        jnp.concatenate([pieces[(dy, -1)], pieces[(dy, 0)], pieces[(dy, 1)]], axis=-1)
-        for dy in (-1, 0, 1)
-    ]
-    return jnp.concatenate(bands, axis=-2)
-
-
 def relax_sweep(padded, mask_pad, target, count):
     centre = padded[:, 1:-1, 1:-1]
     mask_c = mask_pad[1:-1, 1:-1]
@@ -200,7 +174,8 @@
     mask = node_mask.astype(f32)
     w = ITERS_R
     arrived = lax.all_to_all(outgoing, "tx", split_axis=0, concat_axis=0, tiled=True)
-    b_wide = padded_2(section_b, (("ty", 0), ("tx", 1)), RADIUS)
+    b_tall = padded_2(section_b, (("ty", 0),), RADIUS)
+    b_wide = padded_2(b_tall, (("tx", 1),), RADIUS)
 
     wrow_pick = one_hot(window_corner[0, 0], WIN, b_wide.shape[0])
     wcol_pick = one_hot(window_corner[1, 0], WIN, b_wide.shape[1])

time: 76.9 us -> 76.9 us (level)
  no operation moved by 1% of the time
where the time goes in v11:
time: 76.9 us; the launch traced here: 76.4 us
  starting transfers between devices  36.4 us (47%)
  Pallas kernels  11.9 us (15%)
  waiting for transfers between devices  11.6 us (15%)
  local copies, waits for them, and re-layouts  6.38 us (8%)
  matrix products  6.14 us (8%)
  other arithmetic  3.03 us (4%)
  between operations  0.97 us (1%)
    pallas_call x1, Pallas kernels, flows_of(): pl.pallas_call(flow_kernel, grid=(n,), in_specs=[pl.BlockSpec((1, PATCH,...  11.9 us
    all_to_all x1, starting transfers between devices, shards(): lax.all_to_all(back, 'tx', split_axis=0, concat_axis=0, tiled=True)  9.27 us
    all_to_all x1, starting transfers between devices, shards(): lax.all_to_all(outgoing, 'tx', split_axis=0, concat_axis=0, tiled=True)  8.56 us
    ppermute x2, starting transfers between devices, padded_2(): lax.ppermute(tail, axis, [(i, (i + 1) % count) for i in range(ends)])  8.22 us
    all_to_all x1, waiting for transfers between devices, shards(): lax.all_to_all(back, 'tx', split_axis=0, concat_axis=0, tiled=True)  6.43 us
    ppermute x2, waiting for transfers between devices, padded_2(): lax.ppermute(head, axis, [((i + 1) % count, i) for i in range(ends)])  4.98 us
    ppermute x1, starting transfers between devices, rows_exchange(): above = lax.ppermute(tail, 'ty', [(i, i + 1) for i in range(count - 1)])  4.84 us
    dot_general x1, matrix products, shards(): jnp.einsum('mrc,msc->mrs', by_row.astype(jnp.bfloat16), wcol_pick, prefer...  3.8 us
  transfers between devices with their start and end apart: 8, of which 4 were waited for; matrix products, arithmetic and copies ran while one was open for 7% of the time, Pallas kernels for 0%

profile of v11, /device:TPU:1, one launch (start us, length us, event | category | flops | bytes accessed | tf_op | source)
XLA Modules:
  0.0 76.4 jit_solution(15577852478845660712)
XLA Ops:
  0.7 0.7 slice_bitcast_fusion.5
  1.5 0.2 copy-done
  1.7 1.1 %fusion.11 = bf16[8,128,128]{2,1,0:T(8,128)(2,1)S(1)} fusion(s32[8,128]{1,0:T(8,128)S(1)} %get-tuple-element.43, s32[8,128]{1,0:T(8,128)S(1)} %get-tuple-element.44, bf16[512,512]{1,0:T(8,128)(2,1)S(1)} %copy-done), kind=kOutput, calls=%fused_computation.14 | convolution fusion | flops 672792576 | bytes 794624 | tf_op jit(solution)/shard_map/kra,kia->kri/dot_general | solution.py:132
  2.9 0.6 convolution_convert_fusion
  3.4 1.4 %copy.36 = bf16[32,128,128]{2,1,0:T(8,128)(2,1)} copy(bf16[32,128,128]{2,0,1:T(8,128)(2,1)S(1)} %convolution_convert_fusion) | data formatting | bytes 2097152 | tf_op jit(solution)/shard_map/convert_element_type | solution.py:137
  4.8 8.6 %all-to-all-start = ((bf16[32,128,128]{2,1,0:T(8,128)(2,1)}), bf16[32,128,128]{2,1,0:T(8,128)(2,1)S(1)}, u32[]{:S(2)}, u32[]{:S(2)}) async-start(bf16[32,128,128]{2,1,0:T(8,128)(2,1)} %copy.36), calls=%async_computation | async-start | bytes 2097152 | tf_op jit(solution)/shard_map/all_to_all | solution.py:176
  13.4 4.0 %collective-permute-start = (bf16[32,512]{1,0:T(8,128)(2,1)S(1)}, bf16[32,512]{1,0:T(8,128)(2,1)S(1)}, u32[]{:S(2)}, u32[]{:S(2)}) collective-permute-start(bf16[32,512]{1,0:T(8,128)(2,1)S(1)} %get-tuple-element.20), channel_id=1, source_target_pairs={{0,16},{16,32},{32,48},{48,64},{64,80},{80,96},{96,112},{1,17},{17... | collective-permute-start | bytes 98312 | tf_op jit(solution)/shard_map/ppermute | solution.py:89
  17.4 1.9 %collective-permute-start.1 = (bf16[32,512]{1,0:T(8,128)(2,1)S(1)}, bf16[32,512]{1,0:T(8,128)(2,1)S(1)}, u32[]{:S(2)}, u32[]{:S(2)}) collective-permute-start(bf16[32,512]{1,0:T(8,128)(2,1)S(1)} %get-tuple-element.19), channel_id=1, source_target_pairs={{16,0},{32,16},{48,32},{64,48},{80,64},{96,80},{112,96},{17,1},{33... | collective-permute-start | bytes 98312 | tf_op jit(solution)/shard_map/ppermute | solution.py:91
  19.9 3.0 %collective-permute-done.1 = bf16[32,512]{1,0:T(8,128)(2,1)S(1)} collective-permute-done((bf16[32,512]{1,0:T(8,128)(2,1)S(1)}, bf16[32,512]{1,0:T(8,128)(2,1)S(1)}, u32[]{:S(2)}, u32[]{:S(2)}) %collective-permute-start.1) | collective-permute-done | bytes 32800 | tf_op jit(solution)/shard_map/ppermute | solution.py:91
  23.0 0.1 fusion.59
  23.1 1.3 %collective-permute-start.3 = (bf16[576,32]{1,0:T(8,128)(2,1)S(1)}, bf16[576,32]{1,0:T(8,128)(2,1)S(1)}, u32[]{:S(2)}, u32[]{:S(2)}) collective-permute-start(bf16[576,32]{1,0:T(8,128)(2,1)S(1)} %get-tuple-element.18), channel_id=1, source_target_pairs={{1,0},{2,1},{3,2},{4,3},{5,4},{6,5},{7,6},{8,7},{9,8},{10,9},{11,1... | collective-permute-start | bytes 110600 | tf_op jit(solution)/shard_map/ppermute | solution.py:91
  24.4 4.2 %collective-permute-start.2 = (bf16[576,32]{1,0:T(8,128)(2,1)S(1)}, bf16[576,32]{1,0:T(8,128)(2,1)S(1)}, u32[]{:S(2)}, u32[]{:S(2)}) collective-permute-start(bf16[576,32]{1,0:T(8,128)(2,1)S(1)} %get-tuple-element.17), channel_id=1, source_target_pairs={{0,1},{1,2},{2,3},{3,4},{4,5},{5,6},{6,7},{7,8},{8,9},{9,10},{10,1... | collective-permute-start | bytes 110600 | tf_op jit(solution)/shard_map/ppermute | solution.py:89
  28.7 2.0 %collective-permute-done.3 = bf16[576,32]{1,0:T(8,128)(2,1)S(1)} collective-permute-done((bf16[576,32]{1,0:T(8,128)(2,1)S(1)}, bf16[576,32]{1,0:T(8,128)(2,1)S(1)}, u32[]{:S(2)}, u32[]{:S(2)}) %collective-permute-start.3) | collective-permute-done | bytes 36896 | tf_op jit(solution)/shard_map/ppermute | solution.py:91
  30.7 3.8 %fusion.8.w_ref = bf16[8,192,192]{2,1,0:T(8,128)(2,1)} fusion(s32[8,192]{1,0:T(8,128)S(1)} %get-tuple-element.45, s32[8,192]{1,0:T(8,128)S(1)} %get-tuple-element.46, bf16[576,32]{1,0:T(8,128)(2,1)S(1)} %collective-permute-done.3, bf16[576,512]{1,0:T(8,128)(2,1)S(1)} %constant_dynamic-update-slice_fusion, bf16[576,32]{1,0:T(8,128)(2,1)S(1)} %collective-permute-done.2), kind=kOutput, calls=%fused_computation.13 | convolution fusion | flops 1363894272 | bytes 1265664 | tf_op jit(solution)/shard_map/mrc,msc->mrs/dot_general | solution.py:183
  34.5 0.7 fusion.12
  35.1 0.8 copy.53.tf_ref
  35.9 11.9 %shard_map.94 = f32[8,8,128]{2,1,0:T(8,128)} custom-call(bf16[8,128,128]{2,1,0:T(8,128)(2,1)} %copy.53.tf_ref, bf16[8,192,192]{2,1,0:T(8,128)(2,1)} %fusion.8.w_ref), custom_call_target="tpu_custom_call" | custom-call | tf_op jit(solution)/shard_map/pallas_call | solution.py:67
  47.8 0.8 slice.192
  49.2 0.2 broadcast_in_dim.163
  49.4 0.2 broadcast_in_dim.160
  49.7 0.6 reshape.316
  50.4 9.3 %all-to-all-start.1 = ((f32[16,4,128]{2,1,0:T(4,128)}), f32[16,4,128]{2,1,0:T(4,128)S(1)}, u32[]{:S(2)}, u32[]{:S(2)}) async-start(f32[16,4,128]{2,1,0:T(4,128)} %reshape.316), calls=%async_computation.1 | async-start | bytes 65536 | tf_op jit(solution)/shard_map/all_to_all | solution.py:204
  59.7 6.4 %all-to-all-done.1 = f32[16,4,128]{2,1,0:T(4,128)S(1)} async-done(((f32[16,4,128]{2,1,0:T(4,128)}), f32[16,4,128]{2,1,0:T(4,128)S(1)}, u32[]{:S(2)}, u32[]{:S(2)}) %all-to-all-start.1) | async-done | bytes 32800 | tf_op jit(solution)/shard_map/all_to_all | solution.py:204
  66.5 0.2 select_n.76
  66.7 0.2 select_n.72
  67.0 2.3 %collective-permute-start.5 = (f32[4,3,38]{2,1,0:T(4,128)S(1)}, f32[4,3,38]{2,1,0:T(4,128)S(1)}, u32[]{:S(2)}, u32[]{:S(2)}) collective-permute-start(f32[4,3,38]{2,1,0:T(4,128)S(1)} %get-tuple-element.22), channel_id=1, source_target_pairs={{16,0},{32,16},{48,32},{64,48},{80,64},{96,80},{112,96},{17,1},{33... | collective-permute-start | bytes 5480 | tf_op jit(solution)/shard_map/ppermute | solution.py:164
  69.3 4.8 %collective-permute-start.4 = (f32[4,3,38]{2,1,0:T(4,128)S(1)}, f32[4,3,38]{2,1,0:T(4,128)S(1)}, u32[]{:S(2)}, u32[]{:S(2)}) collective-permute-start(f32[4,3,38]{2,1,0:T(4,128)S(1)} %get-tuple-element.21), channel_id=1, source_target_pairs={{0,16},{16,32},{32,48},{48,64},{64,80},{80,96},{96,112},{1,17},{17... | collective-permute-start | bytes 5480 | tf_op jit(solution)/shard_map/ppermute | solution.py:163
  74.2 0.7 select_reduce_fusion.1
  74.8 0.1 collective-permute-done.4
  74.9 0.1 pad_maximum_fusion
  75.6 0.1 fusion.29
  75.7 0.7 fusion.45
  (61 shorter events, 2.4 us)
Async XLA Ops:
  0.6 1.1 %copy-start = (bf16[512,512]{1,0:T(8,128)(2,1)S(1)}, bf16[512,512]{1,0:T(8,128)(2,1)}, u32[]{:S(2)}) copy-start(bf16[512,512]{1,0:T(8,128)(2,1)} %param.7) | copy-start | bytes 1572868
  1.7 1.1 %copy-start.6 = (s32[1,8]{1,0:T(1,128)S(1)}, s32[1,8]{1,0:T(1,128)}, u32[]{:S(2)}) copy-start(s32[1,8]{1,0:T(1,128)} %param.10) | copy-start | bytes 100
  4.8 8.6 %copy-start.1 = (bf16[512,512]{1,0:T(8,128)(2,1)S(1)}, bf16[512,512]{1,0:T(8,128)(2,1)}, u32[]{:S(2)}) copy-start(bf16[512,512]{1,0:T(8,128)(2,1)} %param.8) | copy-start | bytes 1572868
  4.8 14.6 %copy-start.4 = (s32[2,1,8]{2,1,0:T(1,128)S(1)}, s32[2,1,8]{2,1,0:T(1,128)}, u32[]{:S(2)}) copy-start(s32[2,1,8]{2,1,0:T(1,128)} %param.11) | copy-start | bytes 196
  4.8 14.6 %copy-start.5 = (s32[1,8]{1,0:T(1,128)S(1)}, s32[1,8]{1,0:T(1,128)}, u32[]{:S(2)}) copy-start(s32[1,8]{1,0:T(1,128)} %param.12) | copy-start | bytes 100
  4.8 14.7 %copy-start.2 = (s32[32,32]{1,0:T(8,128)S(1)}, s32[32,32]{1,0:T(8,128)}, u32[]{:S(2)}) copy-start(s32[32,32]{1,0:T(8,128)} %param.13) | copy-start | bytes 12292
  4.8 29.6 %all-to-all-start = ((bf16[32,128,128]{2,1,0:T(8,128)(2,1)}), bf16[32,128,128]{2,1,0:T(8,128)(2,1)S(1)}, u32[]{:S(2)}, u32[]{:S(2)}) async-start(bf16[32,128,128]{2,1,0:T(8,128)(2,1)} %copy.36), calls=%async_computation | async-start | bytes 2097152 | tf_op jit(solution)/shard_map/all_to_all | solution.py:176
  13.4 6.5 %collective-permute-start = (bf16[32,512]{1,0:T(8,128)(2,1)S(1)}, bf16[32,512]{1,0:T(8,128)(2,1)S(1)}, u32[]{:S(2)}, u32[]{:S(2)}) collective-permute-start(bf16[32,512]{1,0:T(8,128)(2,1)S(1)} %get-tuple-element.20), channel_id=1, source_target_pairs={{0,16},{16,32},{32,48},{48,64},{64,80},{80,96},{96,112},{1,17},{17... | collective-permute-start | bytes 98312 | tf_op jit(solution)/shard_map/ppermute | solution.py:89
  17.4 5.5 %collective-permute-start.1 = (bf16[32,512]{1,0:T(8,128)(2,1)S(1)}, bf16[32,512]{1,0:T(8,128)(2,1)S(1)}, u32[]{:S(2)}, u32[]{:S(2)}) collective-permute-start(bf16[32,512]{1,0:T(8,128)(2,1)S(1)} %get-tuple-element.19), channel_id=1, source_target_pairs={{16,0},{32,16},{48,32},{64,48},{80,64},{96,80},{112,96},{17,1},{33... | collective-permute-start | bytes 98312 | tf_op jit(solution)/shard_map/ppermute | solution.py:91
  23.1 7.5 %collective-permute-start.3 = (bf16[576,32]{1,0:T(8,128)(2,1)S(1)}, bf16[576,32]{1,0:T(8,128)(2,1)S(1)}, u32[]{:S(2)}, u32[]{:S(2)}) collective-permute-start(bf16[576,32]{1,0:T(8,128)(2,1)S(1)} %get-tuple-element.18), channel_id=1, source_target_pairs={{1,0},{2,1},{3,2},{4,3},{5,4},{6,5},{7,6},{8,7},{9,8},{10,9},{11,1... | collective-permute-start | bytes 110600 | tf_op jit(solution)/shard_map/ppermute | solution.py:91
  24.4 6.3 %collective-permute-start.2 = (bf16[576,32]{1,0:T(8,128)(2,1)S(1)}, bf16[576,32]{1,0:T(8,128)(2,1)S(1)}, u32[]{:S(2)}, u32[]{:S(2)}) collective-permute-start(bf16[576,32]{1,0:T(8,128)(2,1)S(1)} %get-tuple-element.17), channel_id=1, source_target_pairs={{0,1},{1,2},{2,3},{3,4},{4,5},{5,6},{6,7},{7,8},{8,9},{9,10},{10,1... | collective-permute-start | bytes 110600 | tf_op jit(solution)/shard_map/ppermute | solution.py:89
  48.7 26.7 %copy-start.3 = (f32[2,8]{1,0:T(2,128)}, f32[2,8]{1,0:T(2,128)S(1)}, u32[]{:S(2)}) copy-start(f32[2,8]{1,0:T(2,128)S(1)} %bitcast_negate_fusion) | copy-start | bytes 196
  50.4 15.8 %all-to-all-start.1 = ((f32[16,4,128]{2,1,0:T(4,128)}), f32[16,4,128]{2,1,0:T(4,128)S(1)}, u32[]{:S(2)}, u32[]{:S(2)}) async-start(f32[16,4,128]{2,1,0:T(4,128)} %reshape.316), calls=%async_computation.1 | async-start | bytes 65536 | tf_op jit(solution)/shard_map/all_to_all | solution.py:204
  67.0 7.9 %collective-permute-start.5 = (f32[4,3,38]{2,1,0:T(4,128)S(1)}, f32[4,3,38]{2,1,0:T(4,128)S(1)}, u32[]{:S(2)}, u32[]{:S(2)}) collective-permute-start(f32[4,3,38]{2,1,0:T(4,128)S(1)} %get-tuple-element.22), channel_id=1, source_target_pairs={{16,0},{32,16},{48,32},{64,48},{80,64},{96,80},{112,96},{17,1},{33... | collective-permute-start | bytes 5480 | tf_op jit(solution)/shard_map/ppermute | solution.py:164
  69.3 5.6 %collective-permute-start.4 = (f32[4,3,38]{2,1,0:T(4,128)S(1)}, f32[4,3,38]{2,1,0:T(4,128)S(1)}, u32[]{:S(2)}, u32[]{:S(2)}) collective-permute-start(f32[4,3,38]{2,1,0:T(4,128)S(1)} %get-tuple-element.21), channel_id=1, source_target_pairs={{0,16},{16,32},{32,48},{48,64},{64,80},{80,96},{96,112},{1,17},{17... | collective-permute-start | bytes 5480 | tf_op jit(solution)/shard_map/ppermute | solution.py:163

commit v12 on v11

--- a/solution.py
+++ b/solution.py
@@ -175,14 +175,28 @@
     w = ITERS_R
     arrived = lax.all_to_all(outgoing, "tx", split_axis=0, concat_axis=0, tiled=True)
     b_tall = padded_2(section_b, (("ty", 0),), RADIUS)
-    b_wide = padded_2(b_tall, (("tx", 1),), RADIUS)
-
-    wrow_pick = one_hot(window_corner[0, 0], WIN, b_wide.shape[0])
-    wcol_pick = one_hot(window_corner[1, 0], WIN, b_wide.shape[1])
-    by_row = jnp.einsum("mra,ac->mrc", wrow_pick, b_wide, preferred_element_type=f32)
-    windows = jnp.einsum(
-        "mrc,msc->mrs", by_row.astype(jnp.bfloat16), wcol_pick, preferred_element_type=f32
-    ).astype(jnp.bfloat16)
+    tall_cols = b_tall.shape[1]
+    rim_left = lax.ppermute(
+        b_tall[:, tall_cols - RADIUS :], "tx", [(i, i + 1) for i in range(n_tx - 1)]
+    )
+    rim_right = lax.ppermute(b_tall[:, 0:RADIUS], "tx", [(i + 1, i) for i in range(n_tx - 1)])
+    wrow_pick = one_hot(window_corner[0, 0], WIN, b_tall.shape[0])
+    wcol_pick = one_hot(window_corner[1, 0], WIN, tall_cols + 2 * RADIUS)
+    wcol_mid = wcol_pick[:, :, RADIUS : RADIUS + tall_cols]
+    wcol_side = jnp.concatenate(
+        [wcol_pick[:, :, 0:RADIUS], wcol_pick[:, :, RADIUS + tall_cols :]], axis=2
+    )
+    by_row_mid = jnp.einsum("mra,ac->mrc", wrow_pick, b_tall, preferred_element_type=f32)
+    win_mid = jnp.einsum(
+        "mrc,msc->mrs", by_row_mid.astype(jnp.bfloat16), wcol_mid, preferred_element_type=f32
+    )
+    win_mid = lax.optimization_barrier(win_mid)
+    rims = jnp.concatenate([rim_left, rim_right], axis=1)
+    by_row_side = jnp.einsum("mra,ac->mrc", wrow_pick, rims, preferred_element_type=f32)
+    win_side = jnp.einsum(
+        "mrc,msc->mrs", by_row_side.astype(jnp.bfloat16), wcol_side, preferred_element_type=f32
+    )
+    windows = (win_mid + win_side).astype(jnp.bfloat16)
     matched = jnp.einsum(
         "ms,sri->mri", source_picker.astype(jnp.bfloat16), arrived, preferred_element_type=f32
     ).astype(jnp.bfloat16)

time: 76.9 us -> 86.2 us (1.12)
  other arithmetic: 3.03 us -> 7.66 us
  matrix products: 6.14 us -> 9.84 us
  local copies, waits for them, and re-layouts: 6.38 us -> 9.32 us
  starting transfers between devices: 36.4 us -> 34.2 us
    ppermute x0 -> x2, starting transfers between devices: none -> 5.19 us  [the longest x1 3.91 us: shards(): lax.ppermute(b_tall[:, tall_cols - RADIUS:], 'tx', [(i, i + 1) for i in r...]
    ppermute x2 -> x1, starting transfers between devices: 8.22 us -> 3.21 us  [padded_2(): lax.ppermute(tail, axis, [(i, (i + 1) % count) for i in range(ends)])]
    ppermute x2 -> x1, waiting for transfers between devices: 4.98 us -> 0.01 us  [padded_2(): lax.ppermute(head, axis, [((i + 1) % count, i) for i in range(ends)])]
    dot_general x1 -> x2, matrix products: 3.8 us -> 6.83 us  [the longest x1 3.54 us: shards(): jnp.einsum('mrc,msc->mrs', by_row_side.astype(jnp.bfloat16), wcol_side, p...]
    ppermute x0 -> x2, waiting for transfers between devices: none -> 2.87 us  [the longest x1 2.39 us: shards(): lax.ppermute(b_tall[:, 0:RADIUS], 'tx', [(i + 1, i) for i in range(n_tx -...]
    ppermute x1, waiting for transfers between devices: 0.01 us -> 2.39 us  [rows_exchange(): below = lax.ppermute(head, 'ty', [(i + 1, i) for i in range(count - 1)])]
    all_to_all x1, starting transfers between devices: 9.27 us -> 7.36 us  [shards(): lax.all_to_all(back, 'tx', split_axis=0, concat_axis=0, tiled=True)]
    slice x1 -> x2, local copies, waits for them, and re-layouts: 0.11 us -> 1.87 us  [the longest x1 0.97 us: shards(): wcol_pick[:, :, 0:RADIUS]]
  transfers between devices with their start and end apart: 8 -> 8, of which waited for: 4 -> 4; matrix products, arithmetic and copies ran while one was open for 7% -> 22% of each run, Pallas kernels for 0% -> 0%
where the time goes in v12:
time: 86.2 us; the launch traced here: 85.6 us
  starting transfers between devices  34.2 us (40%)
  Pallas kernels  11.9 us (14%)
  waiting for transfers between devices  11.6 us (13%)
  matrix products  9.84 us (11%)
  local copies, waits for them, and re-layouts  9.32 us (11%)
  other arithmetic  7.66 us (9%)
  between operations  1.02 us (1%)
    pallas_call x1, Pallas kernels, flows_of(): pl.pallas_call(flow_kernel, grid=(n,), in_specs=[pl.BlockSpec((1, PATCH,...  11.9 us
    all_to_all x1, starting transfers between devices, shards(): lax.all_to_all(outgoing, 'tx', split_axis=0, concat_axis=0, tiled=True)  7.6 us
    all_to_all x1, starting transfers between devices, shards(): lax.all_to_all(back, 'tx', split_axis=0, concat_axis=0, tiled=True)  7.36 us
    all_to_all x1, waiting for transfers between devices, shards(): lax.all_to_all(back, 'tx', split_axis=0, concat_axis=0, tiled=True)  6.37 us
    ppermute x1, starting transfers between devices, rows_exchange(): above = lax.ppermute(tail, 'ty', [(i, i + 1) for i in range(count - 1)])  5.52 us
    ppermute x1, starting transfers between devices, shards(): lax.ppermute(b_tall[:, tall_cols - RADIUS:], 'tx', [(i, i + 1) for i in r...  3.91 us
    dot_general x1, matrix products, shards(): jnp.einsum('mrc,msc->mrs', by_row_side.astype(jnp.bfloat16), wcol_side, p...  3.54 us
    ppermute x1, starting transfers between devices, padded_2(): lax.ppermute(head, axis, [((i + 1) % count, i) for i in range(ends)])  3.41 us
  transfers between devices with their start and end apart: 8, of which 4 were waited for; matrix products, arithmetic and copies ran while one was open for 22% of the time, Pallas kernels for 0%

profile of v12, /device:TPU:1, one launch (start us, length us, event | category | flops | bytes accessed | tf_op | source)
XLA Modules:
  0.0 85.6 jit_solution(3089814864801207088)
XLA Ops:
  0.6 0.8 fusion.63
  1.5 3.4 %collective-permute-start.1 = (bf16[32,512]{1,0:T(8,128)(2,1)S(1)}, bf16[32,512]{1,0:T(8,128)(2,1)S(1)}, u32[]{:S(2)}, u32[]{:S(2)}) collective-permute-start(bf16[32,512]{1,0:T(8,128)(2,1)S(1)} %get-tuple-element.21), channel_id=1, source_target_pairs={{16,0},{32,16},{48,32},{64,48},{80,64},{96,80},{112,96},{17,1},{33... | collective-permute-start | bytes 98312 | tf_op jit(solution)/shard_map/ppermute | solution.py:91
  4.9 3.2 %collective-permute-start = (bf16[32,512]{1,0:T(8,128)(2,1)S(1)}, bf16[32,512]{1,0:T(8,128)(2,1)S(1)}, u32[]{:S(2)}, u32[]{:S(2)}) collective-permute-start(bf16[32,512]{1,0:T(8,128)(2,1)S(1)} %get-tuple-element.22), channel_id=1, source_target_pairs={{0,16},{16,32},{32,48},{48,64},{64,80},{80,96},{96,112},{1,17},{17... | collective-permute-start | bytes 98312 | tf_op jit(solution)/shard_map/ppermute | solution.py:89
  8.1 0.7 slice_bitcast_fusion.5
  8.9 1.1 %fusion.11 = bf16[8,128,128]{2,1,0:T(8,128)(2,1)S(1)} fusion(s32[8,128]{1,0:T(8,128)S(1)} %get-tuple-element.47, s32[8,128]{1,0:T(8,128)S(1)} %get-tuple-element.48, bf16[512,512]{1,0:T(8,128)(2,1)S(1)} %copy-done), kind=kOutput, calls=%fused_computation.17 | convolution fusion | flops 672792576 | bytes 794624 | tf_op jit(solution)/shard_map/kra,kia->kri/dot_general | solution.py:132
  10.6 1.4 %copy.40 = bf16[32,128,128]{2,1,0:T(8,128)(2,1)} copy(bf16[32,128,128]{2,0,1:T(8,128)(2,1)S(1)} %convolution_convert_fusion) | data formatting | bytes 2097152 | tf_op jit(solution)/shard_map/convert_element_type | solution.py:137
  12.0 7.6 %all-to-all-start = ((bf16[32,128,128]{2,1,0:T(8,128)(2,1)}), bf16[32,128,128]{2,1,0:T(8,128)(2,1)S(1)}, u32[]{:S(2)}, u32[]{:S(2)}) async-start(bf16[32,128,128]{2,1,0:T(8,128)(2,1)} %copy.40), calls=%async_computation | async-start | bytes 2097152 | tf_op jit(solution)/shard_map/all_to_all | solution.py:176
  19.9 0.7 broadcast_and_fusion
  20.6 0.6 iota_compare_fusion.24
  21.2 0.7 iota_add_fusion.1
  22.0 0.6 convert_bitcast_fusion
  22.6 1.7 %fusion.29 = (bf16[8,192,576]{2,1,0:T(8,128)(2,1)S(1)}, pred[8,192,576]{2,1,0:T(32,128)(4,1)}) fusion(s32[8,192]{1,0:T(8,128)S(1)} %iota_add_fusion), kind=kLoop, calls=%fused_computation.34 | loop fusion | flops 1769472 | bytes 2660352 | tf_op jit(solution)/shard_map/convert_element_type | solution.py:116
  24.2 1.0 %fusion.61 = (bf16[8,192,32]{2,1,0:T(8,128)(2,1)S(1)}, bf16[8,192,32]{2,1,0:T(8,128)(2,1)}) fusion(bf16[8,192,576]{2,1,0:T(8,128)(2,1)S(1)} %get-tuple-element.39), kind=kLoop, calls=%fused_computation.135 | loop fusion | bytes 393216 | tf_op jit(solution)/shard_map/slice | solution.py:187
  25.7 0.7 pad.14.clone
  26.5 0.9 %fusion.62 = (bf16[576,32]{1,0:T(8,128)(2,1)}, bf16[576,32]{1,0:T(8,128)(2,1)}) fusion(bf16[576,512]{1,0:T(8,128)(2,1)S(1)} %constant_dynamic-update-slice_fusion), kind=kLoop, calls=%fused_computation.136 | loop fusion | bytes 147456 | tf_op jit(solution)/shard_map/slice | solution.py:180
  27.4 3.9 %collective-permute-start.2 = (bf16[576,32]{1,0:T(8,128)(2,1)}, bf16[576,32]{1,0:T(8,128)(2,1)}, u32[]{:S(2)}, u32[]{:S(2)}) collective-permute-start(bf16[576,32]{1,0:T(8,128)(2,1)} %get-tuple-element.19), channel_id=1, source_target_pairs={{0,1},{1,2},{2,3},{3,4},{4,5},{5,6},{6,7},{7,8},{8,9},{9,10},{10,1... | collective-permute-start | bytes 110600 | tf_op jit(solution)/shard_map/ppermute | solution.py:179
  31.3 1.3 %collective-permute-start.3 = (bf16[576,32]{1,0:T(8,128)(2,1)}, bf16[576,32]{1,0:T(8,128)(2,1)}, u32[]{:S(2)}, u32[]{:S(2)}) collective-permute-start(bf16[576,32]{1,0:T(8,128)(2,1)} %get-tuple-element.20), channel_id=1, source_target_pairs={{1,0},{2,1},{3,2},{4,3},{5,4},{6,5},{7,6},{8,7},{9,8},{10,9},{11,1... | collective-permute-start | bytes 110600 | tf_op jit(solution)/shard_map/ppermute | solution.py:182
  32.6 3.3 %fusion.2 = f32[8,192,192]{2,1,0:T(8,128)S(1)} fusion(pred[8,192,576]{2,1,0:T(32,128)(4,1)} %get-tuple-element.40, s32[8,192]{1,0:T(8,128)} %iota_add_fusion.1, bf16[576,512]{1,0:T(8,128)(2,1)} %copy-done.3), kind=kOutput, calls=%fused_computation.4 | convolution fusion | flops 1209630720 | bytes 2564096 | tf_op jit(solution)/shard_map/mrc,msc->mrs/dot_general | solution.py:190
  36.4 2.4 %collective-permute-done.3 = bf16[576,32]{1,0:T(8,128)(2,1)} collective-permute-done((bf16[576,32]{1,0:T(8,128)(2,1)}, bf16[576,32]{1,0:T(8,128)(2,1)}, u32[]{:S(2)}, u32[]{:S(2)}) %collective-permute-start.3) | collective-permute-done | bytes 36896 | tf_op jit(solution)/shard_map/ppermute | solution.py:182
  38.8 3.5 %add_convert_fusion.w_ref = bf16[8,192,192]{2,1,0:T(8,128)(2,1)} fusion(f32[8,192,192]{2,1,0:T(8,128)S(1)} %fusion.2, s32[8,192]{1,0:T(8,128)} %iota_add_fusion.1, bf16[8,192,32]{2,1,0:T(8,128)(2,1)} %get-tuple-element.18, bf16[8,192,32]{2,1,0:T(8,128)(2,1)S(1)} %get-tuple-element.17, bf16[576,32]{1,0:T(8,128)(2,1)} %collective-permute-done.3, ...), kind=kOutput, calls=%fused_computation.13 | convolution fusion | flops 153108480 | bytes 2045952 | tf_op jit(solution)/shard_map/mrc,msc->mrs/dot_general | solution.py:196
  42.4 1.3 %fusion.12 = bf16[8,128,128]{2,0,1:T(8,128)(2,1)S(1)} fusion(bf16[32,128,128]{2,1,0:T(8,128)(2,1)S(1)} %all-to-all-done, s32[8]{0:T(128)} %bitcast.76), kind=kOutput, calls=%fused_computation.18 | convolution fusion | flops 8388864 | bytes 1310752 | tf_op jit(solution)/shard_map/ms,sri->mri/dot_general | solution.py:200
  43.7 0.8 copy.62.tf_ref
  44.5 11.9 %shard_map.94 = f32[8,8,128]{2,1,0:T(8,128)} custom-call(bf16[8,128,128]{2,1,0:T(8,128)(2,1)} %copy.62.tf_ref, bf16[8,192,192]{2,1,0:T(8,128)(2,1)} %add_convert_fusion.w_ref), custom_call_target="tpu_custom_call" | custom-call | tf_op jit(solution)/shard_map/pallas_call | solution.py:67
  56.4 0.8 slice.207
  58.3 0.6 reshape.316
  59.0 7.4 %all-to-all-start.1 = ((f32[16,4,128]{2,1,0:T(4,128)}), f32[16,4,128]{2,1,0:T(4,128)S(1)}, u32[]{:S(2)}, u32[]{:S(2)}) async-start(f32[16,4,128]{2,1,0:T(4,128)} %reshape.316), calls=%async_computation.1 | async-start | bytes 65536 | tf_op jit(solution)/shard_map/all_to_all | solution.py:218
  66.4 6.4 %all-to-all-done.1 = f32[16,4,128]{2,1,0:T(4,128)S(1)} async-done(((f32[16,4,128]{2,1,0:T(4,128)}), f32[16,4,128]{2,1,0:T(4,128)S(1)}, u32[]{:S(2)}, u32[]{:S(2)}) %all-to-all-start.1) | async-done | bytes 32800 | tf_op jit(solution)/shard_map/all_to_all | solution.py:218
  73.6 5.5 %collective-permute-start.4 = (f32[4,3,38]{2,1,0:T(4,128)S(1)}, f32[4,3,38]{2,1,0:T(4,128)S(1)}, u32[]{:S(2)}, u32[]{:S(2)}) collective-permute-start(f32[4,3,38]{2,1,0:T(4,128)S(1)} %get-tuple-element.23), channel_id=1, source_target_pairs={{0,16},{16,32},{32,48},{48,64},{64,80},{80,96},{96,112},{1,17},{17... | collective-permute-start | bytes 5480 | tf_op jit(solution)/shard_map/ppermute | solution.py:163
  79.1 1.9 %collective-permute-start.5 = (f32[4,3,38]{2,1,0:T(4,128)S(1)}, f32[4,3,38]{2,1,0:T(4,128)S(1)}, u32[]{:S(2)}, u32[]{:S(2)}) collective-permute-start(f32[4,3,38]{2,1,0:T(4,128)S(1)} %get-tuple-element.24), channel_id=1, source_target_pairs={{16,0},{32,16},{48,32},{64,48},{80,64},{96,80},{112,96},{17,1},{33... | collective-permute-start | bytes 5480 | tf_op jit(solution)/shard_map/ppermute | solution.py:164
  81.1 0.7 select_reduce_fusion.1
  81.7 2.4 %collective-permute-done.5 = f32[4,3,38]{2,1,0:T(4,128)S(1)} collective-permute-done((f32[4,3,38]{2,1,0:T(4,128)S(1)}, f32[4,3,38]{2,1,0:T(4,128)S(1)}, u32[]{:S(2)}, u32[]{:S(2)}) %collective-permute-start.5) | collective-permute-done | bytes 1856 | tf_op jit(solution)/shard_map/ppermute | solution.py:164
  84.9 0.7 fusion.47
  (81 shorter events, 4.8 us)
Async XLA Ops:
  0.6 8.3 %copy-start = (bf16[512,512]{1,0:T(8,128)(2,1)S(1)}, bf16[512,512]{1,0:T(8,128)(2,1)}, u32[]{:S(2)}) copy-start(bf16[512,512]{1,0:T(8,128)(2,1)} %param.7) | copy-start | bytes 1572868
  1.5 8.5 %copy-start.13 = (s32[1,8]{1,0:T(1,128)S(1)}, s32[1,8]{1,0:T(1,128)}, u32[]{:S(2)}) copy-start(s32[1,8]{1,0:T(1,128)} %param.10) | copy-start | bytes 100
  1.5 25.0 %collective-permute-start.1 = (bf16[32,512]{1,0:T(8,128)(2,1)S(1)}, bf16[32,512]{1,0:T(8,128)(2,1)S(1)}, u32[]{:S(2)}, u32[]{:S(2)}) collective-permute-start(bf16[32,512]{1,0:T(8,128)(2,1)S(1)} %get-tuple-element.21), channel_id=1, source_target_pairs={{16,0},{32,16},{48,32},{64,48},{80,64},{96,80},{112,96},{17,1},{33... | collective-permute-start | bytes 98312 | tf_op jit(solution)/shard_map/ppermute | solution.py:91
  4.9 21.5 %collective-permute-start = (bf16[32,512]{1,0:T(8,128)(2,1)S(1)}, bf16[32,512]{1,0:T(8,128)(2,1)S(1)}, u32[]{:S(2)}, u32[]{:S(2)}) collective-permute-start(bf16[32,512]{1,0:T(8,128)(2,1)S(1)} %get-tuple-element.22), channel_id=1, source_target_pairs={{0,16},{16,32},{32,48},{48,64},{64,80},{80,96},{96,112},{1,17},{17... | collective-permute-start | bytes 98312 | tf_op jit(solution)/shard_map/ppermute | solution.py:89
  10.6 9.0 %copy-start.8 = (s32[2,1,8]{2,1,0:T(1,128)S(1)}, s32[2,1,8]{2,1,0:T(1,128)}, u32[]{:S(2)}) copy-start(s32[2,1,8]{2,1,0:T(1,128)} %param.11) | copy-start | bytes 196
  10.6 10.0 %copy-start.12 = (s32[1,8]{1,0:T(1,128)S(1)}, s32[1,8]{1,0:T(1,128)}, u32[]{:S(2)}) copy-start(s32[1,8]{1,0:T(1,128)} %param.12) | copy-start | bytes 100
  10.6 11.3 %copy-start.5 = (s32[32,32]{1,0:T(8,128)S(1)}, s32[32,32]{1,0:T(8,128)}, u32[]{:S(2)}) copy-start(s32[32,32]{1,0:T(8,128)} %param.13) | copy-start | bytes 12292
  12.0 30.3 %all-to-all-start = ((bf16[32,128,128]{2,1,0:T(8,128)(2,1)}), bf16[32,128,128]{2,1,0:T(8,128)(2,1)S(1)}, u32[]{:S(2)}, u32[]{:S(2)}) async-start(bf16[32,128,128]{2,1,0:T(8,128)(2,1)} %copy.40), calls=%async_computation | async-start | bytes 2097152 | tf_op jit(solution)/shard_map/all_to_all | solution.py:176
  22.6 3.9 %copy-start.1 = (bf16[512,512]{1,0:T(8,128)(2,1)S(1)}, bf16[512,512]{1,0:T(8,128)(2,1)}, u32[]{:S(2)}) copy-start(bf16[512,512]{1,0:T(8,128)(2,1)} %param.8) | copy-start | bytes 1572868
  26.5 6.1 %copy-start.3 = (bf16[576,512]{1,0:T(8,128)(2,1)}, bf16[576,512]{1,0:T(8,128)(2,1)S(1)}, u32[]{:S(2)}) copy-start(bf16[576,512]{1,0:T(8,128)(2,1)S(1)} %constant_dynamic-update-slice_fusion) | copy-start | bytes 1769476
  27.4 9.0 %collective-permute-start.2 = (bf16[576,32]{1,0:T(8,128)(2,1)}, bf16[576,32]{1,0:T(8,128)(2,1)}, u32[]{:S(2)}, u32[]{:S(2)}) collective-permute-start(bf16[576,32]{1,0:T(8,128)(2,1)} %get-tuple-element.19), channel_id=1, source_target_pairs={{0,1},{1,2},{2,3},{3,4},{4,5},{5,6},{6,7},{7,8},{8,9},{9,10},{10,1... | collective-permute-start | bytes 110600 | tf_op jit(solution)/shard_map/ppermute | solution.py:179
  31.3 7.5 %collective-permute-start.3 = (bf16[576,32]{1,0:T(8,128)(2,1)}, bf16[576,32]{1,0:T(8,128)(2,1)}, u32[]{:S(2)}, u32[]{:S(2)}) collective-permute-start(bf16[576,32]{1,0:T(8,128)(2,1)} %get-tuple-element.20), channel_id=1, source_target_pairs={{1,0},{2,1},{3,2},{4,3},{5,4},{6,5},{7,6},{8,7},{9,8},{10,9},{11,1... | collective-permute-start | bytes 110600 | tf_op jit(solution)/shard_map/ppermute | solution.py:182
  42.3 14.9 %copy-start.11 = (pred[8,32]{1,0:T(8,128)(4,1)S(1)}, pred[8,32]{1,0:T(8,128)(4,1)}, u32[]{:S(2)}) copy-start(pred[8,32]{1,0:T(8,128)(4,1)} %iota_compare_fusion.24) | copy-start | bytes 772
  42.3 15.3 %copy-start.4 = (pred[8,32,32]{2,1,0:T(8,128)(4,1)S(1)}, pred[8,32,32]{2,1,0:T(8,128)(4,1)}, u32[]{:S(2)}) copy-start(pred[8,32,32]{2,1,0:T(8,128)(4,1)} %broadcast_and_fusion) | copy-start | bytes 24580
  42.3 15.4 %copy-start.2 = (f32[1,32,32]{2,1,0:T(8,128)S(1)}, f32[1,32,32]{2,1,0:T(8,128)}, u32[]{:S(2)}) copy-start(f32[1,32,32]{2,1,0:T(8,128)} %convert_bitcast_fusion) | copy-start | bytes 12292
  42.3 15.9 %copy-start.9 = (pred[16]{0:T(512)(128)(4,1)S(1)}, pred[16]{0:T(512)(128)(4,1)}, u32[]{:S(2)}) copy-start(pred[16]{0:T(512)(128)(4,1)} %get-tuple-element.51) | copy-start | bytes 52
  42.3 15.9 %copy-start.10 = (pred[16]{0:T(512)(128)(4,1)S(1)}, pred[16]{0:T(512)(128)(4,1)}, u32[]{:S(2)}) copy-start(pred[16]{0:T(512)(128)(4,1)} %get-tuple-element.52) | copy-start | bytes 52
  42.3 16.0 %copy-start.6 = (f32[512]{0:T(512)S(1)}, f32[512]{0:T(512)}, u32[]{:S(2)}) copy-start(f32[512]{0:T(512)} %pad.14.clone) | copy-start | bytes 6148
  42.3 24.0 %copy-start.14 = (s32[1,8]{1,0:T(1,128)S(1)}, s32[1,8]{1,0:T(1,128)}, u32[]{:S(2)}) copy-start(s32[1,8]{1,0:T(1,128)} %param.10) | copy-start | bytes 100
  57.2 28.4 %copy-start.7 = (f32[2,8]{1,0:T(2,128)}, f32[2,8]{1,0:T(2,128)S(1)}, u32[]{:S(2)}) copy-start(f32[2,8]{1,0:T(2,128)S(1)} %bitcast_negate_fusion) | copy-start | bytes 196
  59.0 13.8 %all-to-all-start.1 = ((f32[16,4,128]{2,1,0:T(4,128)}), f32[16,4,128]{2,1,0:T(4,128)S(1)}, u32[]{:S(2)}, u32[]{:S(2)}) async-start(f32[16,4,128]{2,1,0:T(4,128)} %reshape.316), calls=%async_computation.1 | async-start | bytes 65536 | tf_op jit(solution)/shard_map/all_to_all | solution.py:218
  73.6 8.1 %collective-permute-start.4 = (f32[4,3,38]{2,1,0:T(4,128)S(1)}, f32[4,3,38]{2,1,0:T(4,128)S(1)}, u32[]{:S(2)}, u32[]{:S(2)}) collective-permute-start(f32[4,3,38]{2,1,0:T(4,128)S(1)} %get-tuple-element.23), channel_id=1, source_target_pairs={{0,16},{16,32},{32,48},{48,64},{64,80},{80,96},{96,112},{1,17},{17... | collective-permute-start | bytes 5480 | tf_op jit(solution)/shard_map/ppermute | solution.py:163
  79.1 5.0 %collective-permute-start.5 = (f32[4,3,38]{2,1,0:T(4,128)S(1)}, f32[4,3,38]{2,1,0:T(4,128)S(1)}, u32[]{:S(2)}, u32[]{:S(2)}) collective-permute-start(f32[4,3,38]{2,1,0:T(4,128)S(1)} %get-tuple-element.24), channel_id=1, source_target_pairs={{16,0},{32,16},{48,32},{64,48},{80,64},{96,80},{112,96},{17,1},{33... | collective-permute-start | bytes 5480 | tf_op jit(solution)/shard_map/ppermute | solution.py:164

commit v13 on v10

--- a/solution.py
+++ b/solution.py
@@ -20,29 +20,34 @@
 EPSILON = 1e-05
 
 HALF = PATCH // 2
+PER = 2
 
 
 def flow_kernel(tf_ref, w_ref, out_ref, wlo, whi, corr):
-    wf = w_ref[0].astype(jnp.float32)
-    wlo[...] = wf[:, 0:PATCH]
-    whi[...] = jnp.zeros(whi.shape, jnp.float32)
-    whi[:, 0:WIN - HALF] = wf[:, HALF:WIN]
-    tfv = tf_ref[0].astype(jnp.float32)
-    t_cat = jnp.concatenate([tf_ref[0, 0:HALF, :], tf_ref[0, HALF:PATCH, :]], axis=1)
-    corr[...] = jnp.zeros(corr.shape, jnp.float32)
-
-    def step(dy, carry):
-        w_cat = jnp.concatenate(
-            [whi[pl.ds(dy, PATCH), :], wlo[pl.ds(dy, PATCH), :]], axis=0
-        ).astype(jnp.bfloat16)
-        m = jnp.dot(t_cat, w_cat, preferred_element_type=jnp.float32)
-        r = pltpu.roll(m, 0, axis=1, stride=1, stride_axis=0)
-        corr[pl.ds(dy, 1), :] = jnp.sum(r, axis=0, keepdims=True)
-        return carry
-
-    lax.fori_loop(0, SHIFTS, step, 0, unroll=SHIFTS)
-
-    c = corr[...]
+    cats = []
+    for q in range(PER):
+        wf = w_ref[q].astype(jnp.float32)
+        wlo[q] = wf[:, 0:PATCH]
+        whi[q] = jnp.zeros(whi.shape[1:], jnp.float32)
+        whi[q, :, 0:WIN - HALF] = wf[:, HALF:WIN]
+        cats.append(jnp.concatenate([tf_ref[q, 0:HALF, :], tf_ref[q, HALF:PATCH, :]], axis=1))
+        corr[q] = jnp.zeros(corr.shape[1:], jnp.float32)
+    for dy in range(SHIFTS):
+        for q in range(PER):
+            w_cat = jnp.concatenate(
+                [whi[q, dy : dy + PATCH, :], wlo[q, dy : dy + PATCH, :]], axis=0
+            ).astype(jnp.bfloat16)
+            m = jnp.dot(cats[q], w_cat, preferred_element_type=jnp.float32)
+            r = pltpu.roll(m, 0, axis=1, stride=1, stride_axis=0)
+            corr[q, dy : dy + 1, :] = jnp.sum(r, axis=0, keepdims=True)
+    for q in range(PER):
+        _epilogue(tf_ref, w_ref, out_ref, corr, q)
+
+
+def _epilogue(tf_ref, w_ref, out_ref, corr, q):
+    wf = w_ref[q].astype(jnp.float32)
+    tfv = tf_ref[q].astype(jnp.float32)
+    c = corr[q]
     rows = lax.broadcasted_iota(jnp.int32, c.shape, 0)
     lanes = lax.broadcasted_iota(jnp.int32, c.shape, 1)
     valid = (rows < SHIFTS) & (lanes >= HALF - 1)
@@ -59,20 +64,20 @@
     fy = jnp.sum(w * sy, keepdims=True) / FLOW_UNIT
     fx = jnp.sum(w * sx, keepdims=True) / FLOW_UNIT
     orow = lax.broadcasted_iota(jnp.int32, (8, 128), 0)
-    out_ref[0] = jnp.where(orow == 0, fy, jnp.where(orow == 1, fx, 0.0))
+    out_ref[q] = jnp.where(orow == 0, fy, jnp.where(orow == 1, fx, 0.0))
 
 def flows_of(tflipped, windows):
     n = tflipped.shape[0]
     out = pl.pallas_call(
         flow_kernel,
-        grid=(n,),
-        in_specs=[pl.BlockSpec((1, PATCH, PATCH), lambda i: (i, 0, 0)),
-                  pl.BlockSpec((1, WIN, WIN), lambda i: (i, 0, 0))],
-        out_specs=pl.BlockSpec((1, 8, 128), lambda i: (i, 0, 0)),
+        grid=(n // PER,),
+        in_specs=[pl.BlockSpec((PER, PATCH, PATCH), lambda i: (i, 0, 0)),
+                  pl.BlockSpec((PER, WIN, WIN), lambda i: (i, 0, 0))],
+        out_specs=pl.BlockSpec((PER, 8, 128), lambda i: (i, 0, 0)),
         out_shape=jax.ShapeDtypeStruct((n, 8, 128), jnp.float32),
-        scratch_shapes=[pltpu.VMEM((WIN, PATCH), jnp.float32),
-                        pltpu.VMEM((WIN, PATCH), jnp.float32),
-                        pltpu.VMEM((72, PATCH), jnp.float32)],
+        scratch_shapes=[pltpu.VMEM((PER, WIN, PATCH), jnp.float32),
+                        pltpu.VMEM((PER, WIN, PATCH), jnp.float32),
+                        pltpu.VMEM((PER, 72, PATCH), jnp.float32)],
     )(tflipped, windows)
     return out[:, 0:2, 0].T
 

time: 76.9 us -> 75.6 us (0.983)
  Pallas kernels: 11.9 us -> 10.6 us
    pallas_call x1, Pallas kernels: 11.9 us -> 10.6 us  [flows_of(): pl.pallas_call(flow_kernel, grid=(n // PER,), in_specs=[pl.BlockSpec((PER...]
where the time goes in v13:
time: 75.6 us; the launch traced here: 75.1 us
  starting transfers between devices  36.4 us (48%)
  waiting for transfers between devices  11.6 us (15%)
  Pallas kernels  10.6 us (14%)
  local copies, waits for them, and re-layouts  6.38 us (8%)
  matrix products  6.14 us (8%)
  other arithmetic  3.03 us (4%)
  between operations  0.97 us (1%)
    pallas_call x1, Pallas kernels, flows_of(): pl.pallas_call(flow_kernel, grid=(n // PER,), in_specs=[pl.BlockSpec((PER...  10.6 us
    all_to_all x1, starting transfers between devices, shards(): lax.all_to_all(back, 'tx', split_axis=0, concat_axis=0, tiled=True)  9.27 us
    all_to_all x1, starting transfers between devices, shards(): lax.all_to_all(outgoing, 'tx', split_axis=0, concat_axis=0, tiled=True)  8.56 us
    ppermute x2, starting transfers between devices, padded_2(): lax.ppermute(tail, axis, [(i, (i + 1) % count) for i in range(ends)])  8.22 us
    all_to_all x1, waiting for transfers between devices, shards(): lax.all_to_all(back, 'tx', split_axis=0, concat_axis=0, tiled=True)  6.43 us
    ppermute x2, waiting for transfers between devices, padded_2(): lax.ppermute(head, axis, [((i + 1) % count, i) for i in range(ends)])  4.98 us
    ppermute x1, starting transfers between devices, rows_exchange(): above = lax.ppermute(tail, 'ty', [(i, i + 1) for i in range(count - 1)])  4.84 us
    dot_general x1, matrix products, shards(): jnp.einsum('mrc,msc->mrs', by_row.astype(jnp.bfloat16), wcol_pick, prefer...  3.8 us
  transfers between devices with their start and end apart: 8, of which 4 were waited for; matrix products, arithmetic and copies ran while one was open for 7% of the time, Pallas kernels for 0%

profile of v13, /device:TPU:1, one launch (start us, length us, event | category | flops | bytes accessed | tf_op | source)
XLA Modules:
  0.0 75.1 jit_solution(131218679769439535)
XLA Ops:
  0.7 0.7 slice_bitcast_fusion.5
  1.5 0.2 copy-done
  1.7 1.1 %fusion.11 = bf16[8,128,128]{2,1,0:T(8,128)(2,1)S(1)} fusion(s32[8,128]{1,0:T(8,128)S(1)} %get-tuple-element.43, s32[8,128]{1,0:T(8,128)S(1)} %get-tuple-element.44, bf16[512,512]{1,0:T(8,128)(2,1)S(1)} %copy-done), kind=kOutput, calls=%fused_computation.14 | convolution fusion | flops 672792576 | bytes 794624 | tf_op jit(solution)/shard_map/kra,kia->kri/dot_general | solution.py:163
  2.9 0.6 convolution_convert_fusion
  3.4 1.4 %copy.36 = bf16[32,128,128]{2,1,0:T(8,128)(2,1)} copy(bf16[32,128,128]{2,0,1:T(8,128)(2,1)S(1)} %convolution_convert_fusion) | data formatting | bytes 2097152 | tf_op jit(solution)/shard_map/convert_element_type | solution.py:168
  4.8 8.6 %all-to-all-start = ((bf16[32,128,128]{2,1,0:T(8,128)(2,1)}), bf16[32,128,128]{2,1,0:T(8,128)(2,1)S(1)}, u32[]{:S(2)}, u32[]{:S(2)}) async-start(bf16[32,128,128]{2,1,0:T(8,128)(2,1)} %copy.36), calls=%async_computation | async-start | bytes 2097152 | tf_op jit(solution)/shard_map/all_to_all | solution.py:207
  13.4 4.0 %collective-permute-start = (bf16[32,512]{1,0:T(8,128)(2,1)S(1)}, bf16[32,512]{1,0:T(8,128)(2,1)S(1)}, u32[]{:S(2)}, u32[]{:S(2)}) collective-permute-start(bf16[32,512]{1,0:T(8,128)(2,1)S(1)} %get-tuple-element.20), channel_id=1, source_target_pairs={{0,16},{16,32},{32,48},{48,64},{64,80},{80,96},{96,112},{1,17},{17... | collective-permute-start | bytes 98312 | tf_op jit(solution)/shard_map/ppermute | solution.py:93
  17.4 1.9 %collective-permute-start.1 = (bf16[32,512]{1,0:T(8,128)(2,1)S(1)}, bf16[32,512]{1,0:T(8,128)(2,1)S(1)}, u32[]{:S(2)}, u32[]{:S(2)}) collective-permute-start(bf16[32,512]{1,0:T(8,128)(2,1)S(1)} %get-tuple-element.19), channel_id=1, source_target_pairs={{16,0},{32,16},{48,32},{64,48},{80,64},{96,80},{112,96},{17,1},{33... | collective-permute-start | bytes 98312 | tf_op jit(solution)/shard_map/ppermute | solution.py:95
  19.9 3.0 %collective-permute-done.1 = bf16[32,512]{1,0:T(8,128)(2,1)S(1)} collective-permute-done((bf16[32,512]{1,0:T(8,128)(2,1)S(1)}, bf16[32,512]{1,0:T(8,128)(2,1)S(1)}, u32[]{:S(2)}, u32[]{:S(2)}) %collective-permute-start.1) | collective-permute-done | bytes 32800 | tf_op jit(solution)/shard_map/ppermute | solution.py:95
  23.0 0.1 fusion.59
  23.1 1.3 %collective-permute-start.3 = (bf16[576,32]{1,0:T(8,128)(2,1)S(1)}, bf16[576,32]{1,0:T(8,128)(2,1)S(1)}, u32[]{:S(2)}, u32[]{:S(2)}) collective-permute-start(bf16[576,32]{1,0:T(8,128)(2,1)S(1)} %get-tuple-element.18), channel_id=1, source_target_pairs={{1,0},{2,1},{3,2},{4,3},{5,4},{6,5},{7,6},{8,7},{9,8},{10,9},{11,1... | collective-permute-start | bytes 110600 | tf_op jit(solution)/shard_map/ppermute | solution.py:95
  24.4 4.2 %collective-permute-start.2 = (bf16[576,32]{1,0:T(8,128)(2,1)S(1)}, bf16[576,32]{1,0:T(8,128)(2,1)S(1)}, u32[]{:S(2)}, u32[]{:S(2)}) collective-permute-start(bf16[576,32]{1,0:T(8,128)(2,1)S(1)} %get-tuple-element.17), channel_id=1, source_target_pairs={{0,1},{1,2},{2,3},{3,4},{4,5},{5,6},{6,7},{7,8},{8,9},{9,10},{10,1... | collective-permute-start | bytes 110600 | tf_op jit(solution)/shard_map/ppermute | solution.py:93
  28.7 2.0 %collective-permute-done.3 = bf16[576,32]{1,0:T(8,128)(2,1)S(1)} collective-permute-done((bf16[576,32]{1,0:T(8,128)(2,1)S(1)}, bf16[576,32]{1,0:T(8,128)(2,1)S(1)}, u32[]{:S(2)}, u32[]{:S(2)}) %collective-permute-start.3) | collective-permute-done | bytes 36896 | tf_op jit(solution)/shard_map/ppermute | solution.py:95
  30.7 3.8 %fusion.8.w_ref = bf16[8,192,192]{2,1,0:T(8,128)(2,1)} fusion(s32[8,192]{1,0:T(8,128)S(1)} %get-tuple-element.45, s32[8,192]{1,0:T(8,128)S(1)} %get-tuple-element.46, bf16[576,32]{1,0:T(8,128)(2,1)S(1)} %collective-permute-done.3, bf16[576,512]{1,0:T(8,128)(2,1)S(1)} %constant_dynamic-update-slice_fusion, bf16[576,32]{1,0:T(8,128)(2,1)S(1)} %collective-permute-done.2), kind=kOutput, calls=%fused_computation.13 | convolution fusion | flops 1363894272 | bytes 1265664 | tf_op jit(solution)/shard_map/mrc,msc->mrs/dot_general | solution.py:213
  34.5 0.7 fusion.12
  35.1 0.8 %copy.53.tf_ref = bf16[8,128,128]{2,1,0:T(8,128)(2,1)} copy(bf16[8,128,128]{2,0,1:T(8,128)(2,1)S(1)} %fusion.12) | data formatting | bytes 524288 | tf_op jit(solution)/shard_map/ms,sri->mri/dot_general | solution.py:216
  35.9 10.6 %shard_map.94 = f32[8,8,128]{2,1,0:T(8,128)} custom-call(bf16[8,128,128]{2,1,0:T(8,128)(2,1)} %copy.53.tf_ref, bf16[8,192,192]{2,1,0:T(8,128)(2,1)} %fusion.8.w_ref), custom_call_target="tpu_custom_call" | custom-call | tf_op jit(solution)/shard_map/pallas_call | solution.py:71
  46.4 0.8 %slice.192 = f32[8,2,1]{2,1,0:T(2,128)S(1)} slice(f32[8,8,128]{2,1,0:T(8,128)} %shard_map.94), slice={[0:8], [0:2], [0:1]} | slice | bytes 128 | tf_op jit(solution)/shard_map/slice | solution.py:82
  47.9 0.2 broadcast_in_dim.163
  48.1 0.2 broadcast_in_dim.160
  48.4 0.6 reshape.316
  49.0 9.3 %all-to-all-start.1 = ((f32[16,4,128]{2,1,0:T(4,128)}), f32[16,4,128]{2,1,0:T(4,128)S(1)}, u32[]{:S(2)}, u32[]{:S(2)}) async-start(f32[16,4,128]{2,1,0:T(4,128)} %reshape.316), calls=%async_computation.1 | async-start | bytes 65536 | tf_op jit(solution)/shard_map/all_to_all | solution.py:234
  58.4 6.4 %all-to-all-done.1 = f32[16,4,128]{2,1,0:T(4,128)S(1)} async-done(((f32[16,4,128]{2,1,0:T(4,128)}), f32[16,4,128]{2,1,0:T(4,128)S(1)}, u32[]{:S(2)}, u32[]{:S(2)}) %all-to-all-start.1) | async-done | bytes 32800 | tf_op jit(solution)/shard_map/all_to_all | solution.py:234
  65.1 0.2 select_n.76
  65.3 0.2 select_n.72
  65.6 2.3 %collective-permute-start.5 = (f32[4,3,38]{2,1,0:T(4,128)S(1)}, f32[4,3,38]{2,1,0:T(4,128)S(1)}, u32[]{:S(2)}, u32[]{:S(2)}) collective-permute-start(f32[4,3,38]{2,1,0:T(4,128)S(1)} %get-tuple-element.22), channel_id=1, source_target_pairs={{16,0},{32,16},{48,32},{64,48},{80,64},{96,80},{112,96},{17,1},{33... | collective-permute-start | bytes 5480 | tf_op jit(solution)/shard_map/ppermute | solution.py:195
  68.0 4.8 %collective-permute-start.4 = (f32[4,3,38]{2,1,0:T(4,128)S(1)}, f32[4,3,38]{2,1,0:T(4,128)S(1)}, u32[]{:S(2)}, u32[]{:S(2)}) collective-permute-start(f32[4,3,38]{2,1,0:T(4,128)S(1)} %get-tuple-element.21), channel_id=1, source_target_pairs={{0,16},{16,32},{32,48},{48,64},{64,80},{80,96},{96,112},{1,17},{17... | collective-permute-start | bytes 5480 | tf_op jit(solution)/shard_map/ppermute | solution.py:194
  72.8 0.7 select_reduce_fusion.1
  73.5 0.1 collective-permute-done.4
  73.6 0.1 pad_maximum_fusion
  74.2 0.1 fusion.29
  74.4 0.7 fusion.45
  (61 shorter events, 2.4 us)
Async XLA Ops:
  0.6 1.1 %copy-start = (bf16[512,512]{1,0:T(8,128)(2,1)S(1)}, bf16[512,512]{1,0:T(8,128)(2,1)}, u32[]{:S(2)}) copy-start(bf16[512,512]{1,0:T(8,128)(2,1)} %param.7) | copy-start | bytes 1572868
  1.7 1.1 %copy-start.6 = (s32[1,8]{1,0:T(1,128)S(1)}, s32[1,8]{1,0:T(1,128)}, u32[]{:S(2)}) copy-start(s32[1,8]{1,0:T(1,128)} %param.10) | copy-start | bytes 100
  4.8 8.6 %copy-start.1 = (bf16[512,512]{1,0:T(8,128)(2,1)S(1)}, bf16[512,512]{1,0:T(8,128)(2,1)}, u32[]{:S(2)}) copy-start(bf16[512,512]{1,0:T(8,128)(2,1)} %param.8) | copy-start | bytes 1572868
  4.8 14.6 %copy-start.4 = (s32[2,1,8]{2,1,0:T(1,128)S(1)}, s32[2,1,8]{2,1,0:T(1,128)}, u32[]{:S(2)}) copy-start(s32[2,1,8]{2,1,0:T(1,128)} %param.11) | copy-start | bytes 196
  4.8 14.6 %copy-start.5 = (s32[1,8]{1,0:T(1,128)S(1)}, s32[1,8]{1,0:T(1,128)}, u32[]{:S(2)}) copy-start(s32[1,8]{1,0:T(1,128)} %param.12) | copy-start | bytes 100
  4.8 14.7 %copy-start.2 = (s32[32,32]{1,0:T(8,128)S(1)}, s32[32,32]{1,0:T(8,128)}, u32[]{:S(2)}) copy-start(s32[32,32]{1,0:T(8,128)} %param.13) | copy-start | bytes 12292
  4.8 29.6 %all-to-all-start = ((bf16[32,128,128]{2,1,0:T(8,128)(2,1)}), bf16[32,128,128]{2,1,0:T(8,128)(2,1)S(1)}, u32[]{:S(2)}, u32[]{:S(2)}) async-start(bf16[32,128,128]{2,1,0:T(8,128)(2,1)} %copy.36), calls=%async_computation | async-start | bytes 2097152 | tf_op jit(solution)/shard_map/all_to_all | solution.py:207
  13.4 6.5 %collective-permute-start = (bf16[32,512]{1,0:T(8,128)(2,1)S(1)}, bf16[32,512]{1,0:T(8,128)(2,1)S(1)}, u32[]{:S(2)}, u32[]{:S(2)}) collective-permute-start(bf16[32,512]{1,0:T(8,128)(2,1)S(1)} %get-tuple-element.20), channel_id=1, source_target_pairs={{0,16},{16,32},{32,48},{48,64},{64,80},{80,96},{96,112},{1,17},{17... | collective-permute-start | bytes 98312 | tf_op jit(solution)/shard_map/ppermute | solution.py:93
  17.4 5.5 %collective-permute-start.1 = (bf16[32,512]{1,0:T(8,128)(2,1)S(1)}, bf16[32,512]{1,0:T(8,128)(2,1)S(1)}, u32[]{:S(2)}, u32[]{:S(2)}) collective-permute-start(bf16[32,512]{1,0:T(8,128)(2,1)S(1)} %get-tuple-element.19), channel_id=1, source_target_pairs={{16,0},{32,16},{48,32},{64,48},{80,64},{96,80},{112,96},{17,1},{33... | collective-permute-start | bytes 98312 | tf_op jit(solution)/shard_map/ppermute | solution.py:95
  23.1 7.5 %collective-permute-start.3 = (bf16[576,32]{1,0:T(8,128)(2,1)S(1)}, bf16[576,32]{1,0:T(8,128)(2,1)S(1)}, u32[]{:S(2)}, u32[]{:S(2)}) collective-permute-start(bf16[576,32]{1,0:T(8,128)(2,1)S(1)} %get-tuple-element.18), channel_id=1, source_target_pairs={{1,0},{2,1},{3,2},{4,3},{5,4},{6,5},{7,6},{8,7},{9,8},{10,9},{11,1... | collective-permute-start | bytes 110600 | tf_op jit(solution)/shard_map/ppermute | solution.py:95
  24.4 6.3 %collective-permute-start.2 = (bf16[576,32]{1,0:T(8,128)(2,1)S(1)}, bf16[576,32]{1,0:T(8,128)(2,1)S(1)}, u32[]{:S(2)}, u32[]{:S(2)}) collective-permute-start(bf16[576,32]{1,0:T(8,128)(2,1)S(1)} %get-tuple-element.17), channel_id=1, source_target_pairs={{0,1},{1,2},{2,3},{3,4},{4,5},{5,6},{6,7},{7,8},{8,9},{9,10},{10,1... | collective-permute-start | bytes 110600 | tf_op jit(solution)/shard_map/ppermute | solution.py:93
  47.3 26.7 %copy-start.3 = (f32[2,8]{1,0:T(2,128)}, f32[2,8]{1,0:T(2,128)S(1)}, u32[]{:S(2)}) copy-start(f32[2,8]{1,0:T(2,128)S(1)} %bitcast_negate_fusion) | copy-start | bytes 196
  49.0 15.8 %all-to-all-start.1 = ((f32[16,4,128]{2,1,0:T(4,128)}), f32[16,4,128]{2,1,0:T(4,128)S(1)}, u32[]{:S(2)}, u32[]{:S(2)}) async-start(f32[16,4,128]{2,1,0:T(4,128)} %reshape.316), calls=%async_computation.1 | async-start | bytes 65536 | tf_op jit(solution)/shard_map/all_to_all | solution.py:234
  65.6 7.9 %collective-permute-start.5 = (f32[4,3,38]{2,1,0:T(4,128)S(1)}, f32[4,3,38]{2,1,0:T(4,128)S(1)}, u32[]{:S(2)}, u32[]{:S(2)}) collective-permute-start(f32[4,3,38]{2,1,0:T(4,128)S(1)} %get-tuple-element.22), channel_id=1, source_target_pairs={{16,0},{32,16},{48,32},{64,48},{80,64},{96,80},{112,96},{17,1},{33... | collective-permute-start | bytes 5480 | tf_op jit(solution)/shard_map/ppermute | solution.py:195
  68.0 5.6 %collective-permute-start.4 = (f32[4,3,38]{2,1,0:T(4,128)S(1)}, f32[4,3,38]{2,1,0:T(4,128)S(1)}, u32[]{:S(2)}, u32[]{:S(2)}) collective-permute-start(f32[4,3,38]{2,1,0:T(4,128)S(1)} %get-tuple-element.21), channel_id=1, source_target_pairs={{0,16},{16,32},{32,48},{48,64},{64,80},{80,96},{96,112},{1,17},{17... | collective-permute-start | bytes 5480 | tf_op jit(solution)/shard_map/ppermute | solution.py:194

commit v14 on v13

--- a/solution.py
+++ b/solution.py
@@ -20,7 +20,7 @@
 EPSILON = 1e-05
 
 HALF = PATCH // 2
-PER = 2
+PER = 4
 
 
 def flow_kernel(tf_ref, w_ref, out_ref, wlo, whi, corr):

time: 75.6 us -> 75.2 us (level)
  no operation moved by 1% of the time
where the time goes in v14:
time: 75.2 us; the launch traced here: 74.7 us
  starting transfers between devices  36.4 us (48%)
  waiting for transfers between devices  11.6 us (15%)
  Pallas kernels  10.2 us (14%)
  local copies, waits for them, and re-layouts  6.38 us (8%)
  matrix products  6.14 us (8%)
  other arithmetic  3.03 us (4%)
  between operations  0.97 us (1%)
    pallas_call x1, Pallas kernels, flows_of(): pl.pallas_call(flow_kernel, grid=(n // PER,), in_specs=[pl.BlockSpec((PER...  10.2 us
    all_to_all x1, starting transfers between devices, shards(): lax.all_to_all(back, 'tx', split_axis=0, concat_axis=0, tiled=True)  9.27 us
    all_to_all x1, starting transfers between devices, shards(): lax.all_to_all(outgoing, 'tx', split_axis=0, concat_axis=0, tiled=True)  8.56 us
    ppermute x2, starting transfers between devices, padded_2(): lax.ppermute(tail, axis, [(i, (i + 1) % count) for i in range(ends)])  8.22 us
    all_to_all x1, waiting for transfers between devices, shards(): lax.all_to_all(back, 'tx', split_axis=0, concat_axis=0, tiled=True)  6.43 us
    ppermute x2, waiting for transfers between devices, padded_2(): lax.ppermute(head, axis, [((i + 1) % count, i) for i in range(ends)])  4.98 us
    ppermute x1, starting transfers between devices, rows_exchange(): above = lax.ppermute(tail, 'ty', [(i, i + 1) for i in range(count - 1)])  4.84 us
    dot_general x1, matrix products, shards(): jnp.einsum('mrc,msc->mrs', by_row.astype(jnp.bfloat16), wcol_pick, prefer...  3.8 us
  transfers between devices with their start and end apart: 8, of which 4 were waited for; matrix products, arithmetic and copies ran while one was open for 7% of the time, Pallas kernels for 0%

profile of v14, /device:TPU:1, one launch (start us, length us, event | category | flops | bytes accessed | tf_op | source)
XLA Modules:
  0.0 74.7 jit_solution(18089650458440414601)
XLA Ops:
  0.7 0.7 slice_bitcast_fusion.5
  1.5 0.2 copy-done
  1.7 1.1 %fusion.11 = bf16[8,128,128]{2,1,0:T(8,128)(2,1)S(1)} fusion(s32[8,128]{1,0:T(8,128)S(1)} %get-tuple-element.43, s32[8,128]{1,0:T(8,128)S(1)} %get-tuple-element.44, bf16[512,512]{1,0:T(8,128)(2,1)S(1)} %copy-done), kind=kOutput, calls=%fused_computation.14 | convolution fusion | flops 672792576 | bytes 794624 | tf_op jit(solution)/shard_map/kra,kia->kri/dot_general | solution.py:163
  2.9 0.6 convolution_convert_fusion
  3.4 1.4 %copy.36 = bf16[32,128,128]{2,1,0:T(8,128)(2,1)} copy(bf16[32,128,128]{2,0,1:T(8,128)(2,1)S(1)} %convolution_convert_fusion) | data formatting | bytes 2097152 | tf_op jit(solution)/shard_map/convert_element_type | solution.py:168
  4.8 8.6 %all-to-all-start = ((bf16[32,128,128]{2,1,0:T(8,128)(2,1)}), bf16[32,128,128]{2,1,0:T(8,128)(2,1)S(1)}, u32[]{:S(2)}, u32[]{:S(2)}) async-start(bf16[32,128,128]{2,1,0:T(8,128)(2,1)} %copy.36), calls=%async_computation | async-start | bytes 2097152 | tf_op jit(solution)/shard_map/all_to_all | solution.py:207
  13.4 4.0 %collective-permute-start = (bf16[32,512]{1,0:T(8,128)(2,1)S(1)}, bf16[32,512]{1,0:T(8,128)(2,1)S(1)}, u32[]{:S(2)}, u32[]{:S(2)}) collective-permute-start(bf16[32,512]{1,0:T(8,128)(2,1)S(1)} %get-tuple-element.20), channel_id=1, source_target_pairs={{0,16},{16,32},{32,48},{48,64},{64,80},{80,96},{96,112},{1,17},{17... | collective-permute-start | bytes 98312 | tf_op jit(solution)/shard_map/ppermute | solution.py:93
  17.4 1.9 %collective-permute-start.1 = (bf16[32,512]{1,0:T(8,128)(2,1)S(1)}, bf16[32,512]{1,0:T(8,128)(2,1)S(1)}, u32[]{:S(2)}, u32[]{:S(2)}) collective-permute-start(bf16[32,512]{1,0:T(8,128)(2,1)S(1)} %get-tuple-element.19), channel_id=1, source_target_pairs={{16,0},{32,16},{48,32},{64,48},{80,64},{96,80},{112,96},{17,1},{33... | collective-permute-start | bytes 98312 | tf_op jit(solution)/shard_map/ppermute | solution.py:95
  19.9 3.0 %collective-permute-done.1 = bf16[32,512]{1,0:T(8,128)(2,1)S(1)} collective-permute-done((bf16[32,512]{1,0:T(8,128)(2,1)S(1)}, bf16[32,512]{1,0:T(8,128)(2,1)S(1)}, u32[]{:S(2)}, u32[]{:S(2)}) %collective-permute-start.1) | collective-permute-done | bytes 32800 | tf_op jit(solution)/shard_map/ppermute | solution.py:95
  23.0 0.1 fusion.59
  23.1 1.3 %collective-permute-start.3 = (bf16[576,32]{1,0:T(8,128)(2,1)S(1)}, bf16[576,32]{1,0:T(8,128)(2,1)S(1)}, u32[]{:S(2)}, u32[]{:S(2)}) collective-permute-start(bf16[576,32]{1,0:T(8,128)(2,1)S(1)} %get-tuple-element.18), channel_id=1, source_target_pairs={{1,0},{2,1},{3,2},{4,3},{5,4},{6,5},{7,6},{8,7},{9,8},{10,9},{11,1... | collective-permute-start | bytes 110600 | tf_op jit(solution)/shard_map/ppermute | solution.py:95
  24.4 4.2 %collective-permute-start.2 = (bf16[576,32]{1,0:T(8,128)(2,1)S(1)}, bf16[576,32]{1,0:T(8,128)(2,1)S(1)}, u32[]{:S(2)}, u32[]{:S(2)}) collective-permute-start(bf16[576,32]{1,0:T(8,128)(2,1)S(1)} %get-tuple-element.17), channel_id=1, source_target_pairs={{0,1},{1,2},{2,3},{3,4},{4,5},{5,6},{6,7},{7,8},{8,9},{9,10},{10,1... | collective-permute-start | bytes 110600 | tf_op jit(solution)/shard_map/ppermute | solution.py:93
  28.7 2.0 %collective-permute-done.3 = bf16[576,32]{1,0:T(8,128)(2,1)S(1)} collective-permute-done((bf16[576,32]{1,0:T(8,128)(2,1)S(1)}, bf16[576,32]{1,0:T(8,128)(2,1)S(1)}, u32[]{:S(2)}, u32[]{:S(2)}) %collective-permute-start.3) | collective-permute-done | bytes 36896 | tf_op jit(solution)/shard_map/ppermute | solution.py:95
  30.7 3.8 %fusion.8.w_ref = bf16[8,192,192]{2,1,0:T(8,128)(2,1)} fusion(s32[8,192]{1,0:T(8,128)S(1)} %get-tuple-element.45, s32[8,192]{1,0:T(8,128)S(1)} %get-tuple-element.46, bf16[576,32]{1,0:T(8,128)(2,1)S(1)} %collective-permute-done.3, bf16[576,512]{1,0:T(8,128)(2,1)S(1)} %constant_dynamic-update-slice_fusion, bf16[576,32]{1,0:T(8,128)(2,1)S(1)} %collective-permute-done.2), kind=kOutput, calls=%fused_computation.13 | convolution fusion | flops 1363894272 | bytes 1265664 | tf_op jit(solution)/shard_map/mrc,msc->mrs/dot_general | solution.py:213
  34.5 0.7 fusion.12
  35.1 0.8 %copy.53.tf_ref = bf16[8,128,128]{2,1,0:T(8,128)(2,1)} copy(bf16[8,128,128]{2,0,1:T(8,128)(2,1)S(1)} %fusion.12) | data formatting | bytes 524288 | tf_op jit(solution)/shard_map/ms,sri->mri/dot_general | solution.py:216
  35.9 10.2 %shard_map.94 = f32[8,8,128]{2,1,0:T(8,128)} custom-call(bf16[8,128,128]{2,1,0:T(8,128)(2,1)} %copy.53.tf_ref, bf16[8,192,192]{2,1,0:T(8,128)(2,1)} %fusion.8.w_ref), custom_call_target="tpu_custom_call" | custom-call | tf_op jit(solution)/shard_map/pallas_call | solution.py:71
  46.0 0.8 %slice.192 = f32[8,2,1]{2,1,0:T(2,128)S(1)} slice(f32[8,8,128]{2,1,0:T(8,128)} %shard_map.94), slice={[0:8], [0:2], [0:1]} | slice | bytes 128 | tf_op jit(solution)/shard_map/slice | solution.py:82
  47.5 0.2 broadcast_in_dim.163
  47.7 0.2 broadcast_in_dim.160
  48.0 0.6 reshape.316
  48.6 9.3 %all-to-all-start.1 = ((f32[16,4,128]{2,1,0:T(4,128)}), f32[16,4,128]{2,1,0:T(4,128)S(1)}, u32[]{:S(2)}, u32[]{:S(2)}) async-start(f32[16,4,128]{2,1,0:T(4,128)} %reshape.316), calls=%async_computation.1 | async-start | bytes 65536 | tf_op jit(solution)/shard_map/all_to_all | solution.py:234
  58.0 6.4 %all-to-all-done.1 = f32[16,4,128]{2,1,0:T(4,128)S(1)} async-done(((f32[16,4,128]{2,1,0:T(4,128)}), f32[16,4,128]{2,1,0:T(4,128)S(1)}, u32[]{:S(2)}, u32[]{:S(2)}) %all-to-all-start.1) | async-done | bytes 32800 | tf_op jit(solution)/shard_map/all_to_all | solution.py:234
  64.7 0.2 select_n.76
  64.9 0.2 select_n.72
  65.2 2.3 %collective-permute-start.5 = (f32[4,3,38]{2,1,0:T(4,128)S(1)}, f32[4,3,38]{2,1,0:T(4,128)S(1)}, u32[]{:S(2)}, u32[]{:S(2)}) collective-permute-start(f32[4,3,38]{2,1,0:T(4,128)S(1)} %get-tuple-element.22), channel_id=1, source_target_pairs={{16,0},{32,16},{48,32},{64,48},{80,64},{96,80},{112,96},{17,1},{33... | collective-permute-start | bytes 5480 | tf_op jit(solution)/shard_map/ppermute | solution.py:195
  67.6 4.8 %collective-permute-start.4 = (f32[4,3,38]{2,1,0:T(4,128)S(1)}, f32[4,3,38]{2,1,0:T(4,128)S(1)}, u32[]{:S(2)}, u32[]{:S(2)}) collective-permute-start(f32[4,3,38]{2,1,0:T(4,128)S(1)} %get-tuple-element.21), channel_id=1, source_target_pairs={{0,16},{16,32},{32,48},{48,64},{64,80},{80,96},{96,112},{1,17},{17... | collective-permute-start | bytes 5480 | tf_op jit(solution)/shard_map/ppermute | solution.py:194
  72.4 0.7 select_reduce_fusion.1
  73.1 0.1 collective-permute-done.4
  73.2 0.1 pad_maximum_fusion
  73.8 0.1 fusion.29
  74.0 0.7 fusion.45
  (61 shorter events, 2.4 us)
Async XLA Ops:
  0.6 1.1 %copy-start = (bf16[512,512]{1,0:T(8,128)(2,1)S(1)}, bf16[512,512]{1,0:T(8,128)(2,1)}, u32[]{:S(2)}) copy-start(bf16[512,512]{1,0:T(8,128)(2,1)} %param.7) | copy-start | bytes 1572868
  1.7 1.1 %copy-start.6 = (s32[1,8]{1,0:T(1,128)S(1)}, s32[1,8]{1,0:T(1,128)}, u32[]{:S(2)}) copy-start(s32[1,8]{1,0:T(1,128)} %param.10) | copy-start | bytes 100
  4.8 8.6 %copy-start.1 = (bf16[512,512]{1,0:T(8,128)(2,1)S(1)}, bf16[512,512]{1,0:T(8,128)(2,1)}, u32[]{:S(2)}) copy-start(bf16[512,512]{1,0:T(8,128)(2,1)} %param.8) | copy-start | bytes 1572868
  4.8 14.6 %copy-start.4 = (s32[2,1,8]{2,1,0:T(1,128)S(1)}, s32[2,1,8]{2,1,0:T(1,128)}, u32[]{:S(2)}) copy-start(s32[2,1,8]{2,1,0:T(1,128)} %param.11) | copy-start | bytes 196
  4.8 14.6 %copy-start.5 = (s32[1,8]{1,0:T(1,128)S(1)}, s32[1,8]{1,0:T(1,128)}, u32[]{:S(2)}) copy-start(s32[1,8]{1,0:T(1,128)} %param.12) | copy-start | bytes 100
  4.8 14.7 %copy-start.2 = (s32[32,32]{1,0:T(8,128)S(1)}, s32[32,32]{1,0:T(8,128)}, u32[]{:S(2)}) copy-start(s32[32,32]{1,0:T(8,128)} %param.13) | copy-start | bytes 12292
  4.8 29.6 %all-to-all-start = ((bf16[32,128,128]{2,1,0:T(8,128)(2,1)}), bf16[32,128,128]{2,1,0:T(8,128)(2,1)S(1)}, u32[]{:S(2)}, u32[]{:S(2)}) async-start(bf16[32,128,128]{2,1,0:T(8,128)(2,1)} %copy.36), calls=%async_computation | async-start | bytes 2097152 | tf_op jit(solution)/shard_map/all_to_all | solution.py:207
  13.4 6.5 %collective-permute-start = (bf16[32,512]{1,0:T(8,128)(2,1)S(1)}, bf16[32,512]{1,0:T(8,128)(2,1)S(1)}, u32[]{:S(2)}, u32[]{:S(2)}) collective-permute-start(bf16[32,512]{1,0:T(8,128)(2,1)S(1)} %get-tuple-element.20), channel_id=1, source_target_pairs={{0,16},{16,32},{32,48},{48,64},{64,80},{80,96},{96,112},{1,17},{17... | collective-permute-start | bytes 98312 | tf_op jit(solution)/shard_map/ppermute | solution.py:93
  17.4 5.5 %collective-permute-start.1 = (bf16[32,512]{1,0:T(8,128)(2,1)S(1)}, bf16[32,512]{1,0:T(8,128)(2,1)S(1)}, u32[]{:S(2)}, u32[]{:S(2)}) collective-permute-start(bf16[32,512]{1,0:T(8,128)(2,1)S(1)} %get-tuple-element.19), channel_id=1, source_target_pairs={{16,0},{32,16},{48,32},{64,48},{80,64},{96,80},{112,96},{17,1},{33... | collective-permute-start | bytes 98312 | tf_op jit(solution)/shard_map/ppermute | solution.py:95
  23.1 7.5 %collective-permute-start.3 = (bf16[576,32]{1,0:T(8,128)(2,1)S(1)}, bf16[576,32]{1,0:T(8,128)(2,1)S(1)}, u32[]{:S(2)}, u32[]{:S(2)}) collective-permute-start(bf16[576,32]{1,0:T(8,128)(2,1)S(1)} %get-tuple-element.18), channel_id=1, source_target_pairs={{1,0},{2,1},{3,2},{4,3},{5,4},{6,5},{7,6},{8,7},{9,8},{10,9},{11,1... | collective-permute-start | bytes 110600 | tf_op jit(solution)/shard_map/ppermute | solution.py:95
  24.4 6.3 %collective-permute-start.2 = (bf16[576,32]{1,0:T(8,128)(2,1)S(1)}, bf16[576,32]{1,0:T(8,128)(2,1)S(1)}, u32[]{:S(2)}, u32[]{:S(2)}) collective-permute-start(bf16[576,32]{1,0:T(8,128)(2,1)S(1)} %get-tuple-element.17), channel_id=1, source_target_pairs={{0,1},{1,2},{2,3},{3,4},{4,5},{5,6},{6,7},{7,8},{8,9},{9,10},{10,1... | collective-permute-start | bytes 110600 | tf_op jit(solution)/shard_map/ppermute | solution.py:93
  46.9 26.7 %copy-start.3 = (f32[2,8]{1,0:T(2,128)}, f32[2,8]{1,0:T(2,128)S(1)}, u32[]{:S(2)}) copy-start(f32[2,8]{1,0:T(2,128)S(1)} %bitcast_negate_fusion) | copy-start | bytes 196
  48.6 15.8 %all-to-all-start.1 = ((f32[16,4,128]{2,1,0:T(4,128)}), f32[16,4,128]{2,1,0:T(4,128)S(1)}, u32[]{:S(2)}, u32[]{:S(2)}) async-start(f32[16,4,128]{2,1,0:T(4,128)} %reshape.316), calls=%async_computation.1 | async-start | bytes 65536 | tf_op jit(solution)/shard_map/all_to_all | solution.py:234
  65.2 7.9 %collective-permute-start.5 = (f32[4,3,38]{2,1,0:T(4,128)S(1)}, f32[4,3,38]{2,1,0:T(4,128)S(1)}, u32[]{:S(2)}, u32[]{:S(2)}) collective-permute-start(f32[4,3,38]{2,1,0:T(4,128)S(1)} %get-tuple-element.22), channel_id=1, source_target_pairs={{16,0},{32,16},{48,32},{64,48},{80,64},{96,80},{112,96},{17,1},{33... | collective-permute-start | bytes 5480 | tf_op jit(solution)/shard_map/ppermute | solution.py:195
  67.6 5.6 %collective-permute-start.4 = (f32[4,3,38]{2,1,0:T(4,128)S(1)}, f32[4,3,38]{2,1,0:T(4,128)S(1)}, u32[]{:S(2)}, u32[]{:S(2)}) collective-permute-start(f32[4,3,38]{2,1,0:T(4,128)S(1)} %get-tuple-element.21), channel_id=1, source_target_pairs={{0,16},{16,32},{32,48},{48,64},{64,80},{80,96},{96,112},{1,17},{17... | collective-permute-start | bytes 5480 | tf_op jit(solution)/shard_map/ppermute | solution.py:194

commit v15 on v13

--- a/solution.py
+++ b/solution.py
@@ -205,7 +205,8 @@
     mask = node_mask.astype(f32)
     w = ITERS_R
     arrived = lax.all_to_all(outgoing, "tx", split_axis=0, concat_axis=0, tiled=True)
-    b_wide = padded_2(section_b, (("ty", 0), ("tx", 1)), RADIUS)
+    b_tall = padded_2(section_b, (("ty", 0),), RADIUS)
+    b_wide = padded_2(b_tall.T, (("tx", 0),), RADIUS).T
 
     wrow_pick = one_hot(window_corner[0, 0], WIN, b_wide.shape[0])
     wcol_pick = one_hot(window_corner[1, 0], WIN, b_wide.shape[1])

time: 75.6 us -> 75.2 us (level)
  waiting for transfers between devices: 11.6 us -> 8.89 us
  starting transfers between devices: 36.4 us -> 38.2 us
    ppermute x2, waiting for transfers between devices: 4.98 us -> 0.57 us  [padded_2(): lax.ppermute(head, axis, [((i + 1) % count, i) for i in range(ends)])]
    ppermute x2, waiting for transfers between devices: 0.03 us -> 1.82 us  [padded_2(): lax.ppermute(tail, axis, [(i, (i + 1) % count) for i in range(ends)])]
    ppermute x1, starting transfers between devices: 4.84 us -> 6 us  [rows_exchange(): above = lax.ppermute(tail, 'ty', [(i, i + 1) for i in range(count - 1)])]
    ppermute x2, starting transfers between devices: 8.22 us -> 7.27 us  [padded_2(): lax.ppermute(tail, axis, [(i, (i + 1) % count) for i in range(ends)])]
    ppermute x2, starting transfers between devices: 3.21 us -> 4.15 us  [padded_2(): lax.ppermute(head, axis, [((i + 1) % count, i) for i in range(ends)])]
    ppermute x1, starting transfers between devices: 2.35 us -> 3.12 us  [rows_exchange(): below = lax.ppermute(head, 'ty', [(i + 1, i) for i in range(count - 1)])]
  transfers between devices with their start and end apart: 8 -> 8, of which waited for: 4 -> 6; matrix products, arithmetic and copies ran while one was open for 7% -> 8% of each run, Pallas kernels for 0% -> 0%
where the time goes in v15:
time: 75.2 us; the launch traced here: 74.7 us
  starting transfers between devices  38.2 us (51%)
  Pallas kernels  10.6 us (14%)
  waiting for transfers between devices  8.89 us (12%)
  local copies, waits for them, and re-layouts  6.56 us (9%)
  matrix products  6.09 us (8%)
  other arithmetic  3.4 us (5%)
  between operations  0.98 us (1%)
    pallas_call x1, Pallas kernels, flows_of(): pl.pallas_call(flow_kernel, grid=(n // PER,), in_specs=[pl.BlockSpec((PER...  10.6 us
    all_to_all x1, starting transfers between devices, shards(): lax.all_to_all(back, 'tx', split_axis=0, concat_axis=0, tiled=True)  9.14 us
    all_to_all x1, starting transfers between devices, shards(): lax.all_to_all(outgoing, 'tx', split_axis=0, concat_axis=0, tiled=True)  8.55 us
    ppermute x2, starting transfers between devices, padded_2(): lax.ppermute(tail, axis, [(i, (i + 1) % count) for i in range(ends)])  7.27 us
    all_to_all x1, waiting for transfers between devices, shards(): lax.all_to_all(back, 'tx', split_axis=0, concat_axis=0, tiled=True)  6.38 us
    ppermute x1, starting transfers between devices, rows_exchange(): above = lax.ppermute(tail, 'ty', [(i, i + 1) for i in range(count - 1)])  6 us
    ppermute x2, starting transfers between devices, padded_2(): lax.ppermute(head, axis, [((i + 1) % count, i) for i in range(ends)])  4.15 us
    dot_general x1, matrix products, shards(): jnp.einsum('mrc,msc->mrs', by_row.astype(jnp.bfloat16), wcol_pick, prefer...  3.75 us
  transfers between devices with their start and end apart: 8, of which 6 were waited for; matrix products, arithmetic and copies ran while one was open for 8% of the time, Pallas kernels for 0%

profile of v15, /device:TPU:1, one launch (start us, length us, event | category | flops | bytes accessed | tf_op | source)
XLA Modules:
  0.0 74.7 jit_solution(14512181154681983476)
XLA Ops:
  0.7 0.7 slice_bitcast_fusion.5
  1.5 0.2 copy-done
  1.7 1.1 %fusion.11 = bf16[8,128,128]{2,1,0:T(8,128)(2,1)S(1)} fusion(s32[8,128]{1,0:T(8,128)S(1)} %get-tuple-element.43, s32[8,128]{1,0:T(8,128)S(1)} %get-tuple-element.44, bf16[512,512]{1,0:T(8,128)(2,1)S(1)} %copy-done), kind=kOutput, calls=%fused_computation.14 | convolution fusion | flops 672792576 | bytes 794624 | tf_op jit(solution)/shard_map/kra,kia->kri/dot_general | solution.py:163
  2.9 0.6 convolution_convert_fusion
  3.4 1.4 %copy.39 = bf16[32,128,128]{2,1,0:T(8,128)(2,1)} copy(bf16[32,128,128]{2,0,1:T(8,128)(2,1)S(1)} %convolution_convert_fusion) | data formatting | bytes 2097152 | tf_op jit(solution)/shard_map/convert_element_type | solution.py:168
  4.8 8.5 %all-to-all-start = ((bf16[32,128,128]{2,1,0:T(8,128)(2,1)}), bf16[32,128,128]{2,1,0:T(8,128)(2,1)S(1)}, u32[]{:S(2)}, u32[]{:S(2)}) async-start(bf16[32,128,128]{2,1,0:T(8,128)(2,1)} %copy.39), calls=%async_computation | async-start | bytes 2097152 | tf_op jit(solution)/shard_map/all_to_all | solution.py:207
  13.4 0.2 copy.42
  13.7 2.9 %collective-permute-start.1 = (bf16[32,512]{0,1:T(8,128)(2,1)S(1)}, bf16[32,512]{0,1:T(8,128)(2,1)S(1)}, u32[]{:S(2)}, u32[]{:S(2)}) collective-permute-start(bf16[32,512]{0,1:T(8,128)(2,1)S(1)} %get-tuple-element.20), channel_id=1, source_target_pairs={{16,0},{32,16},{48,32},{64,48},{80,64},{96,80},{112,96},{17,1},{33... | collective-permute-start | bytes 98312 | tf_op jit(solution)/shard_map/ppermute | solution.py:95
  16.6 3.1 %collective-permute-start = (bf16[32,512]{0,1:T(8,128)(2,1)S(1)}, bf16[32,512]{0,1:T(8,128)(2,1)S(1)}, u32[]{:S(2)}, u32[]{:S(2)}) collective-permute-start(bf16[32,512]{0,1:T(8,128)(2,1)S(1)} %get-tuple-element.19), channel_id=1, source_target_pairs={{0,16},{16,32},{32,48},{48,64},{64,80},{80,96},{96,112},{1,17},{17... | collective-permute-start | bytes 98312 | tf_op jit(solution)/shard_map/ppermute | solution.py:93
  20.2 0.5 collective-permute-done.1
  20.7 0.9 %collective-permute-done = bf16[32,512]{0,1:T(8,128)(2,1)S(1)} collective-permute-done((bf16[32,512]{0,1:T(8,128)(2,1)S(1)}, bf16[32,512]{0,1:T(8,128)(2,1)S(1)}, u32[]{:S(2)}, u32[]{:S(2)}) %collective-permute-start) | collective-permute-done | bytes 32800 | tf_op jit(solution)/shard_map/ppermute | solution.py:93
  21.6 0.4 maximum_bitcast_fusion.3
  22.0 1.3 %collective-permute-start.3 = (bf16[32,576]{1,0:T(8,128)(2,1)S(1)}, bf16[32,576]{1,0:T(8,128)(2,1)S(1)}, u32[]{:S(2)}, u32[]{:S(2)}) collective-permute-start(bf16[32,576]{1,0:T(8,128)(2,1)S(1)} %get-tuple-element.18), channel_id=1, source_target_pairs={{1,0},{2,1},{3,2},{4,3},{5,4},{6,5},{7,6},{8,7},{9,8},{10,9},{11,1... | collective-permute-start | bytes 110600 | tf_op jit(solution)/shard_map/ppermute | solution.py:95
  23.3 4.2 %collective-permute-start.2 = (bf16[32,576]{1,0:T(8,128)(2,1)S(1)}, bf16[32,576]{1,0:T(8,128)(2,1)S(1)}, u32[]{:S(2)}, u32[]{:S(2)}) collective-permute-start(bf16[32,576]{1,0:T(8,128)(2,1)S(1)} %get-tuple-element.17), channel_id=1, source_target_pairs={{0,1},{1,2},{2,3},{3,4},{4,5},{5,6},{6,7},{7,8},{8,9},{9,10},{10,1... | collective-permute-start | bytes 110600 | tf_op jit(solution)/shard_map/ppermute | solution.py:93
  27.7 0.9 %collective-permute-done.2 = bf16[32,576]{1,0:T(8,128)(2,1)S(1)} collective-permute-done((bf16[32,576]{1,0:T(8,128)(2,1)S(1)}, bf16[32,576]{1,0:T(8,128)(2,1)S(1)}, u32[]{:S(2)}, u32[]{:S(2)}) %collective-permute-start.2) | collective-permute-done | bytes 36896 | tf_op jit(solution)/shard_map/ppermute | solution.py:93
  28.6 3.7 %fusion.8.w_ref = bf16[8,192,192]{2,1,0:T(8,128)(2,1)} fusion(s32[8,192]{1,0:T(8,128)S(1)} %get-tuple-element.45, s32[8,192]{1,0:T(8,128)S(1)} %get-tuple-element.46, bf16[32,576]{1,0:T(8,128)(2,1)S(1)} %collective-permute-done.3, bf16[512,576]{1,0:T(8,128)(2,1)S(1)} %maximum_bitcast_fusion.3, bf16[32,576]{1,0:T(8,128)(2,1)S(1)} %collective-permute-done.2), kind=kOutput, calls=%fused_computation.13 | convolution fusion | flops 1363894272 | bytes 1265664 | tf_op jit(solution)/shard_map/mrc,msc->mrs/dot_general | solution.py:214
  32.3 0.7 fusion.12
  33.0 0.8 %copy.59.tf_ref = bf16[8,128,128]{2,1,0:T(8,128)(2,1)} copy(bf16[8,128,128]{2,0,1:T(8,128)(2,1)S(1)} %fusion.12) | data formatting | bytes 524288 | tf_op jit(solution)/shard_map/ms,sri->mri/dot_general | solution.py:217
  33.8 10.6 %shard_map.94 = f32[8,8,128]{2,1,0:T(8,128)} custom-call(bf16[8,128,128]{2,1,0:T(8,128)(2,1)} %copy.59.tf_ref, bf16[8,192,192]{2,1,0:T(8,128)(2,1)} %fusion.8.w_ref), custom_call_target="tpu_custom_call" | custom-call | tf_op jit(solution)/shard_map/pallas_call | solution.py:71
  44.3 0.8 %slice.194 = f32[8,2,1]{2,1,0:T(2,128)S(1)} slice(f32[8,8,128]{2,1,0:T(8,128)} %shard_map.94), slice={[0:8], [0:2], [0:1]} | slice | bytes 128 | tf_op jit(solution)/shard_map/slice | solution.py:82
  45.7 0.2 broadcast_in_dim.163
  46.0 0.2 broadcast_in_dim.160
  46.3 0.6 reshape.316
  46.9 9.1 %all-to-all-start.1 = ((f32[16,4,128]{2,1,0:T(4,128)}), f32[16,4,128]{2,1,0:T(4,128)S(1)}, u32[]{:S(2)}, u32[]{:S(2)}) async-start(f32[16,4,128]{2,1,0:T(4,128)} %reshape.316), calls=%async_computation.1 | async-start | bytes 65536 | tf_op jit(solution)/shard_map/all_to_all | solution.py:235
  56.1 6.4 %all-to-all-done.1 = f32[16,4,128]{2,1,0:T(4,128)S(1)} async-done(((f32[16,4,128]{2,1,0:T(4,128)}), f32[16,4,128]{2,1,0:T(4,128)S(1)}, u32[]{:S(2)}, u32[]{:S(2)}) %all-to-all-start.1) | async-done | bytes 32800 | tf_op jit(solution)/shard_map/all_to_all | solution.py:235
  62.8 0.2 select_n.76
  63.0 0.2 select_n.72
  63.3 3.1 %collective-permute-start.5 = (f32[4,3,38]{2,1,0:T(4,128)S(1)}, f32[4,3,38]{2,1,0:T(4,128)S(1)}, u32[]{:S(2)}, u32[]{:S(2)}) collective-permute-start(f32[4,3,38]{2,1,0:T(4,128)S(1)} %get-tuple-element.22), channel_id=1, source_target_pairs={{16,0},{32,16},{48,32},{64,48},{80,64},{96,80},{112,96},{17,1},{33... | collective-permute-start | bytes 5480 | tf_op jit(solution)/shard_map/ppermute | solution.py:195
  66.4 6.0 %collective-permute-start.4 = (f32[4,3,38]{2,1,0:T(4,128)S(1)}, f32[4,3,38]{2,1,0:T(4,128)S(1)}, u32[]{:S(2)}, u32[]{:S(2)}) collective-permute-start(f32[4,3,38]{2,1,0:T(4,128)S(1)} %get-tuple-element.21), channel_id=1, source_target_pairs={{0,16},{16,32},{32,48},{48,64},{64,80},{80,96},{96,112},{1,17},{17... | collective-permute-start | bytes 5480 | tf_op jit(solution)/shard_map/ppermute | solution.py:194
  72.4 0.7 select_reduce_fusion.1
  73.9 0.1 fusion.29
  74.0 0.7 fusion.45
  (60 shorter events, 2.7 us)
Async XLA Ops:
  0.6 1.1 %copy-start = (bf16[512,512]{1,0:T(8,128)(2,1)S(1)}, bf16[512,512]{1,0:T(8,128)(2,1)}, u32[]{:S(2)}) copy-start(bf16[512,512]{1,0:T(8,128)(2,1)} %param.7) | copy-start | bytes 1572868
  1.7 1.1 %copy-start.6 = (s32[1,8]{1,0:T(1,128)S(1)}, s32[1,8]{1,0:T(1,128)}, u32[]{:S(2)}) copy-start(s32[1,8]{1,0:T(1,128)} %param.10) | copy-start | bytes 100
  4.8 8.6 %copy-start.1 = (bf16[512,512]{1,0:T(8,128)(2,1)S(1)}, bf16[512,512]{1,0:T(8,128)(2,1)}, u32[]{:S(2)}) copy-start(bf16[512,512]{1,0:T(8,128)(2,1)} %param.8) | copy-start | bytes 1572868
  4.8 27.5 %all-to-all-start = ((bf16[32,128,128]{2,1,0:T(8,128)(2,1)}), bf16[32,128,128]{2,1,0:T(8,128)(2,1)S(1)}, u32[]{:S(2)}, u32[]{:S(2)}) async-start(bf16[32,128,128]{2,1,0:T(8,128)(2,1)} %copy.39), calls=%async_computation | async-start | bytes 2097152 | tf_op jit(solution)/shard_map/all_to_all | solution.py:207
  13.4 6.3 %copy-start.4 = (s32[2,1,8]{2,1,0:T(1,128)S(1)}, s32[2,1,8]{2,1,0:T(1,128)}, u32[]{:S(2)}) copy-start(s32[2,1,8]{2,1,0:T(1,128)} %param.11) | copy-start | bytes 196
  13.4 6.4 %copy-start.2 = (s32[32,32]{1,0:T(8,128)S(1)}, s32[32,32]{1,0:T(8,128)}, u32[]{:S(2)}) copy-start(s32[32,32]{1,0:T(8,128)} %param.13) | copy-start | bytes 12292
  13.4 6.6 %copy-start.5 = (s32[1,8]{1,0:T(1,128)S(1)}, s32[1,8]{1,0:T(1,128)}, u32[]{:S(2)}) copy-start(s32[1,8]{1,0:T(1,128)} %param.12) | copy-start | bytes 100
  13.7 7.0 %collective-permute-start.1 = (bf16[32,512]{0,1:T(8,128)(2,1)S(1)}, bf16[32,512]{0,1:T(8,128)(2,1)S(1)}, u32[]{:S(2)}, u32[]{:S(2)}) collective-permute-start(bf16[32,512]{0,1:T(8,128)(2,1)S(1)} %get-tuple-element.20), channel_id=1, source_target_pairs={{16,0},{32,16},{48,32},{64,48},{80,64},{96,80},{112,96},{17,1},{33... | collective-permute-start | bytes 98312 | tf_op jit(solution)/shard_map/ppermute | solution.py:95
  16.6 5.0 %collective-permute-start = (bf16[32,512]{0,1:T(8,128)(2,1)S(1)}, bf16[32,512]{0,1:T(8,128)(2,1)S(1)}, u32[]{:S(2)}, u32[]{:S(2)}) collective-permute-start(bf16[32,512]{0,1:T(8,128)(2,1)S(1)} %get-tuple-element.19), channel_id=1, source_target_pairs={{0,16},{16,32},{32,48},{48,64},{64,80},{80,96},{96,112},{1,17},{17... | collective-permute-start | bytes 98312 | tf_op jit(solution)/shard_map/ppermute | solution.py:93
  22.0 5.7 %collective-permute-start.3 = (bf16[32,576]{1,0:T(8,128)(2,1)S(1)}, bf16[32,576]{1,0:T(8,128)(2,1)S(1)}, u32[]{:S(2)}, u32[]{:S(2)}) collective-permute-start(bf16[32,576]{1,0:T(8,128)(2,1)S(1)} %get-tuple-element.18), channel_id=1, source_target_pairs={{1,0},{2,1},{3,2},{4,3},{5,4},{6,5},{7,6},{8,7},{9,8},{10,9},{11,1... | collective-permute-start | bytes 110600 | tf_op jit(solution)/shard_map/ppermute | solution.py:95
  23.3 5.3 %collective-permute-start.2 = (bf16[32,576]{1,0:T(8,128)(2,1)S(1)}, bf16[32,576]{1,0:T(8,128)(2,1)S(1)}, u32[]{:S(2)}, u32[]{:S(2)}) collective-permute-start(bf16[32,576]{1,0:T(8,128)(2,1)S(1)} %get-tuple-element.17), channel_id=1, source_target_pairs={{0,1},{1,2},{2,3},{3,4},{4,5},{5,6},{6,7},{7,8},{8,9},{9,10},{10,1... | collective-permute-start | bytes 110600 | tf_op jit(solution)/shard_map/ppermute | solution.py:93
  45.2 28.5 %copy-start.3 = (f32[2,8]{1,0:T(2,128)}, f32[2,8]{1,0:T(2,128)S(1)}, u32[]{:S(2)}) copy-start(f32[2,8]{1,0:T(2,128)S(1)} %bitcast_negate_fusion) | copy-start | bytes 196
  46.9 15.6 %all-to-all-start.1 = ((f32[16,4,128]{2,1,0:T(4,128)}), f32[16,4,128]{2,1,0:T(4,128)S(1)}, u32[]{:S(2)}, u32[]{:S(2)}) async-start(f32[16,4,128]{2,1,0:T(4,128)} %reshape.316), calls=%async_computation.1 | async-start | bytes 65536 | tf_op jit(solution)/shard_map/all_to_all | solution.py:235
  63.3 9.8 %collective-permute-start.5 = (f32[4,3,38]{2,1,0:T(4,128)S(1)}, f32[4,3,38]{2,1,0:T(4,128)S(1)}, u32[]{:S(2)}, u32[]{:S(2)}) collective-permute-start(f32[4,3,38]{2,1,0:T(4,128)S(1)} %get-tuple-element.22), channel_id=1, source_target_pairs={{16,0},{32,16},{48,32},{64,48},{80,64},{96,80},{112,96},{17,1},{33... | collective-permute-start | bytes 5480 | tf_op jit(solution)/shard_map/ppermute | solution.py:195
  66.4 6.8 %collective-permute-start.4 = (f32[4,3,38]{2,1,0:T(4,128)S(1)}, f32[4,3,38]{2,1,0:T(4,128)S(1)}, u32[]{:S(2)}, u32[]{:S(2)}) collective-permute-start(f32[4,3,38]{2,1,0:T(4,128)S(1)} %get-tuple-element.21), channel_id=1, source_target_pairs={{0,16},{16,32},{32,48},{48,64},{64,80},{80,96},{96,112},{1,17},{17... | collective-permute-start | bytes 5480 | tf_op jit(solution)/shard_map/ppermute | solution.py:194

commit v16 on v15

--- a/solution.py
+++ b/solution.py
@@ -224,8 +224,10 @@
     target = jnp.sum(jnp.where(attach[None], source_flow[:, :, None, None], 0.0), axis=1)
     fields = jnp.concatenate([target, count[None], mask[None]], axis=0)
     returned = jnp.sum(jnp.where(source_picker[None], flows[:, :, None], 0.0), axis=1)
+    f_above, f_below = rows_exchange(fields, w)
+    fields_ty = jnp.concatenate([f_above, fields, f_below], axis=1)
     lane = 128
-    sides = side_payload(fields[:, :, 0:w], fields[:, :, node_cols - w :])
+    sides = side_payload(fields_ty[:, :, 0:w], fields_ty[:, :, node_cols - w :])
     flows_out = returned.reshape(2, n_tx, CAP).transpose(1, 0, 2).reshape(n_tx, -1)
     side_len = sides.shape[1]
     chunk = -(-(side_len + flows_out.shape[1]) // lane) * lane
@@ -235,10 +237,8 @@
     came = lax.all_to_all(back, "tx", split_axis=0, concat_axis=0, tiled=True).reshape(n_tx, chunk)
     landed = came[:, side_len : side_len + 2 * CAP].reshape(n_tx, 2, CAP).transpose(1, 0, 2).reshape(2, -1)
     owner_flow = jnp.sum(jnp.where(owner_picker[None], landed[:, None, :], 0.0), axis=2)
-    f_left, f_right = side_arrivals(came[:, 0:side_len], (fields.shape[0], node_rows, w))
-    fields_tx = jnp.concatenate([f_left, fields, f_right], axis=2)
-    f_above, f_below = rows_exchange(fields_tx, w)
-    wide = jnp.concatenate([f_above, fields_tx, f_below], axis=1)
+    f_left, f_right = side_arrivals(came[:, 0:side_len], (fields.shape[0], fields_ty.shape[1], w))
+    wide = jnp.concatenate([f_left, fields_ty, f_right], axis=2)
 
     displace = jnp.zeros((2,) + wide.shape[1:], f32)
     for sweep in range(ITERS_R):

time: 75.2 us -> 75.2 us (level)
  the two profiles are of different devices: /device:TPU:1 before, /device:TPU:24 now
where the time goes in v16:
time: 75.2 us; the launch traced here: 74.7 us
  starting transfers between devices  32.4 us (43%)
  waiting for transfers between devices  14.6 us (19%)
  Pallas kernels  10.6 us (14%)
  local copies, waits for them, and re-layouts  6.64 us (9%)
  matrix products  6.09 us (8%)
  other arithmetic  3.4 us (5%)
  between operations  0.98 us (1%)
    pallas_call x1, Pallas kernels, flows_of(): pl.pallas_call(flow_kernel, grid=(n // PER,), in_specs=[pl.BlockSpec((PER...  10.6 us
    all_to_all x1, starting transfers between devices, shards(): lax.all_to_all(back, 'tx', split_axis=0, concat_axis=0, tiled=True)  9.89 us
    all_to_all x1, starting transfers between devices, shards(): lax.all_to_all(outgoing, 'tx', split_axis=0, concat_axis=0, tiled=True)  8.01 us
    all_to_all x1, waiting for transfers between devices, shards(): lax.all_to_all(back, 'tx', split_axis=0, concat_axis=0, tiled=True)  7.53 us
    ppermute x2, starting transfers between devices, padded_2(): lax.ppermute(tail, axis, [(i, (i + 1) % count) for i in range(ends)])  6.96 us
    ppermute x2, waiting for transfers between devices, padded_2(): lax.ppermute(tail, axis, [(i, (i + 1) % count) for i in range(ends)])  4.89 us
    dot_general x1, matrix products, shards(): jnp.einsum('mrc,msc->mrs', by_row.astype(jnp.bfloat16), wcol_pick, prefer...  3.75 us
    ppermute x2, starting transfers between devices, padded_2(): lax.ppermute(head, axis, [((i + 1) % count, i) for i in range(ends)])  3.21 us
  transfers between devices with their start and end apart: 8, of which 4 were waited for; matrix products, arithmetic and copies ran while one was open for 7% of the time, Pallas kernels for 0%

profile of v16, /device:TPU:24, one launch (start us, length us, event | category | flops | bytes accessed | tf_op | source)
XLA Modules:
  0.0 74.7 jit_solution(18377621049522923041)
XLA Ops:
  0.7 0.7 slice_bitcast_fusion.5
  1.5 0.2 copy-done
  1.7 1.1 %fusion.11 = bf16[8,128,128]{2,1,0:T(8,128)(2,1)S(1)} fusion(s32[8,128]{1,0:T(8,128)S(1)} %get-tuple-element.43, s32[8,128]{1,0:T(8,128)S(1)} %get-tuple-element.44, bf16[512,512]{1,0:T(8,128)(2,1)S(1)} %copy-done), kind=kOutput, calls=%fused_computation.14 | convolution fusion | flops 672792576 | bytes 794624 | tf_op jit(solution)/shard_map/kra,kia->kri/dot_general | solution.py:163
  2.9 0.6 convolution_convert_fusion
  3.4 1.4 %copy.39 = bf16[32,128,128]{2,1,0:T(8,128)(2,1)} copy(bf16[32,128,128]{2,0,1:T(8,128)(2,1)S(1)} %convolution_convert_fusion) | data formatting | bytes 2097152 | tf_op jit(solution)/shard_map/convert_element_type | solution.py:168
  4.8 8.0 %all-to-all-start = ((bf16[32,128,128]{2,1,0:T(8,128)(2,1)}), bf16[32,128,128]{2,1,0:T(8,128)(2,1)S(1)}, u32[]{:S(2)}, u32[]{:S(2)}) async-start(bf16[32,128,128]{2,1,0:T(8,128)(2,1)} %copy.39), calls=%async_computation | async-start | bytes 2097152 | tf_op jit(solution)/shard_map/all_to_all | solution.py:207
  12.9 0.2 copy.42
  13.2 1.9 %collective-permute-start.1 = (bf16[32,512]{0,1:T(8,128)(2,1)S(1)}, bf16[32,512]{0,1:T(8,128)(2,1)S(1)}, u32[]{:S(2)}, u32[]{:S(2)}) collective-permute-start(bf16[32,512]{0,1:T(8,128)(2,1)S(1)} %get-tuple-element.20), channel_id=1, source_target_pairs={{16,0},{32,16},{48,32},{64,48},{80,64},{96,80},{112,96},{17,1},{33... | collective-permute-start | bytes 98312 | tf_op jit(solution)/shard_map/ppermute | solution.py:95
  15.1 2.4 %collective-permute-start = (bf16[32,512]{0,1:T(8,128)(2,1)S(1)}, bf16[32,512]{0,1:T(8,128)(2,1)S(1)}, u32[]{:S(2)}, u32[]{:S(2)}) collective-permute-start(bf16[32,512]{0,1:T(8,128)(2,1)S(1)} %get-tuple-element.19), channel_id=1, source_target_pairs={{0,16},{16,32},{32,48},{48,64},{64,80},{80,96},{96,112},{1,17},{17... | collective-permute-start | bytes 98312 | tf_op jit(solution)/shard_map/ppermute | solution.py:93
  18.1 3.3 %collective-permute-done = bf16[32,512]{0,1:T(8,128)(2,1)S(1)} collective-permute-done((bf16[32,512]{0,1:T(8,128)(2,1)S(1)}, bf16[32,512]{0,1:T(8,128)(2,1)S(1)}, u32[]{:S(2)}, u32[]{:S(2)}) %collective-permute-start) | collective-permute-done | bytes 32800 | tf_op jit(solution)/shard_map/ppermute | solution.py:93
  21.4 0.4 maximum_bitcast_fusion.3
  21.8 1.3 %collective-permute-start.3 = (bf16[32,576]{1,0:T(8,128)(2,1)S(1)}, bf16[32,576]{1,0:T(8,128)(2,1)S(1)}, u32[]{:S(2)}, u32[]{:S(2)}) collective-permute-start(bf16[32,576]{1,0:T(8,128)(2,1)S(1)} %get-tuple-element.18), channel_id=1, source_target_pairs={{1,0},{2,1},{3,2},{4,3},{5,4},{6,5},{7,6},{8,7},{9,8},{10,9},{11,1... | collective-permute-start | bytes 110600 | tf_op jit(solution)/shard_map/ppermute | solution.py:95
  23.1 4.5 %collective-permute-start.2 = (bf16[32,576]{1,0:T(8,128)(2,1)S(1)}, bf16[32,576]{1,0:T(8,128)(2,1)S(1)}, u32[]{:S(2)}, u32[]{:S(2)}) collective-permute-start(bf16[32,576]{1,0:T(8,128)(2,1)S(1)} %get-tuple-element.17), channel_id=1, source_target_pairs={{0,1},{1,2},{2,3},{3,4},{4,5},{5,6},{6,7},{7,8},{8,9},{9,10},{10,1... | collective-permute-start | bytes 110600 | tf_op jit(solution)/shard_map/ppermute | solution.py:93
  27.8 1.6 %collective-permute-done.2 = bf16[32,576]{1,0:T(8,128)(2,1)S(1)} collective-permute-done((bf16[32,576]{1,0:T(8,128)(2,1)S(1)}, bf16[32,576]{1,0:T(8,128)(2,1)S(1)}, u32[]{:S(2)}, u32[]{:S(2)}) %collective-permute-start.2) | collective-permute-done | bytes 36896 | tf_op jit(solution)/shard_map/ppermute | solution.py:93
  29.3 3.7 %fusion.8.w_ref = bf16[8,192,192]{2,1,0:T(8,128)(2,1)} fusion(s32[8,192]{1,0:T(8,128)S(1)} %get-tuple-element.45, s32[8,192]{1,0:T(8,128)S(1)} %get-tuple-element.46, bf16[32,576]{1,0:T(8,128)(2,1)S(1)} %collective-permute-done.3, bf16[512,576]{1,0:T(8,128)(2,1)S(1)} %maximum_bitcast_fusion.3, bf16[32,576]{1,0:T(8,128)(2,1)S(1)} %collective-permute-done.2), kind=kOutput, calls=%fused_computation.13 | convolution fusion | flops 1363894272 | bytes 1265664 | tf_op jit(solution)/shard_map/mrc,msc->mrs/dot_general | solution.py:214
  33.1 0.7 fusion.12
  33.7 0.8 %copy.59.tf_ref = bf16[8,128,128]{2,1,0:T(8,128)(2,1)} copy(bf16[8,128,128]{2,0,1:T(8,128)(2,1)S(1)} %fusion.12) | data formatting | bytes 524288 | tf_op jit(solution)/shard_map/ms,sri->mri/dot_general | solution.py:217
  34.5 10.6 %shard_map.94 = f32[8,8,128]{2,1,0:T(8,128)} custom-call(bf16[8,128,128]{2,1,0:T(8,128)(2,1)} %copy.59.tf_ref, bf16[8,192,192]{2,1,0:T(8,128)(2,1)} %fusion.8.w_ref), custom_call_target="tpu_custom_call" | custom-call | tf_op jit(solution)/shard_map/pallas_call | solution.py:71
  45.1 0.8 %slice.194 = f32[8,2,1]{2,1,0:T(2,128)S(1)} slice(f32[8,8,128]{2,1,0:T(8,128)} %shard_map.94), slice={[0:8], [0:2], [0:1]} | slice | bytes 128 | tf_op jit(solution)/shard_map/slice | solution.py:82
  46.0 1.9 %collective-permute-start.5 = (f32[4,3,32]{2,1,0:T(4,128)S(1)}, f32[4,3,32]{2,1,0:T(4,128)S(1)}, u32[]{:S(2)}, u32[]{:S(2)}) collective-permute-start(f32[4,3,32]{2,1,0:T(4,128)S(1)} %get-tuple-element.28), channel_id=1, source_target_pairs={{16,0},{32,16},{48,32},{64,48},{80,64},{96,80},{112,96},{17,1},{33... | collective-permute-start | bytes 4616 | tf_op jit(solution)/shard_map/ppermute | solution.py:195
  48.0 2.4 %collective-permute-start.4 = (f32[4,3,32]{2,1,0:T(4,128)S(1)}, f32[4,3,32]{2,1,0:T(4,128)S(1)}, u32[]{:S(2)}, u32[]{:S(2)}) collective-permute-start(f32[4,3,32]{2,1,0:T(4,128)S(1)} %get-tuple-element.27), channel_id=1, source_target_pairs={{0,16},{16,32},{32,48},{48,64},{64,80},{80,96},{96,112},{1,17},{17... | collective-permute-start | bytes 4616 | tf_op jit(solution)/shard_map/ppermute | solution.py:194
  50.7 2.2 %collective-permute-done.4 = f32[4,3,32]{2,1,0:T(4,128)S(1)} collective-permute-done((f32[4,3,32]{2,1,0:T(4,128)S(1)}, f32[4,3,32]{2,1,0:T(4,128)S(1)}, u32[]{:S(2)}, u32[]{:S(2)}) %collective-permute-start.4) | collective-permute-done | bytes 1568 | tf_op jit(solution)/shard_map/ppermute | solution.py:194
  53.0 0.2 broadcast_in_dim.163
  53.3 0.2 broadcast_in_dim.160
  53.6 0.6 reshape.316
  54.3 9.9 %all-to-all-start.1 = ((f32[16,4,128]{2,1,0:T(4,128)}), f32[16,4,128]{2,1,0:T(4,128)S(1)}, u32[]{:S(2)}, u32[]{:S(2)}) async-start(f32[16,4,128]{2,1,0:T(4,128)} %reshape.316), calls=%async_computation.1 | async-start | bytes 65536 | tf_op jit(solution)/shard_map/all_to_all | solution.py:237
  64.2 7.5 %all-to-all-done.1 = f32[16,4,128]{2,1,0:T(4,128)S(1)} async-done(((f32[16,4,128]{2,1,0:T(4,128)}), f32[16,4,128]{2,1,0:T(4,128)S(1)}, u32[]{:S(2)}, u32[]{:S(2)}) %all-to-all-start.1) | async-done | bytes 32800 | tf_op jit(solution)/shard_map/all_to_all | solution.py:237
  71.9 0.2 select_n.76
  72.1 0.2 select_n.72
  73.1 0.7 select_reduce_fusion.1
  73.9 0.1 fusion.29
  74.0 0.7 fusion.45
  (59 shorter events, 2.6 us)
Async XLA Ops:
  0.6 1.1 %copy-start = (bf16[512,512]{1,0:T(8,128)(2,1)S(1)}, bf16[512,512]{1,0:T(8,128)(2,1)}, u32[]{:S(2)}) copy-start(bf16[512,512]{1,0:T(8,128)(2,1)} %param.7) | copy-start | bytes 1572868
  1.7 1.1 %copy-start.6 = (s32[1,8]{1,0:T(1,128)S(1)}, s32[1,8]{1,0:T(1,128)}, u32[]{:S(2)}) copy-start(s32[1,8]{1,0:T(1,128)} %param.10) | copy-start | bytes 100
  4.8 8.0 %copy-start.1 = (bf16[512,512]{1,0:T(8,128)(2,1)S(1)}, bf16[512,512]{1,0:T(8,128)(2,1)}, u32[]{:S(2)}) copy-start(bf16[512,512]{1,0:T(8,128)(2,1)} %param.8) | copy-start | bytes 1572868
  4.8 28.3 %all-to-all-start = ((bf16[32,128,128]{2,1,0:T(8,128)(2,1)}), bf16[32,128,128]{2,1,0:T(8,128)(2,1)S(1)}, u32[]{:S(2)}, u32[]{:S(2)}) async-start(bf16[32,128,128]{2,1,0:T(8,128)(2,1)} %copy.39), calls=%async_computation | async-start | bytes 2097152 | tf_op jit(solution)/shard_map/all_to_all | solution.py:207
  12.8 4.7 %copy-start.4 = (s32[2,1,8]{2,1,0:T(1,128)S(1)}, s32[2,1,8]{2,1,0:T(1,128)}, u32[]{:S(2)}) copy-start(s32[2,1,8]{2,1,0:T(1,128)} %param.11) | copy-start | bytes 196
  12.8 4.7 %copy-start.2 = (s32[32,32]{1,0:T(8,128)S(1)}, s32[32,32]{1,0:T(8,128)}, u32[]{:S(2)}) copy-start(s32[32,32]{1,0:T(8,128)} %param.13) | copy-start | bytes 12292
  12.9 5.0 %copy-start.5 = (s32[1,8]{1,0:T(1,128)S(1)}, s32[1,8]{1,0:T(1,128)}, u32[]{:S(2)}) copy-start(s32[1,8]{1,0:T(1,128)} %param.12) | copy-start | bytes 100
  13.2 4.9 %collective-permute-start.1 = (bf16[32,512]{0,1:T(8,128)(2,1)S(1)}, bf16[32,512]{0,1:T(8,128)(2,1)S(1)}, u32[]{:S(2)}, u32[]{:S(2)}) collective-permute-start(bf16[32,512]{0,1:T(8,128)(2,1)S(1)} %get-tuple-element.20), channel_id=1, source_target_pairs={{16,0},{32,16},{48,32},{64,48},{80,64},{96,80},{112,96},{17,1},{33... | collective-permute-start | bytes 98312 | tf_op jit(solution)/shard_map/ppermute | solution.py:95
  15.1 6.3 %collective-permute-start = (bf16[32,512]{0,1:T(8,128)(2,1)S(1)}, bf16[32,512]{0,1:T(8,128)(2,1)S(1)}, u32[]{:S(2)}, u32[]{:S(2)}) collective-permute-start(bf16[32,512]{0,1:T(8,128)(2,1)S(1)} %get-tuple-element.19), channel_id=1, source_target_pairs={{0,16},{16,32},{32,48},{48,64},{64,80},{80,96},{96,112},{1,17},{17... | collective-permute-start | bytes 98312 | tf_op jit(solution)/shard_map/ppermute | solution.py:93
  21.8 6.0 %collective-permute-start.3 = (bf16[32,576]{1,0:T(8,128)(2,1)S(1)}, bf16[32,576]{1,0:T(8,128)(2,1)S(1)}, u32[]{:S(2)}, u32[]{:S(2)}) collective-permute-start(bf16[32,576]{1,0:T(8,128)(2,1)S(1)} %get-tuple-element.18), channel_id=1, source_target_pairs={{1,0},{2,1},{3,2},{4,3},{5,4},{6,5},{7,6},{8,7},{9,8},{10,9},{11,1... | collective-permute-start | bytes 110600 | tf_op jit(solution)/shard_map/ppermute | solution.py:95
  23.1 6.2 %collective-permute-start.2 = (bf16[32,576]{1,0:T(8,128)(2,1)S(1)}, bf16[32,576]{1,0:T(8,128)(2,1)S(1)}, u32[]{:S(2)}, u32[]{:S(2)}) collective-permute-start(bf16[32,576]{1,0:T(8,128)(2,1)S(1)} %get-tuple-element.17), channel_id=1, source_target_pairs={{0,1},{1,2},{2,3},{3,4},{4,5},{5,6},{6,7},{7,8},{8,9},{9,10},{10,1... | collective-permute-start | bytes 110600 | tf_op jit(solution)/shard_map/ppermute | solution.py:93
  45.9 27.0 %copy-start.3 = (f32[2,8]{1,0:T(2,128)}, f32[2,8]{1,0:T(2,128)S(1)}, u32[]{:S(2)}) copy-start(f32[2,8]{1,0:T(2,128)S(1)} %bitcast_negate_fusion) | copy-start | bytes 196
  46.0 4.7 %collective-permute-start.5 = (f32[4,3,32]{2,1,0:T(4,128)S(1)}, f32[4,3,32]{2,1,0:T(4,128)S(1)}, u32[]{:S(2)}, u32[]{:S(2)}) collective-permute-start(f32[4,3,32]{2,1,0:T(4,128)S(1)} %get-tuple-element.28), channel_id=1, source_target_pairs={{16,0},{32,16},{48,32},{64,48},{80,64},{96,80},{112,96},{17,1},{33... | collective-permute-start | bytes 4616 | tf_op jit(solution)/shard_map/ppermute | solution.py:195
  48.0 5.0 %collective-permute-start.4 = (f32[4,3,32]{2,1,0:T(4,128)S(1)}, f32[4,3,32]{2,1,0:T(4,128)S(1)}, u32[]{:S(2)}, u32[]{:S(2)}) collective-permute-start(f32[4,3,32]{2,1,0:T(4,128)S(1)} %get-tuple-element.27), channel_id=1, source_target_pairs={{0,16},{16,32},{32,48},{48,64},{64,80},{80,96},{96,112},{1,17},{17... | collective-permute-start | bytes 4616 | tf_op jit(solution)/shard_map/ppermute | solution.py:194
  54.3 17.5 %all-to-all-start.1 = ((f32[16,4,128]{2,1,0:T(4,128)}), f32[16,4,128]{2,1,0:T(4,128)S(1)}, u32[]{:S(2)}, u32[]{:S(2)}) async-start(f32[16,4,128]{2,1,0:T(4,128)} %reshape.316), calls=%async_computation.1 | async-start | bytes 65536 | tf_op jit(solution)/shard_map/all_to_all | solution.py:237

commit v17 on v15

--- a/solution.py
+++ b/solution.py
@@ -210,9 +210,9 @@
 
     wrow_pick = one_hot(window_corner[0, 0], WIN, b_wide.shape[0])
     wcol_pick = one_hot(window_corner[1, 0], WIN, b_wide.shape[1])
-    by_row = jnp.einsum("mra,ac->mrc", wrow_pick, b_wide, preferred_element_type=f32)
+    by_col = jnp.einsum("ac,msc->mas", b_wide, wcol_pick, preferred_element_type=f32)
     windows = jnp.einsum(
-        "mrc,msc->mrs", by_row.astype(jnp.bfloat16), wcol_pick, preferred_element_type=f32
+        "mra,mas->mrs", wrow_pick, by_col.astype(jnp.bfloat16), preferred_element_type=f32
     ).astype(jnp.bfloat16)
     matched = jnp.einsum(
         "ms,sri->mri", source_picker.astype(jnp.bfloat16), arrived, preferred_element_type=f32

time: 75.2 us -> 75.3 us (level)
  no operation moved by 1% of the time
where the time goes in v17:
time: 75.3 us; the launch traced here: 74.8 us
  starting transfers between devices  38.2 us (51%)
  Pallas kernels  10.6 us (14%)
  waiting for transfers between devices  8.89 us (12%)
  local copies, waits for them, and re-layouts  6.56 us (9%)
  matrix products  6.15 us (8%)
  other arithmetic  3.4 us (5%)
  between operations  0.98 us (1%)
    pallas_call x1, Pallas kernels, flows_of(): pl.pallas_call(flow_kernel, grid=(n // PER,), in_specs=[pl.BlockSpec((PER...  10.6 us
    all_to_all x1, starting transfers between devices, shards(): lax.all_to_all(back, 'tx', split_axis=0, concat_axis=0, tiled=True)  9.13 us
    all_to_all x1, starting transfers between devices, shards(): lax.all_to_all(outgoing, 'tx', split_axis=0, concat_axis=0, tiled=True)  8.55 us
    ppermute x2, starting transfers between devices, padded_2(): lax.ppermute(tail, axis, [(i, (i + 1) % count) for i in range(ends)])  7.27 us
    all_to_all x1, waiting for transfers between devices, shards(): lax.all_to_all(back, 'tx', split_axis=0, concat_axis=0, tiled=True)  6.38 us
    ppermute x1, starting transfers between devices, rows_exchange(): above = lax.ppermute(tail, 'ty', [(i, i + 1) for i in range(count - 1)])  6 us
    ppermute x2, starting transfers between devices, padded_2(): lax.ppermute(head, axis, [((i + 1) % count, i) for i in range(ends)])  4.15 us
    dot_general x1, matrix products, shards(): jnp.einsum('mra,mas->mrs', wrow_pick, by_col.astype(jnp.bfloat16), prefer...  3.81 us
  transfers between devices with their start and end apart: 8, of which 6 were waited for; matrix products, arithmetic and copies ran while one was open for 8% of the time, Pallas kernels for 0%

profile of v17, /device:TPU:1, one launch (start us, length us, event | category | flops | bytes accessed | tf_op | source)
XLA Modules:
  0.0 74.8 jit_solution(9845940817268405217)
XLA Ops:
  0.7 0.7 slice_bitcast_fusion.5
  1.5 0.2 copy-done
  1.7 1.1 %fusion.11 = bf16[8,128,128]{2,1,0:T(8,128)(2,1)S(1)} fusion(s32[8,128]{1,0:T(8,128)S(1)} %get-tuple-element.43, s32[8,128]{1,0:T(8,128)S(1)} %get-tuple-element.44, bf16[512,512]{1,0:T(8,128)(2,1)S(1)} %copy-done), kind=kOutput, calls=%fused_computation.14 | convolution fusion | flops 672792576 | bytes 794624 | tf_op jit(solution)/shard_map/kra,kia->kri/dot_general | solution.py:163
  2.9 0.6 convolution_convert_fusion
  3.4 1.4 %copy.39 = bf16[32,128,128]{2,1,0:T(8,128)(2,1)} copy(bf16[32,128,128]{2,0,1:T(8,128)(2,1)S(1)} %convolution_convert_fusion) | data formatting | bytes 2097152 | tf_op jit(solution)/shard_map/convert_element_type | solution.py:168
  4.8 8.5 %all-to-all-start = ((bf16[32,128,128]{2,1,0:T(8,128)(2,1)}), bf16[32,128,128]{2,1,0:T(8,128)(2,1)S(1)}, u32[]{:S(2)}, u32[]{:S(2)}) async-start(bf16[32,128,128]{2,1,0:T(8,128)(2,1)} %copy.39), calls=%async_computation | async-start | bytes 2097152 | tf_op jit(solution)/shard_map/all_to_all | solution.py:207
  13.4 0.2 copy.42
  13.7 2.9 %collective-permute-start.1 = (bf16[32,512]{0,1:T(8,128)(2,1)S(1)}, bf16[32,512]{0,1:T(8,128)(2,1)S(1)}, u32[]{:S(2)}, u32[]{:S(2)}) collective-permute-start(bf16[32,512]{0,1:T(8,128)(2,1)S(1)} %get-tuple-element.20), channel_id=1, source_target_pairs={{16,0},{32,16},{48,32},{64,48},{80,64},{96,80},{112,96},{17,1},{33... | collective-permute-start | bytes 98312 | tf_op jit(solution)/shard_map/ppermute | solution.py:95
  16.6 3.1 %collective-permute-start = (bf16[32,512]{0,1:T(8,128)(2,1)S(1)}, bf16[32,512]{0,1:T(8,128)(2,1)S(1)}, u32[]{:S(2)}, u32[]{:S(2)}) collective-permute-start(bf16[32,512]{0,1:T(8,128)(2,1)S(1)} %get-tuple-element.19), channel_id=1, source_target_pairs={{0,16},{16,32},{32,48},{48,64},{64,80},{80,96},{96,112},{1,17},{17... | collective-permute-start | bytes 98312 | tf_op jit(solution)/shard_map/ppermute | solution.py:93
  20.2 0.5 collective-permute-done.1
  20.7 0.9 %collective-permute-done = bf16[32,512]{0,1:T(8,128)(2,1)S(1)} collective-permute-done((bf16[32,512]{0,1:T(8,128)(2,1)S(1)}, bf16[32,512]{0,1:T(8,128)(2,1)S(1)}, u32[]{:S(2)}, u32[]{:S(2)}) %collective-permute-start) | collective-permute-done | bytes 32800 | tf_op jit(solution)/shard_map/ppermute | solution.py:93
  21.6 0.4 maximum_bitcast_fusion.3
  22.0 1.3 %collective-permute-start.3 = (bf16[32,576]{1,0:T(8,128)(2,1)S(1)}, bf16[32,576]{1,0:T(8,128)(2,1)S(1)}, u32[]{:S(2)}, u32[]{:S(2)}) collective-permute-start(bf16[32,576]{1,0:T(8,128)(2,1)S(1)} %get-tuple-element.18), channel_id=1, source_target_pairs={{1,0},{2,1},{3,2},{4,3},{5,4},{6,5},{7,6},{8,7},{9,8},{10,9},{11,1... | collective-permute-start | bytes 110600 | tf_op jit(solution)/shard_map/ppermute | solution.py:95
  23.3 4.2 %collective-permute-start.2 = (bf16[32,576]{1,0:T(8,128)(2,1)S(1)}, bf16[32,576]{1,0:T(8,128)(2,1)S(1)}, u32[]{:S(2)}, u32[]{:S(2)}) collective-permute-start(bf16[32,576]{1,0:T(8,128)(2,1)S(1)} %get-tuple-element.17), channel_id=1, source_target_pairs={{0,1},{1,2},{2,3},{3,4},{4,5},{5,6},{6,7},{7,8},{8,9},{9,10},{10,1... | collective-permute-start | bytes 110600 | tf_op jit(solution)/shard_map/ppermute | solution.py:93
  27.7 0.9 %collective-permute-done.2 = bf16[32,576]{1,0:T(8,128)(2,1)S(1)} collective-permute-done((bf16[32,576]{1,0:T(8,128)(2,1)S(1)}, bf16[32,576]{1,0:T(8,128)(2,1)S(1)}, u32[]{:S(2)}, u32[]{:S(2)}) %collective-permute-start.2) | collective-permute-done | bytes 36896 | tf_op jit(solution)/shard_map/ppermute | solution.py:93
  28.6 3.8 %fusion.8.w_ref = bf16[8,192,192]{2,1,0:T(8,128)(2,1)} fusion(s32[8,192]{1,0:T(8,128)S(1)} %get-tuple-element.45, s32[8,192]{1,0:T(8,128)S(1)} %get-tuple-element.46, bf16[32,576]{1,0:T(8,128)(2,1)S(1)} %collective-permute-done.3, bf16[512,576]{1,0:T(8,128)(2,1)S(1)} %maximum_bitcast_fusion.3, bf16[32,576]{1,0:T(8,128)(2,1)S(1)} %collective-permute-done.2), kind=kOutput, calls=%fused_computation.13 | convolution fusion | flops 1363894272 | bytes 1265664 | tf_op jit(solution)/shard_map/mra,mas->mrs/dot_general | solution.py:214
  32.4 0.7 fusion.12
  33.1 0.8 %copy.59.tf_ref = bf16[8,128,128]{2,1,0:T(8,128)(2,1)} copy(bf16[8,128,128]{2,0,1:T(8,128)(2,1)S(1)} %fusion.12) | data formatting | bytes 524288 | tf_op jit(solution)/shard_map/ms,sri->mri/dot_general | solution.py:217
  33.8 10.6 %shard_map.94 = f32[8,8,128]{2,1,0:T(8,128)} custom-call(bf16[8,128,128]{2,1,0:T(8,128)(2,1)} %copy.59.tf_ref, bf16[8,192,192]{2,1,0:T(8,128)(2,1)} %fusion.8.w_ref), custom_call_target="tpu_custom_call" | custom-call | tf_op jit(solution)/shard_map/pallas_call | solution.py:71
  44.4 0.8 %slice.194 = f32[8,2,1]{2,1,0:T(2,128)S(1)} slice(f32[8,8,128]{2,1,0:T(8,128)} %shard_map.94), slice={[0:8], [0:2], [0:1]} | slice | bytes 128 | tf_op jit(solution)/shard_map/slice | solution.py:82
  45.8 0.2 broadcast_in_dim.163
  46.0 0.2 broadcast_in_dim.160
  46.3 0.6 reshape.316
  47.0 9.1 %all-to-all-start.1 = ((f32[16,4,128]{2,1,0:T(4,128)}), f32[16,4,128]{2,1,0:T(4,128)S(1)}, u32[]{:S(2)}, u32[]{:S(2)}) async-start(f32[16,4,128]{2,1,0:T(4,128)} %reshape.316), calls=%async_computation.1 | async-start | bytes 65536 | tf_op jit(solution)/shard_map/all_to_all | solution.py:235
  56.2 6.4 %all-to-all-done.1 = f32[16,4,128]{2,1,0:T(4,128)S(1)} async-done(((f32[16,4,128]{2,1,0:T(4,128)}), f32[16,4,128]{2,1,0:T(4,128)S(1)}, u32[]{:S(2)}, u32[]{:S(2)}) %all-to-all-start.1) | async-done | bytes 32800 | tf_op jit(solution)/shard_map/all_to_all | solution.py:235
  62.9 0.2 select_n.76
  63.1 0.2 select_n.72
  63.4 3.1 %collective-permute-start.5 = (f32[4,3,38]{2,1,0:T(4,128)S(1)}, f32[4,3,38]{2,1,0:T(4,128)S(1)}, u32[]{:S(2)}, u32[]{:S(2)}) collective-permute-start(f32[4,3,38]{2,1,0:T(4,128)S(1)} %get-tuple-element.22), channel_id=1, source_target_pairs={{16,0},{32,16},{48,32},{64,48},{80,64},{96,80},{112,96},{17,1},{33... | collective-permute-start | bytes 5480 | tf_op jit(solution)/shard_map/ppermute | solution.py:195
  66.5 6.0 %collective-permute-start.4 = (f32[4,3,38]{2,1,0:T(4,128)S(1)}, f32[4,3,38]{2,1,0:T(4,128)S(1)}, u32[]{:S(2)}, u32[]{:S(2)}) collective-permute-start(f32[4,3,38]{2,1,0:T(4,128)S(1)} %get-tuple-element.21), channel_id=1, source_target_pairs={{0,16},{16,32},{32,48},{48,64},{64,80},{80,96},{96,112},{1,17},{17... | collective-permute-start | bytes 5480 | tf_op jit(solution)/shard_map/ppermute | solution.py:194
  72.5 0.7 select_reduce_fusion.1
  73.9 0.1 fusion.29
  74.1 0.7 fusion.45
  (60 shorter events, 2.7 us)
Async XLA Ops:
  0.6 1.1 %copy-start = (bf16[512,512]{1,0:T(8,128)(2,1)S(1)}, bf16[512,512]{1,0:T(8,128)(2,1)}, u32[]{:S(2)}) copy-start(bf16[512,512]{1,0:T(8,128)(2,1)} %param.7) | copy-start | bytes 1572868
  1.7 1.1 %copy-start.6 = (s32[1,8]{1,0:T(1,128)S(1)}, s32[1,8]{1,0:T(1,128)}, u32[]{:S(2)}) copy-start(s32[1,8]{1,0:T(1,128)} %param.10) | copy-start | bytes 100
  4.8 8.6 %copy-start.1 = (bf16[512,512]{1,0:T(8,128)(2,1)S(1)}, bf16[512,512]{1,0:T(8,128)(2,1)}, u32[]{:S(2)}) copy-start(bf16[512,512]{1,0:T(8,128)(2,1)} %param.8) | copy-start | bytes 1572868
  4.8 27.6 %all-to-all-start = ((bf16[32,128,128]{2,1,0:T(8,128)(2,1)}), bf16[32,128,128]{2,1,0:T(8,128)(2,1)S(1)}, u32[]{:S(2)}, u32[]{:S(2)}) async-start(bf16[32,128,128]{2,1,0:T(8,128)(2,1)} %copy.39), calls=%async_computation | async-start | bytes 2097152 | tf_op jit(solution)/shard_map/all_to_all | solution.py:207
  13.4 6.3 %copy-start.4 = (s32[2,1,8]{2,1,0:T(1,128)S(1)}, s32[2,1,8]{2,1,0:T(1,128)}, u32[]{:S(2)}) copy-start(s32[2,1,8]{2,1,0:T(1,128)} %param.11) | copy-start | bytes 196
  13.4 6.4 %copy-start.2 = (s32[32,32]{1,0:T(8,128)S(1)}, s32[32,32]{1,0:T(8,128)}, u32[]{:S(2)}) copy-start(s32[32,32]{1,0:T(8,128)} %param.13) | copy-start | bytes 12292
  13.4 6.6 %copy-start.5 = (s32[1,8]{1,0:T(1,128)S(1)}, s32[1,8]{1,0:T(1,128)}, u32[]{:S(2)}) copy-start(s32[1,8]{1,0:T(1,128)} %param.12) | copy-start | bytes 100
  13.7 7.0 %collective-permute-start.1 = (bf16[32,512]{0,1:T(8,128)(2,1)S(1)}, bf16[32,512]{0,1:T(8,128)(2,1)S(1)}, u32[]{:S(2)}, u32[]{:S(2)}) collective-permute-start(bf16[32,512]{0,1:T(8,128)(2,1)S(1)} %get-tuple-element.20), channel_id=1, source_target_pairs={{16,0},{32,16},{48,32},{64,48},{80,64},{96,80},{112,96},{17,1},{33... | collective-permute-start | bytes 98312 | tf_op jit(solution)/shard_map/ppermute | solution.py:95
  16.6 5.0 %collective-permute-start = (bf16[32,512]{0,1:T(8,128)(2,1)S(1)}, bf16[32,512]{0,1:T(8,128)(2,1)S(1)}, u32[]{:S(2)}, u32[]{:S(2)}) collective-permute-start(bf16[32,512]{0,1:T(8,128)(2,1)S(1)} %get-tuple-element.19), channel_id=1, source_target_pairs={{0,16},{16,32},{32,48},{48,64},{64,80},{80,96},{96,112},{1,17},{17... | collective-permute-start | bytes 98312 | tf_op jit(solution)/shard_map/ppermute | solution.py:93
  22.0 5.7 %collective-permute-start.3 = (bf16[32,576]{1,0:T(8,128)(2,1)S(1)}, bf16[32,576]{1,0:T(8,128)(2,1)S(1)}, u32[]{:S(2)}, u32[]{:S(2)}) collective-permute-start(bf16[32,576]{1,0:T(8,128)(2,1)S(1)} %get-tuple-element.18), channel_id=1, source_target_pairs={{1,0},{2,1},{3,2},{4,3},{5,4},{6,5},{7,6},{8,7},{9,8},{10,9},{11,1... | collective-permute-start | bytes 110600 | tf_op jit(solution)/shard_map/ppermute | solution.py:95
  23.3 5.3 %collective-permute-start.2 = (bf16[32,576]{1,0:T(8,128)(2,1)S(1)}, bf16[32,576]{1,0:T(8,128)(2,1)S(1)}, u32[]{:S(2)}, u32[]{:S(2)}) collective-permute-start(bf16[32,576]{1,0:T(8,128)(2,1)S(1)} %get-tuple-element.17), channel_id=1, source_target_pairs={{0,1},{1,2},{2,3},{3,4},{4,5},{5,6},{6,7},{7,8},{8,9},{9,10},{10,1... | collective-permute-start | bytes 110600 | tf_op jit(solution)/shard_map/ppermute | solution.py:93
  45.3 28.5 %copy-start.3 = (f32[2,8]{1,0:T(2,128)}, f32[2,8]{1,0:T(2,128)S(1)}, u32[]{:S(2)}) copy-start(f32[2,8]{1,0:T(2,128)S(1)} %bitcast_negate_fusion) | copy-start | bytes 196
  47.0 15.6 %all-to-all-start.1 = ((f32[16,4,128]{2,1,0:T(4,128)}), f32[16,4,128]{2,1,0:T(4,128)S(1)}, u32[]{:S(2)}, u32[]{:S(2)}) async-start(f32[16,4,128]{2,1,0:T(4,128)} %reshape.316), calls=%async_computation.1 | async-start | bytes 65536 | tf_op jit(solution)/shard_map/all_to_all | solution.py:235
  63.4 9.8 %collective-permute-start.5 = (f32[4,3,38]{2,1,0:T(4,128)S(1)}, f32[4,3,38]{2,1,0:T(4,128)S(1)}, u32[]{:S(2)}, u32[]{:S(2)}) collective-permute-start(f32[4,3,38]{2,1,0:T(4,128)S(1)} %get-tuple-element.22), channel_id=1, source_target_pairs={{16,0},{32,16},{48,32},{64,48},{80,64},{96,80},{112,96},{17,1},{33... | collective-permute-start | bytes 5480 | tf_op jit(solution)/shard_map/ppermute | solution.py:195
  66.5 6.8 %collective-permute-start.4 = (f32[4,3,38]{2,1,0:T(4,128)S(1)}, f32[4,3,38]{2,1,0:T(4,128)S(1)}, u32[]{:S(2)}, u32[]{:S(2)}) collective-permute-start(f32[4,3,38]{2,1,0:T(4,128)S(1)} %get-tuple-element.21), channel_id=1, source_target_pairs={{0,16},{16,32},{32,48},{48,64},{64,80},{80,96},{96,112},{1,17},{17... | collective-permute-start | bytes 5480 | tf_op jit(solution)/shard_map/ppermute | solution.py:194

commit v18 on v15

--- a/solution.py
+++ b/solution.py
@@ -157,14 +157,16 @@
     source_picker = window_slot[0][:, None] == slot_ids[None, :]
     f32 = jnp.float32
 
-    col_pick = one_hot(template_corner[1, 0], PATCH, section_a.shape[1], flip=True)
-    row_pick = one_hot(template_corner[0, 0], PATCH, section_a.shape[0])
-    by_col = jnp.einsum("krc,ac->kra", col_pick, section_a, preferred_element_type=f32)
-    tflipped = jnp.einsum(
-        "kra,kia->kri", by_col.astype(jnp.bfloat16), row_pick, preferred_element_type=f32
-    ).astype(jnp.bfloat16)
+    slot_has = jnp.any(owner_picker, axis=0)
+    no_col = section_a.shape[1] + PATCH
+    slot_top = jnp.sum(jnp.where(owner_picker, template_corner[0, 0][:, None], 0), axis=0)
+    slot_left = jnp.sum(jnp.where(owner_picker, template_corner[1, 0][:, None], 0), axis=0)
+    slot_left = jnp.where(slot_has, slot_left, no_col)
+    col_pick = one_hot(slot_left, PATCH, section_a.shape[1], flip=True)
+    row_pick = one_hot(slot_top, PATCH, section_a.shape[0])
+    by_col = jnp.einsum("src,ac->sra", col_pick, section_a, preferred_element_type=f32)
     outgoing = jnp.einsum(
-        "ks,kri->sri", owner_picker.astype(jnp.bfloat16), tflipped, preferred_element_type=f32
+        "sra,sia->sri", by_col.astype(jnp.bfloat16), row_pick, preferred_element_type=f32
     ).astype(jnp.bfloat16)
 
     n_tx = lax.axis_size("tx")

time: 75.2 us -> 78.4 us (1.043)
  matrix products: 6.09 us -> 9.41 us
  local copies, waits for them, and re-layouts: 6.56 us -> 4.92 us
  other arithmetic: 3.4 us -> 4.81 us
    dot_general x2 -> x1, matrix products: 1.68 us -> 5.01 us  [shards(): jnp.einsum('sra,sia->sri', by_col.astype(jnp.bfloat16), row_pick, preferr...]
    convert_element_type x1 -> x0, local copies, waits for them, and re-layouts: 1.39 us -> none  [shards(): outgoing = jnp.einsum('ks,kri->sri', owner_picker.astype(jnp.bfloat16), t...]
  transfers between devices with their start and end apart: 8 -> 8, of which waited for: 6 -> 6; matrix products, arithmetic and copies ran while one was open for 8% -> 7% of each run, Pallas kernels for 0% -> 0%
where the time goes in v18:
time: 78.4 us; the launch traced here: 77.9 us
  starting transfers between devices  38.2 us (49%)
  Pallas kernels  10.6 us (14%)
  matrix products  9.41 us (12%)
  waiting for transfers between devices  8.95 us (11%)
  local copies, waits for them, and re-layouts  4.92 us (6%)
  other arithmetic  4.81 us (6%)
  between operations  0.98 us (1%)
    pallas_call x1, Pallas kernels, flows_of(): pl.pallas_call(flow_kernel, grid=(n // PER,), in_specs=[pl.BlockSpec((PER...  10.6 us
    all_to_all x1, starting transfers between devices, shards(): lax.all_to_all(back, 'tx', split_axis=0, concat_axis=0, tiled=True)  9.13 us
    all_to_all x1, starting transfers between devices, shards(): lax.all_to_all(outgoing, 'tx', split_axis=0, concat_axis=0, tiled=True)  8.55 us
    ppermute x2, starting transfers between devices, padded_2(): lax.ppermute(tail, axis, [(i, (i + 1) % count) for i in range(ends)])  7.28 us
    all_to_all x1, waiting for transfers between devices, shards(): lax.all_to_all(back, 'tx', split_axis=0, concat_axis=0, tiled=True)  6.43 us
    ppermute x1, starting transfers between devices, rows_exchange(): above = lax.ppermute(tail, 'ty', [(i, i + 1) for i in range(count - 1)])  6 us
    dot_general x1, matrix products, shards(): jnp.einsum('sra,sia->sri', by_col.astype(jnp.bfloat16), row_pick, preferr...  5.01 us
    ppermute x2, starting transfers between devices, padded_2(): lax.ppermute(head, axis, [((i + 1) % count, i) for i in range(ends)])  4.16 us
  transfers between devices with their start and end apart: 8, of which 6 were waited for; matrix products, arithmetic and copies ran while one was open for 7% of the time, Pallas kernels for 0%

profile of v18, /device:TPU:1, one launch (start us, length us, event | category | flops | bytes accessed | tf_op | source)
XLA Modules:
  0.0 77.9 jit_solution(15287685269849438292)
XLA Ops:
  0.7 0.7 slice_bitcast_fusion.4
  1.4 0.7 iota_compare_fusion.27
  2.1 0.7 select_reduce_fusion.4
  3.0 5.0 %fusion.10 = bf16[32,128,128]{2,1,0:T(8,128)(2,1)} fusion(s32[32,128]{1,0:T(8,128)S(1)} %get-tuple-element.47, s32[32,128]{1,0:T(8,128)S(1)} %get-tuple-element.48, bf16[512,512]{1,0:T(8,128)(2,1)S(1)} %copy-done), kind=kOutput, calls=%fused_computation.14 | convolution fusion | flops 2691170304 | bytes 1605632 | tf_op jit(solution)/shard_map/sra,sia->sri/dot_general | solution.py:168
  8.0 8.5 %all-to-all-start = ((bf16[32,128,128]{2,1,0:T(8,128)(2,1)}), bf16[32,128,128]{2,1,0:T(8,128)(2,1)S(1)}, u32[]{:S(2)}, u32[]{:S(2)}) async-start(bf16[32,128,128]{2,1,0:T(8,128)(2,1)} %fusion.10), calls=%async_computation | async-start | bytes 2097152 | tf_op jit(solution)/shard_map/all_to_all | solution.py:209
  16.6 0.2 copy.38
  16.9 2.9 %collective-permute-start.1 = (bf16[32,512]{0,1:T(8,128)(2,1)S(1)}, bf16[32,512]{0,1:T(8,128)(2,1)S(1)}, u32[]{:S(2)}, u32[]{:S(2)}) collective-permute-start(bf16[32,512]{0,1:T(8,128)(2,1)S(1)} %get-tuple-element.22), channel_id=1, source_target_pairs={{16,0},{32,16},{48,32},{64,48},{80,64},{96,80},{112,96},{17,1},{33... | collective-permute-start | bytes 98312 | tf_op jit(solution)/shard_map/ppermute | solution.py:95
  19.8 3.1 %collective-permute-start = (bf16[32,512]{0,1:T(8,128)(2,1)S(1)}, bf16[32,512]{0,1:T(8,128)(2,1)S(1)}, u32[]{:S(2)}, u32[]{:S(2)}) collective-permute-start(bf16[32,512]{0,1:T(8,128)(2,1)S(1)} %get-tuple-element.21), channel_id=1, source_target_pairs={{0,16},{16,32},{32,48},{48,64},{64,80},{80,96},{96,112},{1,17},{17... | collective-permute-start | bytes 98312 | tf_op jit(solution)/shard_map/ppermute | solution.py:93
  23.4 0.5 collective-permute-done.1
  23.9 0.9 %collective-permute-done = bf16[32,512]{0,1:T(8,128)(2,1)S(1)} collective-permute-done((bf16[32,512]{0,1:T(8,128)(2,1)S(1)}, bf16[32,512]{0,1:T(8,128)(2,1)S(1)}, u32[]{:S(2)}, u32[]{:S(2)}) %collective-permute-start) | collective-permute-done | bytes 32800 | tf_op jit(solution)/shard_map/ppermute | solution.py:93
  24.8 0.4 maximum_bitcast_fusion.3
  25.2 1.3 %collective-permute-start.3 = (bf16[32,576]{1,0:T(8,128)(2,1)S(1)}, bf16[32,576]{1,0:T(8,128)(2,1)S(1)}, u32[]{:S(2)}, u32[]{:S(2)}) collective-permute-start(bf16[32,576]{1,0:T(8,128)(2,1)S(1)} %get-tuple-element.20), channel_id=1, source_target_pairs={{1,0},{2,1},{3,2},{4,3},{5,4},{6,5},{7,6},{8,7},{9,8},{10,9},{11,1... | collective-permute-start | bytes 110600 | tf_op jit(solution)/shard_map/ppermute | solution.py:95
  26.5 4.2 %collective-permute-start.2 = (bf16[32,576]{1,0:T(8,128)(2,1)S(1)}, bf16[32,576]{1,0:T(8,128)(2,1)S(1)}, u32[]{:S(2)}, u32[]{:S(2)}) collective-permute-start(bf16[32,576]{1,0:T(8,128)(2,1)S(1)} %get-tuple-element.19), channel_id=1, source_target_pairs={{0,1},{1,2},{2,3},{3,4},{4,5},{5,6},{6,7},{7,8},{8,9},{9,10},{10,1... | collective-permute-start | bytes 110600 | tf_op jit(solution)/shard_map/ppermute | solution.py:93
  30.9 0.9 %collective-permute-done.2 = bf16[32,576]{1,0:T(8,128)(2,1)S(1)} collective-permute-done((bf16[32,576]{1,0:T(8,128)(2,1)S(1)}, bf16[32,576]{1,0:T(8,128)(2,1)S(1)}, u32[]{:S(2)}, u32[]{:S(2)}) %collective-permute-start.2) | collective-permute-done | bytes 36896 | tf_op jit(solution)/shard_map/ppermute | solution.py:93
  31.8 3.7 %fusion.13.w_ref = bf16[8,192,192]{2,1,0:T(8,128)(2,1)} fusion(s32[8,192]{1,0:T(8,128)S(1)} %get-tuple-element.49, s32[8,192]{1,0:T(8,128)S(1)} %get-tuple-element.50, bf16[32,576]{1,0:T(8,128)(2,1)S(1)} %collective-permute-done.3, bf16[512,576]{1,0:T(8,128)(2,1)S(1)} %maximum_bitcast_fusion.3, bf16[32,576]{1,0:T(8,128)(2,1)S(1)} %collective-permute-done.2), kind=kOutput, calls=%fused_computation.15 | convolution fusion | flops 1363894272 | bytes 1265664 | tf_op jit(solution)/shard_map/mrc,msc->mrs/dot_general | solution.py:216
  35.5 0.7 fusion.16
  36.2 0.8 copy.53.tf_ref
  36.9 10.6 %shard_map.94 = f32[8,8,128]{2,1,0:T(8,128)} custom-call(bf16[8,128,128]{2,1,0:T(8,128)(2,1)} %copy.53.tf_ref, bf16[8,192,192]{2,1,0:T(8,128)(2,1)} %fusion.13.w_ref), custom_call_target="tpu_custom_call" | custom-call | tf_op jit(solution)/shard_map/pallas_call | solution.py:71
  47.5 0.8 slice.194
  48.9 0.2 broadcast_in_dim.197
  49.1 0.2 broadcast_in_dim.194
  49.4 0.6 reshape.316
  50.1 9.1 %all-to-all-start.1 = ((f32[16,4,128]{2,1,0:T(4,128)}), f32[16,4,128]{2,1,0:T(4,128)S(1)}, u32[]{:S(2)}, u32[]{:S(2)}) async-start(f32[16,4,128]{2,1,0:T(4,128)} %reshape.316), calls=%async_computation.1 | async-start | bytes 65536 | tf_op jit(solution)/shard_map/all_to_all | solution.py:237
  59.2 6.4 %all-to-all-done.1 = f32[16,4,128]{2,1,0:T(4,128)S(1)} async-done(((f32[16,4,128]{2,1,0:T(4,128)}), f32[16,4,128]{2,1,0:T(4,128)S(1)}, u32[]{:S(2)}, u32[]{:S(2)}) %all-to-all-start.1) | async-done | bytes 32800 | tf_op jit(solution)/shard_map/all_to_all | solution.py:237
  66.0 0.2 select_n.94
  66.2 0.2 select_n.90
  66.5 3.1 %collective-permute-start.5 = (f32[4,3,38]{2,1,0:T(4,128)S(1)}, f32[4,3,38]{2,1,0:T(4,128)S(1)}, u32[]{:S(2)}, u32[]{:S(2)}) collective-permute-start(f32[4,3,38]{2,1,0:T(4,128)S(1)} %get-tuple-element.24), channel_id=1, source_target_pairs={{16,0},{32,16},{48,32},{64,48},{80,64},{96,80},{112,96},{17,1},{33... | collective-permute-start | bytes 5480 | tf_op jit(solution)/shard_map/ppermute | solution.py:197
  69.6 6.0 %collective-permute-start.4 = (f32[4,3,38]{2,1,0:T(4,128)S(1)}, f32[4,3,38]{2,1,0:T(4,128)S(1)}, u32[]{:S(2)}, u32[]{:S(2)}) collective-permute-start(f32[4,3,38]{2,1,0:T(4,128)S(1)} %get-tuple-element.23), channel_id=1, source_target_pairs={{0,16},{16,32},{32,48},{48,64},{64,80},{80,96},{96,112},{1,17},{17... | collective-permute-start | bytes 5480 | tf_op jit(solution)/shard_map/ppermute | solution.py:196
  75.6 0.7 select_reduce_fusion.1
  76.3 0.1 collective-permute-done.4
  77.0 0.1 fusion.29
  77.2 0.7 fusion.45
  (58 shorter events, 2.6 us)
Async XLA Ops:
  0.6 2.3 %copy-start = (bf16[512,512]{1,0:T(8,128)(2,1)S(1)}, bf16[512,512]{1,0:T(8,128)(2,1)}, u32[]{:S(2)}) copy-start(bf16[512,512]{1,0:T(8,128)(2,1)} %param.7) | copy-start | bytes 1572868
  8.0 8.6 %copy-start.1 = (bf16[512,512]{1,0:T(8,128)(2,1)S(1)}, bf16[512,512]{1,0:T(8,128)(2,1)}, u32[]{:S(2)}) copy-start(bf16[512,512]{1,0:T(8,128)(2,1)} %param.8) | copy-start | bytes 1572868
  8.0 27.5 %all-to-all-start = ((bf16[32,128,128]{2,1,0:T(8,128)(2,1)}), bf16[32,128,128]{2,1,0:T(8,128)(2,1)S(1)}, u32[]{:S(2)}, u32[]{:S(2)}) async-start(bf16[32,128,128]{2,1,0:T(8,128)(2,1)} %fusion.10), calls=%async_computation | async-start | bytes 2097152 | tf_op jit(solution)/shard_map/all_to_all | solution.py:209
  16.5 6.3 %copy-start.4 = (s32[2,1,8]{2,1,0:T(1,128)S(1)}, s32[2,1,8]{2,1,0:T(1,128)}, u32[]{:S(2)}) copy-start(s32[2,1,8]{2,1,0:T(1,128)} %param.11) | copy-start | bytes 196
  16.6 6.4 %copy-start.2 = (s32[32,32]{1,0:T(8,128)S(1)}, s32[32,32]{1,0:T(8,128)}, u32[]{:S(2)}) copy-start(s32[32,32]{1,0:T(8,128)} %param.13) | copy-start | bytes 12292
  16.6 6.6 %copy-start.5 = (s32[1,8]{1,0:T(1,128)S(1)}, s32[1,8]{1,0:T(1,128)}, u32[]{:S(2)}) copy-start(s32[1,8]{1,0:T(1,128)} %param.12) | copy-start | bytes 100
  16.9 7.0 %collective-permute-start.1 = (bf16[32,512]{0,1:T(8,128)(2,1)S(1)}, bf16[32,512]{0,1:T(8,128)(2,1)S(1)}, u32[]{:S(2)}, u32[]{:S(2)}) collective-permute-start(bf16[32,512]{0,1:T(8,128)(2,1)S(1)} %get-tuple-element.22), channel_id=1, source_target_pairs={{16,0},{32,16},{48,32},{64,48},{80,64},{96,80},{112,96},{17,1},{33... | collective-permute-start | bytes 98312 | tf_op jit(solution)/shard_map/ppermute | solution.py:95
  19.8 5.0 %collective-permute-start = (bf16[32,512]{0,1:T(8,128)(2,1)S(1)}, bf16[32,512]{0,1:T(8,128)(2,1)S(1)}, u32[]{:S(2)}, u32[]{:S(2)}) collective-permute-start(bf16[32,512]{0,1:T(8,128)(2,1)S(1)} %get-tuple-element.21), channel_id=1, source_target_pairs={{0,16},{16,32},{32,48},{48,64},{64,80},{80,96},{96,112},{1,17},{17... | collective-permute-start | bytes 98312 | tf_op jit(solution)/shard_map/ppermute | solution.py:93
  25.2 5.7 %collective-permute-start.3 = (bf16[32,576]{1,0:T(8,128)(2,1)S(1)}, bf16[32,576]{1,0:T(8,128)(2,1)S(1)}, u32[]{:S(2)}, u32[]{:S(2)}) collective-permute-start(bf16[32,576]{1,0:T(8,128)(2,1)S(1)} %get-tuple-element.20), channel_id=1, source_target_pairs={{1,0},{2,1},{3,2},{4,3},{5,4},{6,5},{7,6},{8,7},{9,8},{10,9},{11,1... | collective-permute-start | bytes 110600 | tf_op jit(solution)/shard_map/ppermute | solution.py:95
  26.5 5.3 %collective-permute-start.2 = (bf16[32,576]{1,0:T(8,128)(2,1)S(1)}, bf16[32,576]{1,0:T(8,128)(2,1)S(1)}, u32[]{:S(2)}, u32[]{:S(2)}) collective-permute-start(bf16[32,576]{1,0:T(8,128)(2,1)S(1)} %get-tuple-element.19), channel_id=1, source_target_pairs={{0,1},{1,2},{2,3},{3,4},{4,5},{5,6},{6,7},{7,8},{8,9},{9,10},{10,1... | collective-permute-start | bytes 110600 | tf_op jit(solution)/shard_map/ppermute | solution.py:93
  48.4 28.5 %copy-start.3 = (f32[2,8]{1,0:T(2,128)}, f32[2,8]{1,0:T(2,128)S(1)}, u32[]{:S(2)}) copy-start(f32[2,8]{1,0:T(2,128)S(1)} %bitcast_negate_fusion) | copy-start | bytes 196
  50.1 15.6 %all-to-all-start.1 = ((f32[16,4,128]{2,1,0:T(4,128)}), f32[16,4,128]{2,1,0:T(4,128)S(1)}, u32[]{:S(2)}, u32[]{:S(2)}) async-start(f32[16,4,128]{2,1,0:T(4,128)} %reshape.316), calls=%async_computation.1 | async-start | bytes 65536 | tf_op jit(solution)/shard_map/all_to_all | solution.py:237
  66.5 9.8 %collective-permute-start.5 = (f32[4,3,38]{2,1,0:T(4,128)S(1)}, f32[4,3,38]{2,1,0:T(4,128)S(1)}, u32[]{:S(2)}, u32[]{:S(2)}) collective-permute-start(f32[4,3,38]{2,1,0:T(4,128)S(1)} %get-tuple-element.24), channel_id=1, source_target_pairs={{16,0},{32,16},{48,32},{64,48},{80,64},{96,80},{112,96},{17,1},{33... | collective-permute-start | bytes 5480 | tf_op jit(solution)/shard_map/ppermute | solution.py:197
  69.6 6.8 %collective-permute-start.4 = (f32[4,3,38]{2,1,0:T(4,128)S(1)}, f32[4,3,38]{2,1,0:T(4,128)S(1)}, u32[]{:S(2)}, u32[]{:S(2)}) collective-permute-start(f32[4,3,38]{2,1,0:T(4,128)S(1)} %get-tuple-element.23), channel_id=1, source_target_pairs={{0,16},{16,32},{32,48},{48,64},{64,80},{80,96},{96,112},{1,17},{17... | collective-permute-start | bytes 5480 | tf_op jit(solution)/shard_map/ppermute | solution.py:196

commit v19 on v15

--- a/solution.py
+++ b/solution.py
@@ -20,7 +20,7 @@
 EPSILON = 1e-05
 
 HALF = PATCH // 2
-PER = 2
+PER = 4
 
 
 def flow_kernel(tf_ref, w_ref, out_ref, wlo, whi, corr):

time: 75.2 us -> 74.8 us (level)
  no operation moved by 1% of the time
where the time goes in v19:
time: 74.8 us; the launch traced here: 74.3 us
  starting transfers between devices  38.2 us (51%)
  Pallas kernels  10.2 us (14%)
  waiting for transfers between devices  8.89 us (12%)
  local copies, waits for them, and re-layouts  6.56 us (9%)
  matrix products  6.09 us (8%)
  other arithmetic  3.4 us (5%)
  between operations  0.98 us (1%)
    pallas_call x1, Pallas kernels, flows_of(): pl.pallas_call(flow_kernel, grid=(n // PER,), in_specs=[pl.BlockSpec((PER...  10.2 us
    all_to_all x1, starting transfers between devices, shards(): lax.all_to_all(back, 'tx', split_axis=0, concat_axis=0, tiled=True)  9.14 us
    all_to_all x1, starting transfers between devices, shards(): lax.all_to_all(outgoing, 'tx', split_axis=0, concat_axis=0, tiled=True)  8.55 us
    ppermute x2, starting transfers between devices, padded_2(): lax.ppermute(tail, axis, [(i, (i + 1) % count) for i in range(ends)])  7.27 us
    all_to_all x1, waiting for transfers between devices, shards(): lax.all_to_all(back, 'tx', split_axis=0, concat_axis=0, tiled=True)  6.38 us
    ppermute x1, starting transfers between devices, rows_exchange(): above = lax.ppermute(tail, 'ty', [(i, i + 1) for i in range(count - 1)])  6 us
    ppermute x2, starting transfers between devices, padded_2(): lax.ppermute(head, axis, [((i + 1) % count, i) for i in range(ends)])  4.15 us
    dot_general x1, matrix products, shards(): jnp.einsum('mrc,msc->mrs', by_row.astype(jnp.bfloat16), wcol_pick, prefer...  3.75 us
  transfers between devices with their start and end apart: 8, of which 6 were waited for; matrix products, arithmetic and copies ran while one was open for 8% of the time, Pallas kernels for 0%

profile of v19, /device:TPU:1, one launch (start us, length us, event | category | flops | bytes accessed | tf_op | source)
XLA Modules:
  0.0 74.3 jit_solution(2459553521318853285)
XLA Ops:
  0.7 0.7 slice_bitcast_fusion.5
  1.5 0.2 copy-done
  1.7 1.1 %fusion.11 = bf16[8,128,128]{2,1,0:T(8,128)(2,1)S(1)} fusion(s32[8,128]{1,0:T(8,128)S(1)} %get-tuple-element.43, s32[8,128]{1,0:T(8,128)S(1)} %get-tuple-element.44, bf16[512,512]{1,0:T(8,128)(2,1)S(1)} %copy-done), kind=kOutput, calls=%fused_computation.14 | convolution fusion | flops 672792576 | bytes 794624 | tf_op jit(solution)/shard_map/kra,kia->kri/dot_general | solution.py:163
  2.9 0.6 convolution_convert_fusion
  3.4 1.4 %copy.39 = bf16[32,128,128]{2,1,0:T(8,128)(2,1)} copy(bf16[32,128,128]{2,0,1:T(8,128)(2,1)S(1)} %convolution_convert_fusion) | data formatting | bytes 2097152 | tf_op jit(solution)/shard_map/convert_element_type | solution.py:168
  4.8 8.5 %all-to-all-start = ((bf16[32,128,128]{2,1,0:T(8,128)(2,1)}), bf16[32,128,128]{2,1,0:T(8,128)(2,1)S(1)}, u32[]{:S(2)}, u32[]{:S(2)}) async-start(bf16[32,128,128]{2,1,0:T(8,128)(2,1)} %copy.39), calls=%async_computation | async-start | bytes 2097152 | tf_op jit(solution)/shard_map/all_to_all | solution.py:207
  13.4 0.2 copy.42
  13.7 2.9 %collective-permute-start.1 = (bf16[32,512]{0,1:T(8,128)(2,1)S(1)}, bf16[32,512]{0,1:T(8,128)(2,1)S(1)}, u32[]{:S(2)}, u32[]{:S(2)}) collective-permute-start(bf16[32,512]{0,1:T(8,128)(2,1)S(1)} %get-tuple-element.20), channel_id=1, source_target_pairs={{16,0},{32,16},{48,32},{64,48},{80,64},{96,80},{112,96},{17,1},{33... | collective-permute-start | bytes 98312 | tf_op jit(solution)/shard_map/ppermute | solution.py:95
  16.6 3.1 %collective-permute-start = (bf16[32,512]{0,1:T(8,128)(2,1)S(1)}, bf16[32,512]{0,1:T(8,128)(2,1)S(1)}, u32[]{:S(2)}, u32[]{:S(2)}) collective-permute-start(bf16[32,512]{0,1:T(8,128)(2,1)S(1)} %get-tuple-element.19), channel_id=1, source_target_pairs={{0,16},{16,32},{32,48},{48,64},{64,80},{80,96},{96,112},{1,17},{17... | collective-permute-start | bytes 98312 | tf_op jit(solution)/shard_map/ppermute | solution.py:93
  20.2 0.5 collective-permute-done.1
  20.7 0.9 %collective-permute-done = bf16[32,512]{0,1:T(8,128)(2,1)S(1)} collective-permute-done((bf16[32,512]{0,1:T(8,128)(2,1)S(1)}, bf16[32,512]{0,1:T(8,128)(2,1)S(1)}, u32[]{:S(2)}, u32[]{:S(2)}) %collective-permute-start) | collective-permute-done | bytes 32800 | tf_op jit(solution)/shard_map/ppermute | solution.py:93
  21.6 0.4 maximum_bitcast_fusion.3
  22.0 1.3 %collective-permute-start.3 = (bf16[32,576]{1,0:T(8,128)(2,1)S(1)}, bf16[32,576]{1,0:T(8,128)(2,1)S(1)}, u32[]{:S(2)}, u32[]{:S(2)}) collective-permute-start(bf16[32,576]{1,0:T(8,128)(2,1)S(1)} %get-tuple-element.18), channel_id=1, source_target_pairs={{1,0},{2,1},{3,2},{4,3},{5,4},{6,5},{7,6},{8,7},{9,8},{10,9},{11,1... | collective-permute-start | bytes 110600 | tf_op jit(solution)/shard_map/ppermute | solution.py:95
  23.3 4.2 %collective-permute-start.2 = (bf16[32,576]{1,0:T(8,128)(2,1)S(1)}, bf16[32,576]{1,0:T(8,128)(2,1)S(1)}, u32[]{:S(2)}, u32[]{:S(2)}) collective-permute-start(bf16[32,576]{1,0:T(8,128)(2,1)S(1)} %get-tuple-element.17), channel_id=1, source_target_pairs={{0,1},{1,2},{2,3},{3,4},{4,5},{5,6},{6,7},{7,8},{8,9},{9,10},{10,1... | collective-permute-start | bytes 110600 | tf_op jit(solution)/shard_map/ppermute | solution.py:93
  27.7 0.9 %collective-permute-done.2 = bf16[32,576]{1,0:T(8,128)(2,1)S(1)} collective-permute-done((bf16[32,576]{1,0:T(8,128)(2,1)S(1)}, bf16[32,576]{1,0:T(8,128)(2,1)S(1)}, u32[]{:S(2)}, u32[]{:S(2)}) %collective-permute-start.2) | collective-permute-done | bytes 36896 | tf_op jit(solution)/shard_map/ppermute | solution.py:93
  28.6 3.7 %fusion.8.w_ref = bf16[8,192,192]{2,1,0:T(8,128)(2,1)} fusion(s32[8,192]{1,0:T(8,128)S(1)} %get-tuple-element.45, s32[8,192]{1,0:T(8,128)S(1)} %get-tuple-element.46, bf16[32,576]{1,0:T(8,128)(2,1)S(1)} %collective-permute-done.3, bf16[512,576]{1,0:T(8,128)(2,1)S(1)} %maximum_bitcast_fusion.3, bf16[32,576]{1,0:T(8,128)(2,1)S(1)} %collective-permute-done.2), kind=kOutput, calls=%fused_computation.13 | convolution fusion | flops 1363894272 | bytes 1265664 | tf_op jit(solution)/shard_map/mrc,msc->mrs/dot_general | solution.py:214
  32.3 0.7 fusion.12
  33.0 0.8 %copy.59.tf_ref = bf16[8,128,128]{2,1,0:T(8,128)(2,1)} copy(bf16[8,128,128]{2,0,1:T(8,128)(2,1)S(1)} %fusion.12) | data formatting | bytes 524288 | tf_op jit(solution)/shard_map/ms,sri->mri/dot_general | solution.py:217
  33.8 10.2 %shard_map.94 = f32[8,8,128]{2,1,0:T(8,128)} custom-call(bf16[8,128,128]{2,1,0:T(8,128)(2,1)} %copy.59.tf_ref, bf16[8,192,192]{2,1,0:T(8,128)(2,1)} %fusion.8.w_ref), custom_call_target="tpu_custom_call" | custom-call | tf_op jit(solution)/shard_map/pallas_call | solution.py:71
  43.9 0.8 %slice.194 = f32[8,2,1]{2,1,0:T(2,128)S(1)} slice(f32[8,8,128]{2,1,0:T(8,128)} %shard_map.94), slice={[0:8], [0:2], [0:1]} | slice | bytes 128 | tf_op jit(solution)/shard_map/slice | solution.py:82
  45.3 0.2 broadcast_in_dim.163
  45.6 0.2 broadcast_in_dim.160
  45.9 0.6 reshape.316
  46.5 9.1 %all-to-all-start.1 = ((f32[16,4,128]{2,1,0:T(4,128)}), f32[16,4,128]{2,1,0:T(4,128)S(1)}, u32[]{:S(2)}, u32[]{:S(2)}) async-start(f32[16,4,128]{2,1,0:T(4,128)} %reshape.316), calls=%async_computation.1 | async-start | bytes 65536 | tf_op jit(solution)/shard_map/all_to_all | solution.py:235
  55.7 6.4 %all-to-all-done.1 = f32[16,4,128]{2,1,0:T(4,128)S(1)} async-done(((f32[16,4,128]{2,1,0:T(4,128)}), f32[16,4,128]{2,1,0:T(4,128)S(1)}, u32[]{:S(2)}, u32[]{:S(2)}) %all-to-all-start.1) | async-done | bytes 32800 | tf_op jit(solution)/shard_map/all_to_all | solution.py:235
  62.4 0.2 select_n.76
  62.6 0.2 select_n.72
  62.9 3.1 %collective-permute-start.5 = (f32[4,3,38]{2,1,0:T(4,128)S(1)}, f32[4,3,38]{2,1,0:T(4,128)S(1)}, u32[]{:S(2)}, u32[]{:S(2)}) collective-permute-start(f32[4,3,38]{2,1,0:T(4,128)S(1)} %get-tuple-element.22), channel_id=1, source_target_pairs={{16,0},{32,16},{48,32},{64,48},{80,64},{96,80},{112,96},{17,1},{33... | collective-permute-start | bytes 5480 | tf_op jit(solution)/shard_map/ppermute | solution.py:195
  66.0 6.0 %collective-permute-start.4 = (f32[4,3,38]{2,1,0:T(4,128)S(1)}, f32[4,3,38]{2,1,0:T(4,128)S(1)}, u32[]{:S(2)}, u32[]{:S(2)}) collective-permute-start(f32[4,3,38]{2,1,0:T(4,128)S(1)} %get-tuple-element.21), channel_id=1, source_target_pairs={{0,16},{16,32},{32,48},{48,64},{64,80},{80,96},{96,112},{1,17},{17... | collective-permute-start | bytes 5480 | tf_op jit(solution)/shard_map/ppermute | solution.py:194
  72.0 0.7 select_reduce_fusion.1
  73.5 0.1 fusion.29
  73.6 0.7 fusion.45
  (60 shorter events, 2.7 us)
Async XLA Ops:
  0.6 1.1 %copy-start = (bf16[512,512]{1,0:T(8,128)(2,1)S(1)}, bf16[512,512]{1,0:T(8,128)(2,1)}, u32[]{:S(2)}) copy-start(bf16[512,512]{1,0:T(8,128)(2,1)} %param.7) | copy-start | bytes 1572868
  1.7 1.1 %copy-start.6 = (s32[1,8]{1,0:T(1,128)S(1)}, s32[1,8]{1,0:T(1,128)}, u32[]{:S(2)}) copy-start(s32[1,8]{1,0:T(1,128)} %param.10) | copy-start | bytes 100
  4.8 8.6 %copy-start.1 = (bf16[512,512]{1,0:T(8,128)(2,1)S(1)}, bf16[512,512]{1,0:T(8,128)(2,1)}, u32[]{:S(2)}) copy-start(bf16[512,512]{1,0:T(8,128)(2,1)} %param.8) | copy-start | bytes 1572868
  4.8 27.5 %all-to-all-start = ((bf16[32,128,128]{2,1,0:T(8,128)(2,1)}), bf16[32,128,128]{2,1,0:T(8,128)(2,1)S(1)}, u32[]{:S(2)}, u32[]{:S(2)}) async-start(bf16[32,128,128]{2,1,0:T(8,128)(2,1)} %copy.39), calls=%async_computation | async-start | bytes 2097152 | tf_op jit(solution)/shard_map/all_to_all | solution.py:207
  13.4 6.3 %copy-start.4 = (s32[2,1,8]{2,1,0:T(1,128)S(1)}, s32[2,1,8]{2,1,0:T(1,128)}, u32[]{:S(2)}) copy-start(s32[2,1,8]{2,1,0:T(1,128)} %param.11) | copy-start | bytes 196
  13.4 6.4 %copy-start.2 = (s32[32,32]{1,0:T(8,128)S(1)}, s32[32,32]{1,0:T(8,128)}, u32[]{:S(2)}) copy-start(s32[32,32]{1,0:T(8,128)} %param.13) | copy-start | bytes 12292
  13.4 6.6 %copy-start.5 = (s32[1,8]{1,0:T(1,128)S(1)}, s32[1,8]{1,0:T(1,128)}, u32[]{:S(2)}) copy-start(s32[1,8]{1,0:T(1,128)} %param.12) | copy-start | bytes 100
  13.7 7.0 %collective-permute-start.1 = (bf16[32,512]{0,1:T(8,128)(2,1)S(1)}, bf16[32,512]{0,1:T(8,128)(2,1)S(1)}, u32[]{:S(2)}, u32[]{:S(2)}) collective-permute-start(bf16[32,512]{0,1:T(8,128)(2,1)S(1)} %get-tuple-element.20), channel_id=1, source_target_pairs={{16,0},{32,16},{48,32},{64,48},{80,64},{96,80},{112,96},{17,1},{33... | collective-permute-start | bytes 98312 | tf_op jit(solution)/shard_map/ppermute | solution.py:95
  16.6 5.0 %collective-permute-start = (bf16[32,512]{0,1:T(8,128)(2,1)S(1)}, bf16[32,512]{0,1:T(8,128)(2,1)S(1)}, u32[]{:S(2)}, u32[]{:S(2)}) collective-permute-start(bf16[32,512]{0,1:T(8,128)(2,1)S(1)} %get-tuple-element.19), channel_id=1, source_target_pairs={{0,16},{16,32},{32,48},{48,64},{64,80},{80,96},{96,112},{1,17},{17... | collective-permute-start | bytes 98312 | tf_op jit(solution)/shard_map/ppermute | solution.py:93
  22.0 5.7 %collective-permute-start.3 = (bf16[32,576]{1,0:T(8,128)(2,1)S(1)}, bf16[32,576]{1,0:T(8,128)(2,1)S(1)}, u32[]{:S(2)}, u32[]{:S(2)}) collective-permute-start(bf16[32,576]{1,0:T(8,128)(2,1)S(1)} %get-tuple-element.18), channel_id=1, source_target_pairs={{1,0},{2,1},{3,2},{4,3},{5,4},{6,5},{7,6},{8,7},{9,8},{10,9},{11,1... | collective-permute-start | bytes 110600 | tf_op jit(solution)/shard_map/ppermute | solution.py:95
  23.3 5.3 %collective-permute-start.2 = (bf16[32,576]{1,0:T(8,128)(2,1)S(1)}, bf16[32,576]{1,0:T(8,128)(2,1)S(1)}, u32[]{:S(2)}, u32[]{:S(2)}) collective-permute-start(bf16[32,576]{1,0:T(8,128)(2,1)S(1)} %get-tuple-element.17), channel_id=1, source_target_pairs={{0,1},{1,2},{2,3},{3,4},{4,5},{5,6},{6,7},{7,8},{8,9},{9,10},{10,1... | collective-permute-start | bytes 110600 | tf_op jit(solution)/shard_map/ppermute | solution.py:93
  44.8 28.5 %copy-start.3 = (f32[2,8]{1,0:T(2,128)}, f32[2,8]{1,0:T(2,128)S(1)}, u32[]{:S(2)}) copy-start(f32[2,8]{1,0:T(2,128)S(1)} %bitcast_negate_fusion) | copy-start | bytes 196
  46.5 15.6 %all-to-all-start.1 = ((f32[16,4,128]{2,1,0:T(4,128)}), f32[16,4,128]{2,1,0:T(4,128)S(1)}, u32[]{:S(2)}, u32[]{:S(2)}) async-start(f32[16,4,128]{2,1,0:T(4,128)} %reshape.316), calls=%async_computation.1 | async-start | bytes 65536 | tf_op jit(solution)/shard_map/all_to_all | solution.py:235
  62.9 9.8 %collective-permute-start.5 = (f32[4,3,38]{2,1,0:T(4,128)S(1)}, f32[4,3,38]{2,1,0:T(4,128)S(1)}, u32[]{:S(2)}, u32[]{:S(2)}) collective-permute-start(f32[4,3,38]{2,1,0:T(4,128)S(1)} %get-tuple-element.22), channel_id=1, source_target_pairs={{16,0},{32,16},{48,32},{64,48},{80,64},{96,80},{112,96},{17,1},{33... | collective-permute-start | bytes 5480 | tf_op jit(solution)/shard_map/ppermute | solution.py:195
  66.0 6.8 %collective-permute-start.4 = (f32[4,3,38]{2,1,0:T(4,128)S(1)}, f32[4,3,38]{2,1,0:T(4,128)S(1)}, u32[]{:S(2)}, u32[]{:S(2)}) collective-permute-start(f32[4,3,38]{2,1,0:T(4,128)S(1)} %get-tuple-element.21), channel_id=1, source_target_pairs={{0,16},{16,32},{32,48},{48,64},{64,80},{80,96},{96,112},{1,17},{17... | collective-permute-start | bytes 5480 | tf_op jit(solution)/shard_map/ppermute | solution.py:194

commit v20 on v19

--- a/solution.py
+++ b/solution.py
@@ -20,7 +20,7 @@
 EPSILON = 1e-05
 
 HALF = PATCH // 2
-PER = 4
+PER = 8
 
 
 def flow_kernel(tf_ref, w_ref, out_ref, wlo, whi, corr):

time: 74.8 us -> 74.7 us (level)
  transfers between devices with their start and end apart: 8 -> 8, of which waited for: 6 -> 5; matrix products, arithmetic and copies ran while one was open for 8% -> 8% of each run, Pallas kernels for 0% -> 0%
where the time goes in v20:
time: 74.7 us; the launch traced here: 74.1 us
  starting transfers between devices  38.4 us (51%)
  Pallas kernels  9.98 us (13%)
  waiting for transfers between devices  8.71 us (12%)
  local copies, waits for them, and re-layouts  6.56 us (9%)
  matrix products  6.08 us (8%)
  other arithmetic  3.4 us (5%)
  between operations  0.98 us (1%)
    pallas_call x1, Pallas kernels, flows_of(): pl.pallas_call(flow_kernel, grid=(n // PER,), in_specs=[pl.BlockSpec((PER...  9.98 us
    all_to_all x1, starting transfers between devices, shards(): lax.all_to_all(back, 'tx', split_axis=0, concat_axis=0, tiled=True)  9.14 us
    all_to_all x1, starting transfers between devices, shards(): lax.all_to_all(outgoing, 'tx', split_axis=0, concat_axis=0, tiled=True)  8.55 us
    ppermute x2, starting transfers between devices, padded_2(): lax.ppermute(tail, axis, [(i, (i + 1) % count) for i in range(ends)])  7.46 us
    all_to_all x1, waiting for transfers between devices, shards(): lax.all_to_all(back, 'tx', split_axis=0, concat_axis=0, tiled=True)  6.38 us
    ppermute x1, starting transfers between devices, rows_exchange(): above = lax.ppermute(tail, 'ty', [(i, i + 1) for i in range(count - 1)])  6.01 us
    ppermute x2, starting transfers between devices, padded_2(): lax.ppermute(head, axis, [((i + 1) % count, i) for i in range(ends)])  4.15 us
    dot_general x1, matrix products, shards(): jnp.einsum('mrc,msc->mrs', by_row.astype(jnp.bfloat16), wcol_pick, prefer...  3.74 us
  transfers between devices with their start and end apart: 8, of which 5 were waited for; matrix products, arithmetic and copies ran while one was open for 8% of the time, Pallas kernels for 0%

profile of v20, /device:TPU:1, one launch (start us, length us, event | category | flops | bytes accessed | tf_op | source)
XLA Modules:
  0.0 74.1 jit_solution(1298945086509339544)
XLA Ops:
  0.7 0.7 slice_bitcast_fusion.5
  1.5 0.2 copy-done
  1.7 1.1 %fusion.11 = bf16[8,128,128]{2,1,0:T(8,128)(2,1)S(1)} fusion(s32[8,128]{1,0:T(8,128)S(1)} %get-tuple-element.43, s32[8,128]{1,0:T(8,128)S(1)} %get-tuple-element.44, bf16[512,512]{1,0:T(8,128)(2,1)S(1)} %copy-done), kind=kOutput, calls=%fused_computation.14 | convolution fusion | flops 672792576 | bytes 794624 | tf_op jit(solution)/shard_map/kra,kia->kri/dot_general | solution.py:163
  2.9 0.5 convolution_convert_fusion
  3.4 1.4 %copy.39 = bf16[32,128,128]{2,1,0:T(8,128)(2,1)} copy(bf16[32,128,128]{2,0,1:T(8,128)(2,1)S(1)} %convolution_convert_fusion) | data formatting | bytes 2097152 | tf_op jit(solution)/shard_map/convert_element_type | solution.py:168
  4.8 8.5 %all-to-all-start = ((bf16[32,128,128]{2,1,0:T(8,128)(2,1)}), bf16[32,128,128]{2,1,0:T(8,128)(2,1)S(1)}, u32[]{:S(2)}, u32[]{:S(2)}) async-start(bf16[32,128,128]{2,1,0:T(8,128)(2,1)} %copy.39), calls=%async_computation | async-start | bytes 2097152 | tf_op jit(solution)/shard_map/all_to_all | solution.py:207
  13.4 0.2 copy.42
  13.7 2.9 %collective-permute-start.1 = (bf16[32,512]{0,1:T(8,128)(2,1)S(1)}, bf16[32,512]{0,1:T(8,128)(2,1)S(1)}, u32[]{:S(2)}, u32[]{:S(2)}) collective-permute-start(bf16[32,512]{0,1:T(8,128)(2,1)S(1)} %get-tuple-element.20), channel_id=1, source_target_pairs={{16,0},{32,16},{48,32},{64,48},{80,64},{96,80},{112,96},{17,1},{33... | collective-permute-start | bytes 98312 | tf_op jit(solution)/shard_map/ppermute | solution.py:95
  16.6 3.1 %collective-permute-start = (bf16[32,512]{0,1:T(8,128)(2,1)S(1)}, bf16[32,512]{0,1:T(8,128)(2,1)S(1)}, u32[]{:S(2)}, u32[]{:S(2)}) collective-permute-start(bf16[32,512]{0,1:T(8,128)(2,1)S(1)} %get-tuple-element.19), channel_id=1, source_target_pairs={{0,16},{16,32},{32,48},{48,64},{64,80},{80,96},{96,112},{1,17},{17... | collective-permute-start | bytes 98312 | tf_op jit(solution)/shard_map/ppermute | solution.py:93
  20.2 0.5 collective-permute-done.1
  20.7 0.9 %collective-permute-done = bf16[32,512]{0,1:T(8,128)(2,1)S(1)} collective-permute-done((bf16[32,512]{0,1:T(8,128)(2,1)S(1)}, bf16[32,512]{0,1:T(8,128)(2,1)S(1)}, u32[]{:S(2)}, u32[]{:S(2)}) %collective-permute-start) | collective-permute-done | bytes 32800 | tf_op jit(solution)/shard_map/ppermute | solution.py:93
  21.6 0.4 maximum_bitcast_fusion.3
  22.0 1.3 %collective-permute-start.3 = (bf16[32,576]{1,0:T(8,128)(2,1)S(1)}, bf16[32,576]{1,0:T(8,128)(2,1)S(1)}, u32[]{:S(2)}, u32[]{:S(2)}) collective-permute-start(bf16[32,576]{1,0:T(8,128)(2,1)S(1)} %get-tuple-element.18), channel_id=1, source_target_pairs={{1,0},{2,1},{3,2},{4,3},{5,4},{6,5},{7,6},{8,7},{9,8},{10,9},{11,1... | collective-permute-start | bytes 110600 | tf_op jit(solution)/shard_map/ppermute | solution.py:95
  23.3 4.4 %collective-permute-start.2 = (bf16[32,576]{1,0:T(8,128)(2,1)S(1)}, bf16[32,576]{1,0:T(8,128)(2,1)S(1)}, u32[]{:S(2)}, u32[]{:S(2)}) collective-permute-start(bf16[32,576]{1,0:T(8,128)(2,1)S(1)} %get-tuple-element.17), channel_id=1, source_target_pairs={{0,1},{1,2},{2,3},{3,4},{4,5},{5,6},{6,7},{7,8},{8,9},{9,10},{10,1... | collective-permute-start | bytes 110600 | tf_op jit(solution)/shard_map/ppermute | solution.py:93
  27.8 0.8 %collective-permute-done.2 = bf16[32,576]{1,0:T(8,128)(2,1)S(1)} collective-permute-done((bf16[32,576]{1,0:T(8,128)(2,1)S(1)}, bf16[32,576]{1,0:T(8,128)(2,1)S(1)}, u32[]{:S(2)}, u32[]{:S(2)}) %collective-permute-start.2) | collective-permute-done | bytes 36896 | tf_op jit(solution)/shard_map/ppermute | solution.py:93
  28.6 3.7 %fusion.8.w_ref = bf16[8,192,192]{2,1,0:T(8,128)(2,1)} fusion(s32[8,192]{1,0:T(8,128)S(1)} %get-tuple-element.45, s32[8,192]{1,0:T(8,128)S(1)} %get-tuple-element.46, bf16[32,576]{1,0:T(8,128)(2,1)S(1)} %collective-permute-done.3, bf16[512,576]{1,0:T(8,128)(2,1)S(1)} %maximum_bitcast_fusion.3, bf16[32,576]{1,0:T(8,128)(2,1)S(1)} %collective-permute-done.2), kind=kOutput, calls=%fused_computation.13 | convolution fusion | flops 1363894272 | bytes 1265664 | tf_op jit(solution)/shard_map/mrc,msc->mrs/dot_general | solution.py:214
  32.3 0.7 fusion.12
  33.0 0.8 %copy.59.tf_ref = bf16[8,128,128]{2,1,0:T(8,128)(2,1)} copy(bf16[8,128,128]{2,0,1:T(8,128)(2,1)S(1)} %fusion.12) | data formatting | bytes 524288 | tf_op jit(solution)/shard_map/ms,sri->mri/dot_general | solution.py:217
  33.8 10.0 %shard_map.94 = f32[8,8,128]{2,1,0:T(8,128)} custom-call(bf16[8,128,128]{2,1,0:T(8,128)(2,1)} %copy.59.tf_ref, bf16[8,192,192]{2,1,0:T(8,128)(2,1)} %fusion.8.w_ref), custom_call_target="tpu_custom_call" | custom-call | tf_op jit(solution)/shard_map/pallas_call | solution.py:71
  43.7 0.8 %slice.194 = f32[8,2,1]{2,1,0:T(2,128)S(1)} slice(f32[8,8,128]{2,1,0:T(8,128)} %shard_map.94), slice={[0:8], [0:2], [0:1]} | slice | bytes 128 | tf_op jit(solution)/shard_map/slice | solution.py:82
  45.1 0.2 broadcast_in_dim.163
  45.4 0.2 broadcast_in_dim.160
  45.7 0.6 reshape.316
  46.3 9.1 %all-to-all-start.1 = ((f32[16,4,128]{2,1,0:T(4,128)}), f32[16,4,128]{2,1,0:T(4,128)S(1)}, u32[]{:S(2)}, u32[]{:S(2)}) async-start(f32[16,4,128]{2,1,0:T(4,128)} %reshape.316), calls=%async_computation.1 | async-start | bytes 65536 | tf_op jit(solution)/shard_map/all_to_all | solution.py:235
  55.5 6.4 %all-to-all-done.1 = f32[16,4,128]{2,1,0:T(4,128)S(1)} async-done(((f32[16,4,128]{2,1,0:T(4,128)}), f32[16,4,128]{2,1,0:T(4,128)S(1)}, u32[]{:S(2)}, u32[]{:S(2)}) %all-to-all-start.1) | async-done | bytes 32800 | tf_op jit(solution)/shard_map/all_to_all | solution.py:235
  62.2 0.2 select_n.76
  62.4 0.2 select_n.72
  62.7 3.1 %collective-permute-start.5 = (f32[4,3,38]{2,1,0:T(4,128)S(1)}, f32[4,3,38]{2,1,0:T(4,128)S(1)}, u32[]{:S(2)}, u32[]{:S(2)}) collective-permute-start(f32[4,3,38]{2,1,0:T(4,128)S(1)} %get-tuple-element.22), channel_id=1, source_target_pairs={{16,0},{32,16},{48,32},{64,48},{80,64},{96,80},{112,96},{17,1},{33... | collective-permute-start | bytes 5480 | tf_op jit(solution)/shard_map/ppermute | solution.py:195
  65.8 6.0 %collective-permute-start.4 = (f32[4,3,38]{2,1,0:T(4,128)S(1)}, f32[4,3,38]{2,1,0:T(4,128)S(1)}, u32[]{:S(2)}, u32[]{:S(2)}) collective-permute-start(f32[4,3,38]{2,1,0:T(4,128)S(1)} %get-tuple-element.21), channel_id=1, source_target_pairs={{0,16},{16,32},{32,48},{48,64},{64,80},{80,96},{96,112},{1,17},{17... | collective-permute-start | bytes 5480 | tf_op jit(solution)/shard_map/ppermute | solution.py:194
  71.9 0.7 select_reduce_fusion.1
  73.3 0.1 fusion.29
  73.4 0.7 fusion.45
  (60 shorter events, 2.7 us)
Async XLA Ops:
  0.6 1.1 %copy-start = (bf16[512,512]{1,0:T(8,128)(2,1)S(1)}, bf16[512,512]{1,0:T(8,128)(2,1)}, u32[]{:S(2)}) copy-start(bf16[512,512]{1,0:T(8,128)(2,1)} %param.7) | copy-start | bytes 1572868
  1.7 1.1 %copy-start.6 = (s32[1,8]{1,0:T(1,128)S(1)}, s32[1,8]{1,0:T(1,128)}, u32[]{:S(2)}) copy-start(s32[1,8]{1,0:T(1,128)} %param.10) | copy-start | bytes 100
  4.8 8.6 %copy-start.1 = (bf16[512,512]{1,0:T(8,128)(2,1)S(1)}, bf16[512,512]{1,0:T(8,128)(2,1)}, u32[]{:S(2)}) copy-start(bf16[512,512]{1,0:T(8,128)(2,1)} %param.8) | copy-start | bytes 1572868
  4.8 27.5 %all-to-all-start = ((bf16[32,128,128]{2,1,0:T(8,128)(2,1)}), bf16[32,128,128]{2,1,0:T(8,128)(2,1)S(1)}, u32[]{:S(2)}, u32[]{:S(2)}) async-start(bf16[32,128,128]{2,1,0:T(8,128)(2,1)} %copy.39), calls=%async_computation | async-start | bytes 2097152 | tf_op jit(solution)/shard_map/all_to_all | solution.py:207
  13.4 6.3 %copy-start.4 = (s32[2,1,8]{2,1,0:T(1,128)S(1)}, s32[2,1,8]{2,1,0:T(1,128)}, u32[]{:S(2)}) copy-start(s32[2,1,8]{2,1,0:T(1,128)} %param.11) | copy-start | bytes 196
  13.4 6.4 %copy-start.2 = (s32[32,32]{1,0:T(8,128)S(1)}, s32[32,32]{1,0:T(8,128)}, u32[]{:S(2)}) copy-start(s32[32,32]{1,0:T(8,128)} %param.13) | copy-start | bytes 12292
  13.4 6.6 %copy-start.5 = (s32[1,8]{1,0:T(1,128)S(1)}, s32[1,8]{1,0:T(1,128)}, u32[]{:S(2)}) copy-start(s32[1,8]{1,0:T(1,128)} %param.12) | copy-start | bytes 100
  13.7 7.0 %collective-permute-start.1 = (bf16[32,512]{0,1:T(8,128)(2,1)S(1)}, bf16[32,512]{0,1:T(8,128)(2,1)S(1)}, u32[]{:S(2)}, u32[]{:S(2)}) collective-permute-start(bf16[32,512]{0,1:T(8,128)(2,1)S(1)} %get-tuple-element.20), channel_id=1, source_target_pairs={{16,0},{32,16},{48,32},{64,48},{80,64},{96,80},{112,96},{17,1},{33... | collective-permute-start | bytes 98312 | tf_op jit(solution)/shard_map/ppermute | solution.py:95
  16.6 5.0 %collective-permute-start = (bf16[32,512]{0,1:T(8,128)(2,1)S(1)}, bf16[32,512]{0,1:T(8,128)(2,1)S(1)}, u32[]{:S(2)}, u32[]{:S(2)}) collective-permute-start(bf16[32,512]{0,1:T(8,128)(2,1)S(1)} %get-tuple-element.19), channel_id=1, source_target_pairs={{0,16},{16,32},{32,48},{48,64},{64,80},{80,96},{96,112},{1,17},{17... | collective-permute-start | bytes 98312 | tf_op jit(solution)/shard_map/ppermute | solution.py:93
  22.0 5.8 %collective-permute-start.3 = (bf16[32,576]{1,0:T(8,128)(2,1)S(1)}, bf16[32,576]{1,0:T(8,128)(2,1)S(1)}, u32[]{:S(2)}, u32[]{:S(2)}) collective-permute-start(bf16[32,576]{1,0:T(8,128)(2,1)S(1)} %get-tuple-element.18), channel_id=1, source_target_pairs={{1,0},{2,1},{3,2},{4,3},{5,4},{6,5},{7,6},{8,7},{9,8},{10,9},{11,1... | collective-permute-start | bytes 110600 | tf_op jit(solution)/shard_map/ppermute | solution.py:95
  23.3 5.3 %collective-permute-start.2 = (bf16[32,576]{1,0:T(8,128)(2,1)S(1)}, bf16[32,576]{1,0:T(8,128)(2,1)S(1)}, u32[]{:S(2)}, u32[]{:S(2)}) collective-permute-start(bf16[32,576]{1,0:T(8,128)(2,1)S(1)} %get-tuple-element.17), channel_id=1, source_target_pairs={{0,1},{1,2},{2,3},{3,4},{4,5},{5,6},{6,7},{7,8},{8,9},{9,10},{10,1... | collective-permute-start | bytes 110600 | tf_op jit(solution)/shard_map/ppermute | solution.py:93
  44.6 28.5 %copy-start.3 = (f32[2,8]{1,0:T(2,128)}, f32[2,8]{1,0:T(2,128)S(1)}, u32[]{:S(2)}) copy-start(f32[2,8]{1,0:T(2,128)S(1)} %bitcast_negate_fusion) | copy-start | bytes 196
  46.3 15.6 %all-to-all-start.1 = ((f32[16,4,128]{2,1,0:T(4,128)}), f32[16,4,128]{2,1,0:T(4,128)S(1)}, u32[]{:S(2)}, u32[]{:S(2)}) async-start(f32[16,4,128]{2,1,0:T(4,128)} %reshape.316), calls=%async_computation.1 | async-start | bytes 65536 | tf_op jit(solution)/shard_map/all_to_all | solution.py:235
  62.7 9.8 %collective-permute-start.5 = (f32[4,3,38]{2,1,0:T(4,128)S(1)}, f32[4,3,38]{2,1,0:T(4,128)S(1)}, u32[]{:S(2)}, u32[]{:S(2)}) collective-permute-start(f32[4,3,38]{2,1,0:T(4,128)S(1)} %get-tuple-element.22), channel_id=1, source_target_pairs={{16,0},{32,16},{48,32},{64,48},{80,64},{96,80},{112,96},{17,1},{33... | collective-permute-start | bytes 5480 | tf_op jit(solution)/shard_map/ppermute | solution.py:195
  65.8 6.8 %collective-permute-start.4 = (f32[4,3,38]{2,1,0:T(4,128)S(1)}, f32[4,3,38]{2,1,0:T(4,128)S(1)}, u32[]{:S(2)}, u32[]{:S(2)}) collective-permute-start(f32[4,3,38]{2,1,0:T(4,128)S(1)} %get-tuple-element.21), channel_id=1, source_target_pairs={{0,16},{16,32},{32,48},{48,64},{64,80},{80,96},{96,112},{1,17},{17... | collective-permute-start | bytes 5480 | tf_op jit(solution)/shard_map/ppermute | solution.py:194
